TPU v7x, 32 devices: a whole 2x2x4 slice. The times are simulated.
32 devices in a mesh: uv: 8 (over y, x, core), chan: 4 (over z).
Axes of the slice: x: 2, y: 2, z: 4, core: 2. Of those that a mesh axis runs over, the one named last changes fastest.
Arguments:
- vis: bfloat16 [98304, 2, 1024], P('uv', None, 'chan'), may hold values from -6 to 6
- row_cell: int32 [98304], P('uv'), may hold values from 0 to 127
- tap_weight: bfloat16 [8, 98304], P(None, 'uv'), may hold values from 0.029907227 to 0.29882812
- tap_offset: int32 [8], replicated, may hold values from -32 to 32
- block_tile: int32 [768], P('uv'), may hold values from 0 to 79, as said below
- tile_owner: int32 [80], replicated, may hold values from 0 to 7, as said below
- galaxy: bfloat16 [152, 128, 2048], P('uv', 'chan'), may hold values from -6 to 6
Outputs:
- delay_cube: bfloat16 [152, 128, 2048], P('uv', 'chan')
- cross_power: float32 [152, 1024], P('uv')
Inputs may be any that keep to these rules, and one draw needn't show every extreme that they name: `tile_owner`: each of the 8 owners holds 1 to 19 tiles, and some owner exactly 19. `block_tile`: of the 96 row blocks of one index of uv, at most 22 lie in tiles of one owner, and exactly 22 lie in the tiles of some owner.
All inputs are finite; a program needn't handle non-finite values.
Results may differ from a plain program's by a relative error of at most 0.0059.
Values may be sent and summed in bfloat16 or wider, within the bound.
No kernel may reach another device: no remote copies, remote signals or barrier semaphores. Data moves between devices by JAX's collectives and lax.ppermute only.
A program may use at most 128 MiB of HBM per device.

v0:
```python
import math

import jax
import jax.numpy as jnp
from jax import lax
from jax.sharding import PartitionSpec as P

CH = 1024
BR = 128
TC = 128
KT = 8
TILES_DEV = 10


def tile_ranks(tile_owner, owners):
    onehot = (tile_owner[:, None] == jnp.arange(owners, dtype=jnp.int32)[None, :]).astype(jnp.int32)
    before = jnp.cumsum(onehot, axis=0) - onehot
    return jnp.sum(before * onehot, axis=1)


def kernel_matrix(cells, weights, tap_offset):
    positions = jnp.arange(TC, dtype=jnp.int32)
    total = jnp.zeros(cells.shape[:-1] + (TC, cells.shape[-1]), jnp.float32)
    for k in range(KT):
        target = cells + tap_offset[k]
        hit = target[..., None, :] == positions[:, None]
        total = total + jnp.where(
            hit, weights[..., k, :].astype(jnp.float32)[..., None, :], jnp.float32(0.0)
        )
    return total.astype(jnp.bfloat16)


def delay_table():
    freq = jnp.arange(CH, dtype=jnp.int32)
    phase = (freq[:, None] * freq[None, :] % CH).astype(jnp.float32) * jnp.float32(
        2.0 * math.pi / CH
    )
    cosine = jnp.cos(phase)
    sine = jnp.sin(phase)
    x = freq.astype(jnp.float32) * jnp.float32(2.0 * math.pi / CH)
    taper = 0.35875 - 0.48829 * jnp.cos(x) + 0.14128 * jnp.cos(2.0 * x) - 0.01168 * jnp.cos(3.0 * x)
    scale = (taper / jnp.float32(math.sqrt(CH)))[:, None]
    upper = jnp.concatenate([cosine * scale, -sine * scale], axis=1)
    lower = jnp.concatenate([sine * scale, cosine * scale], axis=1)
    return jnp.concatenate([upper, lower], axis=0).astype(jnp.bfloat16)


def body(vis, row_cell, tap_weight, tap_offset, block_tile, tile_owner, galaxy):
    n_owners = lax.axis_size("uv")
    nblocks = block_tile.shape[0]
    mean_load = nblocks // n_owners
    capacity = mean_load + (TILES_DEV - 1) * mean_load // TILES_DEV
    slots_dev = 2 * TILES_DEV - 1
    chan_dev = vis.shape[2]
    buffer_size = n_owners * capacity
    rank_of_tile = tile_ranks(tile_owner, n_owners)
    target_owner = tile_owner[block_tile]
    owner_hot = (target_owner[:, None] == jnp.arange(n_owners, dtype=jnp.int32)[None, :]).astype(
        jnp.int32
    )
    earlier = jnp.cumsum(owner_hot, axis=0) - owner_hot
    place = target_owner * capacity + jnp.sum(earlier * owner_hot, axis=1)
    blocks = vis.reshape(nblocks, BR, 2 * chan_dev)
    cells = row_cell.reshape(nblocks, BR)
    weights = jnp.transpose(tap_weight.reshape(KT, nblocks, BR), (1, 0, 2))
    sent_vis = jnp.zeros((buffer_size, BR, 2 * chan_dev), jnp.bfloat16).at[place].set(blocks)
    sent_tile = jnp.full((buffer_size,), -1, jnp.int32).at[place].set(block_tile)
    sent_cells = jnp.zeros((buffer_size, BR), jnp.int32).at[place].set(cells)
    sent_weights = jnp.zeros((buffer_size, KT, BR), jnp.bfloat16).at[place].set(weights)
    got_vis, got_tile, got_cells, got_weights = (
        lax.all_to_all(sent_vis, "uv", split_axis=0, concat_axis=0, tiled=True),
        lax.all_to_all(sent_tile, "uv", split_axis=0, concat_axis=0, tiled=True),
        lax.all_to_all(sent_cells, "uv", split_axis=0, concat_axis=0, tiled=True),
        lax.all_to_all(sent_weights, "uv", split_axis=0, concat_axis=0, tiled=True),
    )
    got_matrix = kernel_matrix(got_cells, got_weights, tap_offset)
    contrib = jnp.einsum("bcr,brf->bcf", got_matrix, got_vis, preferred_element_type=jnp.float32)
    slot = jnp.where(got_tile >= 0, rank_of_tile[jnp.maximum(got_tile, 0)], -1)
    pick = (slot[:, None] == jnp.arange(slots_dev, dtype=jnp.int32)[None, :]).astype(jnp.float32)
    grid = jnp.einsum("bs,bcf->scf", pick, contrib, precision=lax.Precision.HIGHEST)
    gridded = grid.astype(jnp.bfloat16).reshape(slots_dev, TC, 2, chan_dev)
    table = delay_table()
    piece = lax.all_to_all(gridded, "chan", split_axis=1, concat_axis=3, tiled=True)
    count = piece.shape[0]
    cells_part = piece.shape[1]
    flat = piece.reshape(count * cells_part, 2 * CH)
    out = jnp.dot(flat, table, preferred_element_type=jnp.float32)
    delay = out.reshape(count, cells_part, 2 * CH)
    galaxy_f = galaxy.astype(jnp.float32)
    product = delay[..., :CH] * galaxy_f[..., :CH] + delay[..., CH:] * galaxy_f[..., CH:]
    local_power = jnp.sum(product, axis=1)
    power = lax.psum(local_power, "chan") / jnp.float32(math.sqrt(TC))
    return (delay.astype(jnp.bfloat16), power)


def solution(mesh):
    return jax.shard_map(
        body,
        mesh=mesh,
        in_specs=(
            P("uv", None, "chan"),
            P("uv"),
            P(None, "uv"),
            P(),
            P("uv"),
            P(),
            P("uv", "chan", None),
        ),
        out_specs=(P("uv", "chan", None), P("uv", None)),
        check_vma=False,
    )
```

profile of v0, /device:TPU:0, one launch (start us, length us, event | category | flops | bytes accessed | tf_op | source)
XLA Modules:
  0.0 569.5 jit_solution(16998166635543470072)
XLA Ops:
  11.6 5.2 all-to-all-start
  18.2 3.1 all-to-all-done
  21.4 3.4 all-to-all-start.1
  25.5 10.6 %scatter_fusion = bf16[176,8,128]{2,1,0:T(8,128)(2,1)} fusion(bf16[176,8,128]{2,1,0:T(8,128)(2,1)} %broadcast_in_dim.144, s32[96]{0:T(128)S(1)} %fusion.47, bf16[96,8,128]{2,1,0:T(8,128)(2,1)} %bitcast.45), kind=kCustom, calls=%fused_computation.4 | custom fusion | bytes 590208 | tf_op jit(solution)/shard_map/scatter | solution.py:69
  36.1 4.1 all-to-all-start.2
  40.3 20.5 %reshape.204 = bf16[96,128,512]{2,1,0:T(8,128)(2,1)} reshape(bf16[12288,2,256]{2,1,0:T(2,128)(2,1)} %param.7) | data formatting | bytes 25165824 | tf_op jit(solution)/shard_map/reshape | solution.py:63
  60.7 7.9 %broadcast_in_dim.170 = bf16[176,128,512]{2,1,0:T(8,128)(2,1)} broadcast(bf16[]{:T(256)} %constant.24.clone.1), dimensions={} | broadcast | bytes 23068674 | tf_op jit(solution)/shard_map/broadcast_in_dim | solution.py:66
  68.6 33.0 %scatter_fusion.1 = bf16[176,128,512]{2,1,0:T(8,128)(2,1)} fusion(bf16[176,128,512]{2,1,0:T(8,128)(2,1)} %broadcast_in_dim.170, s32[96]{0:T(128)S(1)} %fusion.47, bf16[96,128,512]{2,1,0:T(8,128)(2,1)} %reshape.204), kind=kCustom, calls=%fused_computation.5 | custom fusion | bytes 37749120 | tf_op jit(solution)/shard_map/scatter | solution.py:66
  101.6 6.4 %all-to-all-start.3 = ((bf16[176,128,512]{2,1,0:T(8,128)(2,1)}), bf16[176,128,512]{2,1,0:T(8,128)(2,1)}, u32[]{:S(2)}, u32[]{:S(2)}) async-start(bf16[176,128,512]{2,1,0:T(8,128)(2,1)} %scatter_fusion.1), calls=%async_computation.3 | async-start | bytes 46137344 | tf_op jit(solution)/shard_map/all_to_all | solution.py:71
  110.9 5.1 broadcast_add_fusion.7
  116.6 242.7 %all-to-all-done.3 = bf16[176,128,512]{2,1,0:T(8,128)(2,1)} async-done(((bf16[176,128,512]{2,1,0:T(8,128)(2,1)}), bf16[176,128,512]{2,1,0:T(8,128)(2,1)}, u32[]{:S(2)}, u32[]{:S(2)}) %all-to-all-start.3) | async-done | bytes 23068704 | tf_op jit(solution)/shard_map/all_to_all | solution.py:71
  359.4 29.0 %fusion.9 = f32[176,128,512]{2,1,0:T(8,128)} fusion(bf16[176,128,512]{2,1,0:T(8,128)(2,1)} %all-to-all-done.3, f32[176,128]{1,0:T(8,128)S(1)} %bitcast.47, s32[176,128]{1,0:T(8,128)S(1)} %add.223, f32[176,128]{1,0:T(8,128)S(1)} %bitcast.48, s32[176,128]{1,0:T(8,128)S(1)} %add.219, f32[176,128]{1,0:T(8,128)S(1)} %bitcast.49, s32[176,128]{1,0:T(8,128)S(1)} %add.215, ...), kind=kOutput, calls=%fused_computation.28 | convolution fusion | flops 3021996032 | bytes 70647808 | tf_op jit(solution)/shard_map/bcr,brf->bcf/dot_general | solution.py:77
  388.4 49.7 %fusion.35 = bf16[19,128,512]{2,0,1:T(8,128)(2,1)S(1)} fusion(f32[176,128,512]{2,1,0:T(8,128)} %fusion.9, s32[176]{0:T(256)S(1)} %broadcast_select_fusion), kind=kOutput, calls=%fused_computation.59 | convolution fusion | flops 2631077120 | bytes 48628416 | tf_op jit(solution)/shard_map/bs,bcf->scf/dot_general | solution.py:80
  438.1 3.4 copy.18
  441.5 7.4 %copy.19 = bf16[19,128,2,256]{3,2,0,1:T(2,128)(2,1)} copy(bf16[19,128,2,256]{1,3,2,0:T(8,128)(2,1)} %bitcast.43) | data formatting | bytes 4980736 | tf_op jit(solution)/shard_map/reshape | solution.py:81
  448.9 4.9 all-to-all-start.4
  453.8 4.6 convert_element_type.65
  458.4 19.1 %multiply_convert_fusion.1 = (bf16[1024,1024]{1,0:T(8,128)(2,1)}, bf16[1024,1024]{1,0:T(8,128)(2,1)}, bf16[1024,1024]{1,0:T(8,128)(2,1)}) fusion(f32[1024]{0:T(1024)S(1)} %subtract_multiply_fusion), kind=kLoop, calls=%fused_computation.50 | loop fusion | flops 22020096 | bytes 6295552 | tf_op jit(solution)/shard_map/convert.13
  477.5 30.0 %all-to-all-done.4 = bf16[19,128,2,256]{3,2,0,1:T(2,128)(2,1)S(1)} async-done(((bf16[19,128,2,256]{3,2,0,1:T(2,128)(2,1)}), bf16[19,128,2,256]{3,2,0,1:T(2,128)(2,1)S(1)}, u32[]{:S(2)}, u32[]{:S(2)}) %all-to-all-start.4) | async-done | bytes 2490400 | tf_op jit(solution)/shard_map/all_to_all | solution.py:83
  507.9 2.2 copy.21
  510.1 3.0 dot_general.13
  513.1 11.1 %fusion.53 = (bf16[19,32,2048]{2,1,0:T(8,128)(2,1)}, f32[19,32,2048]{2,1,0:T(8,128)S(1)}) fusion(bf16[19,32,2048]{2,1,0:T(8,128)(2,1)} %dot_general.13, bf16[1024,1024]{1,0:T(8,128)(2,1)} %get-tuple-element.20, bf16[1024,1024]{1,0:T(8,128)(2,1)} %get-tuple-element.19, bf16[1024,1024]{1,0:T(8,128)(2,1)} %get-tuple-element.18), kind=kOutput, calls=%fused_computation.104 | convolution fusion | flops 5135073280 | bytes 16252928 | tf_op jit(solution)/shard_map/dot_general | solution.py:87
  524.2 2.0 fusion.34
  526.2 34.9 %all-reduce.2.cloned.1.call-done = f32[19,1024]{1,0:T(8,128)} async-done(((f32[19,1024]{1,0:T(8,128)}), f32[19,1024]{1,0:T(8,128)}) %all-reduce.2.cloned.1.call-update) | async-done | bytes 77840 | tf_op jit(solution)/shard_map/psum | solution.py:92
  (52 shorter events, 12.1 us)
Async XLA Ops:
  7.2 9.6 %copy-start = (s32[12288]{0:T(1024)S(1)}, s32[12288]{0:T(1024)}, u32[]{:S(2)}) copy-start(s32[12288]{0:T(1024)} %param.8) | copy-start | bytes 147460
  11.6 9.8 %all-to-all-start = ((s32[8,22,1]{1,2,0:T(1,128)}), s32[8,22,1]{1,2,0:T(1,128)S(1)}, u32[]{:S(2)}, u32[]{:S(2)}) async-start(s32[8,22,1]{1,2,0:T(1,128)} %bitcast.2), calls=%async_computation | async-start | bytes 8192 | tf_op jit(solution)/shard_map/all_to_all | solution.py:72
  21.4 14.8 %all-to-all-start.1 = ((s32[8,22,128]{2,1,0:T(8,128)}), s32[8,22,128]{2,1,0:T(8,128)S(1)}, u32[]{:S(2)}, u32[]{:S(2)}) async-start(s32[8,22,128]{2,1,0:T(8,128)} %all_to_all.31), calls=%async_computation.1 | async-start | bytes 196608 | tf_op jit(solution)/shard_map/all_to_all | solution.py:73
  36.1 65.5 %all-to-all-start.2 = ((bf16[176,8,128]{2,1,0:T(8,128)(2,1)}), bf16[176,8,128]{2,1,0:T(8,128)(2,1)S(1)}, u32[]{:S(2)}, u32[]{:S(2)}) async-start(bf16[176,8,128]{2,1,0:T(8,128)(2,1)} %scatter_fusion), calls=%async_computation.2 | async-start | bytes 720896 | tf_op jit(solution)/shard_map/all_to_all | solution.py:74
  101.6 6.5 %copy-start.2 = (s32[80]{0:T(128)S(1)}, s32[80]{0:T(128)}, u32[]{:S(2)}) copy-start(s32[80]{0:T(128)} %param.12) | copy-start | bytes 964
  101.6 6.7 %copy-start.3 = (s32[8]{0:T(128)S(1)}, s32[8]{0:T(128)}, u32[]{:S(2)}) copy-start(s32[8]{0:T(128)} %param.10) | copy-start | bytes 100
  101.6 257.8 %all-to-all-start.3 = ((bf16[176,128,512]{2,1,0:T(8,128)(2,1)}), bf16[176,128,512]{2,1,0:T(8,128)(2,1)}, u32[]{:S(2)}, u32[]{:S(2)}) async-start(bf16[176,128,512]{2,1,0:T(8,128)(2,1)} %scatter_fusion.1), calls=%async_computation.3 | async-start | bytes 46137344 | tf_op jit(solution)/shard_map/all_to_all | solution.py:71
  448.9 58.6 %all-to-all-start.4 = ((bf16[19,128,2,256]{3,2,0,1:T(2,128)(2,1)}), bf16[19,128,2,256]{3,2,0,1:T(2,128)(2,1)S(1)}, u32[]{:S(2)}, u32[]{:S(2)}) async-start(bf16[19,128,2,256]{3,2,0,1:T(2,128)(2,1)} %copy.19), calls=%async_computation.4 | async-start | bytes 4980736 | tf_op jit(solution)/shard_map/all_to_all | solution.py:83
  453.8 107.4 %all-reduce.2.cloned.1.call-start = ((), (), s32[]{:S(2)}) async-start(), calls=%async_computation.5 | async-start | bytes 196608 | tf_op jit(solution)/shard_map/psum | solution.py:92
  510.1 14.1 %slice-start = ((s8[4980736]{0:T(1024)(128)(4,1)}), s8[786432]{0:T(1024)(128)(4,1)S(1)}, s32[]{:S(2)}) async-start(s8[4980736]{0:T(1024)(128)(4,1)} %bitcast.41), calls=%async_computation.6 | async-start | bytes 1572864
  513.1 11.1 %slice-start.1 = ((s8[4980736]{0:T(1024)(128)(4,1)}), s8[4194304]{0:T(1024)(128)(4,1)S(1)}, s32[]{:S(2)}) async-start(s8[4980736]{0:T(1024)(128)(4,1)} %bitcast.41), calls=%async_computation.7 | async-start | bytes 8388608
  513.1 49.6 %copy-start.1 = (s32[12288]{0:T(1024)S(1)}, s32[12288]{0:T(1024)}, u32[]{:S(2)}) copy-start(s32[12288]{0:T(1024)} %param.8) | copy-start | bytes 147460
Sparse Core Ops, SparseCore 0:
  526.3 34.7 all-reduce.1
where the time goes:
time: 572 us; the launch traced here: 570 us
  waiting for transfers between devices  311 us (54%)
  local copies, waits for them, and re-layouts  96.4 us (17%)
  matrix products  89.8 us (16%)
  other arithmetic  34.3 us (6%)
  starting transfers between devices  24 us (4%)
  between operations  14.3 us (2%)
    all_to_all x1, waiting for transfers between devices, body(): lax.all_to_all(sent_vis, 'uv', split_axis=0, concat_axis=0, tiled=True)  243 us
    dot_general x1, matrix products, body(): jnp.einsum('bs,bcf->scf', pick, contrib, precision=lax.Precision.HIGHEST)  49.7 us
    psum x1, waiting for transfers between devices, body(): power = lax.psum(local_power, 'chan') / jnp.float32(math.sqrt(TC))  34.9 us
    scatter x1, local copies, waits for them, and re-layouts, body(): jnp.zeros((buffer_size, BR, 2 * chan_dev), jnp.bfloat16).at[place]  33 us
    all_to_all x1, waiting for transfers between devices, body(): lax.all_to_all(gridded, 'chan', split_axis=1, concat_axis=3, tiled=True)  30 us
    dot_general x1, matrix products, body(): jnp.einsum('bcr,brf->bcf', got_matrix, got_vis, preferred_element_type=jn...  29 us
    reshape x1, local copies, waits for them, and re-layouts, body(): blocks = vis.reshape(nblocks, BR, 2 * chan_dev)  20.5 us
    another operation x1, other arithmetic  19.1 us
  transfers between devices with their start and end apart: 6, of which 4 were waited for; matrix products, arithmetic and copies ran while one was open for 19% of the time, Pallas kernels for 0%

commit v1 on v0

--- a/solution.py
+++ b/solution.py
@@ -9,7 +9,6 @@
 BR = 128
 TC = 128
 KT = 8
-TILES_DEV = 10
 
 
 def tile_ranks(tile_owner, owners):
@@ -45,39 +44,75 @@
     return jnp.concatenate([upper, lower], axis=0).astype(jnp.bfloat16)
 
 
+def _partner_pairs(n, fn):
+    return [(i, fn(i)) for i in range(n)]
+
+
+def _allreduce_sum(x, axis, n):
+    if n & (n - 1):
+        return lax.psum(x, axis)
+    d = 1
+    while d < n:
+        x = x + lax.ppermute(x, axis, _partner_pairs(n, lambda i, d=d: i ^ d))
+        d *= 2
+    return x
+
+
 def body(vis, row_cell, tap_weight, tap_offset, block_tile, tile_owner, galaxy):
     n_owners = lax.axis_size("uv")
+    n_chan = lax.axis_size("chan")
+    pairs = n_owners // 2
+    me = lax.axis_index("uv")
+    parity = me % 2
+    chip = me // 2
     nblocks = block_tile.shape[0]
-    mean_load = nblocks // n_owners
-    capacity = mean_load + (TILES_DEV - 1) * mean_load // TILES_DEV
-    slots_dev = 2 * TILES_DEV - 1
+    slots_dev = galaxy.shape[0]
     chan_dev = vis.shape[2]
-    buffer_size = n_owners * capacity
+    width = 2 * chan_dev
+
     rank_of_tile = tile_ranks(tile_owner, n_owners)
-    target_owner = tile_owner[block_tile]
-    owner_hot = (target_owner[:, None] == jnp.arange(n_owners, dtype=jnp.int32)[None, :]).astype(
-        jnp.int32
-    )
-    earlier = jnp.cumsum(owner_hot, axis=0) - owner_hot
-    place = target_owner * capacity + jnp.sum(earlier * owner_hot, axis=1)
-    blocks = vis.reshape(nblocks, BR, 2 * chan_dev)
+    owner = tile_owner[block_tile]
+    rank = rank_of_tile[block_tile]
+    slot = (owner % 2) * (pairs * slots_dev) + (owner // 2) * slots_dev + rank
+    n_slots = n_owners * slots_dev
+    pick = (jnp.arange(n_slots, dtype=jnp.int32)[:, None] == slot[None, :]).astype(jnp.bfloat16)
+
+    blocks = vis.reshape(nblocks, BR, width)
     cells = row_cell.reshape(nblocks, BR)
     weights = jnp.transpose(tap_weight.reshape(KT, nblocks, BR), (1, 0, 2))
-    sent_vis = jnp.zeros((buffer_size, BR, 2 * chan_dev), jnp.bfloat16).at[place].set(blocks)
-    sent_tile = jnp.full((buffer_size,), -1, jnp.int32).at[place].set(block_tile)
-    sent_cells = jnp.zeros((buffer_size, BR), jnp.int32).at[place].set(cells)
-    sent_weights = jnp.zeros((buffer_size, KT, BR), jnp.bfloat16).at[place].set(weights)
-    got_vis, got_tile, got_cells, got_weights = (
-        lax.all_to_all(sent_vis, "uv", split_axis=0, concat_axis=0, tiled=True),
-        lax.all_to_all(sent_tile, "uv", split_axis=0, concat_axis=0, tiled=True),
-        lax.all_to_all(sent_cells, "uv", split_axis=0, concat_axis=0, tiled=True),
-        lax.all_to_all(sent_weights, "uv", split_axis=0, concat_axis=0, tiled=True),
-    )
-    got_matrix = kernel_matrix(got_cells, got_weights, tap_offset)
-    contrib = jnp.einsum("bcr,brf->bcf", got_matrix, got_vis, preferred_element_type=jnp.float32)
-    slot = jnp.where(got_tile >= 0, rank_of_tile[jnp.maximum(got_tile, 0)], -1)
-    pick = (slot[:, None] == jnp.arange(slots_dev, dtype=jnp.int32)[None, :]).astype(jnp.float32)
-    grid = jnp.einsum("bs,bcf->scf", pick, contrib, precision=lax.Precision.HIGHEST)
+    matrix = kernel_matrix(cells, weights, tap_offset)
+    contrib = jnp.einsum("bcr,brf->bcf", matrix, blocks, preferred_element_type=jnp.float32)
+    contrib = contrib.reshape(nblocks, TC * width)
+    high = contrib.astype(jnp.bfloat16)
+    low = (contrib - high.astype(jnp.float32)).astype(jnp.bfloat16)
+    partial = jnp.dot(
+        jnp.concatenate([pick, pick], axis=1),
+        jnp.concatenate([high, low], axis=0),
+        preferred_element_type=jnp.float32,
+    ).astype(jnp.bfloat16)
+    partial = partial.reshape(2, pairs, slots_dev, TC, width)
+
+    mine = lax.dynamic_index_in_dim(partial, parity, axis=0, keepdims=False)
+    other = lax.dynamic_index_in_dim(partial, 1 - parity, axis=0, keepdims=False)
+    got = lax.ppermute(other, "uv", _partner_pairs(n_owners, lambda i: i ^ 1))
+    pair_sum = mine.astype(jnp.float32) + got.astype(jnp.float32)
+    pair_send = pair_sum.astype(jnp.bfloat16)
+
+    grid = lax.dynamic_index_in_dim(pair_sum, chip, axis=0, keepdims=False)
+    for d in range(1, pairs):
+        if pairs & (pairs - 1):
+            dest = lambda c, d=d: (c + d) % pairs
+            src_chip = (chip - d) % pairs
+        else:
+            dest = lambda c, d=d: c ^ d
+            src_chip = chip ^ d
+        del src_chip
+        send = lax.dynamic_index_in_dim(pair_send, dest(chip), axis=0, keepdims=False)
+        recv = lax.ppermute(
+            send, "uv", _partner_pairs(n_owners, lambda i, dest=dest: dest(i // 2) * 2 + i % 2)
+        )
+        grid = grid + recv.astype(jnp.float32)
+
     gridded = grid.astype(jnp.bfloat16).reshape(slots_dev, TC, 2, chan_dev)
     table = delay_table()
     piece = lax.all_to_all(gridded, "chan", split_axis=1, concat_axis=3, tiled=True)
@@ -89,7 +124,7 @@
     galaxy_f = galaxy.astype(jnp.float32)
     product = delay[..., :CH] * galaxy_f[..., :CH] + delay[..., CH:] * galaxy_f[..., CH:]
     local_power = jnp.sum(product, axis=1)
-    power = lax.psum(local_power, "chan") / jnp.float32(math.sqrt(TC))
+    power = _allreduce_sum(local_power, "chan", n_chan) / jnp.float32(math.sqrt(TC))
     return (delay.astype(jnp.bfloat16), power)
 
 

time: 572 us -> 384 us (0.67)
  waiting for transfers between devices: 311 us -> 152 us
  matrix products: 89.8 us -> 44.8 us
  other arithmetic: 34.3 us -> 64.1 us
  local copies, waits for them, and re-layouts: 96.4 us -> 111 us
  starting transfers between devices: 24 us -> 9.88 us
  between operations: 14.3 us -> 0.81 us
    all_to_all x4 -> x0, waiting for transfers between devices: 246 us -> none  [the longest x1 243 us: body(): lax.all_to_all(sent_vis, 'uv', split_axis=0, concat_axis=0, tiled=True)]
    ppermute x0 -> x6, waiting for transfers between devices: none -> 120 us  [the longest x3 94 us: body(): lax.ppermute(send, 'uv', _partner_pairs(n_owners, lambda i, dest=dest: de...]
    scatter x4 -> x0, local copies, waits for them, and re-layouts: 45.4 us -> none  [the longest x1 33 us: body(): jnp.zeros((buffer_size, BR, 2 * chan_dev), jnp.bfloat16).at[place]]
    dot_general x2, matrix products: 78.7 us -> 33.7 us  [the longest x1 18.2 us: body(): jnp.dot(jnp.concatenate([pick, pick], axis=1), jnp.concatenate([high, low...]
    unnamed x12, local copies, waits for them, and re-layouts: 0.03 us -> 41.8 us
    psum x1 -> x0, waiting for transfers between devices: 34.9 us -> none  [body(): power = lax.psum(local_power, 'chan') / jnp.float32(math.sqrt(TC))]
    convert_element_type x1 -> x3, other arithmetic: 0.09 us -> 30.7 us  [the longest x1 16 us: body(): pair_send = pair_sum.astype(jnp.bfloat16)]
    dynamic_slice x0 -> x6, local copies, waits for them, and re-layouts: none -> 25.5 us  [the longest x4 14.3 us: body(): lax.dynamic_index_in_dim(pair_send, dest(chip), axis=0, keepdims=False)]
  transfers between devices with their start and end apart: 6 -> 7, of which waited for: 4 -> 6; matrix products, arithmetic and copies ran while one was open for 19% -> 11% of each run, Pallas kernels for 0% -> 0%
where the time goes in v1:
time: 384 us; the launch traced here: 383 us
  waiting for transfers between devices  152 us (40%)
  local copies, waits for them, and re-layouts  111 us (29%)
  other arithmetic  64.1 us (17%)
  matrix products  44.8 us (12%)
  starting transfers between devices  9.88 us (3%)
    ppermute x3, waiting for transfers between devices, body(): lax.ppermute(send, 'uv', _partner_pairs(n_owners, lambda i, dest=dest: de...  94 us
    unnamed x12, local copies, waits for them, and re-layouts  41.8 us
    all_to_all x1, waiting for transfers between devices, body(): lax.all_to_all(gridded, 'chan', split_axis=1, concat_axis=3, tiled=True)  32 us
    reshape x1, local copies, waits for them, and re-layouts, body(): blocks = vis.reshape(nblocks, BR, width)  20.5 us
    another operation x1, other arithmetic  19.1 us
    dot_general x1, matrix products, body(): jnp.dot(jnp.concatenate([pick, pick], axis=1), jnp.concatenate([high, low...  18.2 us
    convert_element_type x1, other arithmetic, body(): pair_send = pair_sum.astype(jnp.bfloat16)  16 us
    dot_general x1, matrix products, body(): jnp.einsum('bcr,brf->bcf', matrix, blocks, preferred_element_type=jnp.flo...  15.6 us
  transfers between devices with their start and end apart: 7, of which 6 were waited for; matrix products, arithmetic and copies ran while one was open for 11% of the time, Pallas kernels for 0%

profile of v1, /device:TPU:0, one launch (start us, length us, event | category | flops | bytes accessed | tf_op | source)
XLA Modules:
  0.0 383.0 jit_solution(7505906053888566513)
XLA Ops:
  4.4 20.5 %reshape.136 = bf16[96,128,512]{2,1,0:T(8,128)(2,1)} reshape(bf16[12288,2,256]{2,1,0:T(2,128)(2,1)} %param.7) | data formatting | bytes 25165824 | tf_op jit(solution)/shard_map/reshape | solution.py:80
  24.9 5.1 %add_bitcast_fusion.7 = (s32[96,128]{1,0:T(8,128)S(1)}, s32[96,128]{1,0:T(8,128)S(1)}, s32[96,128]{1,0:T(8,128)S(1)}, s32[96,128]{1,0:T(8,128)S(1)}, s32[96,128]...) fusion(s32[12288]{0:T(1024)S(1)} %copy-done.1, s32[]{:T(128)} %bitcast, ...), kind=kLoop, calls=%fused_computation.85 | loop fusion | flops 98304 | bytes 442400 | tf_op jit(solution)/shard_map/add | solution.py:24
  30.1 15.6 %fusion.19 = f32[96,128,512]{2,1,0:T(8,128)} fusion(bf16[96,128,512]{2,1,0:T(8,128)(2,1)} %reshape.136, f32[96,128]{1,0:T(8,128)S(1)} %bitcast.82, s32[96,128]{1,0:T(8,128)S(1)} %get-tuple-element.23, f32[96,128]{1,0:T(8,128)S(1)} %bitcast.83, s32[96,128]{1,0:T(8,128)S(1)} %get-tuple-element.24, f32[96,128]{1,0:T(8,128)S(1)} %bitcast.84, ...), kind=kOutput, calls=%fused_computation.42 | convolution fusion | flops 1648361472 | bytes 38535168 | tf_op jit(solution)/shard_map/bcr,brf->bcf/dot_general | solution.py:84
  45.6 21.7 %copy.23 = f32[12,8,128,512]{3,1,2,0:T(8,128)S(1)} copy(f32[12,8,128,512]{3,2,1,0:T(8,128)} %bitcast.71) | data formatting | bytes 50331648
  67.4 8.8 %subtract_convert_fusion = (bf16[96,65536]{1,0:T(8,128)(2,1)}, bf16[96,65536]{1,0:T(8,128)(2,1)}) fusion(f32[96,65536]{1,0:T(8,128)S(1)} %bitcast.68), kind=kLoop, calls=%fused_computation.6 | loop fusion | flops 25165824 | bytes 50331648 | tf_op jit(solution)/shard_map/convert_element_type | solution.py:87
  79.1 18.2 %convolution_convert_fusion = bf16[152,65536]{1,0:T(8,128)(2,1)} fusion(bf16[96,65536]{1,0:T(8,128)(2,1)} %get-tuple-element.4, bf16[96,65536]{1,0:T(8,128)(2,1)} %get-tuple-element.5, pred[152,96]{1,0:T(8,128)(4,1)S(1)} %iota_compare_fusion.8), kind=kOutput, calls=%fused_computation.2 | convolution fusion | flops 3885527552 | bytes 45103360 | tf_op jit(solution)/shard_map/dot_general | solution.py:88
  97.3 20.1 %copy.24 = bf16[19,8,128,512]{3,2,1,0:T(8,128)(2,1)} copy(bf16[19,8,128,512]{3,1,2,0:T(8,128)(2,1)} %bitcast.72) | data formatting | bytes 39845888
  117.4 8.8 %dynamic-slice_bitcast_fusion = bf16[4,19,128,512]{3,2,1,0:T(8,128)(2,1)} fusion(bf16[2,4,19,128,512]{4,3,2,1,0:T(8,128)(2,1)} %bitcast.69, s32[]{:T(128)S(6)} %select_n.105), kind=kLoop, calls=%fused_computation.8 | loop fusion | bytes 19922948 | tf_op jit(solution)/shard_map/jit(dynamic_index_in_dim)/squeeze | solution.py:96
  126.7 15.4 %collective-permute-done = bf16[4,19,128,512]{3,2,1,0:T(8,128)(2,1)} collective-permute-done((bf16[4,19,128,512]{3,2,1,0:T(8,128)(2,1)}, bf16[4,19,128,512]{3,2,1,0:T(8,128)(2,1)}, u32[]{:S(2)}, u32[]{:S(2)}) %collective-permute-start) | collective-permute-done | bytes 9961504 | tf_op jit(solution)/shard_map/ppermute | solution.py:97
  142.1 16.0 %fusion.51 = (bf16[4,19,128,512]{3,2,1,0:T(8,128)(2,1)S(1)}, f32[4,19,128,512]{3,2,1,0:T(8,128)}) fusion(bf16[4,19,128,512]{3,2,1,0:T(8,128)(2,1)} %collective-permute-done, bf16[2,4,19,128,512]{4,3,2,1,0:T(8,128)(2,1)} %bitcast.70, s32[]{:T(128)S(6)} %select_n.104), kind=kLoop, calls=%fused_computation.108 | loop fusion | flops 19922944 | bytes 49807364 | tf_op jit(solution)/shard_map/convert_element_type | solution.py:99
  160.8 4.4 %copy.17 = bf16[1,19,128,512]{2,3,1,0:T(8,128)(2,1)} copy(bf16[1,19,128,512]{3,2,1,0:T(8,128)(2,1)} %get-tuple-element.6) | data formatting | bytes 4980736 | tf_op jit(solution)/shard_map/jit(dynamic_index_in_dim)/dynamic_slice | solution.py:110
  176.7 5.4 %constant_dynamic-slice_fusion.3 = f32[1,19,128,512]{3,2,1,0:T(8,128)} fusion(f32[4,19,128,512]{3,2,1,0:T(8,128)} %get-tuple-element.3, s32[]{:T(128)S(6)} %select_n.107), kind=kLoop, calls=%fused_computation.97 | loop fusion | bytes 9961476 | tf_op jit(solution)/shard_map/jit(dynamic_index_in_dim)/dynamic_slice | solution.py:101
  182.1 5.8 %copy.16 = f32[1,19,128,512]{2,3,1,0:T(8,128)} copy(f32[1,19,128,512]{3,2,1,0:T(8,128)} %constant_dynamic-slice_fusion.3) | data formatting | bytes 9961472 | tf_op jit(solution)/shard_map/jit(dynamic_index_in_dim)/dynamic_slice | solution.py:101
  187.9 35.4 %collective-permute-done.1 = bf16[19,128,512]{1,2,0:T(8,128)(2,1)} collective-permute-done((bf16[19,128,512]{1,2,0:T(8,128)(2,1)}, bf16[19,128,512]{1,2,0:T(8,128)(2,1)}, u32[]{:S(2)}, u32[]{:S(2)}) %collective-permute-start.1) | collective-permute-done | bytes 2490400 | tf_op jit(solution)/shard_map/ppermute | solution.py:111
  223.3 58.7 %collective-permute-done.2 = bf16[19,128,512]{1,2,0:T(8,128)(2,1)} collective-permute-done((bf16[19,128,512]{1,2,0:T(8,128)(2,1)}, bf16[19,128,512]{1,2,0:T(8,128)(2,1)}, u32[]{:S(2)}, u32[]{:S(2)}) %collective-permute-start.2) | collective-permute-done | bytes 2490400 | tf_op jit(solution)/shard_map/ppermute | solution.py:111
  282.0 5.9 %fusion.12 = bf16[19,128,512]{1,2,0:T(8,128)(2,1)S(1)} fusion(f32[1,19,128,512]{2,3,1,0:T(8,128)} %copy.16, bf16[19,128,512]{1,2,0:T(8,128)(2,1)} %collective-permute-done.3, bf16[19,128,512]{1,2,0:T(8,128)(2,1)} %collective-permute-done.2, bf16[19,128,512]{1,2,0:T(8,128)(2,1)} %collective-permute-done.1), kind=kLoop, calls=%fused_computation.32 | loop fusion | flops 8716288 | bytes 14942208 | tf_op jit(solution)/shard_map/convert_element_type | solution.py:116
  287.9 4.9 %copy.20 = bf16[19,128,2,256]{3,2,0,1:T(2,128)(2,1)} copy(bf16[19,128,2,256]{1,3,2,0:T(8,128)(2,1)S(1)} %bitcast.75) | data formatting | bytes 4980736 | tf_op jit(solution)/shard_map/reshape | solution.py:116
  292.8 4.9 %all-to-all-start = ((bf16[19,128,2,256]{3,2,0,1:T(2,128)(2,1)}), bf16[19,128,2,256]{3,2,0,1:T(2,128)(2,1)S(1)}, u32[]{:S(2)}, u32[]{:S(2)}) async-start(bf16[19,128,2,256]{3,2,0,1:T(2,128)(2,1)} %copy.20), calls=%async_computation | async-start | bytes 4980736 | tf_op jit(solution)/shard_map/all_to_all | solution.py:118
  297.7 4.6 %convert_element_type.105 = f32[19,32,2048]{2,1,0:T(8,128)} convert(bf16[19,32,2048]{2,1,0:T(8,128)(2,1)} %param.13) | non-fusion elementwise | flops 1245184 | bytes 7471104 | tf_op jit(solution)/shard_map/convert_element_type | solution.py:124
  302.4 19.1 %multiply_convert_fusion.1 = (bf16[1024,1024]{1,0:T(8,128)(2,1)}, bf16[1024,1024]{1,0:T(8,128)(2,1)}, bf16[1024,1024]{1,0:T(8,128)(2,1)}) fusion(f32[1024]{0:T(1024)S(1)} %subtract_multiply_fusion), kind=kLoop, calls=%fused_computation.37 | loop fusion | flops 22020096 | bytes 6295552 | tf_op jit(solution)/shard_map/convert.15
  321.4 32.0 %all-to-all-done = bf16[19,128,2,256]{3,2,0,1:T(2,128)(2,1)S(1)} async-done(((bf16[19,128,2,256]{3,2,0,1:T(2,128)(2,1)}), bf16[19,128,2,256]{3,2,0,1:T(2,128)(2,1)S(1)}, u32[]{:S(2)}, u32[]{:S(2)}) %all-to-all-start) | async-done | bytes 2490400 | tf_op jit(solution)/shard_map/all_to_all | solution.py:118
  359.1 11.1 %fusion.53 = (bf16[19,32,2048]{2,1,0:T(8,128)(2,1)}, f32[19,32,2048]{2,1,0:T(8,128)S(1)}) fusion(bf16[19,32,2048]{2,1,0:T(8,128)(2,1)} %dot_general.13, bf16[1024,1024]{1,0:T(8,128)(2,1)} %get-tuple-element.27, bf16[1024,1024]{1,0:T(8,128)(2,1)} %get-tuple-element.26, bf16[1024,1024]{1,0:T(8,128)(2,1)} %get-tuple-element.25), kind=kOutput, calls=%fused_computation.110 | convolution fusion | flops 5135073280 | bytes 16252928 | tf_op jit(solution)/shard_map/dot_general | solution.py:122
  371.7 4.6 %collective-permute-done.4 = f32[19,1024]{1,0:T(8,128)S(1)} collective-permute-done((f32[19,1024]{1,0:T(8,128)S(1)}, f32[19,1024]{1,0:T(8,128)S(1)}, u32[]{:S(2)}, u32[]{:S(2)}) %collective-permute-start.4) | collective-permute-done | bytes 77856 | tf_op jit(solution)/shard_map/ppermute | solution.py:56
  376.4 6.0 %collective-permute-done.5 = f32[19,1024]{1,0:T(8,128)S(1)} collective-permute-done((f32[19,1024]{1,0:T(8,128)S(1)}, f32[19,1024]{1,0:T(8,128)S(1)}, u32[]{:S(2)}, u32[]{:S(2)}) %collective-permute-start.5) | collective-permute-done | bytes 77856 | tf_op jit(solution)/shard_map/ppermute | solution.py:56
  (39 shorter events, 29.2 us)
Async XLA Ops:
  4.4 20.5 %copy-start.1 = (s32[12288]{0:T(1024)S(1)}, s32[12288]{0:T(1024)}, u32[]{:S(2)}) copy-start(s32[12288]{0:T(1024)} %param.8) | copy-start | bytes 147460
  67.3 8.9 %copy-start.2 = (s32[96]{0:T(128)S(1)}, s32[96]{0:T(128)}, u32[]{:S(2)}) copy-start(s32[96]{0:T(128)} %param.11) | copy-start | bytes 1156
  67.4 8.9 %copy-start = (s32[80]{0:T(128)S(1)}, s32[80]{0:T(128)}, u32[]{:S(2)}) copy-start(s32[80]{0:T(128)} %param.12) | copy-start | bytes 964
  126.2 15.9 %collective-permute-start = (bf16[4,19,128,512]{3,2,1,0:T(8,128)(2,1)}, bf16[4,19,128,512]{3,2,1,0:T(8,128)(2,1)}, u32[]{:S(2)}, u32[]{:S(2)}) collective-permute-start(bf16[4,19,128,512]{3,2,1,0:T(8,128)(2,1)} %dynamic-slice_bitcast_fusion), channel_id=1, source_target_pairs={{0,4},{4,0},{8,12},{12,8},{16,20},{20,16},{24,28},{28,24},{1,5},{5... | collective-permute-start | bytes 29884424 | tf_op jit(solution)/shard_map/ppermute | solution.py:97
  165.3 58.1 %collective-permute-start.1 = (bf16[19,128,512]{1,2,0:T(8,128)(2,1)}, bf16[19,128,512]{1,2,0:T(8,128)(2,1)}, u32[]{:S(2)}, u32[]{:S(2)}) collective-permute-start(bf16[19,128,512]{1,2,0:T(8,128)(2,1)} %bitcast.77), channel_id=1, source_target_pairs={{0,8},{4,12},{8,0},{12,4},{16,24},{20,28},{24,16},{28,20},{1,9},{5... | collective-permute-start | bytes 7471112 | tf_op jit(solution)/shard_map/ppermute | solution.py:111
  172.5 109.5 %collective-permute-start.2 = (bf16[19,128,512]{1,2,0:T(8,128)(2,1)}, bf16[19,128,512]{1,2,0:T(8,128)(2,1)}, u32[]{:S(2)}, u32[]{:S(2)}) collective-permute-start(bf16[19,128,512]{1,2,0:T(8,128)(2,1)} %bitcast.78), channel_id=1, source_target_pairs={{0,16},{4,20},{8,24},{12,28},{16,0},{20,4},{24,8},{28,12},{1,17},{... | collective-permute-start | bytes 7471112 | tf_op jit(solution)/shard_map/ppermute | solution.py:111
  176.7 105.3 %collective-permute-start.3 = (bf16[19,128,512]{1,2,0:T(8,128)(2,1)}, bf16[19,128,512]{1,2,0:T(8,128)(2,1)}, u32[]{:S(2)}, u32[]{:S(2)}) collective-permute-start(bf16[19,128,512]{1,2,0:T(8,128)(2,1)} %bitcast.79), channel_id=1, source_target_pairs={{0,24},{4,28},{8,16},{12,20},{16,8},{20,12},{24,0},{28,4},{1,25},{... | collective-permute-start | bytes 7471112 | tf_op jit(solution)/shard_map/ppermute | solution.py:111
  292.8 60.7 %all-to-all-start = ((bf16[19,128,2,256]{3,2,0,1:T(2,128)(2,1)}), bf16[19,128,2,256]{3,2,0,1:T(2,128)(2,1)S(1)}, u32[]{:S(2)}, u32[]{:S(2)}) async-start(bf16[19,128,2,256]{3,2,0,1:T(2,128)(2,1)} %copy.20), calls=%async_computation | async-start | bytes 4980736 | tf_op jit(solution)/shard_map/all_to_all | solution.py:118
  356.1 14.1 %slice-start = ((s8[4980736]{0:T(1024)(128)(4,1)}), s8[786432]{0:T(1024)(128)(4,1)S(1)}, s32[]{:S(2)}) async-start(s8[4980736]{0:T(1024)(128)(4,1)} %bitcast.73), calls=%async_computation.1 | async-start | bytes 1572864
  359.1 11.1 %slice-start.1 = ((s8[4980736]{0:T(1024)(128)(4,1)}), s8[4194304]{0:T(1024)(128)(4,1)S(1)}, s32[]{:S(2)}) async-start(s8[4980736]{0:T(1024)(128)(4,1)} %bitcast.73), calls=%async_computation.2 | async-start | bytes 8388608
  371.6 4.7 %collective-permute-start.4 = (f32[19,1024]{1,0:T(8,128)S(1)}, f32[19,1024]{1,0:T(8,128)S(1)}, u32[]{:S(2)}, u32[]{:S(2)}) collective-permute-start(f32[19,1024]{1,0:T(8,128)S(1)} %fusion.38), channel_id=1, source_target_pairs={{0,1},{1,0},{2,3},{3,2},{4,5},{5,4},{6,7},{7,6},{8,9},{9,8},{10,11... | collective-permute-start | bytes 233480 | tf_op jit(solution)/shard_map/ppermute | solution.py:56
  376.3 6.1 %collective-permute-start.5 = (f32[19,1024]{1,0:T(8,128)S(1)}, f32[19,1024]{1,0:T(8,128)S(1)}, u32[]{:S(2)}, u32[]{:S(2)}) collective-permute-start(f32[19,1024]{1,0:T(8,128)S(1)} %add.280), channel_id=1, source_target_pairs={{0,2},{1,3},{2,0},{3,1},{4,6},{5,7},{6,4},{7,5},{8,10},{9,11},{10,... | collective-permute-start | bytes 233480 | tf_op jit(solution)/shard_map/ppermute | solution.py:56

commit v2 on v1

--- a/solution.py
+++ b/solution.py
@@ -58,39 +58,18 @@
     return x
 
 
-def body(vis, row_cell, tap_weight, tap_offset, block_tile, tile_owner, galaxy):
-    n_owners = lax.axis_size("uv")
-    n_chan = lax.axis_size("chan")
+def _chunk(part, matrix, pick2, parity, chip, n_owners, slots_dev):
     pairs = n_owners // 2
-    me = lax.axis_index("uv")
-    parity = me % 2
-    chip = me // 2
-    nblocks = block_tile.shape[0]
-    slots_dev = galaxy.shape[0]
-    chan_dev = vis.shape[2]
-    width = 2 * chan_dev
-
-    rank_of_tile = tile_ranks(tile_owner, n_owners)
-    owner = tile_owner[block_tile]
-    rank = rank_of_tile[block_tile]
-    slot = (owner % 2) * (pairs * slots_dev) + (owner // 2) * slots_dev + rank
-    n_slots = n_owners * slots_dev
-    pick = (jnp.arange(n_slots, dtype=jnp.int32)[:, None] == slot[None, :]).astype(jnp.bfloat16)
-
-    blocks = vis.reshape(nblocks, BR, width)
-    cells = row_cell.reshape(nblocks, BR)
-    weights = jnp.transpose(tap_weight.reshape(KT, nblocks, BR), (1, 0, 2))
-    matrix = kernel_matrix(cells, weights, tap_offset)
-    contrib = jnp.einsum("bcr,brf->bcf", matrix, blocks, preferred_element_type=jnp.float32)
-    contrib = contrib.reshape(nblocks, TC * width)
+    contrib = jnp.einsum("bcr,brf->bcf", matrix, part, preferred_element_type=jnp.float32)
     high = contrib.astype(jnp.bfloat16)
     low = (contrib - high.astype(jnp.float32)).astype(jnp.bfloat16)
-    partial = jnp.dot(
-        jnp.concatenate([pick, pick], axis=1),
+    partial = jnp.einsum(
+        "sb,bcf->scf",
+        pick2,
         jnp.concatenate([high, low], axis=0),
         preferred_element_type=jnp.float32,
     ).astype(jnp.bfloat16)
-    partial = partial.reshape(2, pairs, slots_dev, TC, width)
+    partial = partial.reshape((2, pairs, slots_dev) + partial.shape[1:])
 
     mine = lax.dynamic_index_in_dim(partial, parity, axis=0, keepdims=False)
     other = lax.dynamic_index_in_dim(partial, 1 - parity, axis=0, keepdims=False)
@@ -102,24 +81,51 @@
     for d in range(1, pairs):
         if pairs & (pairs - 1):
             dest = lambda c, d=d: (c + d) % pairs
-            src_chip = (chip - d) % pairs
         else:
             dest = lambda c, d=d: c ^ d
-            src_chip = chip ^ d
-        del src_chip
         send = lax.dynamic_index_in_dim(pair_send, dest(chip), axis=0, keepdims=False)
         recv = lax.ppermute(
             send, "uv", _partner_pairs(n_owners, lambda i, dest=dest: dest(i // 2) * 2 + i % 2)
         )
         grid = grid + recv.astype(jnp.float32)
+    gridded = grid.astype(jnp.bfloat16)
+    return lax.all_to_all(gridded, "chan", split_axis=1, concat_axis=2, tiled=True)
 
-    gridded = grid.astype(jnp.bfloat16).reshape(slots_dev, TC, 2, chan_dev)
+
+def body(vis, row_cell, tap_weight, tap_offset, block_tile, tile_owner, galaxy):
+    n_owners = lax.axis_size("uv")
+    n_chan = lax.axis_size("chan")
+    pairs = n_owners // 2
+    me = lax.axis_index("uv")
+    parity = me % 2
+    chip = me // 2
+    nblocks = block_tile.shape[0]
+    slots_dev = galaxy.shape[0]
+    chan_dev = vis.shape[2]
+
+    rank_of_tile = tile_ranks(tile_owner, n_owners)
+    owner = tile_owner[block_tile]
+    rank = rank_of_tile[block_tile]
+    slot = (owner % 2) * (pairs * slots_dev) + (owner // 2) * slots_dev + rank
+    n_slots = n_owners * slots_dev
+    pick = (jnp.arange(n_slots, dtype=jnp.int32)[:, None] == slot[None, :]).astype(jnp.bfloat16)
+    pick2 = jnp.concatenate([pick, pick], axis=1)
+
+    blocks = vis.reshape(nblocks, BR, 2, chan_dev)
+    cells = row_cell.reshape(nblocks, BR)
+    weights = jnp.transpose(tap_weight.reshape(KT, nblocks, BR), (1, 0, 2))
+    matrix = kernel_matrix(cells, weights, tap_offset)
     table = delay_table()
-    piece = lax.all_to_all(gridded, "chan", split_axis=1, concat_axis=3, tiled=True)
-    count = piece.shape[0]
-    cells_part = piece.shape[1]
-    flat = piece.reshape(count * cells_part, 2 * CH)
-    out = jnp.dot(flat, table, preferred_element_type=jnp.float32)
+    out = None
+    for k in range(2):
+        piece = _chunk(blocks[:, :, k, :], matrix, pick2, parity, chip, n_owners, slots_dev)
+        count, cells_part = piece.shape[0], piece.shape[1]
+        term = jnp.dot(
+            piece.reshape(count * cells_part, CH),
+            table[k * CH:(k + 1) * CH],
+            preferred_element_type=jnp.float32,
+        )
+        out = term if out is None else out + term
     delay = out.reshape(count, cells_part, 2 * CH)
     galaxy_f = galaxy.astype(jnp.float32)
     product = delay[..., :CH] * galaxy_f[..., :CH] + delay[..., CH:] * galaxy_f[..., CH:]

time: 384 us -> 339 us (0.88); the launches traced: 383 us -> 333 us
  local copies, waits for them, and re-layouts: 111 us -> 55.6 us
  waiting for transfers between devices: 152 us -> 123 us
  matrix products: 44.8 us -> 58.2 us
  other arithmetic: 64.1 us -> 75.6 us
  starting transfers between devices: 9.88 us -> 19.2 us
    unnamed x12 -> x19, local copies, waits for them, and re-layouts: 41.8 us -> 13.2 us
    dynamic_slice x6 -> x0, local copies, waits for them, and re-layouts: 25.5 us -> none  [the longest x4 14.3 us: body(): lax.dynamic_index_in_dim(pair_send, dest(chip), axis=0, keepdims=False)]
    reshape x2 -> x0, local copies, waits for them, and re-layouts: 25.4 us -> none  [the longest x1 20.5 us: body(): blocks = vis.reshape(nblocks, BR, width)]
    all_to_all x1 -> x2, waiting for transfers between devices: 32 us -> 7.58 us  [_chunk(): lax.all_to_all(gridded, 'chan', split_axis=1, concat_axis=2, tiled=True)]
    convert_element_type x0 -> x4, local copies, waits for them, and re-layouts: none -> 23.8 us  [the longest x2 20 us: _chunk(): partial = jnp.einsum('sb,bcf->scf', pick2, jnp.concatenate([high, low], a...]
    concatenate x0 -> x2, other arithmetic: none -> 14.8 us  [_chunk(): jnp.concatenate([high, low], axis=0)]
    dot_general x3 -> x6, matrix products: 44.8 us -> 58.2 us  [the longest x2 33.9 us: _chunk(): jnp.einsum('sb,bcf->scf', pick2, jnp.concatenate([high, low], axis=0), pr...]
    all_to_all x1 -> x2, starting transfers between devices: 4.88 us -> 9.93 us  [_chunk(): lax.all_to_all(gridded, 'chan', split_axis=1, concat_axis=2, tiled=True)]
  transfers between devices with their start and end apart: 7 -> 12, of which waited for: 6 -> 7; matrix products, arithmetic and copies ran while one was open for 11% -> 32% of each run, Pallas kernels for 0% -> 0%
where the time goes in v2:
time: 339 us; the launch traced here: 333 us
  waiting for transfers between devices  123 us (36%)
  other arithmetic  75.6 us (22%)
  matrix products  58.2 us (17%)
  local copies, waits for them, and re-layouts  55.6 us (16%)
  starting transfers between devices  19.2 us (6%)
    ppermute x6, waiting for transfers between devices, _chunk(): lax.ppermute(send, 'uv', _partner_pairs(n_owners, lambda i, dest=dest: de...  107 us
    dot_general x2, matrix products, _chunk(): jnp.einsum('sb,bcf->scf', pick2, jnp.concatenate([high, low], axis=0), pr...  33.9 us
    convert_element_type x2, other arithmetic, _chunk(): pair_send = pair_sum.astype(jnp.bfloat16)  20.1 us
    convert_element_type x2, local copies, waits for them, and re-layouts, _chunk(): partial = jnp.einsum('sb,bcf->scf', pick2, jnp.concatenate([high, low], a...  20 us
    another operation x1, other arithmetic  19.2 us
    dot_general x2, matrix products, _chunk(): jnp.einsum('bcr,brf->bcf', matrix, part, preferred_element_type=jnp.float32)  18.7 us
    concatenate x2, other arithmetic, _chunk(): jnp.concatenate([high, low], axis=0)  14.8 us
    unnamed x19, local copies, waits for them, and re-layouts  13.2 us
  transfers between devices with their start and end apart: 12, of which 7 were waited for; matrix products, arithmetic and copies ran while one was open for 32% of the time, Pallas kernels for 0%

profile of v2, /device:TPU:0, one launch (start us, length us, event | category | flops | bytes accessed | tf_op | source)
XLA Modules:
  0.0 332.7 jit_solution(7752051113231845115)
XLA Ops:
  4.4 11.7 %copy.33 = bf16[12288,2,256]{2,0,1:T(8,128)(2,1)} copy(bf16[12288,2,256]{2,1,0:T(2,128)(2,1)} %param.7) | data formatting | bytes 25165824 | tf_op args[0]
  19.1 4.9 %add_bitcast_fusion.10 = (s32[96,128]{1,0:T(8,128)S(1)}, s32[96,128]{1,0:T(8,128)S(1)}, s32[96,128]{1,0:T(8,128)S(1)}, s32[96,128]{1,0:T(8,128)S(1)}, s32[96,128...) fusion(s32[12288]{0:T(1024)S(1)} %copy-done.4, s32[]{:T(128)} %bitcast.1, ...), kind=kLoop, calls=%fused_computation.87 | loop fusion | flops 98304 | bytes 442400 | tf_op jit(solution)/shard_map/add | solution.py:24
  24.0 9.4 %subtract_convert_fusion = (bf16[96,128,256]{2,1,0:T(8,128)(2,1)S(1)}, bf16[96,128,256]{2,1,0:T(8,128)(2,1)S(1)}) fusion(bf16[96,128,2,256]{3,1,0,2:T(8,128)(2,1)} %bitcast.115, f32[96,128]{1,0:T(8,128)S(1)} %bitcast.126, s32[96,128]{1,0:T(8,128)S(1)} %get-tuple-element.30, f32[96,128]{1,0:T(8,128)S(1)} %bitcast.128, s32[96,128]{1,0:T(8,128)S(1)} %get-tuple-element.31, ...), kind=kOutput, calls=%fused_computation.8 | convolution fusion | flops 855638016 | bytes 19660800 | tf_op jit(solution)/shard_map/bcr,brf->bcf/dot_general | solution.py:63
  33.4 7.5 %pad_maximum_fusion.1 = bf16[192,128,256]{2,1,0:T(8,128)(2,1)} fusion(bf16[96,128,256]{2,1,0:T(8,128)(2,1)S(1)} %get-tuple-element.4, bf16[96,128,256]{2,1,0:T(8,128)(2,1)S(1)} %get-tuple-element.5), kind=kLoop, calls=%fused_computation.3 | loop fusion | flops 6291456 | bytes 25165824 | tf_op jit(solution)/shard_map/concatenate | solution.py:69
  40.9 17.0 %fusion.7 = bf16[152,128,256]{2,0,1:T(8,128)(2,1)} fusion(bf16[192,128,256]{2,1,0:T(8,128)(2,1)} %pad_maximum_fusion.1, pred[152,96]{1,0:T(8,128)(4,1)S(1)} %iota_compare_fusion.8), kind=kOutput, calls=%fused_computation.13 | convolution fusion | flops 1917612544 | bytes 22558976 | tf_op jit(solution)/shard_map/sb,bcf->scf/dot_general | solution.py:66
  57.9 9.9 %copy.40 = bf16[152,128,256]{2,1,0:T(8,128)(2,1)} copy(bf16[152,128,256]{2,0,1:T(8,128)(2,1)} %fusion.7) | data formatting | bytes 19922944 | tf_op jit(solution)/shard_map/convert_element_type | solution.py:71
  67.8 5.2 %dynamic-slice_bitcast_fusion = bf16[4,19,128,256]{3,2,1,0:T(8,128)(2,1)} fusion(bf16[2,4,19,128,256]{4,3,2,1,0:T(8,128)(2,1)} %bitcast.109, s32[]{:T(128)S(6)} %select_n.111), kind=kLoop, calls=%fused_computation.30 | loop fusion | bytes 9961476 | tf_op jit(solution)/shard_map/jit(dynamic_index_in_dim)/squeeze | solution.py:75
  73.5 9.4 %subtract_convert_fusion.1 = (bf16[96,128,256]{2,1,0:T(8,128)(2,1)S(1)}, bf16[96,128,256]{2,1,0:T(8,128)(2,1)S(1)}) fusion(bf16[96,128,2,256]{3,1,0,2:T(8,128)(2,1)} %bitcast.116, f32[96,128]{1,0:T(8,128)S(1)} %bitcast.127, s32[96,128]{1,0:T(8,128)S(1)} %get-tuple-element.30, f32[96,128]{1,0:T(8,128)S(1)} %bitcast.129, s32[96,128]{1,0:T(8,128)S(1)} %get-tuple-element.31, ...), kind=kOutput, calls=%fused_computation.9 | convolution fusion | flops 855638016 | bytes 19660800 | tf_op jit(solution)/shard_map/bcr,brf->bcf/dot_general | solution.py:63
  82.9 7.3 %pad_maximum_fusion = bf16[192,128,256]{2,1,0:T(8,128)(2,1)} fusion(bf16[96,128,256]{2,1,0:T(8,128)(2,1)S(1)} %get-tuple-element.8, bf16[96,128,256]{2,1,0:T(8,128)(2,1)S(1)} %get-tuple-element.9), kind=kLoop, calls=%fused_computation.2 | loop fusion | flops 6291456 | bytes 25165824 | tf_op jit(solution)/shard_map/concatenate | solution.py:69
  90.2 16.9 %fusion.4 = bf16[152,128,256]{2,0,1:T(8,128)(2,1)} fusion(bf16[192,128,256]{2,1,0:T(8,128)(2,1)} %pad_maximum_fusion, pred[152,96]{1,0:T(8,128)(4,1)S(1)} %iota_compare_fusion.8), kind=kOutput, calls=%fused_computation.12 | convolution fusion | flops 1917612544 | bytes 22558976 | tf_op jit(solution)/shard_map/sb,bcf->scf/dot_general | solution.py:66
  107.2 10.0 %copy.35 = bf16[152,128,256]{2,1,0:T(8,128)(2,1)} copy(bf16[152,128,256]{2,0,1:T(8,128)(2,1)} %fusion.4) | data formatting | bytes 19922944 | tf_op jit(solution)/shard_map/convert_element_type | solution.py:71
  117.2 5.3 %dynamic-slice_bitcast_fusion.1 = bf16[4,19,128,256]{3,2,1,0:T(8,128)(2,1)} fusion(bf16[2,4,19,128,256]{4,3,2,1,0:T(8,128)(2,1)} %bitcast.107, s32[]{:T(128)S(6)} %select_n.111), kind=kLoop, calls=%fused_computation.31 | loop fusion | bytes 9961476 | tf_op jit(solution)/shard_map/jit(dynamic_index_in_dim)/squeeze | solution.py:75
  122.5 10.2 %fusion.46 = (bf16[4,19,128,256]{3,2,1,0:T(8,128)(2,1)S(1)}, f32[4,19,128,256]{3,2,1,0:T(8,128)}) fusion(bf16[4,19,128,256]{3,2,1,0:T(8,128)(2,1)} %collective-permute-done.4, bf16[2,4,19,128,256]{4,3,2,1,0:T(8,128)(2,1)} %bitcast.110, s32[]{:T(128)S(6)} %select_n.110), kind=kLoop, calls=%fused_computation.106 | loop fusion | flops 9961472 | bytes 24903684 | tf_op jit(solution)/shard_map/convert_element_type | solution.py:78
  139.0 26.9 %collective-permute-done.5 = bf16[19,128,256]{2,1,0:T(8,128)(2,1)S(1)} collective-permute-done((bf16[19,128,256]{2,1,0:T(8,128)(2,1)}, bf16[19,128,256]{2,1,0:T(8,128)(2,1)S(1)}, u32[]{:S(2)}, u32[]{:S(2)}) %collective-permute-start.5) | collective-permute-done | bytes 1245216 | tf_op jit(solution)/shard_map/ppermute | solution.py:87
  165.9 27.6 %collective-permute-done.6 = bf16[19,128,256]{2,1,0:T(8,128)(2,1)} collective-permute-done((bf16[19,128,256]{2,1,0:T(8,128)(2,1)}, bf16[19,128,256]{2,1,0:T(8,128)(2,1)}, u32[]{:S(2)}, u32[]{:S(2)}) %collective-permute-start.6) | collective-permute-done | bytes 1245216 | tf_op jit(solution)/shard_map/ppermute | solution.py:87
  198.5 4.9 %all-to-all-start.1 = ((bf16[19,128,256]{2,0,1:T(8,128)(2,1)}), bf16[19,128,256]{2,0,1:T(8,128)(2,1)S(1)}, u32[]{:S(2)}, u32[]{:S(2)}) async-start(bf16[19,128,256]{2,0,1:T(8,128)(2,1)} %copy.41), calls=%async_computation.1 | async-start | bytes 3145728 | tf_op jit(solution)/shard_map/all_to_all | solution.py:92
  203.4 9.9 %fusion.47 = (bf16[4,19,128,256]{3,2,1,0:T(8,128)(2,1)S(1)}, f32[4,19,128,256]{3,2,1,0:T(8,128)}) fusion(bf16[4,19,128,256]{3,2,1,0:T(8,128)(2,1)} %collective-permute-done, bf16[2,4,19,128,256]{4,3,2,1,0:T(8,128)(2,1)} %bitcast.108, s32[]{:T(128)S(6)} %select_n.110), kind=kLoop, calls=%fused_computation.107 | loop fusion | flops 9961472 | bytes 24903684 | tf_op jit(solution)/shard_map/convert_element_type | solution.py:78
  217.1 26.8 %collective-permute-done.1 = bf16[19,128,256]{2,1,0:T(8,128)(2,1)S(1)} collective-permute-done((bf16[19,128,256]{2,1,0:T(8,128)(2,1)S(1)}, bf16[19,128,256]{2,1,0:T(8,128)(2,1)S(1)}, u32[]{:S(2)}, u32[]{:S(2)}) %collective-permute-start.1) | collective-permute-done | bytes 1245216 | tf_op jit(solution)/shard_map/ppermute | solution.py:87
  243.9 25.5 %collective-permute-done.2 = bf16[19,128,256]{2,1,0:T(8,128)(2,1)S(1)} collective-permute-done((bf16[19,128,256]{2,1,0:T(8,128)(2,1)S(1)}, bf16[19,128,256]{2,1,0:T(8,128)(2,1)S(1)}, u32[]{:S(2)}, u32[]{:S(2)}) %collective-permute-start.2) | collective-permute-done | bytes 1245216 | tf_op jit(solution)/shard_map/ppermute | solution.py:87
  273.8 5.1 %all-to-all-start = ((bf16[19,128,256]{2,0,1:T(8,128)(2,1)}), bf16[19,128,256]{2,0,1:T(8,128)(2,1)S(1)}, u32[]{:S(2)}, u32[]{:S(2)}) async-start(bf16[19,128,256]{2,0,1:T(8,128)(2,1)} %copy.36), calls=%async_computation | async-start | bytes 3145728 | tf_op jit(solution)/shard_map/all_to_all | solution.py:92
  278.8 4.6 %convert_element_type.153 = f32[19,32,2048]{2,1,0:T(8,128)} convert(bf16[19,32,2048]{2,1,0:T(8,128)(2,1)} %param.13) | non-fusion elementwise | flops 1245184 | bytes 7471104 | tf_op jit(solution)/shard_map/convert_element_type | solution.py:130
  283.5 19.2 %multiply_convert_fusion = (bf16[1024,1024]{1,0:T(8,128)(2,1)}, bf16[1024,1024]{1,0:T(8,128)(2,1)}, bf16[1024,1024]{1,0:T(8,128)(2,1)}) fusion(f32[1024]{0:T(1024)S(1)} %subtract_multiply_fusion), kind=kLoop, calls=%fused_computation.43 | loop fusion | flops 22020096 | bytes 6295552 | tf_op jit(solution)/shard_map/convert.13
  303.9 7.6 %all-to-all-done = bf16[19,128,256]{2,0,1:T(8,128)(2,1)S(1)} async-done(((bf16[19,128,256]{2,0,1:T(8,128)(2,1)}), bf16[19,128,256]{2,0,1:T(8,128)(2,1)S(1)}, u32[]{:S(2)}, u32[]{:S(2)}) %all-to-all-start) | async-done | bytes 1245216 | tf_op jit(solution)/shard_map/all_to_all | solution.py:92
  320.7 4.6 %collective-permute-done.8 = f32[19,1024]{1,0:T(8,128)S(1)} collective-permute-done((f32[19,1024]{1,0:T(8,128)S(1)}, f32[19,1024]{1,0:T(8,128)S(1)}, u32[]{:S(2)}, u32[]{:S(2)}) %collective-permute-start.8) | collective-permute-done | bytes 77856 | tf_op jit(solution)/shard_map/ppermute | solution.py:56
  (61 shorter events, 44.0 us)
Async XLA Ops:
  4.4 11.7 %copy-start.5 = (s32[96]{0:T(128)S(1)}, s32[96]{0:T(128)}, u32[]{:S(2)}) copy-start(s32[96]{0:T(128)} %param.11) | copy-start | bytes 1156
  4.4 11.7 %copy-start = (s32[80]{0:T(128)S(1)}, s32[80]{0:T(128)}, u32[]{:S(2)}) copy-start(s32[80]{0:T(128)} %param.12) | copy-start | bytes 964
  4.4 14.6 %copy-start.4 = (s32[12288]{0:T(1024)S(1)}, s32[12288]{0:T(1024)}, u32[]{:S(2)}) copy-start(s32[12288]{0:T(1024)} %param.8) | copy-start | bytes 147460
  73.0 49.5 %collective-permute-start.4 = (bf16[4,19,128,256]{3,2,1,0:T(8,128)(2,1)}, bf16[4,19,128,256]{3,2,1,0:T(8,128)(2,1)}, u32[]{:S(2)}, u32[]{:S(2)}) collective-permute-start(bf16[4,19,128,256]{3,2,1,0:T(8,128)(2,1)} %dynamic-slice_bitcast_fusion), channel_id=1, source_target_pairs={{0,4},{4,0},{8,12},{12,8},{16,20},{20,16},{24,28},{28,24},{1,5},{5... | collective-permute-start | bytes 14942216 | tf_op jit(solution)/shard_map/ppermute | solution.py:76
  122.5 80.9 %collective-permute-start = (bf16[4,19,128,256]{3,2,1,0:T(8,128)(2,1)}, bf16[4,19,128,256]{3,2,1,0:T(8,128)(2,1)}, u32[]{:S(2)}, u32[]{:S(2)}) collective-permute-start(bf16[4,19,128,256]{3,2,1,0:T(8,128)(2,1)} %dynamic-slice_bitcast_fusion.1), channel_id=1, source_target_pairs={{0,4},{4,0},{8,12},{12,8},{16,20},{20,16},{24,28},{28,24},{1,5},{5... | collective-permute-start | bytes 14942216 | tf_op jit(solution)/shard_map/ppermute | solution.py:76
  134.5 31.4 %collective-permute-start.5 = (bf16[19,128,256]{2,1,0:T(8,128)(2,1)}, bf16[19,128,256]{2,1,0:T(8,128)(2,1)S(1)}, u32[]{:S(2)}, u32[]{:S(2)}) collective-permute-start(bf16[19,128,256]{2,1,0:T(8,128)(2,1)} %get-tuple-element.10), channel_id=1, source_target_pairs={{0,8},{4,12},{8,0},{12,4},{16,24},{20,28},{24,16},{28,20},{1,9},{5... | collective-permute-start | bytes 3735560 | tf_op jit(solution)/shard_map/ppermute | solution.py:87
  137.5 56.0 %collective-permute-start.6 = (bf16[19,128,256]{2,1,0:T(8,128)(2,1)}, bf16[19,128,256]{2,1,0:T(8,128)(2,1)}, u32[]{:S(2)}, u32[]{:S(2)}) collective-permute-start(bf16[19,128,256]{2,1,0:T(8,128)(2,1)} %get-tuple-element.12), channel_id=1, source_target_pairs={{0,16},{4,20},{8,24},{12,28},{16,0},{20,4},{24,8},{28,12},{1,17},{... | collective-permute-start | bytes 3735560 | tf_op jit(solution)/shard_map/ppermute | solution.py:87
  139.0 54.5 %collective-permute-start.7 = (bf16[19,128,256]{2,1,0:T(8,128)(2,1)S(1)}, bf16[19,128,256]{2,1,0:T(8,128)(2,1)}, u32[]{:S(2)}, u32[]{:S(2)}) collective-permute-start(bf16[19,128,256]{2,1,0:T(8,128)(2,1)S(1)} %get-tuple-element.11), channel_id=1, source_target_pairs={{0,24},{4,28},{8,16},{12,20},{16,8},{20,12},{24,0},{28,4},{1,25},{... | collective-permute-start | bytes 3735560 | tf_op jit(solution)/shard_map/ppermute | solution.py:87
  198.5 75.3 %all-to-all-start.1 = ((bf16[19,128,256]{2,0,1:T(8,128)(2,1)}), bf16[19,128,256]{2,0,1:T(8,128)(2,1)S(1)}, u32[]{:S(2)}, u32[]{:S(2)}) async-start(bf16[19,128,256]{2,0,1:T(8,128)(2,1)} %copy.41), calls=%async_computation.1 | async-start | bytes 3145728 | tf_op jit(solution)/shard_map/all_to_all | solution.py:92
  213.6 30.3 %collective-permute-start.1 = (bf16[19,128,256]{2,1,0:T(8,128)(2,1)S(1)}, bf16[19,128,256]{2,1,0:T(8,128)(2,1)S(1)}, u32[]{:S(2)}, u32[]{:S(2)}) collective-permute-start(bf16[19,128,256]{2,1,0:T(8,128)(2,1)S(1)} %get-tuple-element.13), channel_id=1, source_target_pairs={{0,8},{4,12},{8,0},{12,4},{16,24},{20,28},{24,16},{28,20},{1,9},{5... | collective-permute-start | bytes 3735560 | tf_op jit(solution)/shard_map/ppermute | solution.py:87
  214.9 54.6 %collective-permute-start.2 = (bf16[19,128,256]{2,1,0:T(8,128)(2,1)S(1)}, bf16[19,128,256]{2,1,0:T(8,128)(2,1)S(1)}, u32[]{:S(2)}, u32[]{:S(2)}) collective-permute-start(bf16[19,128,256]{2,1,0:T(8,128)(2,1)S(1)} %get-tuple-element.15), channel_id=1, source_target_pairs={{0,16},{4,20},{8,24},{12,28},{16,0},{20,4},{24,8},{28,12},{1,17},{... | collective-permute-start | bytes 3735560 | tf_op jit(solution)/shard_map/ppermute | solution.py:87
  215.7 53.7 %collective-permute-start.3 = (bf16[19,128,256]{2,1,0:T(8,128)(2,1)S(1)}, bf16[19,128,256]{2,1,0:T(8,128)(2,1)S(1)}, u32[]{:S(2)}, u32[]{:S(2)}) collective-permute-start(bf16[19,128,256]{2,1,0:T(8,128)(2,1)S(1)} %get-tuple-element.14), channel_id=1, source_target_pairs={{0,24},{4,28},{8,16},{12,20},{16,8},{20,12},{24,0},{28,4},{1,25},{... | collective-permute-start | bytes 3735560 | tf_op jit(solution)/shard_map/ppermute | solution.py:87
  273.8 37.7 %all-to-all-start = ((bf16[19,128,256]{2,0,1:T(8,128)(2,1)}), bf16[19,128,256]{2,0,1:T(8,128)(2,1)S(1)}, u32[]{:S(2)}, u32[]{:S(2)}) async-start(bf16[19,128,256]{2,0,1:T(8,128)(2,1)} %copy.36), calls=%async_computation | async-start | bytes 3145728 | tf_op jit(solution)/shard_map/all_to_all | solution.py:92
  311.5 1.6 copy-start.2
  311.5 2.2 copy-start.3
  312.5 6.8 %slice-start = ((s8[4980736]{0:T(1024)(128)(4,1)}), s8[4194304]{0:T(1024)(128)(4,1)S(1)}, s32[]{:S(2)}) async-start(s8[4980736]{0:T(1024)(128)(4,1)} %bitcast.111), calls=%async_computation.2 | async-start | bytes 8388608
  313.7 2.8 copy-start.1
  313.7 5.6 %slice-start.1 = ((s8[4980736]{0:T(1024)(128)(4,1)}), s8[786432]{0:T(1024)(128)(4,1)S(1)}, s32[]{:S(2)}) async-start(s8[4980736]{0:T(1024)(128)(4,1)} %bitcast.111), calls=%async_computation.3 | async-start | bytes 1572864
  320.7 4.7 %collective-permute-start.8 = (f32[19,1024]{1,0:T(8,128)S(1)}, f32[19,1024]{1,0:T(8,128)S(1)}, u32[]{:S(2)}, u32[]{:S(2)}) collective-permute-start(f32[19,1024]{1,0:T(8,128)S(1)} %fusion.30), channel_id=1, source_target_pairs={{0,1},{1,0},{2,3},{3,2},{4,5},{5,4},{6,7},{7,6},{8,9},{9,8},{10,11... | collective-permute-start | bytes 233480 | tf_op jit(solution)/shard_map/ppermute | solution.py:56
  325.4 6.2 %collective-permute-start.9 = (f32[19,1024]{1,0:T(8,128)S(1)}, f32[19,1024]{1,0:T(8,128)S(1)}, u32[]{:S(2)}, u32[]{:S(2)}) collective-permute-start(f32[19,1024]{1,0:T(8,128)S(1)} %add.306), channel_id=1, source_target_pairs={{0,2},{1,3},{2,0},{3,1},{4,6},{5,7},{6,4},{7,5},{8,10},{9,11},{10,... | collective-permute-start | bytes 233480 | tf_op jit(solution)/shard_map/ppermute | solution.py:56

commit v3 on v2

--- a/solution.py
+++ b/solution.py
@@ -58,7 +58,7 @@
     return x
 
 
-def _chunk(part, matrix, pick2, parity, chip, n_owners, slots_dev):
+def _gather_pair(part, matrix, pick2, parity, chip, n_owners, slots_dev):
     pairs = n_owners // 2
     contrib = jnp.einsum("bcr,brf->bcf", matrix, part, preferred_element_type=jnp.float32)
     high = contrib.astype(jnp.bfloat16)
@@ -74,10 +74,16 @@
     mine = lax.dynamic_index_in_dim(partial, parity, axis=0, keepdims=False)
     other = lax.dynamic_index_in_dim(partial, 1 - parity, axis=0, keepdims=False)
     got = lax.ppermute(other, "uv", _partner_pairs(n_owners, lambda i: i ^ 1))
-    pair_sum = mine.astype(jnp.float32) + got.astype(jnp.float32)
-    pair_send = pair_sum.astype(jnp.bfloat16)
+    pair_send = (mine.astype(jnp.float32) + got.astype(jnp.float32)).astype(jnp.bfloat16)
+    own = lax.dynamic_index_in_dim(mine, chip, axis=0, keepdims=False).astype(
+        jnp.float32
+    ) + lax.dynamic_index_in_dim(got, chip, axis=0, keepdims=False).astype(jnp.float32)
+    return pair_send, own
 
-    grid = lax.dynamic_index_in_dim(pair_sum, chip, axis=0, keepdims=False)
+
+def _scatter_pairs(pair_send, own, chip, n_owners):
+    pairs = n_owners // 2
+    grid = own
     for d in range(1, pairs):
         if pairs & (pairs - 1):
             dest = lambda c, d=d: (c + d) % pairs
@@ -116,9 +122,11 @@
     weights = jnp.transpose(tap_weight.reshape(KT, nblocks, BR), (1, 0, 2))
     matrix = kernel_matrix(cells, weights, tap_offset)
     table = delay_table()
+    first = _gather_pair(blocks[:, :, 0, :], matrix, pick2, parity, chip, n_owners, slots_dev)
+    second = _gather_pair(blocks[:, :, 1, :], matrix, pick2, parity, chip, n_owners, slots_dev)
     out = None
-    for k in range(2):
-        piece = _chunk(blocks[:, :, k, :], matrix, pick2, parity, chip, n_owners, slots_dev)
+    for k, (pair_send, own) in enumerate((first, second)):
+        piece = _scatter_pairs(pair_send, own, chip, n_owners)
         count, cells_part = piece.shape[0], piece.shape[1]
         term = jnp.dot(
             piece.reshape(count * cells_part, CH),

time: 339 us -> 332 us (0.979)
  other arithmetic: 75.6 us -> 68.7 us
    convert_element_type x4, other arithmetic: 25.7 us -> 18.5 us  [the longest x2 12.3 us: _gather_pair(): (mine.astype(jnp.float32) + got.astype(jnp.float32)).astype(jnp.bfloat16)]
  transfers between devices with their start and end apart: 12 -> 12, of which waited for: 7 -> 7; matrix products, arithmetic and copies ran while one was open for 32% -> 31% of each run, Pallas kernels for 0% -> 0%
where the time goes in v3:
time: 332 us; the launch traced here: 326 us
  waiting for transfers between devices  123 us (37%)
  other arithmetic  68.7 us (21%)
  matrix products  58.3 us (18%)
  local copies, waits for them, and re-layouts  55.8 us (17%)
  starting transfers between devices  19.2 us (6%)
    ppermute x6, waiting for transfers between devices, _scatter_pairs(): lax.ppermute(send, 'uv', _partner_pairs(n_owners, lambda i, dest=dest: de...  107 us
    dot_general x2, matrix products, _gather_pair(): jnp.einsum('sb,bcf->scf', pick2, jnp.concatenate([high, low], axis=0), pr...  34.1 us
    convert_element_type x2, local copies, waits for them, and re-layouts, _gather_pair(): partial = jnp.einsum('sb,bcf->scf', pick2, jnp.concatenate([high, low], a...  20 us
    another operation x1, other arithmetic  19.2 us
    dot_general x2, matrix products, _gather_pair(): jnp.einsum('bcr,brf->bcf', matrix, part, preferred_element_type=jnp.float32)  18.7 us
    concatenate x2, other arithmetic, _gather_pair(): jnp.concatenate([high, low], axis=0)  14.8 us
    unnamed x19, local copies, waits for them, and re-layouts  13.2 us
    convert_element_type x2, other arithmetic, _gather_pair(): (mine.astype(jnp.float32) + got.astype(jnp.float32)).astype(jnp.bfloat16)  12.3 us
  transfers between devices with their start and end apart: 12, of which 7 were waited for; matrix products, arithmetic and copies ran while one was open for 31% of the time, Pallas kernels for 0%

profile of v3, /device:TPU:0, one launch (start us, length us, event | category | flops | bytes accessed | tf_op | source)
XLA Modules:
  0.0 326.2 jit_solution(16030803658536327914)
XLA Ops:
  4.7 11.7 %copy.21 = bf16[12288,2,256]{2,0,1:T(8,128)(2,1)} copy(bf16[12288,2,256]{2,1,0:T(2,128)(2,1)} %param.7) | data formatting | bytes 25165824 | tf_op args[0]
  19.3 5.0 %add_bitcast_fusion.10 = (s32[96,128]{1,0:T(8,128)S(1)}, s32[96,128]{1,0:T(8,128)S(1)}, s32[96,128]{1,0:T(8,128)S(1)}, s32[96,128]{1,0:T(8,128)S(1)}, s32[96,128...) fusion(s32[12288]{0:T(1024)S(1)} %copy-done.4, s32[]{:T(128)} %bitcast.1, ...), kind=kLoop, calls=%fused_computation.91 | loop fusion | flops 98304 | bytes 442400 | tf_op jit(solution)/shard_map/add | solution.py:24
  24.3 9.4 %subtract_convert_fusion = (bf16[96,128,256]{2,1,0:T(8,128)(2,1)S(1)}, bf16[96,128,256]{2,1,0:T(8,128)(2,1)S(1)}) fusion(bf16[96,128,2,256]{3,1,0,2:T(8,128)(2,1)} %bitcast.109, f32[96,128]{1,0:T(8,128)S(1)} %bitcast.120, s32[96,128]{1,0:T(8,128)S(1)} %get-tuple-element.26, f32[96,128]{1,0:T(8,128)S(1)} %bitcast.122, s32[96,128]{1,0:T(8,128)S(1)} %get-tuple-element.27, ...), kind=kOutput, calls=%fused_computation.8 | convolution fusion | flops 855638016 | bytes 19660800 | tf_op jit(solution)/shard_map/bcr,brf->bcf/dot_general | solution.py:63
  33.7 7.6 %pad_maximum_fusion.1 = bf16[192,128,256]{2,1,0:T(8,128)(2,1)} fusion(bf16[96,128,256]{2,1,0:T(8,128)(2,1)S(1)} %get-tuple-element.2, bf16[96,128,256]{2,1,0:T(8,128)(2,1)S(1)} %get-tuple-element.3), kind=kLoop, calls=%fused_computation.3 | loop fusion | flops 6291456 | bytes 25165824 | tf_op jit(solution)/shard_map/concatenate | solution.py:69
  41.3 17.0 %fusion.9 = bf16[152,128,256]{2,0,1:T(8,128)(2,1)} fusion(bf16[192,128,256]{2,1,0:T(8,128)(2,1)} %pad_maximum_fusion.1, pred[152,96]{1,0:T(8,128)(4,1)S(1)} %iota_compare_fusion.8), kind=kOutput, calls=%fused_computation.15 | convolution fusion | flops 1917612544 | bytes 22558976 | tf_op jit(solution)/shard_map/sb,bcf->scf/dot_general | solution.py:66
  58.3 10.0 %copy.27 = bf16[152,128,256]{2,1,0:T(8,128)(2,1)} copy(bf16[152,128,256]{2,0,1:T(8,128)(2,1)} %fusion.9) | data formatting | bytes 19922944 | tf_op jit(solution)/shard_map/convert_element_type | solution.py:71
  68.3 5.3 %dynamic-slice_bitcast_fusion = bf16[4,19,128,256]{3,2,1,0:T(8,128)(2,1)} fusion(bf16[2,4,19,128,256]{4,3,2,1,0:T(8,128)(2,1)} %bitcast.102, s32[]{:T(128)S(6)} %select_n.120), kind=kLoop, calls=%fused_computation.32 | loop fusion | bytes 9961476 | tf_op jit(solution)/shard_map/jit(dynamic_index_in_dim)/squeeze | solution.py:75
  74.0 9.4 %subtract_convert_fusion.1 = (bf16[96,128,256]{2,1,0:T(8,128)(2,1)S(1)}, bf16[96,128,256]{2,1,0:T(8,128)(2,1)S(1)}) fusion(bf16[96,128,2,256]{3,1,0,2:T(8,128)(2,1)} %bitcast.110, f32[96,128]{1,0:T(8,128)S(1)} %bitcast.121, s32[96,128]{1,0:T(8,128)S(1)} %get-tuple-element.26, f32[96,128]{1,0:T(8,128)S(1)} %bitcast.123, s32[96,128]{1,0:T(8,128)S(1)} %get-tuple-element.27, ...), kind=kOutput, calls=%fused_computation.9 | convolution fusion | flops 855638016 | bytes 19660800 | tf_op jit(solution)/shard_map/bcr,brf->bcf/dot_general | solution.py:63
  83.4 7.3 %pad_maximum_fusion = bf16[192,128,256]{2,1,0:T(8,128)(2,1)} fusion(bf16[96,128,256]{2,1,0:T(8,128)(2,1)S(1)} %get-tuple-element.4, bf16[96,128,256]{2,1,0:T(8,128)(2,1)S(1)} %get-tuple-element.5), kind=kLoop, calls=%fused_computation.2 | loop fusion | flops 6291456 | bytes 25165824 | tf_op jit(solution)/shard_map/concatenate | solution.py:69
  90.7 17.0 %fusion.6 = bf16[152,128,256]{2,0,1:T(8,128)(2,1)} fusion(bf16[192,128,256]{2,1,0:T(8,128)(2,1)} %pad_maximum_fusion, pred[152,96]{1,0:T(8,128)(4,1)S(1)} %iota_compare_fusion.8), kind=kOutput, calls=%fused_computation.14 | convolution fusion | flops 1917612544 | bytes 22558976 | tf_op jit(solution)/shard_map/sb,bcf->scf/dot_general | solution.py:66
  107.7 10.1 %copy.23 = bf16[152,128,256]{2,1,0:T(8,128)(2,1)} copy(bf16[152,128,256]{2,0,1:T(8,128)(2,1)} %fusion.6) | data formatting | bytes 19922944 | tf_op jit(solution)/shard_map/convert_element_type | solution.py:71
  117.8 5.3 %dynamic-slice_bitcast_fusion.1 = bf16[4,19,128,256]{3,2,1,0:T(8,128)(2,1)} fusion(bf16[2,4,19,128,256]{4,3,2,1,0:T(8,128)(2,1)} %bitcast.99, s32[]{:T(128)S(6)} %select_n.120), kind=kLoop, calls=%fused_computation.33 | loop fusion | bytes 9961476 | tf_op jit(solution)/shard_map/jit(dynamic_index_in_dim)/squeeze | solution.py:75
  123.1 6.3 %fusion.4 = bf16[4,19,128,256]{3,2,1,0:T(8,128)(2,1)S(1)} fusion(bf16[4,19,128,256]{3,2,1,0:T(8,128)(2,1)} %collective-permute-done.4, bf16[2,4,19,128,256]{4,3,2,1,0:T(8,128)(2,1)} %bitcast.103, s32[]{:T(128)S(6)} %select_n.115), kind=kLoop, calls=%fused_computation.11 | loop fusion | flops 9961472 | bytes 14942212 | tf_op jit(solution)/shard_map/convert_element_type | solution.py:77
  135.7 26.9 %collective-permute-done.5 = bf16[19,128,256]{2,1,0:T(8,128)(2,1)S(1)} collective-permute-done((bf16[19,128,256]{2,1,0:T(8,128)(2,1)}, bf16[19,128,256]{2,1,0:T(8,128)(2,1)S(1)}, u32[]{:S(2)}, u32[]{:S(2)}) %collective-permute-start.5) | collective-permute-done | bytes 1245216 | tf_op jit(solution)/shard_map/ppermute | solution.py:93
  162.6 27.6 %collective-permute-done.6 = bf16[19,128,256]{2,1,0:T(8,128)(2,1)} collective-permute-done((bf16[19,128,256]{2,1,0:T(8,128)(2,1)}, bf16[19,128,256]{2,1,0:T(8,128)(2,1)}, u32[]{:S(2)}, u32[]{:S(2)}) %collective-permute-start.6) | collective-permute-done | bytes 1245216 | tf_op jit(solution)/shard_map/ppermute | solution.py:93
  195.5 4.9 %all-to-all-start.1 = ((bf16[19,128,256]{2,0,1:T(8,128)(2,1)}), bf16[19,128,256]{2,0,1:T(8,128)(2,1)S(1)}, u32[]{:S(2)}, u32[]{:S(2)}) async-start(bf16[19,128,256]{2,0,1:T(8,128)(2,1)} %copy.28), calls=%async_computation.1 | async-start | bytes 3145728 | tf_op jit(solution)/shard_map/all_to_all | solution.py:98
  200.4 6.1 %fusion.5 = bf16[4,19,128,256]{3,2,1,0:T(8,128)(2,1)S(1)} fusion(bf16[4,19,128,256]{3,2,1,0:T(8,128)(2,1)} %collective-permute-done, bf16[2,4,19,128,256]{4,3,2,1,0:T(8,128)(2,1)} %bitcast.100, s32[]{:T(128)S(6)} %select_n.115), kind=kLoop, calls=%fused_computation.13 | loop fusion | flops 9961472 | bytes 14942212 | tf_op jit(solution)/shard_map/convert_element_type | solution.py:77
  210.4 26.8 %collective-permute-done.1 = bf16[19,128,256]{2,1,0:T(8,128)(2,1)S(1)} collective-permute-done((bf16[19,128,256]{2,1,0:T(8,128)(2,1)S(1)}, bf16[19,128,256]{2,1,0:T(8,128)(2,1)S(1)}, u32[]{:S(2)}, u32[]{:S(2)}) %collective-permute-start.1) | collective-permute-done | bytes 1245216 | tf_op jit(solution)/shard_map/ppermute | solution.py:93
  237.1 25.6 %collective-permute-done.2 = bf16[19,128,256]{2,1,0:T(8,128)(2,1)S(1)} collective-permute-done((bf16[19,128,256]{2,1,0:T(8,128)(2,1)S(1)}, bf16[19,128,256]{2,1,0:T(8,128)(2,1)S(1)}, u32[]{:S(2)}, u32[]{:S(2)}) %collective-permute-start.2) | collective-permute-done | bytes 1245216 | tf_op jit(solution)/shard_map/ppermute | solution.py:93
  267.3 5.1 %all-to-all-start = ((bf16[19,128,256]{2,0,1:T(8,128)(2,1)}), bf16[19,128,256]{2,0,1:T(8,128)(2,1)S(1)}, u32[]{:S(2)}, u32[]{:S(2)}) async-start(bf16[19,128,256]{2,0,1:T(8,128)(2,1)} %copy.24), calls=%async_computation | async-start | bytes 3145728 | tf_op jit(solution)/shard_map/all_to_all | solution.py:98
  272.3 4.6 %convert_element_type.185 = f32[19,32,2048]{2,1,0:T(8,128)} convert(bf16[19,32,2048]{2,1,0:T(8,128)(2,1)} %param.13) | non-fusion elementwise | flops 1245184 | bytes 7471104 | tf_op jit(solution)/shard_map/convert_element_type | solution.py:138
  277.0 19.2 %multiply_convert_fusion = (bf16[1024,1024]{1,0:T(8,128)(2,1)}, bf16[1024,1024]{1,0:T(8,128)(2,1)}, bf16[1024,1024]{1,0:T(8,128)(2,1)}) fusion(f32[1024]{0:T(1024)S(1)} %subtract_multiply_fusion), kind=kLoop, calls=%fused_computation.45 | loop fusion | flops 22020096 | bytes 6295552 | tf_op jit(solution)/shard_map/convert.17
  297.4 7.6 %all-to-all-done = bf16[19,128,256]{2,0,1:T(8,128)(2,1)S(1)} async-done(((bf16[19,128,256]{2,0,1:T(8,128)(2,1)}), bf16[19,128,256]{2,0,1:T(8,128)(2,1)S(1)}, u32[]{:S(2)}, u32[]{:S(2)}) %all-to-all-start) | async-done | bytes 1245216 | tf_op jit(solution)/shard_map/all_to_all | solution.py:98
  314.3 4.6 %collective-permute-done.8 = f32[19,1024]{1,0:T(8,128)S(1)} collective-permute-done((f32[19,1024]{1,0:T(8,128)S(1)}, f32[19,1024]{1,0:T(8,128)S(1)}, u32[]{:S(2)}, u32[]{:S(2)}) %collective-permute-start.8) | collective-permute-done | bytes 77856 | tf_op jit(solution)/shard_map/ppermute | solution.py:56
  (61 shorter events, 44.9 us)
Async XLA Ops:
  4.7 11.7 %copy-start.5 = (s32[96]{0:T(128)S(1)}, s32[96]{0:T(128)}, u32[]{:S(2)}) copy-start(s32[96]{0:T(128)} %param.11) | copy-start | bytes 1156
  4.7 11.7 %copy-start = (s32[80]{0:T(128)S(1)}, s32[80]{0:T(128)}, u32[]{:S(2)}) copy-start(s32[80]{0:T(128)} %param.12) | copy-start | bytes 964
  4.7 14.6 %copy-start.4 = (s32[12288]{0:T(1024)S(1)}, s32[12288]{0:T(1024)}, u32[]{:S(2)}) copy-start(s32[12288]{0:T(1024)} %param.8) | copy-start | bytes 147460
  73.5 49.6 %collective-permute-start.4 = (bf16[4,19,128,256]{3,2,1,0:T(8,128)(2,1)}, bf16[4,19,128,256]{3,2,1,0:T(8,128)(2,1)}, u32[]{:S(2)}, u32[]{:S(2)}) collective-permute-start(bf16[4,19,128,256]{3,2,1,0:T(8,128)(2,1)} %dynamic-slice_bitcast_fusion), channel_id=1, source_target_pairs={{0,4},{4,0},{8,12},{12,8},{16,20},{20,16},{24,28},{28,24},{1,5},{5... | collective-permute-start | bytes 14942216 | tf_op jit(solution)/shard_map/ppermute | solution.py:76
  123.1 77.3 %collective-permute-start = (bf16[4,19,128,256]{3,2,1,0:T(8,128)(2,1)}, bf16[4,19,128,256]{3,2,1,0:T(8,128)(2,1)}, u32[]{:S(2)}, u32[]{:S(2)}) collective-permute-start(bf16[4,19,128,256]{3,2,1,0:T(8,128)(2,1)} %dynamic-slice_bitcast_fusion.1), channel_id=1, source_target_pairs={{0,4},{4,0},{8,12},{12,8},{16,20},{20,16},{24,28},{28,24},{1,5},{5... | collective-permute-start | bytes 14942216 | tf_op jit(solution)/shard_map/ppermute | solution.py:76
  131.2 31.4 %collective-permute-start.5 = (bf16[19,128,256]{2,1,0:T(8,128)(2,1)}, bf16[19,128,256]{2,1,0:T(8,128)(2,1)S(1)}, u32[]{:S(2)}, u32[]{:S(2)}) collective-permute-start(bf16[19,128,256]{2,1,0:T(8,128)(2,1)} %get-tuple-element.6), channel_id=1, source_target_pairs={{0,8},{4,12},{8,0},{12,4},{16,24},{20,28},{24,16},{28,20},{1,9},{5... | collective-permute-start | bytes 3735560 | tf_op jit(solution)/shard_map/ppermute | solution.py:93
  134.2 56.0 %collective-permute-start.6 = (bf16[19,128,256]{2,1,0:T(8,128)(2,1)}, bf16[19,128,256]{2,1,0:T(8,128)(2,1)}, u32[]{:S(2)}, u32[]{:S(2)}) collective-permute-start(bf16[19,128,256]{2,1,0:T(8,128)(2,1)} %get-tuple-element.8), channel_id=1, source_target_pairs={{0,16},{4,20},{8,24},{12,28},{16,0},{20,4},{24,8},{28,12},{1,17},{... | collective-permute-start | bytes 3735560 | tf_op jit(solution)/shard_map/ppermute | solution.py:93
  135.7 54.5 %collective-permute-start.7 = (bf16[19,128,256]{2,1,0:T(8,128)(2,1)S(1)}, bf16[19,128,256]{2,1,0:T(8,128)(2,1)}, u32[]{:S(2)}, u32[]{:S(2)}) collective-permute-start(bf16[19,128,256]{2,1,0:T(8,128)(2,1)S(1)} %get-tuple-element.7), channel_id=1, source_target_pairs={{0,24},{4,28},{8,16},{12,20},{16,8},{20,12},{24,0},{28,4},{1,25},{... | collective-permute-start | bytes 3735560 | tf_op jit(solution)/shard_map/ppermute | solution.py:93
  195.5 71.8 %all-to-all-start.1 = ((bf16[19,128,256]{2,0,1:T(8,128)(2,1)}), bf16[19,128,256]{2,0,1:T(8,128)(2,1)S(1)}, u32[]{:S(2)}, u32[]{:S(2)}) async-start(bf16[19,128,256]{2,0,1:T(8,128)(2,1)} %copy.28), calls=%async_computation.1 | async-start | bytes 3145728 | tf_op jit(solution)/shard_map/all_to_all | solution.py:98
  206.8 30.3 %collective-permute-start.1 = (bf16[19,128,256]{2,1,0:T(8,128)(2,1)S(1)}, bf16[19,128,256]{2,1,0:T(8,128)(2,1)S(1)}, u32[]{:S(2)}, u32[]{:S(2)}) collective-permute-start(bf16[19,128,256]{2,1,0:T(8,128)(2,1)S(1)} %get-tuple-element.9), channel_id=1, source_target_pairs={{0,8},{4,12},{8,0},{12,4},{16,24},{20,28},{24,16},{28,20},{1,9},{5... | collective-permute-start | bytes 3735560 | tf_op jit(solution)/shard_map/ppermute | solution.py:93
  208.1 54.6 %collective-permute-start.2 = (bf16[19,128,256]{2,1,0:T(8,128)(2,1)S(1)}, bf16[19,128,256]{2,1,0:T(8,128)(2,1)S(1)}, u32[]{:S(2)}, u32[]{:S(2)}) collective-permute-start(bf16[19,128,256]{2,1,0:T(8,128)(2,1)S(1)} %get-tuple-element.11), channel_id=1, source_target_pairs={{0,16},{4,20},{8,24},{12,28},{16,0},{20,4},{24,8},{28,12},{1,17},{... | collective-permute-start | bytes 3735560 | tf_op jit(solution)/shard_map/ppermute | solution.py:93
  208.9 53.8 %collective-permute-start.3 = (bf16[19,128,256]{2,1,0:T(8,128)(2,1)S(1)}, bf16[19,128,256]{2,1,0:T(8,128)(2,1)S(1)}, u32[]{:S(2)}, u32[]{:S(2)}) collective-permute-start(bf16[19,128,256]{2,1,0:T(8,128)(2,1)S(1)} %get-tuple-element.10), channel_id=1, source_target_pairs={{0,24},{4,28},{8,16},{12,20},{16,8},{20,12},{24,0},{28,4},{1,25},{... | collective-permute-start | bytes 3735560 | tf_op jit(solution)/shard_map/ppermute | solution.py:93
  267.3 37.7 %all-to-all-start = ((bf16[19,128,256]{2,0,1:T(8,128)(2,1)}), bf16[19,128,256]{2,0,1:T(8,128)(2,1)S(1)}, u32[]{:S(2)}, u32[]{:S(2)}) async-start(bf16[19,128,256]{2,0,1:T(8,128)(2,1)} %copy.24), calls=%async_computation | async-start | bytes 3145728 | tf_op jit(solution)/shard_map/all_to_all | solution.py:98
  305.0 1.6 copy-start.2
  305.0 2.2 copy-start.3
  306.0 6.8 %slice-start = ((s8[4980736]{0:T(1024)(128)(4,1)}), s8[4194304]{0:T(1024)(128)(4,1)S(1)}, s32[]{:S(2)}) async-start(s8[4980736]{0:T(1024)(128)(4,1)} %bitcast.105), calls=%async_computation.2 | async-start | bytes 8388608
  307.2 2.8 copy-start.1
  307.2 5.6 %slice-start.1 = ((s8[4980736]{0:T(1024)(128)(4,1)}), s8[786432]{0:T(1024)(128)(4,1)S(1)}, s32[]{:S(2)}) async-start(s8[4980736]{0:T(1024)(128)(4,1)} %bitcast.105), calls=%async_computation.3 | async-start | bytes 1572864
  314.2 4.7 %collective-permute-start.8 = (f32[19,1024]{1,0:T(8,128)S(1)}, f32[19,1024]{1,0:T(8,128)S(1)}, u32[]{:S(2)}, u32[]{:S(2)}) collective-permute-start(f32[19,1024]{1,0:T(8,128)S(1)} %fusion.32), channel_id=1, source_target_pairs={{0,1},{1,0},{2,3},{3,2},{4,5},{5,4},{6,7},{7,6},{8,9},{9,8},{10,11... | collective-permute-start | bytes 233480 | tf_op jit(solution)/shard_map/ppermute | solution.py:56
  318.9 6.2 %collective-permute-start.9 = (f32[19,1024]{1,0:T(8,128)S(1)}, f32[19,1024]{1,0:T(8,128)S(1)}, u32[]{:S(2)}, u32[]{:S(2)}) collective-permute-start(f32[19,1024]{1,0:T(8,128)S(1)} %add.325), channel_id=1, source_target_pairs={{0,2},{1,3},{2,0},{3,1},{4,6},{5,7},{6,4},{7,5},{8,10},{9,11},{10,... | collective-permute-start | bytes 233480 | tf_op jit(solution)/shard_map/ppermute | solution.py:56

commit v4 on v3

--- a/solution.py
+++ b/solution.py
@@ -74,11 +74,37 @@
     mine = lax.dynamic_index_in_dim(partial, parity, axis=0, keepdims=False)
     other = lax.dynamic_index_in_dim(partial, 1 - parity, axis=0, keepdims=False)
     got = lax.ppermute(other, "uv", _partner_pairs(n_owners, lambda i: i ^ 1))
+    return mine, got
+
+
+def _halving(mine, got, chip, n_owners, order):
+    pairs = n_owners // 2
+    nbits = pairs.bit_length() - 1
+    acc = mine.astype(jnp.float32) + got.astype(jnp.float32)
+    acc = acc.reshape((2,) * nbits + acc.shape[1:])
+    dims = list(range(nbits - 1, -1, -1))
+    for j in order:
+        axis = dims.index(j)
+        dims.pop(axis)
+        bit = (chip >> j) & 1
+        keep = lax.dynamic_index_in_dim(acc, bit, axis=axis, keepdims=False)
+        send = lax.dynamic_index_in_dim(acc, 1 - bit, axis=axis, keepdims=False)
+        recv = lax.ppermute(
+            send.astype(jnp.bfloat16),
+            "uv",
+            _partner_pairs(n_owners, lambda i, j=j: ((i // 2) ^ (1 << j)) * 2 + i % 2),
+        )
+        acc = keep + recv.astype(jnp.float32)
+    gridded = acc.astype(jnp.bfloat16)
+    return lax.all_to_all(gridded, "chan", split_axis=1, concat_axis=2, tiled=True)
+
+
+def _split_pairs(mine, got, chip, n_owners):
     pair_send = (mine.astype(jnp.float32) + got.astype(jnp.float32)).astype(jnp.bfloat16)
     own = lax.dynamic_index_in_dim(mine, chip, axis=0, keepdims=False).astype(
         jnp.float32
     ) + lax.dynamic_index_in_dim(got, chip, axis=0, keepdims=False).astype(jnp.float32)
-    return pair_send, own
+    return _scatter_pairs(pair_send, own, chip, n_owners)
 
 
 def _scatter_pairs(pair_send, own, chip, n_owners):
@@ -125,8 +151,14 @@
     first = _gather_pair(blocks[:, :, 0, :], matrix, pick2, parity, chip, n_owners, slots_dev)
     second = _gather_pair(blocks[:, :, 1, :], matrix, pick2, parity, chip, n_owners, slots_dev)
     out = None
-    for k, (pair_send, own) in enumerate((first, second)):
-        piece = _scatter_pairs(pair_send, own, chip, n_owners)
+    pairs = n_owners // 2
+    nbits = pairs.bit_length() - 1
+    for k, (mine, got) in enumerate((first, second)):
+        if pairs & (pairs - 1) or pairs == 1:
+            piece = _split_pairs(mine, got, chip, n_owners)
+        else:
+            order = list(range(nbits)) if k == 0 else list(range(nbits - 1, -1, -1))
+            piece = _halving(mine, got, chip, n_owners, order)
         count, cells_part = piece.shape[0], piece.shape[1]
         term = jnp.dot(
             piece.reshape(count * cells_part, CH),

time: 332 us -> 344 us (1.036)
  local copies, waits for them, and re-layouts: 55.8 us -> 64.9 us
  other arithmetic: 68.7 us -> 72.4 us
    add x0 -> x4, other arithmetic: none -> 19.7 us  [the longest x2 12 us: _halving(): acc = mine.astype(jnp.float32) + got.astype(jnp.float32)]
    convert_element_type x4 -> x2, other arithmetic: 18.5 us -> 2.45 us  [_halving(): gridded = acc.astype(jnp.bfloat16)]
    unnamed x19 -> x23, local copies, waits for them, and re-layouts: 13.2 us -> 22.1 us
    ppermute x6 -> x4, waiting for transfers between devices: 107 us -> 100 us  [_halving(): lax.ppermute(send.astype(jnp.bfloat16), 'uv', _partner_pairs(n_owners, la...]
    all_to_all x2, waiting for transfers between devices: 7.61 us -> 13.2 us  [_halving(): lax.all_to_all(gridded, 'chan', split_axis=1, concat_axis=2, tiled=True)]
    ppermute x6 -> x4, starting transfers between devices: 8.04 us -> 6.89 us  [_halving(): lax.ppermute(send.astype(jnp.bfloat16), 'uv', _partner_pairs(n_owners, la...]
  transfers between devices with their start and end apart: 12 -> 10, of which waited for: 7 -> 7; matrix products, arithmetic and copies ran while one was open for 31% -> 31% of each run, Pallas kernels for 0% -> 0%
where the time goes in v4:
time: 344 us; the launch traced here: 338 us
  waiting for transfers between devices  122 us (35%)
  other arithmetic  72.4 us (21%)
  local copies, waits for them, and re-layouts  64.9 us (19%)
  matrix products  60.7 us (18%)
  starting transfers between devices  16 us (5%)
    ppermute x4, waiting for transfers between devices, _halving(): lax.ppermute(send.astype(jnp.bfloat16), 'uv', _partner_pairs(n_owners, la...  100 us
    dot_general x2, matrix products, _gather_pair(): jnp.einsum('sb,bcf->scf', pick2, jnp.concatenate([high, low], axis=0), pr...  34.1 us
    unnamed x23, local copies, waits for them, and re-layouts  22.1 us
    convert_element_type x2, local copies, waits for them, and re-layouts, _gather_pair(): partial = jnp.einsum('sb,bcf->scf', pick2, jnp.concatenate([high, low], a...  20 us
    another operation x1, other arithmetic  19.1 us
    dot_general x2, matrix products, _gather_pair(): jnp.einsum('bcr,brf->bcf', matrix, part, preferred_element_type=jnp.float32)  18.7 us
    concatenate x2, other arithmetic, _gather_pair(): jnp.concatenate([high, low], axis=0)  14.8 us
    all_to_all x2, waiting for transfers between devices, _halving(): lax.all_to_all(gridded, 'chan', split_axis=1, concat_axis=2, tiled=True)  13.2 us
  transfers between devices with their start and end apart: 10, of which 7 were waited for; matrix products, arithmetic and copies ran while one was open for 31% of the time, Pallas kernels for 0%

profile of v4, /device:TPU:0, one launch (start us, length us, event | category | flops | bytes accessed | tf_op | source)
XLA Modules:
  0.0 337.5 jit_solution(8228332296763254499)
XLA Ops:
  4.7 11.7 %copy.38 = bf16[12288,2,256]{2,0,1:T(8,128)(2,1)} copy(bf16[12288,2,256]{2,1,0:T(2,128)(2,1)} %param.7) | data formatting | bytes 25165824 | tf_op args[0]
  19.3 5.0 %add_bitcast_fusion.10 = (s32[96,128]{1,0:T(8,128)S(1)}, s32[96,128]{1,0:T(8,128)S(1)}, s32[96,128]{1,0:T(8,128)S(1)}, s32[96,128]{1,0:T(8,128)S(1)}, s32[96,128...) fusion(s32[12288]{0:T(1024)S(1)} %copy-done.6, s32[]{:T(128)} %bitcast.1, ...), kind=kLoop, calls=%fused_computation.87 | loop fusion | flops 98304 | bytes 442400 | tf_op jit(solution)/shard_map/add | solution.py:24
  24.3 9.4 %subtract_convert_fusion = (bf16[96,128,256]{2,1,0:T(8,128)(2,1)S(1)}, bf16[96,128,256]{2,1,0:T(8,128)(2,1)S(1)}) fusion(bf16[96,128,2,256]{3,1,0,2:T(8,128)(2,1)} %bitcast.115, f32[96,128]{1,0:T(8,128)S(1)} %bitcast.126, s32[96,128]{1,0:T(8,128)S(1)} %get-tuple-element.20, f32[96,128]{1,0:T(8,128)S(1)} %bitcast.128, s32[96,128]{1,0:T(8,128)S(1)} %get-tuple-element.21, ...), kind=kOutput, calls=%fused_computation.8 | convolution fusion | flops 855638016 | bytes 19660800 | tf_op jit(solution)/shard_map/bcr,brf->bcf/dot_general | solution.py:63
  33.7 7.3 %pad_maximum_fusion.1 = bf16[192,128,256]{2,1,0:T(8,128)(2,1)} fusion(bf16[96,128,256]{2,1,0:T(8,128)(2,1)S(1)} %get-tuple-element.2, bf16[96,128,256]{2,1,0:T(8,128)(2,1)S(1)} %get-tuple-element.3), kind=kLoop, calls=%fused_computation.3 | loop fusion | flops 6291456 | bytes 25165824 | tf_op jit(solution)/shard_map/concatenate | solution.py:69
  41.0 17.0 %fusion.7 = bf16[152,128,256]{2,0,1:T(8,128)(2,1)} fusion(bf16[192,128,256]{2,1,0:T(8,128)(2,1)} %pad_maximum_fusion.1, pred[152,96]{1,0:T(8,128)(4,1)S(1)} %iota_compare_fusion.8), kind=kOutput, calls=%fused_computation.13 | convolution fusion | flops 1917612544 | bytes 22558976 | tf_op jit(solution)/shard_map/sb,bcf->scf/dot_general | solution.py:66
  58.0 10.0 %copy.46 = bf16[152,128,256]{2,1,0:T(8,128)(2,1)} copy(bf16[152,128,256]{2,0,1:T(8,128)(2,1)} %fusion.7) | data formatting | bytes 19922944 | tf_op jit(solution)/shard_map/convert_element_type | solution.py:71
  68.0 5.2 %dynamic-slice_bitcast_fusion = bf16[4,19,128,256]{3,2,1,0:T(8,128)(2,1)} fusion(bf16[2,4,19,128,256]{4,3,2,1,0:T(8,128)(2,1)} %bitcast.103, s32[]{:T(128)S(6)} %select_n.112), kind=kLoop, calls=%fused_computation.34 | loop fusion | bytes 9961476 | tf_op jit(solution)/shard_map/jit(dynamic_index_in_dim)/squeeze | solution.py:75
  73.7 9.4 %subtract_convert_fusion.1 = (bf16[96,128,256]{2,1,0:T(8,128)(2,1)S(1)}, bf16[96,128,256]{2,1,0:T(8,128)(2,1)S(1)}) fusion(bf16[96,128,2,256]{3,1,0,2:T(8,128)(2,1)} %bitcast.116, f32[96,128]{1,0:T(8,128)S(1)} %bitcast.127, s32[96,128]{1,0:T(8,128)S(1)} %get-tuple-element.20, f32[96,128]{1,0:T(8,128)S(1)} %bitcast.129, s32[96,128]{1,0:T(8,128)S(1)} %get-tuple-element.21, ...), kind=kOutput, calls=%fused_computation.9 | convolution fusion | flops 855638016 | bytes 19660800 | tf_op jit(solution)/shard_map/bcr,brf->bcf/dot_general | solution.py:63
  83.1 7.5 %pad_maximum_fusion = bf16[192,128,256]{2,1,0:T(8,128)(2,1)} fusion(bf16[96,128,256]{2,1,0:T(8,128)(2,1)S(1)} %get-tuple-element.4, bf16[96,128,256]{2,1,0:T(8,128)(2,1)S(1)} %get-tuple-element.5), kind=kLoop, calls=%fused_computation.2 | loop fusion | flops 6291456 | bytes 25165824 | tf_op jit(solution)/shard_map/concatenate | solution.py:69
  90.6 17.1 %fusion.4 = bf16[152,128,256]{2,0,1:T(8,128)(2,1)} fusion(bf16[192,128,256]{2,1,0:T(8,128)(2,1)} %pad_maximum_fusion, pred[152,96]{1,0:T(8,128)(4,1)S(1)} %iota_compare_fusion.8), kind=kOutput, calls=%fused_computation.12 | convolution fusion | flops 1917612544 | bytes 22558976 | tf_op jit(solution)/shard_map/sb,bcf->scf/dot_general | solution.py:66
  107.6 10.1 %copy.40 = bf16[152,128,256]{2,1,0:T(8,128)(2,1)} copy(bf16[152,128,256]{2,0,1:T(8,128)(2,1)} %fusion.4) | data formatting | bytes 19922944 | tf_op jit(solution)/shard_map/convert_element_type | solution.py:71
  117.7 5.3 %dynamic-slice_bitcast_fusion.1 = bf16[4,19,128,256]{3,2,1,0:T(8,128)(2,1)} fusion(bf16[2,4,19,128,256]{4,3,2,1,0:T(8,128)(2,1)} %bitcast.105, s32[]{:T(128)S(6)} %select_n.112), kind=kLoop, calls=%fused_computation.35 | loop fusion | bytes 9961476 | tf_op jit(solution)/shard_map/jit(dynamic_index_in_dim)/squeeze | solution.py:75
  123.0 6.1 %convert_add_fusion = f32[4,19,128,256]{3,2,1,0:T(8,128)S(1)} fusion(bf16[4,19,128,256]{3,2,1,0:T(8,128)(2,1)} %collective-permute-done.3, bf16[2,4,19,128,256]{4,3,2,1,0:T(8,128)(2,1)} %bitcast.104, s32[]{:T(128)S(6)} %select_n.111), kind=kLoop, calls=%fused_computation.10 | loop fusion | flops 7471104 | bytes 19922948 | tf_op jit(solution)/shard_map/add | solution.py:83
  136.2 5.9 %convert_add_fusion.1 = f32[4,19,128,256]{3,2,1,0:T(8,128)S(1)} fusion(bf16[4,19,128,256]{3,2,1,0:T(8,128)(2,1)} %collective-permute-done, bf16[2,4,19,128,256]{4,3,2,1,0:T(8,128)(2,1)} %bitcast.106, s32[]{:T(128)S(6)} %select_n.111), kind=kLoop, calls=%fused_computation.11 | loop fusion | flops 7471104 | bytes 19922948 | tf_op jit(solution)/shard_map/add | solution.py:83
  149.3 41.3 %collective-permute-done.4 = bf16[2,19,128,256]{3,2,1,0:T(8,128)(2,1)} collective-permute-done((bf16[2,19,128,256]{3,2,1,0:T(8,128)(2,1)S(1)}, bf16[2,19,128,256]{3,2,1,0:T(8,128)(2,1)}, u32[]{:S(2)}, u32[]{:S(2)}) %collective-permute-start.4) | collective-permute-done | bytes 2490400 | tf_op jit(solution)/shard_map/ppermute | solution.py:92
  198.7 31.7 %collective-permute-done.5 = bf16[19,128,256]{2,1,0:T(8,128)(2,1)S(1)} collective-permute-done((bf16[19,128,256]{2,1,0:T(8,128)(2,1)S(1)}, bf16[19,128,256]{2,1,0:T(8,128)(2,1)S(1)}, u32[]{:S(2)}, u32[]{:S(2)}) %collective-permute-start.5) | collective-permute-done | bytes 1245216 | tf_op jit(solution)/shard_map/ppermute | solution.py:92
  234.3 4.9 %all-to-all-start.1 = ((bf16[19,128,256]{2,0,1:T(8,128)(2,1)}), bf16[19,128,256]{2,0,1:T(8,128)(2,1)S(1)}, u32[]{:S(2)}, u32[]{:S(2)}) async-start(bf16[19,128,256]{2,0,1:T(8,128)(2,1)} %copy.47), calls=%async_computation.1 | async-start | bytes 3145728 | tf_op jit(solution)/shard_map/all_to_all | solution.py:99
  243.8 27.4 %collective-permute-done.2 = bf16[19,128,256]{2,1,0:T(8,128)(2,1)S(1)} collective-permute-done((bf16[19,128,256]{2,1,0:T(8,128)(2,1)S(1)}, bf16[19,128,256]{2,1,0:T(8,128)(2,1)S(1)}, u32[]{:S(2)}, u32[]{:S(2)}) %collective-permute-start.2) | collective-permute-done | bytes 1245216 | tf_op jit(solution)/shard_map/ppermute | solution.py:92
  278.8 4.6 %convert_element_type.169 = f32[19,32,2048]{2,1,0:T(8,128)} convert(bf16[19,32,2048]{2,1,0:T(8,128)(2,1)} %param.13) | non-fusion elementwise | flops 1245184 | bytes 7471104 | tf_op jit(solution)/shard_map/convert_element_type | solution.py:170
  283.4 19.1 %multiply_convert_fusion = (bf16[1024,1024]{1,0:T(8,128)(2,1)}, bf16[1024,1024]{1,0:T(8,128)(2,1)}, bf16[1024,1024]{1,0:T(8,128)(2,1)}) fusion(f32[1024]{0:T(1024)S(1)} %subtract_multiply_fusion), kind=kLoop, calls=%fused_computation.47 | loop fusion | flops 22020096 | bytes 6295552 | tf_op jit(solution)/shard_map/convert.13
  303.8 11.4 %all-to-all-done = bf16[19,128,256]{2,0,1:T(8,128)(2,1)S(1)} async-done(((bf16[19,128,256]{2,0,1:T(8,128)(2,1)}), bf16[19,128,256]{2,0,1:T(8,128)(2,1)S(1)}, u32[]{:S(2)}, u32[]{:S(2)}) %all-to-all-start) | async-done | bytes 1245216 | tf_op jit(solution)/shard_map/all_to_all | solution.py:99
  316.6 5.1 %fusion.15 = f32[608,2048]{1,0:T(8,128)S(1)} fusion(bf16[608,1024]{1,0:T(8,128)(2,1)S(1)} %bitcast.122, bf16[1024,1024]{1,0:T(8,128)(2,1)} %get-tuple-element.23, bf16[1024,1024]{1,0:T(8,128)(2,1)} %get-tuple-element.24), kind=kOutput, calls=%fused_computation.39 | convolution fusion | flops 2558525440 | bytes 10420224 | tf_op jit(solution)/shard_map/dot_general | solution.py:163
  326.0 4.6 %collective-permute-done.6 = f32[19,1024]{1,0:T(8,128)S(1)} collective-permute-done((f32[19,1024]{1,0:T(8,128)S(1)}, f32[19,1024]{1,0:T(8,128)S(1)}, u32[]{:S(2)}, u32[]{:S(2)}) %collective-permute-start.6) | collective-permute-done | bytes 77856 | tf_op jit(solution)/shard_map/ppermute | solution.py:56
  332.5 4.2 %collective-permute-done.7 = f32[19,1024]{1,0:T(8,128)S(1)} collective-permute-done((f32[19,1024]{1,0:T(8,128)S(1)}, f32[19,1024]{1,0:T(8,128)S(1)}, u32[]{:S(2)}, u32[]{:S(2)}) %collective-permute-start.7) | collective-permute-done | bytes 77856 | tf_op jit(solution)/shard_map/ppermute | solution.py:56
  (65 shorter events, 55.2 us)
Async XLA Ops:
  4.6 11.7 %copy-start.7 = (s32[96]{0:T(128)S(1)}, s32[96]{0:T(128)}, u32[]{:S(2)}) copy-start(s32[96]{0:T(128)} %param.11) | copy-start | bytes 1156
  4.7 11.7 %copy-start = (s32[80]{0:T(128)S(1)}, s32[80]{0:T(128)}, u32[]{:S(2)}) copy-start(s32[80]{0:T(128)} %param.12) | copy-start | bytes 964
  4.7 14.6 %copy-start.6 = (s32[12288]{0:T(1024)S(1)}, s32[12288]{0:T(1024)}, u32[]{:S(2)}) copy-start(s32[12288]{0:T(1024)} %param.8) | copy-start | bytes 147460
  73.2 49.8 %collective-permute-start.3 = (bf16[4,19,128,256]{3,2,1,0:T(8,128)(2,1)}, bf16[4,19,128,256]{3,2,1,0:T(8,128)(2,1)}, u32[]{:S(2)}, u32[]{:S(2)}) collective-permute-start(bf16[4,19,128,256]{3,2,1,0:T(8,128)(2,1)} %dynamic-slice_bitcast_fusion), channel_id=1, source_target_pairs={{0,4},{4,0},{8,12},{12,8},{16,20},{20,16},{24,28},{28,24},{1,5},{5... | collective-permute-start | bytes 14942216 | tf_op jit(solution)/shard_map/ppermute | solution.py:76
  123.0 13.3 %collective-permute-start = (bf16[4,19,128,256]{3,2,1,0:T(8,128)(2,1)}, bf16[4,19,128,256]{3,2,1,0:T(8,128)(2,1)}, u32[]{:S(2)}, u32[]{:S(2)}) collective-permute-start(bf16[4,19,128,256]{3,2,1,0:T(8,128)(2,1)} %dynamic-slice_bitcast_fusion.1), channel_id=1, source_target_pairs={{0,4},{4,0},{8,12},{12,8},{16,20},{20,16},{24,28},{28,24},{1,5},{5... | collective-permute-start | bytes 14942216 | tf_op jit(solution)/shard_map/ppermute | solution.py:76
  129.1 3.8 %copy-start.2 = (f32[4,19,128,256]{3,2,1,0:T(8,128)}, f32[4,19,128,256]{3,2,1,0:T(8,128)S(1)}, u32[]{:S(2)}) copy-start(f32[4,19,128,256]{3,2,1,0:T(8,128)S(1)} %convert_add_fusion) | copy-start | bytes 29884420
  133.2 57.4 %collective-permute-start.4 = (bf16[2,19,128,256]{3,2,1,0:T(8,128)(2,1)S(1)}, bf16[2,19,128,256]{3,2,1,0:T(8,128)(2,1)}, u32[]{:S(2)}, u32[]{:S(2)}) collective-permute-start(bf16[2,19,128,256]{3,2,1,0:T(8,128)(2,1)S(1)} %fusion.29), channel_id=1, source_target_pairs={{0,16},{4,20},{8,24},{12,28},{16,0},{20,4},{24,8},{28,12},{1,17},{... | collective-permute-start | bytes 7471112 | tf_op jit(solution)/shard_map/ppermute | solution.py:92
  142.2 3.8 %copy-start.1 = (f32[4,19,128,256]{3,2,1,0:T(8,128)}, f32[4,19,128,256]{3,2,1,0:T(8,128)S(1)}, u32[]{:S(2)}) copy-start(f32[4,19,128,256]{3,2,1,0:T(8,128)S(1)} %convert_add_fusion.1) | copy-start | bytes 29884420
  147.8 91.4 %collective-permute-start.1 = (bf16[2,19,128,256]{3,2,1,0:T(8,128)(2,1)}, bf16[2,19,128,256]{3,2,1,0:T(8,128)(2,1)}, u32[]{:S(2)}, u32[]{:S(2)}) collective-permute-start(bf16[2,19,128,256]{3,2,1,0:T(8,128)(2,1)} %fusion.30), channel_id=1, source_target_pairs={{0,8},{4,12},{8,0},{12,4},{16,24},{20,28},{24,16},{28,20},{1,9},{5... | collective-permute-start | bytes 7471112 | tf_op jit(solution)/shard_map/ppermute | solution.py:92
  194.5 2.3 copy-start.3
  196.9 33.5 %collective-permute-start.5 = (bf16[19,128,256]{2,1,0:T(8,128)(2,1)S(1)}, bf16[19,128,256]{2,1,0:T(8,128)(2,1)S(1)}, u32[]{:S(2)}, u32[]{:S(2)}) collective-permute-start(bf16[19,128,256]{2,1,0:T(8,128)(2,1)S(1)} %fusion.37), channel_id=1, source_target_pairs={{0,8},{4,12},{8,0},{12,4},{16,24},{20,28},{24,16},{28,20},{1,9},{5... | collective-permute-start | bytes 3735560 | tf_op jit(solution)/shard_map/ppermute | solution.py:92
  234.3 40.9 %all-to-all-start.1 = ((bf16[19,128,256]{2,0,1:T(8,128)(2,1)}), bf16[19,128,256]{2,0,1:T(8,128)(2,1)S(1)}, u32[]{:S(2)}, u32[]{:S(2)}) async-start(bf16[19,128,256]{2,0,1:T(8,128)(2,1)} %copy.47), calls=%async_computation.1 | async-start | bytes 3145728 | tf_op jit(solution)/shard_map/all_to_all | solution.py:99
  243.3 28.0 %collective-permute-start.2 = (bf16[19,128,256]{2,1,0:T(8,128)(2,1)S(1)}, bf16[19,128,256]{2,1,0:T(8,128)(2,1)S(1)}, u32[]{:S(2)}, u32[]{:S(2)}) collective-permute-start(bf16[19,128,256]{2,1,0:T(8,128)(2,1)S(1)} %fusion.36), channel_id=1, source_target_pairs={{0,16},{4,20},{8,24},{12,28},{16,0},{20,4},{24,8},{28,12},{1,17},{... | collective-permute-start | bytes 3735560 | tf_op jit(solution)/shard_map/ppermute | solution.py:92
  275.2 40.1 %all-to-all-start = ((bf16[19,128,256]{2,0,1:T(8,128)(2,1)}), bf16[19,128,256]{2,0,1:T(8,128)(2,1)S(1)}, u32[]{:S(2)}, u32[]{:S(2)}) async-start(bf16[19,128,256]{2,0,1:T(8,128)(2,1)} %copy.42), calls=%async_computation | async-start | bytes 3145728 | tf_op jit(solution)/shard_map/all_to_all | solution.py:99
  316.3 8.2 %slice-start = ((s8[4980736]{0:T(1024)(128)(4,1)}), s8[4194304]{0:T(1024)(128)(4,1)S(1)}, s32[]{:S(2)}) async-start(s8[4980736]{0:T(1024)(128)(4,1)} %bitcast.111), calls=%async_computation.2 | async-start | bytes 8388608
  316.5 5.2 %copy-start.4 = (bf16[1024,1024]{1,0:T(8,128)(2,1)S(1)}, bf16[1024,1024]{1,0:T(8,128)(2,1)}, u32[]{:S(2)}) copy-start(bf16[1024,1024]{1,0:T(8,128)(2,1)} %get-tuple-element.22) | copy-start | bytes 6291460
  316.6 5.2 %copy-start.5 = (bf16[1024,1024]{1,0:T(8,128)(2,1)S(1)}, bf16[1024,1024]{1,0:T(8,128)(2,1)}, u32[]{:S(2)}) copy-start(bf16[1024,1024]{1,0:T(8,128)(2,1)} %get-tuple-element.24) | copy-start | bytes 6291460
  316.6 8.0 %slice-start.1 = ((s8[4980736]{0:T(1024)(128)(4,1)}), s8[786432]{0:T(1024)(128)(4,1)S(1)}, s32[]{:S(2)}) async-start(s8[4980736]{0:T(1024)(128)(4,1)} %bitcast.111), calls=%async_computation.3 | async-start | bytes 1572864
  325.9 4.7 %collective-permute-start.6 = (f32[19,1024]{1,0:T(8,128)S(1)}, f32[19,1024]{1,0:T(8,128)S(1)}, u32[]{:S(2)}, u32[]{:S(2)}) collective-permute-start(f32[19,1024]{1,0:T(8,128)S(1)} %fusion.32), channel_id=1, source_target_pairs={{0,1},{1,0},{2,3},{3,2},{4,5},{5,4},{6,7},{7,6},{8,9},{9,8},{10,11... | collective-permute-start | bytes 233480 | tf_op jit(solution)/shard_map/ppermute | solution.py:56
  330.6 6.1 %collective-permute-start.7 = (f32[19,1024]{1,0:T(8,128)S(1)}, f32[19,1024]{1,0:T(8,128)S(1)}, u32[]{:S(2)}, u32[]{:S(2)}) collective-permute-start(f32[19,1024]{1,0:T(8,128)S(1)} %add.301), channel_id=1, source_target_pairs={{0,2},{1,3},{2,0},{3,1},{4,6},{5,7},{6,4},{7,5},{8,10},{9,11},{10,... | collective-permute-start | bytes 233480 | tf_op jit(solution)/shard_map/ppermute | solution.py:56

commit v5 on v3

--- a/solution.py
+++ b/solution.py
@@ -124,6 +124,7 @@
     table = delay_table()
     first = _gather_pair(blocks[:, :, 0, :], matrix, pick2, parity, chip, n_owners, slots_dev)
     second = _gather_pair(blocks[:, :, 1, :], matrix, pick2, parity, chip, n_owners, slots_dev)
+    table, second = lax.optimization_barrier((table, second))
     out = None
     for k, (pair_send, own) in enumerate((first, second)):
         piece = _scatter_pairs(pair_send, own, chip, n_owners)

time: 332 us -> 329 us (level)
  waiting for transfers between devices: 123 us -> 98 us
  other arithmetic: 68.7 us -> 87.5 us
    ppermute x6, waiting for transfers between devices: 107 us -> 62.8 us  [_scatter_pairs(): lax.ppermute(send, 'uv', _partner_pairs(n_owners, lambda i, dest=dest: de...]
    all_to_all x2, waiting for transfers between devices: 7.61 us -> 26.8 us  [_scatter_pairs(): lax.all_to_all(gridded, 'chan', split_axis=1, concat_axis=2, tiled=True)]
    concatenate x0 -> x1, other arithmetic: none -> 17.1 us  [delay_table(): return jnp.concatenate([upper, lower], axis=0).astype(jnp.bfloat16)]
    unnamed x19 -> x17, local copies, waits for them, and re-layouts: 13.2 us -> 12.2 us
  transfers between devices with their start and end apart: 12 -> 12, of which waited for: 7 -> 6; matrix products, arithmetic and copies ran while one was open for 31% -> 36% of each run, Pallas kernels for 0% -> 0%
where the time goes in v5:
time: 329 us; the launch traced here: 323 us
  waiting for transfers between devices  98 us (30%)
  other arithmetic  87.5 us (27%)
  matrix products  60.4 us (18%)
  local copies, waits for them, and re-layouts  56.7 us (17%)
  starting transfers between devices  19.2 us (6%)
    ppermute x6, waiting for transfers between devices, _scatter_pairs(): lax.ppermute(send, 'uv', _partner_pairs(n_owners, lambda i, dest=dest: de...  62.8 us
    dot_general x2, matrix products, _gather_pair(): jnp.einsum('sb,bcf->scf', pick2, jnp.concatenate([high, low], axis=0), pr...  34.1 us
    all_to_all x2, waiting for transfers between devices, _scatter_pairs(): lax.all_to_all(gridded, 'chan', split_axis=1, concat_axis=2, tiled=True)  26.8 us
    convert_element_type x2, local copies, waits for them, and re-layouts, _gather_pair(): partial = jnp.einsum('sb,bcf->scf', pick2, jnp.concatenate([high, low], a...  20 us
    dot_general x2, matrix products, _gather_pair(): jnp.einsum('bcr,brf->bcf', matrix, part, preferred_element_type=jnp.float32)  18.7 us
    another operation x1, other arithmetic  18.5 us
    concatenate x1, other arithmetic, delay_table(): return jnp.concatenate([upper, lower], axis=0).astype(jnp.bfloat16)  17.1 us
    concatenate x2, other arithmetic, _gather_pair(): jnp.concatenate([high, low], axis=0)  14.9 us
  transfers between devices with their start and end apart: 12, of which 6 were waited for; matrix products, arithmetic and copies ran while one was open for 36% of the time, Pallas kernels for 0%

profile of v5, /device:TPU:0, one launch (start us, length us, event | category | flops | bytes accessed | tf_op | source)
XLA Modules:
  0.0 322.9 jit_solution(12686601151298603156)
XLA Ops:
  4.4 11.7 %copy.22 = bf16[12288,2,256]{2,0,1:T(8,128)(2,1)} copy(bf16[12288,2,256]{2,1,0:T(2,128)(2,1)} %param.7) | data formatting | bytes 25165824 | tf_op args[0]
  19.1 5.2 %add_bitcast_fusion.10 = (s32[96,128]{1,0:T(8,128)S(1)}, s32[96,128]{1,0:T(8,128)S(1)}, s32[96,128]{1,0:T(8,128)S(1)}, s32[96,128]{1,0:T(8,128)S(1)}, s32[96,128...) fusion(s32[12288]{0:T(1024)S(1)} %copy-done.1, s32[]{:T(128)} %bitcast.1, ...), kind=kLoop, calls=%fused_computation.85 | loop fusion | flops 98304 | bytes 442400 | tf_op jit(solution)/shard_map/add | solution.py:24
  24.3 9.4 %subtract_convert_fusion.1 = (bf16[96,128,256]{2,1,0:T(8,128)(2,1)S(1)}, bf16[96,128,256]{2,1,0:T(8,128)(2,1)S(1)}) fusion(bf16[96,128,2,256]{3,1,0,2:T(8,128)(2,1)} %bitcast.109, f32[96,128]{1,0:T(8,128)S(1)} %bitcast.122, s32[96,128]{1,0:T(8,128)S(1)} %get-tuple-element.32, f32[96,128]{1,0:T(8,128)S(1)} %bitcast.124, s32[96,128]{1,0:T(8,128)S(1)} %get-tuple-element.33, ...), kind=kOutput, calls=%fused_computation.9 | convolution fusion | flops 855638016 | bytes 19660800 | tf_op jit(solution)/shard_map/bcr,brf->bcf/dot_general | solution.py:63
  33.7 7.3 %pad_maximum_fusion = bf16[192,128,256]{2,1,0:T(8,128)(2,1)} fusion(bf16[96,128,256]{2,1,0:T(8,128)(2,1)S(1)} %get-tuple-element.8, bf16[96,128,256]{2,1,0:T(8,128)(2,1)S(1)} %get-tuple-element.9), kind=kLoop, calls=%fused_computation.2 | loop fusion | flops 6291456 | bytes 25165824 | tf_op jit(solution)/shard_map/concatenate | solution.py:69
  41.0 17.1 %fusion.6 = bf16[152,128,256]{2,0,1:T(8,128)(2,1)} fusion(bf16[192,128,256]{2,1,0:T(8,128)(2,1)} %pad_maximum_fusion, pred[152,96]{1,0:T(8,128)(4,1)S(1)} %iota_compare_fusion.8), kind=kOutput, calls=%fused_computation.15 | convolution fusion | flops 1917612544 | bytes 22558976 | tf_op jit(solution)/shard_map/sb,bcf->scf/dot_general | solution.py:66
  58.1 10.1 %copy.24 = bf16[152,128,256]{2,1,0:T(8,128)(2,1)} copy(bf16[152,128,256]{2,0,1:T(8,128)(2,1)} %fusion.6) | data formatting | bytes 19922944 | tf_op jit(solution)/shard_map/convert_element_type | solution.py:71
  68.1 5.2 %dynamic-slice_bitcast_fusion.1 = bf16[4,19,128,256]{3,2,1,0:T(8,128)(2,1)} fusion(bf16[2,4,19,128,256]{4,3,2,1,0:T(8,128)(2,1)} %bitcast.99, s32[]{:T(128)S(6)} %select_n.120), kind=kLoop, calls=%fused_computation.34 | loop fusion | bytes 9961476 | tf_op jit(solution)/shard_map/jit(dynamic_index_in_dim)/squeeze | solution.py:75
  73.8 9.4 %subtract_convert_fusion = (bf16[96,128,256]{2,1,0:T(8,128)(2,1)S(1)}, bf16[96,128,256]{2,1,0:T(8,128)(2,1)S(1)}) fusion(bf16[96,128,2,256]{3,1,0,2:T(8,128)(2,1)} %bitcast.110, f32[96,128]{1,0:T(8,128)S(1)} %bitcast.123, s32[96,128]{1,0:T(8,128)S(1)} %get-tuple-element.32, f32[96,128]{1,0:T(8,128)S(1)} %bitcast.125, s32[96,128]{1,0:T(8,128)S(1)} %get-tuple-element.33, ...), kind=kOutput, calls=%fused_computation.8 | convolution fusion | flops 855638016 | bytes 19660800 | tf_op jit(solution)/shard_map/bcr,brf->bcf/dot_general | solution.py:63
  83.2 7.6 %pad_maximum_fusion.1 = bf16[192,128,256]{2,1,0:T(8,128)(2,1)} fusion(bf16[96,128,256]{2,1,0:T(8,128)(2,1)S(1)} %get-tuple-element.10, bf16[96,128,256]{2,1,0:T(8,128)(2,1)S(1)} %get-tuple-element.11), kind=kLoop, calls=%fused_computation.3 | loop fusion | flops 6291456 | bytes 25165824 | tf_op jit(solution)/shard_map/concatenate | solution.py:69
  90.8 17.0 %fusion.9 = bf16[152,128,256]{2,0,1:T(8,128)(2,1)} fusion(bf16[192,128,256]{2,1,0:T(8,128)(2,1)} %pad_maximum_fusion.1, pred[152,96]{1,0:T(8,128)(4,1)S(1)} %iota_compare_fusion.8), kind=kOutput, calls=%fused_computation.16 | convolution fusion | flops 1917612544 | bytes 22558976 | tf_op jit(solution)/shard_map/sb,bcf->scf/dot_general | solution.py:66
  107.8 9.9 %copy.28 = bf16[152,128,256]{2,1,0:T(8,128)(2,1)} copy(bf16[152,128,256]{2,0,1:T(8,128)(2,1)} %fusion.9) | data formatting | bytes 19922944 | tf_op jit(solution)/shard_map/convert_element_type | solution.py:71
  117.8 5.2 %dynamic-slice_bitcast_fusion = bf16[4,19,128,256]{3,2,1,0:T(8,128)(2,1)} fusion(bf16[2,4,19,128,256]{4,3,2,1,0:T(8,128)(2,1)} %bitcast.102, s32[]{:T(128)S(6)} %select_n.120), kind=kLoop, calls=%fused_computation.33 | loop fusion | bytes 9961476 | tf_op jit(solution)/shard_map/jit(dynamic_index_in_dim)/squeeze | solution.py:75
  123.1 6.2 %fusion.5 = bf16[4,19,128,256]{3,2,1,0:T(8,128)(2,1)S(1)} fusion(bf16[4,19,128,256]{3,2,1,0:T(8,128)(2,1)} %collective-permute-done, bf16[2,4,19,128,256]{4,3,2,1,0:T(8,128)(2,1)} %bitcast.100, s32[]{:T(128)S(6)} %select_n.115), kind=kLoop, calls=%fused_computation.13 | loop fusion | flops 9961472 | bytes 14942212 | tf_op jit(solution)/shard_map/convert_element_type | solution.py:77
  135.8 18.5 %multiply_convert_fusion.1 = (bf16[1024,1024]{1,0:T(8,128)(2,1)S(1)}, bf16[1024,1024]{1,0:T(8,128)(2,1)}, bf16[1024,1024]{1,0:T(8,128)(2,1)}) fusion(f32[1024]{0:T(1024)S(1)} %subtract_multiply_fusion), kind=kLoop, calls=%fused_computation.43 | loop fusion | flops 22020096 | bytes 6295552 | tf_op jit(solution)/shard_map/convert.20
  154.3 17.1 %maximum_maximum_fusion = bf16[2048,2048]{1,0:T(8,128)(2,1)} fusion(bf16[1024,1024]{1,0:T(8,128)(2,1)} %get-tuple-element.36, bf16[1024,1024]{1,0:T(8,128)(2,1)} %get-tuple-element.35, bf16[1024,1024]{1,0:T(8,128)(2,1)S(1)} %get-tuple-element.34), kind=kLoop, calls=%fused_computation.14 | loop fusion | flops 33554432 | bytes 14680064 | tf_op jit(solution)/shard_map/concatenate | solution.py:44
  171.4 8.4 %fusion.4 = bf16[4,19,128,256]{3,2,1,0:T(8,128)(2,1)} fusion(bf16[4,19,128,256]{3,2,1,0:T(8,128)(2,1)} %collective-permute-done.4, bf16[2,4,19,128,256]{4,3,2,1,0:T(8,128)(2,1)} %bitcast.103, s32[]{:T(128)S(6)} %select_n.115), kind=kLoop, calls=%fused_computation.11 | loop fusion | flops 9961472 | bytes 14942212 | tf_op jit(solution)/shard_map/convert_element_type | solution.py:77
  179.7 10.5 %collective-permute-done.2 = bf16[19,128,256]{2,1,0:T(8,128)(2,1)} collective-permute-done((bf16[19,128,256]{2,1,0:T(8,128)(2,1)}, bf16[19,128,256]{2,1,0:T(8,128)(2,1)}, u32[]{:S(2)}, u32[]{:S(2)}) %collective-permute-start.2) | collective-permute-done | bytes 1245216 | tf_op jit(solution)/shard_map/ppermute | solution.py:93
  195.5 5.1 %all-to-all-start = ((bf16[19,128,256]{2,0,1:T(8,128)(2,1)}), bf16[19,128,256]{2,0,1:T(8,128)(2,1)S(1)}, u32[]{:S(2)}, u32[]{:S(2)}) async-start(bf16[19,128,256]{2,0,1:T(8,128)(2,1)} %copy.25), calls=%async_computation | async-start | bytes 3145728 | tf_op jit(solution)/shard_map/all_to_all | solution.py:98
  208.5 26.8 %collective-permute-done.5 = bf16[19,128,256]{2,1,0:T(8,128)(2,1)S(1)} collective-permute-done((bf16[19,128,256]{2,1,0:T(8,128)(2,1)S(1)}, bf16[19,128,256]{2,1,0:T(8,128)(2,1)S(1)}, u32[]{:S(2)}, u32[]{:S(2)}) %collective-permute-start.5) | collective-permute-done | bytes 1245216 | tf_op jit(solution)/shard_map/ppermute | solution.py:93
  235.2 25.5 %collective-permute-done.6 = bf16[19,128,256]{2,1,0:T(8,128)(2,1)S(1)} collective-permute-done((bf16[19,128,256]{2,1,0:T(8,128)(2,1)S(1)}, bf16[19,128,256]{2,1,0:T(8,128)(2,1)S(1)}, u32[]{:S(2)}, u32[]{:S(2)}) %collective-permute-start.6) | collective-permute-done | bytes 1245216 | tf_op jit(solution)/shard_map/ppermute | solution.py:93
  263.4 4.8 %all-to-all-start.1 = ((bf16[19,128,256]{2,0,1:T(8,128)(2,1)}), bf16[19,128,256]{2,0,1:T(8,128)(2,1)S(1)}, u32[]{:S(2)}, u32[]{:S(2)}) async-start(bf16[19,128,256]{2,0,1:T(8,128)(2,1)} %copy.29), calls=%async_computation.1 | async-start | bytes 3145728 | tf_op jit(solution)/shard_map/all_to_all | solution.py:98
  274.0 26.8 %all-to-all-done.1 = bf16[19,128,256]{2,0,1:T(8,128)(2,1)S(1)} async-done(((bf16[19,128,256]{2,0,1:T(8,128)(2,1)}), bf16[19,128,256]{2,0,1:T(8,128)(2,1)S(1)}, u32[]{:S(2)}, u32[]{:S(2)}) %all-to-all-start.1) | async-done | bytes 1245216 | tf_op jit(solution)/shard_map/all_to_all | solution.py:98
  302.2 4.7 %fusion.17 = f32[608,2048]{1,0:T(8,128)S(1)} fusion(bf16[608,1024]{1,0:T(8,128)(2,1)S(1)} %bitcast.118, bf16[2048,2048]{1,0:T(8,128)(2,1)} %maximum_maximum_fusion), kind=kOutput, calls=%fused_computation.38 | convolution fusion | flops 2550136832 | bytes 10420224 | tf_op jit(solution)/shard_map/dot_general | solution.py:132
  311.1 4.6 %collective-permute-done.8 = f32[19,1024]{1,0:T(8,128)S(1)} collective-permute-done((f32[19,1024]{1,0:T(8,128)S(1)}, f32[19,1024]{1,0:T(8,128)S(1)}, u32[]{:S(2)}, u32[]{:S(2)}) %collective-permute-start.8) | collective-permute-done | bytes 77856 | tf_op jit(solution)/shard_map/ppermute | solution.py:56
  (62 shorter events, 47.6 us)
Async XLA Ops:
  4.4 11.7 %copy-start.2 = (s32[96]{0:T(128)S(1)}, s32[96]{0:T(128)}, u32[]{:S(2)}) copy-start(s32[96]{0:T(128)} %param.11) | copy-start | bytes 1156
  4.4 11.7 %copy-start = (s32[80]{0:T(128)S(1)}, s32[80]{0:T(128)}, u32[]{:S(2)}) copy-start(s32[80]{0:T(128)} %param.12) | copy-start | bytes 964
  4.4 14.6 %copy-start.1 = (s32[12288]{0:T(1024)S(1)}, s32[12288]{0:T(1024)}, u32[]{:S(2)}) copy-start(s32[12288]{0:T(1024)} %param.8) | copy-start | bytes 147460
  73.3 49.7 %collective-permute-start = (bf16[4,19,128,256]{3,2,1,0:T(8,128)(2,1)}, bf16[4,19,128,256]{3,2,1,0:T(8,128)(2,1)}, u32[]{:S(2)}, u32[]{:S(2)}) collective-permute-start(bf16[4,19,128,256]{3,2,1,0:T(8,128)(2,1)} %dynamic-slice_bitcast_fusion.1), channel_id=1, source_target_pairs={{0,4},{4,0},{8,12},{12,8},{16,20},{20,16},{24,28},{28,24},{1,5},{5... | collective-permute-start | bytes 14942216 | tf_op jit(solution)/shard_map/ppermute | solution.py:76
  123.0 48.4 %collective-permute-start.4 = (bf16[4,19,128,256]{3,2,1,0:T(8,128)(2,1)}, bf16[4,19,128,256]{3,2,1,0:T(8,128)(2,1)}, u32[]{:S(2)}, u32[]{:S(2)}) collective-permute-start(bf16[4,19,128,256]{3,2,1,0:T(8,128)(2,1)} %dynamic-slice_bitcast_fusion), channel_id=1, source_target_pairs={{0,4},{4,0},{8,12},{12,8},{16,20},{20,16},{24,28},{28,24},{1,5},{5... | collective-permute-start | bytes 14942216 | tf_op jit(solution)/shard_map/ppermute | solution.py:76
  131.3 48.4 %collective-permute-start.1 = (bf16[19,128,256]{2,1,0:T(8,128)(2,1)}, bf16[19,128,256]{2,1,0:T(8,128)(2,1)S(1)}, u32[]{:S(2)}, u32[]{:S(2)}) collective-permute-start(bf16[19,128,256]{2,1,0:T(8,128)(2,1)} %get-tuple-element.12), channel_id=1, source_target_pairs={{0,8},{4,12},{8,0},{12,4},{16,24},{20,28},{24,16},{28,20},{1,9},{5... | collective-permute-start | bytes 3735560 | tf_op jit(solution)/shard_map/ppermute | solution.py:93
  134.2 56.0 %collective-permute-start.2 = (bf16[19,128,256]{2,1,0:T(8,128)(2,1)}, bf16[19,128,256]{2,1,0:T(8,128)(2,1)}, u32[]{:S(2)}, u32[]{:S(2)}) collective-permute-start(bf16[19,128,256]{2,1,0:T(8,128)(2,1)} %get-tuple-element.14), channel_id=1, source_target_pairs={{0,16},{4,20},{8,24},{12,28},{16,0},{20,4},{24,8},{28,12},{1,17},{... | collective-permute-start | bytes 3735560 | tf_op jit(solution)/shard_map/ppermute | solution.py:93
  135.8 54.5 %collective-permute-start.3 = (bf16[19,128,256]{2,1,0:T(8,128)(2,1)}, bf16[19,128,256]{2,1,0:T(8,128)(2,1)}, u32[]{:S(2)}, u32[]{:S(2)}) collective-permute-start(bf16[19,128,256]{2,1,0:T(8,128)(2,1)} %get-tuple-element.13), channel_id=1, source_target_pairs={{0,24},{4,28},{8,16},{12,20},{16,8},{20,12},{24,0},{28,4},{1,25},{... | collective-permute-start | bytes 3735560 | tf_op jit(solution)/shard_map/ppermute | solution.py:93
  195.5 67.9 %all-to-all-start = ((bf16[19,128,256]{2,0,1:T(8,128)(2,1)}), bf16[19,128,256]{2,0,1:T(8,128)(2,1)S(1)}, u32[]{:S(2)}, u32[]{:S(2)}) async-start(bf16[19,128,256]{2,0,1:T(8,128)(2,1)} %copy.25), calls=%async_computation | async-start | bytes 3145728 | tf_op jit(solution)/shard_map/all_to_all | solution.py:98
  204.9 30.3 %collective-permute-start.5 = (bf16[19,128,256]{2,1,0:T(8,128)(2,1)S(1)}, bf16[19,128,256]{2,1,0:T(8,128)(2,1)S(1)}, u32[]{:S(2)}, u32[]{:S(2)}) collective-permute-start(bf16[19,128,256]{2,1,0:T(8,128)(2,1)S(1)} %get-tuple-element.15), channel_id=1, source_target_pairs={{0,8},{4,12},{8,0},{12,4},{16,24},{20,28},{24,16},{28,20},{1,9},{5... | collective-permute-start | bytes 3735560 | tf_op jit(solution)/shard_map/ppermute | solution.py:93
  206.2 54.5 %collective-permute-start.6 = (bf16[19,128,256]{2,1,0:T(8,128)(2,1)S(1)}, bf16[19,128,256]{2,1,0:T(8,128)(2,1)S(1)}, u32[]{:S(2)}, u32[]{:S(2)}) collective-permute-start(bf16[19,128,256]{2,1,0:T(8,128)(2,1)S(1)} %get-tuple-element.17), channel_id=1, source_target_pairs={{0,16},{4,20},{8,24},{12,28},{16,0},{20,4},{24,8},{28,12},{1,17},{... | collective-permute-start | bytes 3735560 | tf_op jit(solution)/shard_map/ppermute | solution.py:93
  207.1 53.7 %collective-permute-start.7 = (bf16[19,128,256]{2,1,0:T(8,128)(2,1)S(1)}, bf16[19,128,256]{2,1,0:T(8,128)(2,1)S(1)}, u32[]{:S(2)}, u32[]{:S(2)}) collective-permute-start(bf16[19,128,256]{2,1,0:T(8,128)(2,1)S(1)} %get-tuple-element.16), channel_id=1, source_target_pairs={{0,24},{4,28},{8,16},{12,20},{16,8},{20,12},{24,0},{28,4},{1,25},{... | collective-permute-start | bytes 3735560 | tf_op jit(solution)/shard_map/ppermute | solution.py:93
  263.4 37.5 %all-to-all-start.1 = ((bf16[19,128,256]{2,0,1:T(8,128)(2,1)}), bf16[19,128,256]{2,0,1:T(8,128)(2,1)S(1)}, u32[]{:S(2)}, u32[]{:S(2)}) async-start(bf16[19,128,256]{2,0,1:T(8,128)(2,1)} %copy.29), calls=%async_computation.1 | async-start | bytes 3145728 | tf_op jit(solution)/shard_map/all_to_all | solution.py:98
  301.9 5.0 %slice-start.2 = ((s8[8388608]{0:T(1024)(128)(4,1)}), s8[4194304]{0:T(1024)(128)(4,1)S(1)}, s32[]{:S(2)}) async-start(s8[8388608]{0:T(1024)(128)(4,1)} %bitcast.111), calls=%async_computation.4 | async-start | bytes 8388608
  302.1 4.7 %slice-start.3 = ((s8[8388608]{0:T(1024)(128)(4,1)}), s8[4194304]{0:T(1024)(128)(4,1)S(1)}, s32[]{:S(2)}) async-start(s8[8388608]{0:T(1024)(128)(4,1)} %bitcast.111), calls=%async_computation.5 | async-start | bytes 8388608
  302.1 7.5 %slice-start = ((s8[4980736]{0:T(1024)(128)(4,1)}), s8[4194304]{0:T(1024)(128)(4,1)S(1)}, s32[]{:S(2)}) async-start(s8[4980736]{0:T(1024)(128)(4,1)} %bitcast.105), calls=%async_computation.2 | async-start | bytes 8388608
  306.9 2.8 slice-start.1
  311.1 4.7 %collective-permute-start.8 = (f32[19,1024]{1,0:T(8,128)S(1)}, f32[19,1024]{1,0:T(8,128)S(1)}, u32[]{:S(2)}, u32[]{:S(2)}) collective-permute-start(f32[19,1024]{1,0:T(8,128)S(1)} %fusion.28), channel_id=1, source_target_pairs={{0,1},{1,0},{2,3},{3,2},{4,5},{5,4},{6,7},{7,6},{8,9},{9,8},{10,11... | collective-permute-start | bytes 233480 | tf_op jit(solution)/shard_map/ppermute | solution.py:56
  315.8 6.2 %collective-permute-start.9 = (f32[19,1024]{1,0:T(8,128)S(1)}, f32[19,1024]{1,0:T(8,128)S(1)}, u32[]{:S(2)}, u32[]{:S(2)}) collective-permute-start(f32[19,1024]{1,0:T(8,128)S(1)} %add.325), channel_id=1, source_target_pairs={{0,2},{1,3},{2,0},{3,1},{4,6},{5,7},{6,4},{7,5},{8,10},{9,11},{10,... | collective-permute-start | bytes 233480 | tf_op jit(solution)/shard_map/ppermute | solution.py:56

commit v6 on v5

--- a/solution.py
+++ b/solution.py
@@ -94,8 +94,26 @@
             send, "uv", _partner_pairs(n_owners, lambda i, dest=dest: dest(i // 2) * 2 + i % 2)
         )
         grid = grid + recv.astype(jnp.float32)
-    gridded = grid.astype(jnp.bfloat16)
-    return lax.all_to_all(gridded, "chan", split_axis=1, concat_axis=2, tiled=True)
+    return grid.astype(jnp.bfloat16)
+
+
+def _chan_delay(gridded, table_half, n_chan):
+    me = lax.axis_index("chan")
+    cells_part = gridded.shape[1] // n_chan
+    width = gridded.shape[2]
+    out = None
+    for d in range(n_chan):
+        dest = (me + d) % n_chan
+        send = lax.dynamic_slice_in_dim(gridded, dest * cells_part, cells_part, axis=1)
+        if d == 0:
+            recv = send
+        else:
+            recv = lax.ppermute(send, "chan", [(i, (i + d) % n_chan) for i in range(n_chan)])
+        src = (me - d) % n_chan
+        rows = lax.dynamic_slice_in_dim(table_half, src * width, width, axis=0)
+        term = jnp.dot(recv.reshape(-1, width), rows, preferred_element_type=jnp.float32)
+        out = term if out is None else out + term
+    return out
 
 
 def body(vis, row_cell, tap_weight, tap_offset, block_tile, tile_owner, galaxy):
@@ -127,14 +145,10 @@
     table, second = lax.optimization_barrier((table, second))
     out = None
     for k, (pair_send, own) in enumerate((first, second)):
-        piece = _scatter_pairs(pair_send, own, chip, n_owners)
-        count, cells_part = piece.shape[0], piece.shape[1]
-        term = jnp.dot(
-            piece.reshape(count * cells_part, CH),
-            table[k * CH:(k + 1) * CH],
-            preferred_element_type=jnp.float32,
-        )
+        gridded = _scatter_pairs(pair_send, own, chip, n_owners)
+        term = _chan_delay(gridded, table[k * CH:(k + 1) * CH], n_chan)
         out = term if out is None else out + term
+    count, cells_part = slots_dev, TC // n_chan
     delay = out.reshape(count, cells_part, 2 * CH)
     galaxy_f = galaxy.astype(jnp.float32)
     product = delay[..., :CH] * galaxy_f[..., :CH] + delay[..., CH:] * galaxy_f[..., CH:]

time: 329 us -> 356 us (1.082)
  matrix products: 60.4 us -> 83 us
  starting transfers between devices: 19.2 us -> 33.1 us
  local copies, waits for them, and re-layouts: 56.7 us -> 52.9 us
    all_to_all x2 -> x0, waiting for transfers between devices: 26.8 us -> none  [_scatter_pairs(): lax.all_to_all(gridded, 'chan', split_axis=1, concat_axis=2, tiled=True)]
    dot_general x2 -> x8, matrix products: 7.48 us -> 29.8 us  [_chan_delay(): jnp.dot(recv.reshape(-1, width), rows, preferred_element_type=jnp.float32)]
    ppermute x6, waiting for transfers between devices: 62.8 us -> 82.3 us  [_scatter_pairs(): lax.ppermute(send, 'uv', _partner_pairs(n_owners, lambda i, dest=dest: de...]
    ppermute x0 -> x6, starting transfers between devices: none -> 11.7 us  [_chan_delay(): lax.ppermute(send, 'chan', [(i, (i + d) % n_chan) for i in range(n_chan)])]
    ppermute x2, starting transfers between devices: 0.76 us -> 11 us  [_allreduce_sum(): x = x + lax.ppermute(x, axis, _partner_pairs(n, lambda i, d=d: i ^ d))]
    all_to_all x2 -> x0, starting transfers between devices: 9.9 us -> none  [_scatter_pairs(): lax.all_to_all(gridded, 'chan', split_axis=1, concat_axis=2, tiled=True)]
    ppermute x0 -> x6, waiting for transfers between devices: none -> 8.2 us  [_chan_delay(): lax.ppermute(send, 'chan', [(i, (i + d) % n_chan) for i in range(n_chan)])]
    convert_element_type x2, other arithmetic: 14.6 us -> 10.7 us  [_gather_pair(): (mine.astype(jnp.float32) + got.astype(jnp.float32)).astype(jnp.bfloat16)]
  transfers between devices with their start and end apart: 12 -> 16, of which waited for: 6 -> 5; matrix products, arithmetic and copies ran while one was open for 36% -> 38% of each run, Pallas kernels for 0% -> 0%
where the time goes in v6:
time: 356 us; the launch traced here: 350 us
  waiting for transfers between devices  95.6 us (27%)
  other arithmetic  84 us (24%)
  matrix products  83 us (23%)
  local copies, waits for them, and re-layouts  52.9 us (15%)
  starting transfers between devices  33.1 us (9%)
    ppermute x6, waiting for transfers between devices, _scatter_pairs(): lax.ppermute(send, 'uv', _partner_pairs(n_owners, lambda i, dest=dest: de...  82.3 us
    dot_general x2, matrix products, _gather_pair(): jnp.einsum('sb,bcf->scf', pick2, jnp.concatenate([high, low], axis=0), pr...  34 us
    dot_general x8, matrix products, _chan_delay(): jnp.dot(recv.reshape(-1, width), rows, preferred_element_type=jnp.float32)  29.8 us
    convert_element_type x2, local copies, waits for them, and re-layouts, _gather_pair(): partial = jnp.einsum('sb,bcf->scf', pick2, jnp.concatenate([high, low], a...  20.1 us
    dot_general x2, matrix products, _gather_pair(): jnp.einsum('bcr,brf->bcf', matrix, part, preferred_element_type=jnp.float32)  19.1 us
    another operation x1, other arithmetic  18.7 us
    concatenate x1, other arithmetic, delay_table(): return jnp.concatenate([upper, lower], axis=0).astype(jnp.bfloat16)  17.2 us
    concatenate x2, other arithmetic, _gather_pair(): jnp.concatenate([high, low], axis=0)  14.5 us
  transfers between devices with their start and end apart: 16, of which 5 were waited for; matrix products, arithmetic and copies ran while one was open for 38% of the time, Pallas kernels for 0%

profile of v6, /device:TPU:0, one launch (start us, length us, event | category | flops | bytes accessed | tf_op | source)
XLA Modules:
  0.0 349.7 jit_solution(14033442299499751463)
XLA Ops:
  4.4 11.7 %copy.15 = bf16[12288,2,256]{2,0,1:T(8,128)(2,1)} copy(bf16[12288,2,256]{2,1,0:T(2,128)(2,1)} %param.7) | data formatting | bytes 25165824 | tf_op args[0]
  19.1 5.0 %add_bitcast_fusion.10 = (s32[96,128]{1,0:T(8,128)S(1)}, s32[96,128]{1,0:T(8,128)S(1)}, s32[96,128]{1,0:T(8,128)S(1)}, s32[96,128]{1,0:T(8,128)S(1)}, s32[96,128...) fusion(s32[12288]{0:T(1024)S(1)} %copy-done.2, s32[]{:T(128)} %bitcast.1, ...), kind=kLoop, calls=%fused_computation.97 | loop fusion | flops 98304 | bytes 442400 | tf_op jit(solution)/shard_map/add | solution.py:24
  24.1 9.4 %subtract_convert_fusion.1 = (bf16[96,128,256]{2,1,0:T(8,128)(2,1)S(1)}, bf16[96,128,256]{2,1,0:T(8,128)(2,1)S(1)}) fusion(bf16[96,128,2,256]{3,1,0,2:T(8,128)(2,1)} %bitcast.113, f32[96,128]{1,0:T(8,128)S(1)} %bitcast.126, s32[96,128]{1,0:T(8,128)S(1)} %get-tuple-element.42, f32[96,128]{1,0:T(8,128)S(1)} %bitcast.128, s32[96,128]{1,0:T(8,128)S(1)} %get-tuple-element.43, ...), kind=kOutput, calls=%fused_computation.9 | convolution fusion | flops 855638016 | bytes 19660800 | tf_op jit(solution)/shard_map/bcr,brf->bcf/dot_general | solution.py:63
  33.4 7.3 %pad_maximum_fusion = bf16[192,128,256]{2,1,0:T(8,128)(2,1)} fusion(bf16[96,128,256]{2,1,0:T(8,128)(2,1)S(1)} %get-tuple-element.8, bf16[96,128,256]{2,1,0:T(8,128)(2,1)S(1)} %get-tuple-element.9), kind=kLoop, calls=%fused_computation.2 | loop fusion | flops 6291456 | bytes 25165824 | tf_op jit(solution)/shard_map/concatenate | solution.py:69
  40.7 17.0 %fusion.6 = bf16[152,128,256]{2,0,1:T(8,128)(2,1)} fusion(bf16[192,128,256]{2,1,0:T(8,128)(2,1)} %pad_maximum_fusion, pred[152,96]{1,0:T(8,128)(4,1)S(1)} %iota_compare_fusion.8), kind=kOutput, calls=%fused_computation.15 | convolution fusion | flops 1917612544 | bytes 22558976 | tf_op jit(solution)/shard_map/sb,bcf->scf/dot_general | solution.py:66
  57.7 10.0 %copy.17 = bf16[152,128,256]{2,1,0:T(8,128)(2,1)} copy(bf16[152,128,256]{2,0,1:T(8,128)(2,1)} %fusion.6) | data formatting | bytes 19922944 | tf_op jit(solution)/shard_map/convert_element_type | solution.py:71
  67.7 5.2 %dynamic-slice_bitcast_fusion.1 = bf16[4,19,128,256]{3,2,1,0:T(8,128)(2,1)} fusion(bf16[2,4,19,128,256]{4,3,2,1,0:T(8,128)(2,1)} %bitcast.103, s32[]{:T(128)S(6)} %select_n.198), kind=kLoop, calls=%fused_computation.35 | loop fusion | bytes 9961476 | tf_op jit(solution)/shard_map/jit(dynamic_index_in_dim)/squeeze | solution.py:75
  73.4 9.7 %subtract_convert_fusion = (bf16[96,128,256]{2,1,0:T(8,128)(2,1)S(1)}, bf16[96,128,256]{2,1,0:T(8,128)(2,1)S(1)}) fusion(bf16[96,128,2,256]{3,1,0,2:T(8,128)(2,1)} %bitcast.114, f32[96,128]{1,0:T(8,128)S(1)} %bitcast.127, s32[96,128]{1,0:T(8,128)S(1)} %get-tuple-element.42, f32[96,128]{1,0:T(8,128)S(1)} %bitcast.129, s32[96,128]{1,0:T(8,128)S(1)} %get-tuple-element.43, ...), kind=kOutput, calls=%fused_computation.8 | convolution fusion | flops 855638016 | bytes 19660800 | tf_op jit(solution)/shard_map/bcr,brf->bcf/dot_general | solution.py:63
  83.2 7.2 %pad_maximum_fusion.1 = bf16[192,128,256]{2,1,0:T(8,128)(2,1)} fusion(bf16[96,128,256]{2,1,0:T(8,128)(2,1)S(1)} %get-tuple-element.10, bf16[96,128,256]{2,1,0:T(8,128)(2,1)S(1)} %get-tuple-element.11), kind=kLoop, calls=%fused_computation.3 | loop fusion | flops 6291456 | bytes 25165824 | tf_op jit(solution)/shard_map/concatenate | solution.py:69
  90.4 17.0 %fusion.9 = bf16[152,128,256]{2,0,1:T(8,128)(2,1)} fusion(bf16[192,128,256]{2,1,0:T(8,128)(2,1)} %pad_maximum_fusion.1, pred[152,96]{1,0:T(8,128)(4,1)S(1)} %iota_compare_fusion.8), kind=kOutput, calls=%fused_computation.16 | convolution fusion | flops 1917612544 | bytes 22558976 | tf_op jit(solution)/shard_map/sb,bcf->scf/dot_general | solution.py:66
  107.4 10.1 %copy.19 = bf16[152,128,256]{2,1,0:T(8,128)(2,1)} copy(bf16[152,128,256]{2,0,1:T(8,128)(2,1)} %fusion.9) | data formatting | bytes 19922944 | tf_op jit(solution)/shard_map/convert_element_type | solution.py:71
  117.5 5.4 %dynamic-slice_bitcast_fusion = bf16[4,19,128,256]{3,2,1,0:T(8,128)(2,1)} fusion(bf16[2,4,19,128,256]{4,3,2,1,0:T(8,128)(2,1)} %bitcast.106, s32[]{:T(128)S(6)} %select_n.198), kind=kLoop, calls=%fused_computation.34 | loop fusion | bytes 9961476 | tf_op jit(solution)/shard_map/jit(dynamic_index_in_dim)/squeeze | solution.py:75
  125.8 18.7 %multiply_convert_fusion.1 = (bf16[1024,1024]{1,0:T(8,128)(2,1)S(1)}, bf16[1024,1024]{1,0:T(8,128)(2,1)}, bf16[1024,1024]{1,0:T(8,128)(2,1)}) fusion(f32[1024]{0:T(1024)S(1)} %subtract_multiply_fusion), kind=kLoop, calls=%fused_computation.40 | loop fusion | flops 22020096 | bytes 6295552 | tf_op jit(solution)/shard_map/convert.20
  144.6 6.1 %fusion.5 = bf16[4,19,128,256]{3,2,1,0:T(8,128)(2,1)S(1)} fusion(bf16[4,19,128,256]{3,2,1,0:T(8,128)(2,1)} %collective-permute-done, bf16[2,4,19,128,256]{4,3,2,1,0:T(8,128)(2,1)} %bitcast.104, s32[]{:T(128)S(6)} %select_n.193), kind=kLoop, calls=%fused_computation.13 | loop fusion | flops 9961472 | bytes 14942212 | tf_op jit(solution)/shard_map/convert_element_type | solution.py:77
  155.7 17.2 %maximum_maximum_fusion = bf16[2048,2048]{1,0:T(8,128)(2,1)} fusion(bf16[1024,1024]{1,0:T(8,128)(2,1)} %get-tuple-element.46, bf16[1024,1024]{1,0:T(8,128)(2,1)} %get-tuple-element.45, bf16[1024,1024]{1,0:T(8,128)(2,1)S(1)} %get-tuple-element.44), kind=kLoop, calls=%fused_computation.14 | loop fusion | flops 33554432 | bytes 14680064 | tf_op jit(solution)/shard_map/concatenate | solution.py:44
  175.0 4.6 %fusion.4 = bf16[4,19,128,256]{3,2,1,0:T(8,128)(2,1)S(1)} fusion(bf16[4,19,128,256]{3,2,1,0:T(8,128)(2,1)} %collective-permute-done.4, bf16[2,4,19,128,256]{4,3,2,1,0:T(8,128)(2,1)S(1)} %bitcast.109, s32[]{:T(128)S(6)} %select_n.193), kind=kLoop, calls=%fused_computation.11 | loop fusion | flops 9961472 | bytes 14942212 | tf_op jit(solution)/shard_map/convert_element_type | solution.py:77
  186.3 3.9 %fusion.59 = (bf16[1024,2048]{1,0:T(8,128)(2,1)S(1)}, bf16[1024,2048]{1,0:T(8,128)(2,1)S(1)}) fusion(bf16[2048,2048]{1,0:T(8,128)(2,1)} %maximum_maximum_fusion), kind=kLoop, calls=%fused_computation.130 | loop fusion | bytes 16777216 | tf_op jit(solution)/shard_map/slice | solution.py:149
  190.1 66.6 %collective-permute-done.2 = bf16[19,128,256]{2,1,0:T(8,128)(2,1)} collective-permute-done((bf16[19,128,256]{2,1,0:T(8,128)(2,1)}, bf16[19,128,256]{2,1,0:T(8,128)(2,1)}, u32[]{:S(2)}, u32[]{:S(2)}) %collective-permute-start.2) | collective-permute-done | bytes 1245216 | tf_op jit(solution)/shard_map/ppermute | solution.py:93
  256.8 3.8 %fusion.25 = bf16[19,128,256]{2,1,0:T(8,128)(2,1)S(1)} fusion(bf16[19,128,256]{2,1,0:T(8,128)(2,1)} %collective-permute-done.3, bf16[19,128,256]{2,1,0:T(8,128)(2,1)} %collective-permute-done.2, bf16[19,128,256]{2,1,0:T(8,128)(2,1)} %collective-permute-done.1, bf16[4,19,128,256]{3,2,1,0:T(8,128)(2,1)} %collective-permute-done, s32[]{:T(128)S(6)} %select_n.196, ...), kind=kLoop, calls=%fused_computation.54 | loop fusion | flops 6225920 | bytes 7471116 | tf_op jit(solution)/shard_map/convert_element_type | solution.py:97
  266.7 15.7 %collective-permute-done.9 = bf16[19,128,256]{2,1,0:T(8,128)(2,1)S(1)} collective-permute-done((bf16[19,128,256]{2,1,0:T(8,128)(2,1)S(1)}, bf16[19,128,256]{2,1,0:T(8,128)(2,1)S(1)}, u32[]{:S(2)}, u32[]{:S(2)}) %collective-permute-start.9) | collective-permute-done | bytes 1245216 | tf_op jit(solution)/shard_map/ppermute | solution.py:93
  302.2 8.2 %collective-permute-done.12 = bf16[19,32,256]{2,1,0:T(8,128)(2,1)S(1)} collective-permute-done((bf16[19,32,256]{2,1,0:T(8,128)(2,1)S(1)}, bf16[19,32,256]{2,1,0:T(8,128)(2,1)S(1)}, u32[]{:S(2)}, u32[]{:S(2)}) %collective-permute-start.12) | collective-permute-done | bytes 311328 | tf_op jit(solution)/shard_map/ppermute | solution.py:111
  316.5 10.6 %add_add_fusion = f32[608,2048]{1,0:T(8,128)S(1)} fusion(f32[608,2048]{1,0:T(8,128)} %fusion.31, f32[608,2048]{1,0:T(8,128)} %fusion.35, f32[608,2048]{1,0:T(8,128)} %fusion.33, f32[608,2048]{1,0:T(8,128)} %fusion.37, f32[608,2048]{1,0:T(8,128)} %fusion.39, f32[608,2048]{1,0:T(8,128)S(1)} %fusion.43, f32[608,2048]{1,0:T(8,128)} %fusion.41, ...), kind=kOutput, calls=%fused_computation.33 | convolution fusion | flops 646250496 | bytes 41205764 | tf_op jit(solution)/shard_map/dot_general | solution.py:114
  327.1 3.8 %fusion.21 = f32[19,1024]{1,0:T(8,128)S(1)} fusion(f32[19,32,2048]{2,1,0:T(8,128)} %convert_element_type.185, f32[19,32,2048]{2,1,0:T(8,128)S(1)} %bitcast.111), kind=kLoop, calls=%fused_computation.47 | loop fusion | flops 2470912 | bytes 10039296 | tf_op jit(solution)/shard_map/reduce_sum | solution.py:155
  330.8 7.7 %collective-permute-start.14 = (f32[19,1024]{1,0:T(8,128)S(1)}, f32[19,1024]{1,0:T(8,128)S(1)}, u32[]{:S(2)}, u32[]{:S(2)}) collective-permute-start(f32[19,1024]{1,0:T(8,128)S(1)} %fusion.21), channel_id=1, source_target_pairs={{0,1},{1,0},{2,3},{3,2},{4,5},{5,4},{6,7},{7,6},{8,9},{9,8},{10,11... | collective-permute-start | bytes 233480 | tf_op jit(solution)/shard_map/ppermute | solution.py:56
  (72 shorter events, 66.8 us)
Async XLA Ops:
  4.4 11.8 %copy-start.3 = (s32[96]{0:T(128)S(1)}, s32[96]{0:T(128)}, u32[]{:S(2)}) copy-start(s32[96]{0:T(128)} %param.11) | copy-start | bytes 1156
  4.4 11.8 %copy-start = (s32[80]{0:T(128)S(1)}, s32[80]{0:T(128)}, u32[]{:S(2)}) copy-start(s32[80]{0:T(128)} %param.12) | copy-start | bytes 964
  4.4 14.6 %copy-start.2 = (s32[12288]{0:T(1024)S(1)}, s32[12288]{0:T(1024)}, u32[]{:S(2)}) copy-start(s32[12288]{0:T(1024)} %param.8) | copy-start | bytes 147460
  73.0 71.6 %collective-permute-start = (bf16[4,19,128,256]{3,2,1,0:T(8,128)(2,1)}, bf16[4,19,128,256]{3,2,1,0:T(8,128)(2,1)}, u32[]{:S(2)}, u32[]{:S(2)}) collective-permute-start(bf16[4,19,128,256]{3,2,1,0:T(8,128)(2,1)} %dynamic-slice_bitcast_fusion.1), channel_id=1, source_target_pairs={{0,4},{4,0},{8,12},{12,8},{16,20},{20,16},{24,28},{28,24},{1,5},{5... | collective-permute-start | bytes 14942216 | tf_op jit(solution)/shard_map/ppermute | solution.py:76
  117.5 5.4 %copy-start.1 = (bf16[19,32,2048]{2,1,0:T(8,128)(2,1)S(1)}, bf16[19,32,2048]{2,1,0:T(8,128)(2,1)}, u32[]{:S(2)}) copy-start(bf16[19,32,2048]{2,1,0:T(8,128)(2,1)} %param.13) | copy-start | bytes 7471108
  122.9 52.1 %collective-permute-start.4 = (bf16[4,19,128,256]{3,2,1,0:T(8,128)(2,1)}, bf16[4,19,128,256]{3,2,1,0:T(8,128)(2,1)}, u32[]{:S(2)}, u32[]{:S(2)}) collective-permute-start(bf16[4,19,128,256]{3,2,1,0:T(8,128)(2,1)} %dynamic-slice_bitcast_fusion), channel_id=1, source_target_pairs={{0,4},{4,0},{8,12},{12,8},{16,20},{20,16},{24,28},{28,24},{1,5},{5... | collective-permute-start | bytes 14942216 | tf_op jit(solution)/shard_map/ppermute | solution.py:76
  150.7 24.3 %slice-start = ((s8[9961472]{0:T(1024)(128)(4,1)}), s8[4194304]{0:T(1024)(128)(4,1)S(1)}, s32[]{:S(2)}) async-start(s8[9961472]{0:T(1024)(128)(4,1)} %bitcast.107), calls=%async_computation | async-start | bytes 8388608
  150.7 24.3 %slice-start.1 = ((s8[9961472]{0:T(1024)(128)(4,1)}), s8[4194304]{0:T(1024)(128)(4,1)S(1)}, s32[]{:S(2)}) async-start(s8[9961472]{0:T(1024)(128)(4,1)} %bitcast.107), calls=%async_computation.1 | async-start | bytes 8388608
  152.7 32.4 %collective-permute-start.1 = (bf16[19,128,256]{2,1,0:T(8,128)(2,1)}, bf16[19,128,256]{2,1,0:T(8,128)(2,1)}, u32[]{:S(2)}, u32[]{:S(2)}) collective-permute-start(bf16[19,128,256]{2,1,0:T(8,128)(2,1)} %get-tuple-element.14), channel_id=1, source_target_pairs={{0,8},{4,12},{8,0},{12,4},{16,24},{20,28},{24,16},{28,20},{1,9},{5... | collective-permute-start | bytes 3735560 | tf_op jit(solution)/shard_map/ppermute | solution.py:93
  155.7 19.3 %slice-start.2 = ((s8[9961472]{0:T(1024)(128)(4,1)}), s8[1572864]{0:T(1024)(128)(4,1)S(1)}, s32[]{:S(2)}) async-start(s8[9961472]{0:T(1024)(128)(4,1)} %bitcast.107), calls=%async_computation.2 | async-start | bytes 3145728
  172.8 83.9 %collective-permute-start.2 = (bf16[19,128,256]{2,1,0:T(8,128)(2,1)}, bf16[19,128,256]{2,1,0:T(8,128)(2,1)}, u32[]{:S(2)}, u32[]{:S(2)}) collective-permute-start(bf16[19,128,256]{2,1,0:T(8,128)(2,1)} %get-tuple-element.16), channel_id=1, source_target_pairs={{0,16},{4,20},{8,24},{12,28},{16,0},{20,4},{24,8},{28,12},{1,17},{... | collective-permute-start | bytes 3735560 | tf_op jit(solution)/shard_map/ppermute | solution.py:93
  174.5 82.3 %collective-permute-start.3 = (bf16[19,128,256]{2,1,0:T(8,128)(2,1)}, bf16[19,128,256]{2,1,0:T(8,128)(2,1)}, u32[]{:S(2)}, u32[]{:S(2)}) collective-permute-start(bf16[19,128,256]{2,1,0:T(8,128)(2,1)} %get-tuple-element.15), channel_id=1, source_target_pairs={{0,24},{4,28},{8,16},{12,20},{16,8},{20,12},{24,0},{28,4},{1,25},{... | collective-permute-start | bytes 3735560 | tf_op jit(solution)/shard_map/ppermute | solution.py:93
  181.5 83.6 %collective-permute-start.10 = (bf16[19,128,256]{2,1,0:T(8,128)(2,1)S(1)}, bf16[19,128,256]{2,1,0:T(8,128)(2,1)S(1)}, u32[]{:S(2)}, u32[]{:S(2)}) collective-permute-start(bf16[19,128,256]{2,1,0:T(8,128)(2,1)S(1)} %get-tuple-element.18), channel_id=1, source_target_pairs={{0,24},{4,28},{8,16},{12,20},{16,8},{20,12},{24,0},{28,4},{1,25},{... | collective-permute-start | bytes 3735560 | tf_op jit(solution)/shard_map/ppermute | solution.py:93
  184.0 82.6 %collective-permute-start.8 = (bf16[19,128,256]{2,1,0:T(8,128)(2,1)S(1)}, bf16[19,128,256]{2,1,0:T(8,128)(2,1)S(1)}, u32[]{:S(2)}, u32[]{:S(2)}) collective-permute-start(bf16[19,128,256]{2,1,0:T(8,128)(2,1)S(1)} %get-tuple-element.17), channel_id=1, source_target_pairs={{0,8},{4,12},{8,0},{12,4},{16,24},{20,28},{24,16},{28,20},{1,9},{5... | collective-permute-start | bytes 3735560 | tf_op jit(solution)/shard_map/ppermute | solution.py:93
  185.1 97.2 %collective-permute-start.9 = (bf16[19,128,256]{2,1,0:T(8,128)(2,1)S(1)}, bf16[19,128,256]{2,1,0:T(8,128)(2,1)S(1)}, u32[]{:S(2)}, u32[]{:S(2)}) collective-permute-start(bf16[19,128,256]{2,1,0:T(8,128)(2,1)S(1)} %get-tuple-element.19), channel_id=1, source_target_pairs={{0,16},{4,20},{8,24},{12,28},{16,0},{20,4},{24,8},{28,12},{1,17},{... | collective-permute-start | bytes 3735560 | tf_op jit(solution)/shard_map/ppermute | solution.py:93
  260.7 30.9 %collective-permute-start.5 = (bf16[19,32,256]{2,1,0:T(8,128)(2,1)S(1)}, bf16[19,32,256]{2,1,0:T(8,128)(2,1)S(1)}, u32[]{:S(2)}, u32[]{:S(2)}) collective-permute-start(bf16[19,32,256]{2,1,0:T(8,128)(2,1)S(1)} %get-tuple-element.24), channel_id=1, source_target_pairs={{0,1},{1,2},{2,3},{3,0},{4,5},{5,6},{6,7},{7,4},{8,9},{9,10},{10,1... | collective-permute-start | bytes 933896 | tf_op jit(solution)/shard_map/ppermute | solution.py:111
  262.5 36.7 %collective-permute-start.6 = (bf16[19,32,256]{2,1,0:T(8,128)(2,1)S(1)}, bf16[19,32,256]{2,1,0:T(8,128)(2,1)S(1)}, u32[]{:S(2)}, u32[]{:S(2)}) collective-permute-start(bf16[19,32,256]{2,1,0:T(8,128)(2,1)S(1)} %get-tuple-element.26), channel_id=1, source_target_pairs={{0,2},{1,3},{2,0},{3,1},{4,6},{5,7},{6,4},{7,5},{8,10},{9,11},{10,... | collective-permute-start | bytes 933896 | tf_op jit(solution)/shard_map/ppermute | solution.py:111
  265.1 48.3 %collective-permute-start.7 = (bf16[19,32,256]{2,1,0:T(8,128)(2,1)S(1)}, bf16[19,32,256]{2,1,0:T(8,128)(2,1)S(1)}, u32[]{:S(2)}, u32[]{:S(2)}) collective-permute-start(bf16[19,32,256]{2,1,0:T(8,128)(2,1)S(1)} %get-tuple-element.25), channel_id=1, source_target_pairs={{0,3},{1,0},{2,1},{3,2},{4,7},{5,4},{6,5},{7,6},{8,11},{9,8},{10,9... | collective-permute-start | bytes 933896 | tf_op jit(solution)/shard_map/ppermute | solution.py:111
  283.3 12.8 %collective-permute-start.11 = (bf16[19,32,256]{2,1,0:T(8,128)(2,1)S(1)}, bf16[19,32,256]{2,1,0:T(8,128)(2,1)S(1)}, u32[]{:S(2)}, u32[]{:S(2)}) collective-permute-start(bf16[19,32,256]{2,1,0:T(8,128)(2,1)S(1)} %get-tuple-element.22), channel_id=1, source_target_pairs={{0,1},{1,2},{2,3},{3,0},{4,5},{5,6},{6,7},{7,4},{8,9},{9,10},{10,1... | collective-permute-start | bytes 933896 | tf_op jit(solution)/shard_map/ppermute | solution.py:111
  285.1 25.3 %collective-permute-start.12 = (bf16[19,32,256]{2,1,0:T(8,128)(2,1)S(1)}, bf16[19,32,256]{2,1,0:T(8,128)(2,1)S(1)}, u32[]{:S(2)}, u32[]{:S(2)}) collective-permute-start(bf16[19,32,256]{2,1,0:T(8,128)(2,1)S(1)} %get-tuple-element.21), channel_id=1, source_target_pairs={{0,2},{1,3},{2,0},{3,1},{4,6},{5,7},{6,4},{7,5},{8,10},{9,11},{10,... | collective-permute-start | bytes 933896 | tf_op jit(solution)/shard_map/ppermute | solution.py:111
  291.6 24.9 %collective-permute-start.13 = (bf16[19,32,256]{2,1,0:T(8,128)(2,1)S(1)}, bf16[19,32,256]{2,1,0:T(8,128)(2,1)S(1)}, u32[]{:S(2)}, u32[]{:S(2)}) collective-permute-start(bf16[19,32,256]{2,1,0:T(8,128)(2,1)S(1)} %get-tuple-element.20), channel_id=1, source_target_pairs={{0,3},{1,0},{2,1},{3,2},{4,7},{5,4},{6,5},{7,6},{8,11},{9,8},{10,9... | collective-permute-start | bytes 933896 | tf_op jit(solution)/shard_map/ppermute | solution.py:111
  330.8 10.9 %collective-permute-start.14 = (f32[19,1024]{1,0:T(8,128)S(1)}, f32[19,1024]{1,0:T(8,128)S(1)}, u32[]{:S(2)}, u32[]{:S(2)}) collective-permute-start(f32[19,1024]{1,0:T(8,128)S(1)} %fusion.21), channel_id=1, source_target_pairs={{0,1},{1,0},{2,3},{3,2},{4,5},{5,4},{6,7},{7,6},{8,9},{9,8},{10,11... | collective-permute-start | bytes 233480 | tf_op jit(solution)/shard_map/ppermute | solution.py:56
  341.8 7.0 %collective-permute-start.15 = (f32[19,1024]{1,0:T(8,128)S(1)}, f32[19,1024]{1,0:T(8,128)S(1)}, u32[]{:S(2)}, u32[]{:S(2)}) collective-permute-start(f32[19,1024]{1,0:T(8,128)S(1)} %add.444), channel_id=1, source_target_pairs={{0,2},{1,3},{2,0},{3,1},{4,6},{5,7},{6,4},{7,5},{8,10},{9,11},{10,... | collective-permute-start | bytes 233480 | tf_op jit(solution)/shard_map/ppermute | solution.py:56

commit v7 on v3

--- a/solution.py
+++ b/solution.py
@@ -29,7 +29,7 @@
     return total.astype(jnp.bfloat16)
 
 
-def delay_table():
+def delay_parts():
     freq = jnp.arange(CH, dtype=jnp.int32)
     phase = (freq[:, None] * freq[None, :] % CH).astype(jnp.float32) * jnp.float32(
         2.0 * math.pi / CH
@@ -39,9 +39,7 @@
     x = freq.astype(jnp.float32) * jnp.float32(2.0 * math.pi / CH)
     taper = 0.35875 - 0.48829 * jnp.cos(x) + 0.14128 * jnp.cos(2.0 * x) - 0.01168 * jnp.cos(3.0 * x)
     scale = (taper / jnp.float32(math.sqrt(CH)))[:, None]
-    upper = jnp.concatenate([cosine * scale, -sine * scale], axis=1)
-    lower = jnp.concatenate([sine * scale, cosine * scale], axis=1)
-    return jnp.concatenate([upper, lower], axis=0).astype(jnp.bfloat16)
+    return (cosine * scale).astype(jnp.bfloat16), (sine * scale).astype(jnp.bfloat16)
 
 
 def _partner_pairs(n, fn):
@@ -121,19 +119,22 @@
     cells = row_cell.reshape(nblocks, BR)
     weights = jnp.transpose(tap_weight.reshape(KT, nblocks, BR), (1, 0, 2))
     matrix = kernel_matrix(cells, weights, tap_offset)
-    table = delay_table()
+    cos_part, sin_part = delay_parts()
     first = _gather_pair(blocks[:, :, 0, :], matrix, pick2, parity, chip, n_owners, slots_dev)
     second = _gather_pair(blocks[:, :, 1, :], matrix, pick2, parity, chip, n_owners, slots_dev)
-    out = None
-    for k, (pair_send, own) in enumerate((first, second)):
+    cos_part, sin_part, second = lax.optimization_barrier((cos_part, sin_part, second))
+    flat = []
+    for pair_send, own in (first, second):
         piece = _scatter_pairs(pair_send, own, chip, n_owners)
         count, cells_part = piece.shape[0], piece.shape[1]
-        term = jnp.dot(
-            piece.reshape(count * cells_part, CH),
-            table[k * CH:(k + 1) * CH],
-            preferred_element_type=jnp.float32,
-        )
-        out = term if out is None else out + term
+        flat.append(piece.reshape(count * cells_part, CH))
+
+    def mul(a, b):
+        return jnp.dot(a, b, preferred_element_type=jnp.float32)
+
+    left = mul(flat[0], cos_part) + mul(flat[1], sin_part)
+    right = mul(flat[1], cos_part) - mul(flat[0], sin_part)
+    out = jnp.concatenate([left, right], axis=1)
     delay = out.reshape(count, cells_part, 2 * CH)
     galaxy_f = galaxy.astype(jnp.float32)
     product = delay[..., :CH] * galaxy_f[..., :CH] + delay[..., CH:] * galaxy_f[..., CH:]

time: 332 us -> 348 us (1.048)
  waiting for transfers between devices: 123 us -> 142 us
    all_to_all x2, waiting for transfers between devices: 7.61 us -> 26.8 us  [_scatter_pairs(): lax.all_to_all(gridded, 'chan', split_axis=1, concat_axis=2, tiled=True)]
    another operation x1 -> x0, other arithmetic: 19.2 us -> none
    convert_element_type x0 -> x1, other arithmetic: none -> 18.4 us  [delay_parts(): (sine * scale).astype(jnp.bfloat16)]
    unnamed x19 -> x17, local copies, waits for them, and re-layouts: 13.2 us -> 12.7 us
  transfers between devices with their start and end apart: 12 -> 12, of which waited for: 7 -> 7; matrix products, arithmetic and copies ran while one was open for 31% -> 28% of each run, Pallas kernels for 0% -> 0%
where the time goes in v7:
time: 348 us; the launch traced here: 342 us
  waiting for transfers between devices  142 us (41%)
  other arithmetic  67.6 us (19%)
  matrix products  58.7 us (17%)
  local copies, waits for them, and re-layouts  53.8 us (15%)
  starting transfers between devices  19.3 us (6%)
    ppermute x6, waiting for transfers between devices, _scatter_pairs(): lax.ppermute(send, 'uv', _partner_pairs(n_owners, lambda i, dest=dest: de...  106 us
    dot_general x2, matrix products, _gather_pair(): jnp.einsum('sb,bcf->scf', pick2, jnp.concatenate([high, low], axis=0), pr...  34.1 us
    all_to_all x2, waiting for transfers between devices, _scatter_pairs(): lax.all_to_all(gridded, 'chan', split_axis=1, concat_axis=2, tiled=True)  26.8 us
    convert_element_type x2, local copies, waits for them, and re-layouts, _gather_pair(): partial = jnp.einsum('sb,bcf->scf', pick2, jnp.concatenate([high, low], a...  20 us
    dot_general x2, matrix products, _gather_pair(): jnp.einsum('bcr,brf->bcf', matrix, part, preferred_element_type=jnp.float32)  18.7 us
    convert_element_type x1, other arithmetic, delay_parts(): (sine * scale).astype(jnp.bfloat16)  18.4 us
    concatenate x2, other arithmetic, _gather_pair(): jnp.concatenate([high, low], axis=0)  14.8 us
    unnamed x17, local copies, waits for them, and re-layouts  12.7 us
  transfers between devices with their start and end apart: 12, of which 7 were waited for; matrix products, arithmetic and copies ran while one was open for 28% of the time, Pallas kernels for 0%

profile of v7, /device:TPU:0, one launch (start us, length us, event | category | flops | bytes accessed | tf_op | source)
XLA Modules:
  0.0 342.5 jit_solution(14891929617190092869)
XLA Ops:
  4.7 11.7 %copy.22 = bf16[12288,2,256]{2,0,1:T(8,128)(2,1)} copy(bf16[12288,2,256]{2,1,0:T(2,128)(2,1)} %param.7) | data formatting | bytes 25165824 | tf_op args[0]
  19.3 4.9 %add_bitcast_fusion.10 = (s32[96,128]{1,0:T(8,128)S(1)}, s32[96,128]{1,0:T(8,128)S(1)}, s32[96,128]{1,0:T(8,128)S(1)}, s32[96,128]{1,0:T(8,128)S(1)}, s32[96,128...) fusion(s32[12288]{0:T(1024)S(1)} %copy-done.3, s32[]{:T(128)} %bitcast.1, ...), kind=kLoop, calls=%fused_computation.80 | loop fusion | flops 98304 | bytes 442400 | tf_op jit(solution)/shard_map/add | solution.py:24
  24.2 9.4 %subtract_convert_fusion = (bf16[96,128,256]{2,1,0:T(8,128)(2,1)S(1)}, bf16[96,128,256]{2,1,0:T(8,128)(2,1)S(1)}) fusion(bf16[96,128,2,256]{3,1,0,2:T(8,128)(2,1)} %bitcast.115, f32[96,128]{1,0:T(8,128)S(1)} %bitcast.128, s32[96,128]{1,0:T(8,128)S(1)} %get-tuple-element.34, f32[96,128]{1,0:T(8,128)S(1)} %bitcast.130, s32[96,128]{1,0:T(8,128)S(1)} %get-tuple-element.35, ...), kind=kOutput, calls=%fused_computation.8 | convolution fusion | flops 855638016 | bytes 19660800 | tf_op jit(solution)/shard_map/bcr,brf->bcf/dot_general | solution.py:61
  33.6 7.5 %pad_maximum_fusion.1 = bf16[192,128,256]{2,1,0:T(8,128)(2,1)} fusion(bf16[96,128,256]{2,1,0:T(8,128)(2,1)S(1)} %get-tuple-element.10, bf16[96,128,256]{2,1,0:T(8,128)(2,1)S(1)} %get-tuple-element.11), kind=kLoop, calls=%fused_computation.3 | loop fusion | flops 6291456 | bytes 25165824 | tf_op jit(solution)/shard_map/concatenate | solution.py:67
  41.2 17.0 %fusion.9 = bf16[152,128,256]{2,0,1:T(8,128)(2,1)} fusion(bf16[192,128,256]{2,1,0:T(8,128)(2,1)} %pad_maximum_fusion.1, pred[152,96]{1,0:T(8,128)(4,1)S(1)} %iota_compare_fusion.8), kind=kOutput, calls=%fused_computation.15 | convolution fusion | flops 1917612544 | bytes 22558976 | tf_op jit(solution)/shard_map/sb,bcf->scf/dot_general | solution.py:64
  58.2 10.0 %copy.28 = bf16[152,128,256]{2,1,0:T(8,128)(2,1)} copy(bf16[152,128,256]{2,0,1:T(8,128)(2,1)} %fusion.9) | data formatting | bytes 19922944 | tf_op jit(solution)/shard_map/convert_element_type | solution.py:69
  68.2 5.3 %dynamic-slice_bitcast_fusion = bf16[4,19,128,256]{3,2,1,0:T(8,128)(2,1)} fusion(bf16[2,4,19,128,256]{4,3,2,1,0:T(8,128)(2,1)} %bitcast.108, s32[]{:T(128)S(6)} %select_n.116), kind=kLoop, calls=%fused_computation.33 | loop fusion | bytes 9961476 | tf_op jit(solution)/shard_map/jit(dynamic_index_in_dim)/squeeze | solution.py:73
  73.9 9.4 %subtract_convert_fusion.1 = (bf16[96,128,256]{2,1,0:T(8,128)(2,1)S(1)}, bf16[96,128,256]{2,1,0:T(8,128)(2,1)S(1)}) fusion(bf16[96,128,2,256]{3,1,0,2:T(8,128)(2,1)} %bitcast.116, f32[96,128]{1,0:T(8,128)S(1)} %bitcast.129, s32[96,128]{1,0:T(8,128)S(1)} %get-tuple-element.34, f32[96,128]{1,0:T(8,128)S(1)} %bitcast.131, s32[96,128]{1,0:T(8,128)S(1)} %get-tuple-element.35, ...), kind=kOutput, calls=%fused_computation.9 | convolution fusion | flops 855638016 | bytes 19660800 | tf_op jit(solution)/shard_map/bcr,brf->bcf/dot_general | solution.py:61
  83.3 7.3 %pad_maximum_fusion = bf16[192,128,256]{2,1,0:T(8,128)(2,1)} fusion(bf16[96,128,256]{2,1,0:T(8,128)(2,1)S(1)} %get-tuple-element.12, bf16[96,128,256]{2,1,0:T(8,128)(2,1)S(1)} %get-tuple-element.13), kind=kLoop, calls=%fused_computation.2 | loop fusion | flops 6291456 | bytes 25165824 | tf_op jit(solution)/shard_map/concatenate | solution.py:67
  90.6 17.1 %fusion.6 = bf16[152,128,256]{2,0,1:T(8,128)(2,1)} fusion(bf16[192,128,256]{2,1,0:T(8,128)(2,1)} %pad_maximum_fusion, pred[152,96]{1,0:T(8,128)(4,1)S(1)} %iota_compare_fusion.8), kind=kOutput, calls=%fused_computation.14 | convolution fusion | flops 1917612544 | bytes 22558976 | tf_op jit(solution)/shard_map/sb,bcf->scf/dot_general | solution.py:64
  107.6 10.0 %copy.24 = bf16[152,128,256]{2,1,0:T(8,128)(2,1)} copy(bf16[152,128,256]{2,0,1:T(8,128)(2,1)} %fusion.6) | data formatting | bytes 19922944 | tf_op jit(solution)/shard_map/convert_element_type | solution.py:69
  117.7 5.3 %dynamic-slice_bitcast_fusion.1 = bf16[4,19,128,256]{3,2,1,0:T(8,128)(2,1)} fusion(bf16[2,4,19,128,256]{4,3,2,1,0:T(8,128)(2,1)} %bitcast.105, s32[]{:T(128)S(6)} %select_n.116), kind=kLoop, calls=%fused_computation.34 | loop fusion | bytes 9961476 | tf_op jit(solution)/shard_map/jit(dynamic_index_in_dim)/squeeze | solution.py:73
  123.0 18.4 %multiply_convert_fusion = (bf16[1024,1024]{1,0:T(8,128)(2,1)}, bf16[1024,1024]{1,0:T(8,128)(2,1)}) fusion(f32[1024]{0:T(1024)S(1)} %subtract_multiply_fusion), kind=kLoop, calls=%fused_computation.38 | loop fusion | flops 18874368 | bytes 4198400 | tf_op jit(solution)/shard_map/convert_element_type | solution.py:42
  143.4 6.1 %fusion.4 = bf16[4,19,128,256]{3,2,1,0:T(8,128)(2,1)S(1)} fusion(bf16[4,19,128,256]{3,2,1,0:T(8,128)(2,1)} %collective-permute-done.4, bf16[2,4,19,128,256]{4,3,2,1,0:T(8,128)(2,1)} %bitcast.110, s32[]{:T(128)S(6)} %select_n.111), kind=kLoop, calls=%fused_computation.11 | loop fusion | flops 9961472 | bytes 14942212 | tf_op jit(solution)/shard_map/convert_element_type | solution.py:75
  154.4 26.7 %collective-permute-done.5 = bf16[19,128,256]{2,1,0:T(8,128)(2,1)S(1)} collective-permute-done((bf16[19,128,256]{2,1,0:T(8,128)(2,1)S(1)}, bf16[19,128,256]{2,1,0:T(8,128)(2,1)S(1)}, u32[]{:S(2)}, u32[]{:S(2)}) %collective-permute-start.5) | collective-permute-done | bytes 1245216 | tf_op jit(solution)/shard_map/ppermute | solution.py:91
  181.0 27.5 %collective-permute-done.6 = bf16[19,128,256]{2,1,0:T(8,128)(2,1)S(1)} collective-permute-done((bf16[19,128,256]{2,1,0:T(8,128)(2,1)S(1)}, bf16[19,128,256]{2,1,0:T(8,128)(2,1)S(1)}, u32[]{:S(2)}, u32[]{:S(2)}) %collective-permute-start.6) | collective-permute-done | bytes 1245216 | tf_op jit(solution)/shard_map/ppermute | solution.py:91
  211.3 4.9 %all-to-all-start.1 = ((bf16[19,128,256]{2,0,1:T(8,128)(2,1)}), bf16[19,128,256]{2,0,1:T(8,128)(2,1)S(1)}, u32[]{:S(2)}, u32[]{:S(2)}) async-start(bf16[19,128,256]{2,0,1:T(8,128)(2,1)} %copy.29), calls=%async_computation.1 | async-start | bytes 3145728 | tf_op jit(solution)/shard_map/all_to_all | solution.py:96
  216.1 6.1 %fusion.5 = bf16[4,19,128,256]{3,2,1,0:T(8,128)(2,1)S(1)} fusion(bf16[4,19,128,256]{3,2,1,0:T(8,128)(2,1)} %collective-permute-done, bf16[2,4,19,128,256]{4,3,2,1,0:T(8,128)(2,1)} %bitcast.106, s32[]{:T(128)S(6)} %select_n.111), kind=kLoop, calls=%fused_computation.13 | loop fusion | flops 9961472 | bytes 14942212 | tf_op jit(solution)/shard_map/convert_element_type | solution.py:75
  226.2 26.8 %collective-permute-done.1 = bf16[19,128,256]{2,1,0:T(8,128)(2,1)S(1)} collective-permute-done((bf16[19,128,256]{2,1,0:T(8,128)(2,1)S(1)}, bf16[19,128,256]{2,1,0:T(8,128)(2,1)S(1)}, u32[]{:S(2)}, u32[]{:S(2)}) %collective-permute-start.1) | collective-permute-done | bytes 1245216 | tf_op jit(solution)/shard_map/ppermute | solution.py:91
  252.9 25.5 %collective-permute-done.2 = bf16[19,128,256]{2,1,0:T(8,128)(2,1)S(1)} collective-permute-done((bf16[19,128,256]{2,1,0:T(8,128)(2,1)S(1)}, bf16[19,128,256]{2,1,0:T(8,128)(2,1)S(1)}, u32[]{:S(2)}, u32[]{:S(2)}) %collective-permute-start.2) | collective-permute-done | bytes 1245216 | tf_op jit(solution)/shard_map/ppermute | solution.py:91
  283.1 5.1 %all-to-all-start = ((bf16[19,128,256]{2,0,1:T(8,128)(2,1)}), bf16[19,128,256]{2,0,1:T(8,128)(2,1)S(1)}, u32[]{:S(2)}, u32[]{:S(2)}) async-start(bf16[19,128,256]{2,0,1:T(8,128)(2,1)} %copy.25), calls=%async_computation | async-start | bytes 3145728 | tf_op jit(solution)/shard_map/all_to_all | solution.py:96
  288.1 4.6 %convert_element_type.184 = f32[19,32,2048]{2,1,0:T(8,128)} convert(bf16[19,32,2048]{2,1,0:T(8,128)(2,1)} %param.13) | non-fusion elementwise | flops 1245184 | bytes 7471104 | tf_op jit(solution)/shard_map/convert_element_type | solution.py:139
  294.0 26.8 %all-to-all-done = bf16[19,128,256]{2,0,1:T(8,128)(2,1)S(1)} async-done(((bf16[19,128,256]{2,0,1:T(8,128)(2,1)}), bf16[19,128,256]{2,0,1:T(8,128)(2,1)S(1)}, u32[]{:S(2)}, u32[]{:S(2)}) %all-to-all-start) | async-done | bytes 1245216 | tf_op jit(solution)/shard_map/all_to_all | solution.py:96
  330.5 4.6 %collective-permute-done.8 = f32[19,1024]{1,0:T(8,128)S(1)} collective-permute-done((f32[19,1024]{1,0:T(8,128)S(1)}, f32[19,1024]{1,0:T(8,128)S(1)}, u32[]{:S(2)}, u32[]{:S(2)}) %collective-permute-start.8) | collective-permute-done | bytes 77856 | tf_op jit(solution)/shard_map/ppermute | solution.py:54
  (63 shorter events, 43.4 us)
Async XLA Ops:
  4.6 11.7 %copy-start.4 = (s32[96]{0:T(128)S(1)}, s32[96]{0:T(128)}, u32[]{:S(2)}) copy-start(s32[96]{0:T(128)} %param.11) | copy-start | bytes 1156
  4.6 11.7 %copy-start = (s32[80]{0:T(128)S(1)}, s32[80]{0:T(128)}, u32[]{:S(2)}) copy-start(s32[80]{0:T(128)} %param.12) | copy-start | bytes 964
  4.7 14.6 %copy-start.3 = (s32[12288]{0:T(1024)S(1)}, s32[12288]{0:T(1024)}, u32[]{:S(2)}) copy-start(s32[12288]{0:T(1024)} %param.8) | copy-start | bytes 147460
  73.4 68.0 %collective-permute-start.4 = (bf16[4,19,128,256]{3,2,1,0:T(8,128)(2,1)}, bf16[4,19,128,256]{3,2,1,0:T(8,128)(2,1)}, u32[]{:S(2)}, u32[]{:S(2)}) collective-permute-start(bf16[4,19,128,256]{3,2,1,0:T(8,128)(2,1)} %dynamic-slice_bitcast_fusion), channel_id=1, source_target_pairs={{0,4},{4,0},{8,12},{12,8},{16,20},{20,16},{24,28},{28,24},{1,5},{5... | collective-permute-start | bytes 14942216 | tf_op jit(solution)/shard_map/ppermute | solution.py:74
  123.0 93.2 %collective-permute-start = (bf16[4,19,128,256]{3,2,1,0:T(8,128)(2,1)}, bf16[4,19,128,256]{3,2,1,0:T(8,128)(2,1)}, u32[]{:S(2)}, u32[]{:S(2)}) collective-permute-start(bf16[4,19,128,256]{3,2,1,0:T(8,128)(2,1)} %dynamic-slice_bitcast_fusion.1), channel_id=1, source_target_pairs={{0,4},{4,0},{8,12},{12,8},{16,20},{20,16},{24,28},{28,24},{1,5},{5... | collective-permute-start | bytes 14942216 | tf_op jit(solution)/shard_map/ppermute | solution.py:74
  149.8 31.3 %collective-permute-start.5 = (bf16[19,128,256]{2,1,0:T(8,128)(2,1)S(1)}, bf16[19,128,256]{2,1,0:T(8,128)(2,1)S(1)}, u32[]{:S(2)}, u32[]{:S(2)}) collective-permute-start(bf16[19,128,256]{2,1,0:T(8,128)(2,1)S(1)} %get-tuple-element.14), channel_id=1, source_target_pairs={{0,8},{4,12},{8,0},{12,4},{16,24},{20,28},{24,16},{28,20},{1,9},{5... | collective-permute-start | bytes 3735560 | tf_op jit(solution)/shard_map/ppermute | solution.py:91
  152.8 55.7 %collective-permute-start.6 = (bf16[19,128,256]{2,1,0:T(8,128)(2,1)S(1)}, bf16[19,128,256]{2,1,0:T(8,128)(2,1)S(1)}, u32[]{:S(2)}, u32[]{:S(2)}) collective-permute-start(bf16[19,128,256]{2,1,0:T(8,128)(2,1)S(1)} %get-tuple-element.16), channel_id=1, source_target_pairs={{0,16},{4,20},{8,24},{12,28},{16,0},{20,4},{24,8},{28,12},{1,17},{... | collective-permute-start | bytes 3735560 | tf_op jit(solution)/shard_map/ppermute | solution.py:91
  154.3 54.2 %collective-permute-start.7 = (bf16[19,128,256]{2,1,0:T(8,128)(2,1)S(1)}, bf16[19,128,256]{2,1,0:T(8,128)(2,1)S(1)}, u32[]{:S(2)}, u32[]{:S(2)}) collective-permute-start(bf16[19,128,256]{2,1,0:T(8,128)(2,1)S(1)} %get-tuple-element.15), channel_id=1, source_target_pairs={{0,24},{4,28},{8,16},{12,20},{16,8},{20,12},{24,0},{28,4},{1,25},{... | collective-permute-start | bytes 3735560 | tf_op jit(solution)/shard_map/ppermute | solution.py:91
  211.3 71.8 %all-to-all-start.1 = ((bf16[19,128,256]{2,0,1:T(8,128)(2,1)}), bf16[19,128,256]{2,0,1:T(8,128)(2,1)S(1)}, u32[]{:S(2)}, u32[]{:S(2)}) async-start(bf16[19,128,256]{2,0,1:T(8,128)(2,1)} %copy.29), calls=%async_computation.1 | async-start | bytes 3145728 | tf_op jit(solution)/shard_map/all_to_all | solution.py:96
  222.6 30.3 %collective-permute-start.1 = (bf16[19,128,256]{2,1,0:T(8,128)(2,1)S(1)}, bf16[19,128,256]{2,1,0:T(8,128)(2,1)S(1)}, u32[]{:S(2)}, u32[]{:S(2)}) collective-permute-start(bf16[19,128,256]{2,1,0:T(8,128)(2,1)S(1)} %get-tuple-element.17), channel_id=1, source_target_pairs={{0,8},{4,12},{8,0},{12,4},{16,24},{20,28},{24,16},{28,20},{1,9},{5... | collective-permute-start | bytes 3735560 | tf_op jit(solution)/shard_map/ppermute | solution.py:91
  223.9 54.6 %collective-permute-start.2 = (bf16[19,128,256]{2,1,0:T(8,128)(2,1)S(1)}, bf16[19,128,256]{2,1,0:T(8,128)(2,1)S(1)}, u32[]{:S(2)}, u32[]{:S(2)}) collective-permute-start(bf16[19,128,256]{2,1,0:T(8,128)(2,1)S(1)} %get-tuple-element.19), channel_id=1, source_target_pairs={{0,16},{4,20},{8,24},{12,28},{16,0},{20,4},{24,8},{28,12},{1,17},{... | collective-permute-start | bytes 3735560 | tf_op jit(solution)/shard_map/ppermute | solution.py:91
  224.7 53.7 %collective-permute-start.3 = (bf16[19,128,256]{2,1,0:T(8,128)(2,1)S(1)}, bf16[19,128,256]{2,1,0:T(8,128)(2,1)S(1)}, u32[]{:S(2)}, u32[]{:S(2)}) collective-permute-start(bf16[19,128,256]{2,1,0:T(8,128)(2,1)S(1)} %get-tuple-element.18), channel_id=1, source_target_pairs={{0,24},{4,28},{8,16},{12,20},{16,8},{20,12},{24,0},{28,4},{1,25},{... | collective-permute-start | bytes 3735560 | tf_op jit(solution)/shard_map/ppermute | solution.py:91
  283.1 37.7 %all-to-all-start = ((bf16[19,128,256]{2,0,1:T(8,128)(2,1)}), bf16[19,128,256]{2,0,1:T(8,128)(2,1)S(1)}, u32[]{:S(2)}, u32[]{:S(2)}) async-start(bf16[19,128,256]{2,0,1:T(8,128)(2,1)} %copy.25), calls=%async_computation | async-start | bytes 3145728 | tf_op jit(solution)/shard_map/all_to_all | solution.py:96
  320.8 1.6 copy-start.2
  323.8 1.6 copy-start.1
  325.4 3.6 %slice-start = ((s8[4980736]{0:T(1024)(128)(4,1)}), s8[4194304]{0:T(1024)(128)(4,1)S(1)}, s32[]{:S(2)}) async-start(s8[4980736]{0:T(1024)(128)(4,1)} %bitcast.113), calls=%async_computation.2 | async-start | bytes 8388608
  326.9 2.1 slice-start.1
  330.4 4.7 %collective-permute-start.8 = (f32[19,1024]{1,0:T(8,128)S(1)}, f32[19,1024]{1,0:T(8,128)S(1)}, u32[]{:S(2)}, u32[]{:S(2)}) collective-permute-start(f32[19,1024]{1,0:T(8,128)S(1)} %fusion.21), channel_id=1, source_target_pairs={{0,1},{1,0},{2,3},{3,2},{4,5},{5,4},{6,7},{7,6},{8,9},{9,8},{10,11... | collective-permute-start | bytes 233480 | tf_op jit(solution)/shard_map/ppermute | solution.py:54
  335.1 6.2 %collective-permute-start.9 = (f32[19,1024]{1,0:T(8,128)S(1)}, f32[19,1024]{1,0:T(8,128)S(1)}, u32[]{:S(2)}, u32[]{:S(2)}) collective-permute-start(f32[19,1024]{1,0:T(8,128)S(1)} %add.317), channel_id=1, source_target_pairs={{0,2},{1,3},{2,0},{3,1},{4,6},{5,7},{6,4},{7,5},{8,10},{9,11},{10,... | collective-permute-start | bytes 233480 | tf_op jit(solution)/shard_map/ppermute | solution.py:54

commit v8 on v3

--- a/solution.py
+++ b/solution.py
@@ -58,7 +58,7 @@
     return x
 
 
-def _gather_pair(part, matrix, pick2, parity, chip, n_owners, slots_dev):
+def _gather_pair(part, matrix, pick2, parity, chip, n_owners, slots_dev, after=None):
     pairs = n_owners // 2
     contrib = jnp.einsum("bcr,brf->bcf", matrix, part, preferred_element_type=jnp.float32)
     high = contrib.astype(jnp.bfloat16)
@@ -73,6 +73,8 @@
 
     mine = lax.dynamic_index_in_dim(partial, parity, axis=0, keepdims=False)
     other = lax.dynamic_index_in_dim(partial, 1 - parity, axis=0, keepdims=False)
+    if after is not None:
+        other, _ = lax.optimization_barrier((other, after))
     got = lax.ppermute(other, "uv", _partner_pairs(n_owners, lambda i: i ^ 1))
     pair_send = (mine.astype(jnp.float32) + got.astype(jnp.float32)).astype(jnp.bfloat16)
     own = lax.dynamic_index_in_dim(mine, chip, axis=0, keepdims=False).astype(
@@ -94,8 +96,7 @@
             send, "uv", _partner_pairs(n_owners, lambda i, dest=dest: dest(i // 2) * 2 + i % 2)
         )
         grid = grid + recv.astype(jnp.float32)
-    gridded = grid.astype(jnp.bfloat16)
-    return lax.all_to_all(gridded, "chan", split_axis=1, concat_axis=2, tiled=True)
+    return grid.astype(jnp.bfloat16)
 
 
 def body(vis, row_cell, tap_weight, tap_offset, block_tile, tile_owner, galaxy):
@@ -117,20 +118,30 @@
     pick = (jnp.arange(n_slots, dtype=jnp.int32)[:, None] == slot[None, :]).astype(jnp.bfloat16)
     pick2 = jnp.concatenate([pick, pick], axis=1)
 
-    blocks = vis.reshape(nblocks, BR, 2, chan_dev)
+    width = 2 * chan_dev
+    blocks = vis.reshape(nblocks, BR, width)
     cells = row_cell.reshape(nblocks, BR)
     weights = jnp.transpose(tap_weight.reshape(KT, nblocks, BR), (1, 0, 2))
     matrix = kernel_matrix(cells, weights, tap_offset)
     table = delay_table()
-    first = _gather_pair(blocks[:, :, 0, :], matrix, pick2, parity, chip, n_owners, slots_dev)
-    second = _gather_pair(blocks[:, :, 1, :], matrix, pick2, parity, chip, n_owners, slots_dev)
+    cut = width - width // 4
+    first = _gather_pair(blocks[:, :, :cut], matrix, pick2, parity, chip, n_owners, slots_dev)
+    first_grid = _scatter_pairs(first[0], first[1], chip, n_owners)
+    second = _gather_pair(
+        blocks[:, :, cut:], matrix, pick2, parity, chip, n_owners, slots_dev, after=first_grid
+    )
+    table, first_grid = lax.optimization_barrier((table, first_grid))
+    second_grid = _scatter_pairs(second[0], second[1], chip, n_owners)
+    by_source = table.reshape(2, n_chan, chan_dev, 2 * CH).transpose(1, 0, 2, 3)
+    by_source = by_source.reshape(n_chan, width, 2 * CH)
     out = None
-    for k, (pair_send, own) in enumerate((first, second)):
-        piece = _scatter_pairs(pair_send, own, chip, n_owners)
+    for gridded, lo, hi in ((first_grid, 0, cut), (second_grid, cut, width)):
+        piece = lax.all_to_all(gridded, "chan", split_axis=1, concat_axis=2, tiled=True)
         count, cells_part = piece.shape[0], piece.shape[1]
+        rows = by_source[:, lo:hi, :].reshape(n_chan * (hi - lo), 2 * CH)
         term = jnp.dot(
-            piece.reshape(count * cells_part, CH),
-            table[k * CH:(k + 1) * CH],
+            piece.reshape(count * cells_part, n_chan * (hi - lo)),
+            rows,
             preferred_element_type=jnp.float32,
         )
         out = term if out is None else out + term

time: 332 us -> 404 us (1.22)
  other arithmetic: 68.7 us -> 110 us
  local copies, waits for them, and re-layouts: 55.8 us -> 79.8 us
  matrix products: 58.3 us -> 72.8 us
  waiting for transfers between devices: 123 us -> 116 us
    ppermute x6, waiting for transfers between devices: 107 us -> 60.7 us  [_scatter_pairs(): lax.ppermute(send, 'uv', _partner_pairs(n_owners, lambda i, dest=dest: de...]
    concatenate x0 -> x1, other arithmetic: none -> 36.9 us  [delay_table(): return jnp.concatenate([upper, lower], axis=0).astype(jnp.bfloat16)]
    all_to_all x2, waiting for transfers between devices: 7.61 us -> 35.1 us  [body(): lax.all_to_all(gridded, 'chan', split_axis=1, concat_axis=2, tiled=True)]
    reshape x0 -> x1, local copies, waits for them, and re-layouts: none -> 20.5 us  [body(): blocks = vis.reshape(nblocks, BR, width)]
    ppermute x2, waiting for transfers between devices: 0.01 us -> 11.8 us  [_gather_pair(): got = lax.ppermute(other, 'uv', _partner_pairs(n_owners, lambda i: i ^ 1))]
    unnamed x19 -> x53, local copies, waits for them, and re-layouts: 13.2 us -> 1.78 us
    slice x0 -> x2, local copies, waits for them, and re-layouts: none -> 9.71 us  [body(): rows = by_source[:, lo:hi, :].reshape(n_chan * (hi - lo), 2 * CH)]
    dot_general x2, matrix products: 5.54 us -> 13.9 us  [body(): jnp.dot(piece.reshape(count * cells_part, n_chan * (hi - lo)), rows, pref...]
  transfers between devices with their start and end apart: 12 -> 12, of which waited for: 7 -> 7; matrix products, arithmetic and copies ran while one was open for 31% -> 30% of each run, Pallas kernels for 0% -> 0%
where the time goes in v8:
time: 404 us; the launch traced here: 398 us
  waiting for transfers between devices  116 us (29%)
  other arithmetic  110 us (27%)
  local copies, waits for them, and re-layouts  79.8 us (20%)
  matrix products  72.8 us (18%)
  starting transfers between devices  17.4 us (4%)
    ppermute x6, waiting for transfers between devices, _scatter_pairs(): lax.ppermute(send, 'uv', _partner_pairs(n_owners, lambda i, dest=dest: de...  60.7 us
    concatenate x1, other arithmetic, delay_table(): return jnp.concatenate([upper, lower], axis=0).astype(jnp.bfloat16)  36.9 us
    all_to_all x2, waiting for transfers between devices, body(): lax.all_to_all(gridded, 'chan', split_axis=1, concat_axis=2, tiled=True)  35.1 us
    dot_general x2, matrix products, _gather_pair(): jnp.einsum('sb,bcf->scf', pick2, jnp.concatenate([high, low], axis=0), pr...  34.7 us
    dot_general x2, matrix products, _gather_pair(): jnp.einsum('bcr,brf->bcf', matrix, part, preferred_element_type=jnp.float32)  24.2 us
    reshape x1, local copies, waits for them, and re-layouts, body(): blocks = vis.reshape(nblocks, BR, width)  20.5 us
    concatenate x2, other arithmetic, _gather_pair(): jnp.concatenate([high, low], axis=0)  17.7 us
    another operation x1, other arithmetic  17.7 us
  transfers between devices with their start and end apart: 12, of which 7 were waited for; matrix products, arithmetic and copies ran while one was open for 30% of the time, Pallas kernels for 0%

profile of v8, /device:TPU:0, one launch (start us, length us, event | category | flops | bytes accessed | tf_op | source)
XLA Modules:
  0.0 397.5 jit_solution(489984688012996538)
XLA Ops:
  4.7 20.5 %reshape.165 = bf16[96,128,512]{2,1,0:T(8,128)(2,1)} reshape(bf16[12288,2,256]{2,1,0:T(2,128)(2,1)} %param.7) | data formatting | bytes 25165824 | tf_op jit(solution)/shard_map/reshape | solution.py:122
  28.2 5.0 %add_bitcast_fusion.10 = (s32[96,128]{1,0:T(8,128)S(1)}, s32[96,128]{1,0:T(8,128)S(1)}, s32[96,128]{1,0:T(8,128)S(1)}, s32[96,128]{1,0:T(8,128)S(1)}, s32[96,128...) fusion(s32[12288]{0:T(1024)S(1)} %copy-done.4, s32[]{:T(128)} %bitcast.1, ...), kind=kLoop, calls=%fused_computation.86 | loop fusion | flops 98304 | bytes 442400 | tf_op jit(solution)/shard_map/add | solution.py:24
  33.3 14.2 %subtract_convert_fusion = (bf16[96,128,384]{2,1,0:T(8,128)(2,1)}, bf16[96,128,384]{2,1,0:T(8,128)(2,1)}) fusion(bf16[96,128,512]{2,1,0:T(8,128)(2,1)} %reshape.165, f32[96,128]{1,0:T(8,128)S(1)} %bitcast.120, s32[96,128]{1,0:T(8,128)S(1)} %get-tuple-element.32, f32[96,128]{1,0:T(8,128)S(1)} %bitcast.122, s32[96,128]{1,0:T(8,128)S(1)} %get-tuple-element.33, ...), kind=kOutput, calls=%fused_computation.5 | convolution fusion | flops 1264582656 | bytes 29097984 | tf_op jit(solution)/shard_map/bcr,brf->bcf/dot_general | solution.py:63
  47.5 15.3 %pad_maximum_fusion = bf16[192,128,384]{2,1,0:T(8,128)(2,1)} fusion(bf16[96,128,384]{2,1,0:T(8,128)(2,1)} %get-tuple-element.10, bf16[96,128,384]{2,1,0:T(8,128)(2,1)} %get-tuple-element.11), kind=kLoop, calls=%fused_computation.2 | loop fusion | flops 9437184 | bytes 37748736 | tf_op jit(solution)/shard_map/concatenate | solution.py:69
  62.8 30.0 %fusion.3 = bf16[152,128,384]{2,0,1:T(8,128)(2,1)} fusion(bf16[192,128,384]{2,1,0:T(8,128)(2,1)} %pad_maximum_fusion, pred[152,96]{1,0:T(8,128)(4,1)S(1)} %iota_compare_fusion.8), kind=kOutput, calls=%fused_computation.8 | convolution fusion | flops 2876404224 | bytes 33831168 | tf_op jit(solution)/shard_map/sb,bcf->scf/dot_general | solution.py:66
  92.8 11.9 %copy.27 = bf16[152,128,384]{2,1,0:T(8,128)(2,1)} copy(bf16[152,128,384]{2,0,1:T(8,128)(2,1)} %fusion.3) | data formatting | bytes 29884416 | tf_op jit(solution)/shard_map/convert_element_type | solution.py:71
  104.6 7.6 %dynamic-slice_bitcast_fusion = bf16[4,19,128,384]{3,2,1,0:T(8,128)(2,1)} fusion(bf16[2,4,19,128,384]{4,3,2,1,0:T(8,128)(2,1)} %bitcast.97, s32[]{:T(128)S(6)} %select_n.123), kind=kLoop, calls=%fused_computation.12 | loop fusion | bytes 14942212 | tf_op jit(solution)/shard_map/jit(dynamic_index_in_dim)/squeeze | solution.py:75
  112.7 11.8 %collective-permute-done = bf16[4,19,128,384]{3,2,1,0:T(8,128)(2,1)} collective-permute-done((bf16[4,19,128,384]{3,2,1,0:T(8,128)(2,1)}, bf16[4,19,128,384]{3,2,1,0:T(8,128)(2,1)}, u32[]{:S(2)}, u32[]{:S(2)}) %collective-permute-start) | collective-permute-done | bytes 7471136 | tf_op jit(solution)/shard_map/ppermute | solution.py:78
  124.5 11.9 %fusion.2 = bf16[4,19,128,384]{3,2,1,0:T(8,128)(2,1)} fusion(bf16[4,19,128,384]{3,2,1,0:T(8,128)(2,1)} %collective-permute-done, bf16[2,4,19,128,384]{4,3,2,1,0:T(8,128)(2,1)} %bitcast.98, s32[]{:T(128)S(6)} %select_n.118), kind=kLoop, calls=%fused_computation.7 | loop fusion | flops 14942208 | bytes 22413316 | tf_op jit(solution)/shard_map/convert_element_type | solution.py:79
  136.5 5.5 %dynamic-slice_bitcast_fusion.4 = (bf16[19,128,384]{2,1,0:T(8,128)(2,1)}, bf16[19,128,384]{2,1,0:T(8,128)(2,1)}, bf16[19,128,384]{2,1,0:T(8,128)(2,1)}) fusion(bf16[4,19,128,384]{3,2,1,0:T(8,128)(2,1)} %fusion.2, s32[]{:T(128)S(6)} %select_n.124, s32[]{:T(128)S(6)} %select_n.126, s32[]{:T(128)S(6)} %select_n.125), kind=kLoop, calls=%fused_computation.57 | loop fusion | bytes 11206668 | tf_op jit(solution)/shard_map/jit(dynamic_index_in_dim)/squeeze | solution.py:94
  146.4 10.0 %subtract_convert_fusion.1 = (bf16[96,128,128]{2,1,0:T(8,128)(2,1)S(1)}, bf16[96,128,128]{2,1,0:T(8,128)(2,1)}) fusion(bf16[96,128,512]{2,1,0:T(8,128)(2,1)} %reshape.165, f32[96,128]{1,0:T(8,128)S(1)} %bitcast.121, s32[96,128]{1,0:T(8,128)S(1)} %copy-done.20, f32[96,128]{1,0:T(8,128)S(1)} %bitcast.123, s32[96,128]{1,0:T(8,128)S(1)} %copy-done.22, ...), kind=kOutput, calls=%fused_computation.16 | convolution fusion | flops 446693376 | bytes 10223616 | tf_op jit(solution)/shard_map/bcr,brf->bcf/dot_general | solution.py:63
  158.9 4.7 %fusion.23 = bf16[152,128,128]{2,0,1:T(8,128)(2,1)S(1)} fusion(bf16[192,128,128]{2,1,0:T(8,128)(2,1)S(1)} %pad_maximum_fusion.1, pred[152,96]{1,0:T(8,128)(4,1)S(1)} %iota_compare_fusion.8), kind=kOutput, calls=%fused_computation.48 | convolution fusion | flops 958820864 | bytes 11286784 | tf_op jit(solution)/shard_map/sb,bcf->scf/dot_general | solution.py:66
  167.0 19.7 %collective-permute-done.1 = bf16[19,128,384]{2,1,0:T(8,128)(2,1)} collective-permute-done((bf16[19,128,384]{2,1,0:T(8,128)(2,1)}, bf16[19,128,384]{2,1,0:T(8,128)(2,1)}, u32[]{:S(2)}, u32[]{:S(2)}) %collective-permute-start.1) | collective-permute-done | bytes 1867808 | tf_op jit(solution)/shard_map/ppermute | solution.py:95
  186.7 40.9 %collective-permute-done.2 = bf16[19,128,384]{2,1,0:T(8,128)(2,1)} collective-permute-done((bf16[19,128,384]{2,1,0:T(8,128)(2,1)}, bf16[19,128,384]{2,1,0:T(8,128)(2,1)}, u32[]{:S(2)}, u32[]{:S(2)}) %collective-permute-start.2) | collective-permute-done | bytes 1867808 | tf_op jit(solution)/shard_map/ppermute | solution.py:95
  227.6 5.2 %fusion.20 = bf16[19,128,384]{2,1,0:T(8,128)(2,1)S(1)} fusion(bf16[19,128,384]{2,1,0:T(8,128)(2,1)} %collective-permute-done.3, bf16[19,128,384]{2,1,0:T(8,128)(2,1)} %collective-permute-done.2, bf16[19,128,384]{2,1,0:T(8,128)(2,1)} %collective-permute-done.1, bf16[4,19,128,384]{3,2,1,0:T(8,128)(2,1)} %collective-permute-done, s32[]{:T(128)S(6)} %select_n.121, ...), kind=kLoop, calls=%fused_computation.44 | loop fusion | flops 9338880 | bytes 11206668 | tf_op jit(solution)/shard_map/convert_element_type | solution.py:99
  233.0 17.7 %multiply_convert_fusion.1 = (bf16[1024,1024]{1,0:T(8,128)(2,1)S(1)}, bf16[1024,1024]{1,0:T(8,128)(2,1)S(1)}, bf16[1024,1024]{1,0:T(8,128)(2,1)S(1)}) fusion(f32[1024]{0:T(1024)S(1)} %subtract_multiply_fusion), kind=kLoop, calls=%fused_computation.35 | loop fusion | flops 22020096 | bytes 6295552 | tf_op jit(solution)/shard_map/convert.20
  250.7 36.9 %maximum_maximum_fusion = bf16[2048,2048]{1,0:T(8,128)(2,1)} fusion(bf16[1024,1024]{1,0:T(8,128)(2,1)S(1)} %get-tuple-element.36, bf16[1024,1024]{1,0:T(8,128)(2,1)S(1)} %get-tuple-element.35, bf16[1024,1024]{1,0:T(8,128)(2,1)S(1)} %get-tuple-element.34), kind=kLoop, calls=%fused_computation.11 | loop fusion | flops 33554432 | bytes 14680064 | tf_op jit(solution)/shard_map/concatenate | solution.py:44
  290.1 5.1 %all-to-all-start = ((bf16[19,128,384]{2,0,1:T(8,128)(2,1)}), bf16[19,128,384]{2,0,1:T(8,128)(2,1)S(1)}, u32[]{:S(2)}, u32[]{:S(2)}) async-start(bf16[19,128,384]{2,0,1:T(8,128)(2,1)} %copy.28), calls=%async_computation | async-start | bytes 4718592 | tf_op jit(solution)/shard_map/all_to_all | solution.py:139
  306.5 8.3 %copy.30 = bf16[4,2,256,2048]{3,2,1,0:T(8,128)(2,1)} copy(bf16[4,2,256,2048]{3,2,0,1:T(8,128)(2,1)} %bitcast.102) | data formatting | bytes 16777216 | tf_op jit(solution)/shard_map/transpose | solution.py:135
  314.8 6.5 %slice.109 = bf16[4,384,2048]{2,1,0:T(8,128)(2,1)} slice(bf16[4,512,2048]{2,1,0:T(8,128)(2,1)} %bitcast.103), slice={[0:4], [0:384], [0:2048]} | slice | bytes 12582912 | tf_op jit(solution)/shard_map/slice | solution.py:141
  324.5 25.1 %all-to-all-done = bf16[19,128,384]{2,0,1:T(8,128)(2,1)S(1)} async-done(((bf16[19,128,384]{2,0,1:T(8,128)(2,1)}), bf16[19,128,384]{2,0,1:T(8,128)(2,1)S(1)}, u32[]{:S(2)}, u32[]{:S(2)}) %all-to-all-start) | async-done | bytes 1867808 | tf_op jit(solution)/shard_map/all_to_all | solution.py:139
  360.0 9.8 %fusion.42 = f32[608,2048]{1,0:T(8,128)} fusion(bf16[608,1536]{1,0:T(8,128)(2,1)} %bitcast.116, bf16[1536,2048]{1,0:T(8,128)(2,1)} %bitcast.113), kind=kOutput, calls=%fused_computation.104 | convolution fusion | flops 3825205248 | bytes 13139968 | tf_op jit(solution)/shard_map/dot_general | solution.py:142
  369.8 10.0 %all-to-all-done.1 = bf16[19,128,128]{2,0,1:T(8,128)(2,1)S(1)} async-done(((bf16[19,128,128]{2,0,1:T(8,128)(2,1)}), bf16[19,128,128]{2,0,1:T(8,128)(2,1)S(1)}, u32[]{:S(2)}, u32[]{:S(2)}) %all-to-all-start.1) | async-done | bytes 622624 | tf_op jit(solution)/shard_map/all_to_all | solution.py:139
  385.9 4.6 %collective-permute-done.8 = f32[19,1024]{1,0:T(8,128)S(1)} collective-permute-done((f32[19,1024]{1,0:T(8,128)S(1)}, f32[19,1024]{1,0:T(8,128)S(1)}, u32[]{:S(2)}, u32[]{:S(2)}) %collective-permute-start.8) | collective-permute-done | bytes 77856 | tf_op jit(solution)/shard_map/ppermute | solution.py:56
  (100 shorter events, 57.9 us)
Async XLA Ops:
  4.7 28.6 %copy-start.5 = (f32[96,1,128]{2,1,0:T(1,128)}, f32[96,1,128]{2,1,0:T(1,128)S(1)}, u32[]{:S(2)}) copy-start(f32[96,1,128]{2,1,0:T(1,128)S(1)} %get-tuple-element.25) | copy-start | bytes 147460
  4.7 20.5 %copy-start.23 = (s32[96]{0:T(128)S(1)}, s32[96]{0:T(128)}, u32[]{:S(2)}) copy-start(s32[96]{0:T(128)} %param.11) | copy-start | bytes 1156
  4.7 20.5 %copy-start = (s32[80]{0:T(128)S(1)}, s32[80]{0:T(128)}, u32[]{:S(2)}) copy-start(s32[80]{0:T(128)} %param.12) | copy-start | bytes 964
  4.7 23.4 %copy-start.4 = (s32[12288]{0:T(1024)S(1)}, s32[12288]{0:T(1024)}, u32[]{:S(2)}) copy-start(s32[12288]{0:T(1024)} %param.8) | copy-start | bytes 147460
  33.2 14.3 %copy-start.7 = (s32[96,128]{1,0:T(8,128)}, s32[96,128]{1,0:T(8,128)S(1)}, u32[]{:S(2)}) copy-start(s32[96,128]{1,0:T(8,128)S(1)} %get-tuple-element.26) | copy-start | bytes 147460
  33.2 14.3 %copy-start.9 = (s32[96,128]{1,0:T(8,128)}, s32[96,128]{1,0:T(8,128)S(1)}, u32[]{:S(2)}) copy-start(s32[96,128]{1,0:T(8,128)S(1)} %get-tuple-element.27) | copy-start | bytes 147460
  33.2 14.2 %copy-start.11 = (s32[96,128]{1,0:T(8,128)}, s32[96,128]{1,0:T(8,128)S(1)}, u32[]{:S(2)}) copy-start(s32[96,128]{1,0:T(8,128)S(1)} %get-tuple-element.28) | copy-start | bytes 147460
  33.2 14.2 %copy-start.13 = (s32[96,128]{1,0:T(8,128)}, s32[96,128]{1,0:T(8,128)S(1)}, u32[]{:S(2)}) copy-start(s32[96,128]{1,0:T(8,128)S(1)} %get-tuple-element.29) | copy-start | bytes 147460
  33.2 14.2 %copy-start.15 = (s32[96,128]{1,0:T(8,128)}, s32[96,128]{1,0:T(8,128)S(1)}, u32[]{:S(2)}) copy-start(s32[96,128]{1,0:T(8,128)S(1)} %get-tuple-element.30) | copy-start | bytes 147460
  33.2 14.2 %copy-start.17 = (s32[96,128]{1,0:T(8,128)}, s32[96,128]{1,0:T(8,128)S(1)}, u32[]{:S(2)}) copy-start(s32[96,128]{1,0:T(8,128)S(1)} %get-tuple-element.31) | copy-start | bytes 147460
  112.2 12.3 %collective-permute-start = (bf16[4,19,128,384]{3,2,1,0:T(8,128)(2,1)}, bf16[4,19,128,384]{3,2,1,0:T(8,128)(2,1)}, u32[]{:S(2)}, u32[]{:S(2)}) collective-permute-start(bf16[4,19,128,384]{3,2,1,0:T(8,128)(2,1)} %dynamic-slice_bitcast_fusion), channel_id=1, source_target_pairs={{0,4},{4,0},{8,12},{12,8},{16,20},{20,16},{24,28},{28,24},{1,5},{5... | collective-permute-start | bytes 22413320 | tf_op jit(solution)/shard_map/ppermute | solution.py:78
  142.0 44.7 %collective-permute-start.1 = (bf16[19,128,384]{2,1,0:T(8,128)(2,1)}, bf16[19,128,384]{2,1,0:T(8,128)(2,1)}, u32[]{:S(2)}, u32[]{:S(2)}) collective-permute-start(bf16[19,128,384]{2,1,0:T(8,128)(2,1)} %get-tuple-element.12), channel_id=1, source_target_pairs={{0,8},{4,12},{8,0},{12,4},{16,24},{20,28},{24,16},{28,20},{1,9},{5... | collective-permute-start | bytes 5603336 | tf_op jit(solution)/shard_map/ppermute | solution.py:95
  144.8 82.8 %collective-permute-start.2 = (bf16[19,128,384]{2,1,0:T(8,128)(2,1)}, bf16[19,128,384]{2,1,0:T(8,128)(2,1)}, u32[]{:S(2)}, u32[]{:S(2)}) collective-permute-start(bf16[19,128,384]{2,1,0:T(8,128)(2,1)} %get-tuple-element.14), channel_id=1, source_target_pairs={{0,16},{4,20},{8,24},{12,28},{16,0},{20,4},{24,8},{28,12},{1,17},{... | collective-permute-start | bytes 5603336 | tf_op jit(solution)/shard_map/ppermute | solution.py:95
  146.3 81.3 %collective-permute-start.3 = (bf16[19,128,384]{2,1,0:T(8,128)(2,1)}, bf16[19,128,384]{2,1,0:T(8,128)(2,1)}, u32[]{:S(2)}, u32[]{:S(2)}) collective-permute-start(bf16[19,128,384]{2,1,0:T(8,128)(2,1)} %get-tuple-element.13), channel_id=1, source_target_pairs={{0,24},{4,28},{8,16},{12,20},{16,8},{20,12},{24,0},{28,4},{1,25},{... | collective-permute-start | bytes 5603336 | tf_op jit(solution)/shard_map/ppermute | solution.py:95
  164.9 68.0 %copy-start.1 = (bf16[152,128,128]{2,1,0:T(8,128)(2,1)}, bf16[152,128,128]{2,1,0:T(8,128)(2,1)S(1)}, u32[]{:S(2)}) copy-start(bf16[152,128,128]{2,1,0:T(8,128)(2,1)S(1)} %copy.32) | copy-start | bytes 14942212
  232.9 62.4 %collective-permute-start.4 = (bf16[4,19,128,128]{3,2,1,0:T(8,128)(2,1)}, bf16[4,19,128,128]{3,2,1,0:T(8,128)(2,1)}, u32[]{:S(2)}, u32[]{:S(2)}) collective-permute-start(bf16[4,19,128,128]{3,2,1,0:T(8,128)(2,1)} %dynamic-slice_bitcast_fusion.1), channel_id=1, source_target_pairs={{0,4},{4,0},{8,12},{12,8},{16,20},{20,16},{24,28},{28,24},{1,5},{5... | collective-permute-start | bytes 7471112 | tf_op jit(solution)/shard_map/ppermute | solution.py:78
  290.1 59.5 %all-to-all-start = ((bf16[19,128,384]{2,0,1:T(8,128)(2,1)}), bf16[19,128,384]{2,0,1:T(8,128)(2,1)S(1)}, u32[]{:S(2)}, u32[]{:S(2)}) async-start(bf16[19,128,384]{2,0,1:T(8,128)(2,1)} %copy.28), calls=%async_computation | async-start | bytes 4718592 | tf_op jit(solution)/shard_map/all_to_all | solution.py:139
  300.1 52.7 %collective-permute-start.5 = (bf16[19,128,128]{2,1,0:T(8,128)(2,1)}, bf16[19,128,128]{2,1,0:T(8,128)(2,1)S(1)}, u32[]{:S(2)}, u32[]{:S(2)}) collective-permute-start(bf16[19,128,128]{2,1,0:T(8,128)(2,1)} %get-tuple-element.15), channel_id=1, source_target_pairs={{0,8},{4,12},{8,0},{12,4},{16,24},{20,28},{24,16},{28,20},{1,9},{5... | collective-permute-start | bytes 1867784 | tf_op jit(solution)/shard_map/ppermute | solution.py:95
  301.3 51.4 %collective-permute-start.6 = (bf16[19,128,128]{2,1,0:T(8,128)(2,1)}, bf16[19,128,128]{2,1,0:T(8,128)(2,1)}, u32[]{:S(2)}, u32[]{:S(2)}) collective-permute-start(bf16[19,128,128]{2,1,0:T(8,128)(2,1)} %get-tuple-element.17), channel_id=1, source_target_pairs={{0,16},{4,20},{8,24},{12,28},{16,0},{20,4},{24,8},{28,12},{1,17},{... | collective-permute-start | bytes 1867784 | tf_op jit(solution)/shard_map/ppermute | solution.py:95
  302.2 50.6 %collective-permute-start.7 = (bf16[19,128,128]{2,1,0:T(8,128)(2,1)}, bf16[19,128,128]{2,1,0:T(8,128)(2,1)}, u32[]{:S(2)}, u32[]{:S(2)}) collective-permute-start(bf16[19,128,128]{2,1,0:T(8,128)(2,1)} %get-tuple-element.16), channel_id=1, source_target_pairs={{0,24},{4,28},{8,16},{12,20},{16,8},{20,12},{24,0},{28,4},{1,25},{... | collective-permute-start | bytes 1867784 | tf_op jit(solution)/shard_map/ppermute | solution.py:95
  356.3 23.5 %all-to-all-start.1 = ((bf16[19,128,128]{2,0,1:T(8,128)(2,1)}), bf16[19,128,128]{2,0,1:T(8,128)(2,1)S(1)}, u32[]{:S(2)}, u32[]{:S(2)}) async-start(bf16[19,128,128]{2,0,1:T(8,128)(2,1)} %copy.33), calls=%async_computation.1 | async-start | bytes 1572864 | tf_op jit(solution)/shard_map/all_to_all | solution.py:139
  360.0 20.3 %copy-start.2 = (bf16[4,128,2048]{2,1,0:T(8,128)(2,1)S(1)}, bf16[4,128,2048]{2,1,0:T(8,128)(2,1)}, u32[]{:S(2)}) copy-start(bf16[4,128,2048]{2,1,0:T(8,128)(2,1)} %slice.111) | copy-start | bytes 6291460
  385.8 4.7 %collective-permute-start.8 = (f32[19,1024]{1,0:T(8,128)S(1)}, f32[19,1024]{1,0:T(8,128)S(1)}, u32[]{:S(2)}, u32[]{:S(2)}) collective-permute-start(f32[19,1024]{1,0:T(8,128)S(1)} %fusion.27), channel_id=1, source_target_pairs={{0,1},{1,0},{2,3},{3,2},{4,5},{5,4},{6,7},{7,6},{8,9},{9,8},{10,11... | collective-permute-start | bytes 233480 | tf_op jit(solution)/shard_map/ppermute | solution.py:56
  390.5 6.1 %collective-permute-start.9 = (f32[19,1024]{1,0:T(8,128)S(1)}, f32[19,1024]{1,0:T(8,128)S(1)}, u32[]{:S(2)}, u32[]{:S(2)}) collective-permute-start(f32[19,1024]{1,0:T(8,128)S(1)} %add.327), channel_id=1, source_target_pairs={{0,2},{1,3},{2,0},{3,1},{4,6},{5,7},{6,4},{7,5},{8,10},{9,11},{10,... | collective-permute-start | bytes 233480 | tf_op jit(solution)/shard_map/ppermute | solution.py:56
  (14 other events, 135.1 us)

commit v9 on v3

--- a/solution.py
+++ b/solution.py
@@ -124,6 +124,8 @@
     table = delay_table()
     first = _gather_pair(blocks[:, :, 0, :], matrix, pick2, parity, chip, n_owners, slots_dev)
     second = _gather_pair(blocks[:, :, 1, :], matrix, pick2, parity, chip, n_owners, slots_dev)
+    galaxy_f = galaxy.astype(jnp.float32)
+    table, galaxy_f, second = lax.optimization_barrier((table, galaxy_f, second))
     out = None
     for k, (pair_send, own) in enumerate((first, second)):
         piece = _scatter_pairs(pair_send, own, chip, n_owners)
@@ -135,7 +137,6 @@
         )
         out = term if out is None else out + term
     delay = out.reshape(count, cells_part, 2 * CH)
-    galaxy_f = galaxy.astype(jnp.float32)
     product = delay[..., :CH] * galaxy_f[..., :CH] + delay[..., CH:] * galaxy_f[..., CH:]
     local_power = jnp.sum(product, axis=1)
     power = _allreduce_sum(local_power, "chan", n_chan) / jnp.float32(math.sqrt(TC))

time: 332 us -> 329 us (level)
  waiting for transfers between devices: 123 us -> 99.2 us
  other arithmetic: 68.7 us -> 86.2 us
    ppermute x6, waiting for transfers between devices: 107 us -> 59.5 us  [_scatter_pairs(): lax.ppermute(send, 'uv', _partner_pairs(n_owners, lambda i, dest=dest: de...]
    all_to_all x2, waiting for transfers between devices: 7.61 us -> 31.4 us  [_scatter_pairs(): lax.all_to_all(gridded, 'chan', split_axis=1, concat_axis=2, tiled=True)]
    concatenate x0 -> x1, other arithmetic: none -> 17.1 us  [delay_table(): return jnp.concatenate([upper, lower], axis=0).astype(jnp.bfloat16)]
    unnamed x19 -> x23, local copies, waits for them, and re-layouts: 13.2 us -> 12.2 us
  transfers between devices with their start and end apart: 12 -> 12, of which waited for: 7 -> 6; matrix products, arithmetic and copies ran while one was open for 31% -> 35% of each run, Pallas kernels for 0% -> 0%
where the time goes in v9:
time: 329 us; the launch traced here: 323 us
  waiting for transfers between devices  99.2 us (30%)
  other arithmetic  86.2 us (26%)
  matrix products  60.3 us (18%)
  local copies, waits for them, and re-layouts  56.8 us (17%)
  starting transfers between devices  19.2 us (6%)
    ppermute x6, waiting for transfers between devices, _scatter_pairs(): lax.ppermute(send, 'uv', _partner_pairs(n_owners, lambda i, dest=dest: de...  59.5 us
    dot_general x2, matrix products, _gather_pair(): jnp.einsum('sb,bcf->scf', pick2, jnp.concatenate([high, low], axis=0), pr...  34.1 us
    all_to_all x2, waiting for transfers between devices, _scatter_pairs(): lax.all_to_all(gridded, 'chan', split_axis=1, concat_axis=2, tiled=True)  31.4 us
    convert_element_type x2, local copies, waits for them, and re-layouts, _gather_pair(): partial = jnp.einsum('sb,bcf->scf', pick2, jnp.concatenate([high, low], a...  20 us
    dot_general x2, matrix products, _gather_pair(): jnp.einsum('bcr,brf->bcf', matrix, part, preferred_element_type=jnp.float32)  18.7 us
    another operation x1, other arithmetic  18.5 us
    concatenate x1, other arithmetic, delay_table(): return jnp.concatenate([upper, lower], axis=0).astype(jnp.bfloat16)  17.1 us
    concatenate x2, other arithmetic, _gather_pair(): jnp.concatenate([high, low], axis=0)  14.9 us
  transfers between devices with their start and end apart: 12, of which 6 were waited for; matrix products, arithmetic and copies ran while one was open for 35% of the time, Pallas kernels for 0%

profile of v9, /device:TPU:0, one launch (start us, length us, event | category | flops | bytes accessed | tf_op | source)
XLA Modules:
  0.0 323.0 jit_solution(16518119331680353406)
XLA Ops:
  4.7 11.7 %copy.22 = bf16[12288,2,256]{2,0,1:T(8,128)(2,1)} copy(bf16[12288,2,256]{2,1,0:T(2,128)(2,1)} %param.7) | data formatting | bytes 25165824 | tf_op args[0]
  19.3 5.0 %add_bitcast_fusion.10 = (s32[96,128]{1,0:T(8,128)S(1)}, s32[96,128]{1,0:T(8,128)S(1)}, s32[96,128]{1,0:T(8,128)S(1)}, s32[96,128]{1,0:T(8,128)S(1)}, s32[96,128...) fusion(s32[12288]{0:T(1024)S(1)} %copy-done.1, s32[]{:T(128)} %bitcast.1, ...), kind=kLoop, calls=%fused_computation.85 | loop fusion | flops 98304 | bytes 442400 | tf_op jit(solution)/shard_map/add | solution.py:24
  24.3 9.4 %subtract_convert_fusion.1 = (bf16[96,128,256]{2,1,0:T(8,128)(2,1)S(1)}, bf16[96,128,256]{2,1,0:T(8,128)(2,1)S(1)}) fusion(bf16[96,128,2,256]{3,1,0,2:T(8,128)(2,1)} %bitcast.111, f32[96,128]{1,0:T(8,128)S(1)} %bitcast.124, s32[96,128]{1,0:T(8,128)S(1)} %get-tuple-element.34, f32[96,128]{1,0:T(8,128)S(1)} %bitcast.126, s32[96,128]{1,0:T(8,128)S(1)} %get-tuple-element.35, ...), kind=kOutput, calls=%fused_computation.9 | convolution fusion | flops 855638016 | bytes 19660800 | tf_op jit(solution)/shard_map/bcr,brf->bcf/dot_general | solution.py:63
  33.7 7.4 %pad_maximum_fusion = bf16[192,128,256]{2,1,0:T(8,128)(2,1)} fusion(bf16[96,128,256]{2,1,0:T(8,128)(2,1)S(1)} %get-tuple-element.10, bf16[96,128,256]{2,1,0:T(8,128)(2,1)S(1)} %get-tuple-element.11), kind=kLoop, calls=%fused_computation.2 | loop fusion | flops 6291456 | bytes 25165824 | tf_op jit(solution)/shard_map/concatenate | solution.py:69
  41.1 17.1 %fusion.6 = bf16[152,128,256]{2,0,1:T(8,128)(2,1)} fusion(bf16[192,128,256]{2,1,0:T(8,128)(2,1)} %pad_maximum_fusion, pred[152,96]{1,0:T(8,128)(4,1)S(1)} %iota_compare_fusion.8), kind=kOutput, calls=%fused_computation.15 | convolution fusion | flops 1917612544 | bytes 22558976 | tf_op jit(solution)/shard_map/sb,bcf->scf/dot_general | solution.py:66
  58.2 10.1 %copy.24 = bf16[152,128,256]{2,1,0:T(8,128)(2,1)} copy(bf16[152,128,256]{2,0,1:T(8,128)(2,1)} %fusion.6) | data formatting | bytes 19922944 | tf_op jit(solution)/shard_map/convert_element_type | solution.py:71
  68.3 5.2 %dynamic-slice_bitcast_fusion.1 = bf16[4,19,128,256]{3,2,1,0:T(8,128)(2,1)} fusion(bf16[2,4,19,128,256]{4,3,2,1,0:T(8,128)(2,1)} %bitcast.99, s32[]{:T(128)S(6)} %select_n.120), kind=kLoop, calls=%fused_computation.34 | loop fusion | bytes 9961476 | tf_op jit(solution)/shard_map/jit(dynamic_index_in_dim)/squeeze | solution.py:75
  74.0 9.4 %subtract_convert_fusion = (bf16[96,128,256]{2,1,0:T(8,128)(2,1)S(1)}, bf16[96,128,256]{2,1,0:T(8,128)(2,1)S(1)}) fusion(bf16[96,128,2,256]{3,1,0,2:T(8,128)(2,1)} %bitcast.112, f32[96,128]{1,0:T(8,128)S(1)} %bitcast.125, s32[96,128]{1,0:T(8,128)S(1)} %get-tuple-element.34, f32[96,128]{1,0:T(8,128)S(1)} %bitcast.127, s32[96,128]{1,0:T(8,128)S(1)} %get-tuple-element.35, ...), kind=kOutput, calls=%fused_computation.8 | convolution fusion | flops 855638016 | bytes 19660800 | tf_op jit(solution)/shard_map/bcr,brf->bcf/dot_general | solution.py:63
  83.3 7.5 %pad_maximum_fusion.1 = bf16[192,128,256]{2,1,0:T(8,128)(2,1)} fusion(bf16[96,128,256]{2,1,0:T(8,128)(2,1)S(1)} %get-tuple-element.12, bf16[96,128,256]{2,1,0:T(8,128)(2,1)S(1)} %get-tuple-element.13), kind=kLoop, calls=%fused_computation.3 | loop fusion | flops 6291456 | bytes 25165824 | tf_op jit(solution)/shard_map/concatenate | solution.py:69
  90.9 17.0 %fusion.9 = bf16[152,128,256]{2,0,1:T(8,128)(2,1)} fusion(bf16[192,128,256]{2,1,0:T(8,128)(2,1)} %pad_maximum_fusion.1, pred[152,96]{1,0:T(8,128)(4,1)S(1)} %iota_compare_fusion.8), kind=kOutput, calls=%fused_computation.16 | convolution fusion | flops 1917612544 | bytes 22558976 | tf_op jit(solution)/shard_map/sb,bcf->scf/dot_general | solution.py:66
  107.9 9.9 %copy.28 = bf16[152,128,256]{2,1,0:T(8,128)(2,1)} copy(bf16[152,128,256]{2,0,1:T(8,128)(2,1)} %fusion.9) | data formatting | bytes 19922944 | tf_op jit(solution)/shard_map/convert_element_type | solution.py:71
  117.8 5.2 %dynamic-slice_bitcast_fusion = bf16[4,19,128,256]{3,2,1,0:T(8,128)(2,1)} fusion(bf16[2,4,19,128,256]{4,3,2,1,0:T(8,128)(2,1)} %bitcast.102, s32[]{:T(128)S(6)} %select_n.120), kind=kLoop, calls=%fused_computation.33 | loop fusion | bytes 9961476 | tf_op jit(solution)/shard_map/jit(dynamic_index_in_dim)/squeeze | solution.py:75
  123.1 6.2 %fusion.5 = bf16[4,19,128,256]{3,2,1,0:T(8,128)(2,1)S(1)} fusion(bf16[4,19,128,256]{3,2,1,0:T(8,128)(2,1)} %collective-permute-done, bf16[2,4,19,128,256]{4,3,2,1,0:T(8,128)(2,1)} %bitcast.100, s32[]{:T(128)S(6)} %select_n.115), kind=kLoop, calls=%fused_computation.13 | loop fusion | flops 9961472 | bytes 14942212 | tf_op jit(solution)/shard_map/convert_element_type | solution.py:77
  135.9 18.5 %multiply_convert_fusion.1 = (bf16[1024,1024]{1,0:T(8,128)(2,1)S(1)}, bf16[1024,1024]{1,0:T(8,128)(2,1)}, bf16[1024,1024]{1,0:T(8,128)(2,1)}) fusion(f32[1024]{0:T(1024)S(1)} %subtract_multiply_fusion), kind=kLoop, calls=%fused_computation.43 | loop fusion | flops 22020096 | bytes 6295552 | tf_op jit(solution)/shard_map/convert.20
  154.5 5.0 %convert_element_type.168 = f32[19,32,2048]{2,1,0:T(8,128)} convert(bf16[19,32,2048]{2,1,0:T(8,128)(2,1)} %param.13) | non-fusion elementwise | flops 1245184 | bytes 7471104 | tf_op jit(solution)/shard_map/convert_element_type | solution.py:127
  159.5 17.1 %maximum_maximum_fusion = bf16[2048,2048]{1,0:T(8,128)(2,1)} fusion(bf16[1024,1024]{1,0:T(8,128)(2,1)} %get-tuple-element.38, bf16[1024,1024]{1,0:T(8,128)(2,1)} %get-tuple-element.37, bf16[1024,1024]{1,0:T(8,128)(2,1)S(1)} %get-tuple-element.36), kind=kLoop, calls=%fused_computation.14 | loop fusion | flops 33554432 | bytes 14680064 | tf_op jit(solution)/shard_map/concatenate | solution.py:44
  176.6 6.6 %fusion.4 = bf16[4,19,128,256]{3,2,1,0:T(8,128)(2,1)} fusion(bf16[4,19,128,256]{3,2,1,0:T(8,128)(2,1)} %collective-permute-done.4, bf16[2,4,19,128,256]{4,3,2,1,0:T(8,128)(2,1)S(1)} %bitcast.106, s32[]{:T(128)S(6)} %select_n.115), kind=kLoop, calls=%fused_computation.11 | loop fusion | flops 9961472 | bytes 14942212 | tf_op jit(solution)/shard_map/convert_element_type | solution.py:77
  183.2 7.2 %collective-permute-done.2 = bf16[19,128,256]{2,1,0:T(8,128)(2,1)} collective-permute-done((bf16[19,128,256]{2,1,0:T(8,128)(2,1)}, bf16[19,128,256]{2,1,0:T(8,128)(2,1)}, u32[]{:S(2)}, u32[]{:S(2)}) %collective-permute-start.2) | collective-permute-done | bytes 1245216 | tf_op jit(solution)/shard_map/ppermute | solution.py:93
  195.7 5.1 %all-to-all-start = ((bf16[19,128,256]{2,0,1:T(8,128)(2,1)}), bf16[19,128,256]{2,0,1:T(8,128)(2,1)S(1)}, u32[]{:S(2)}, u32[]{:S(2)}) async-start(bf16[19,128,256]{2,0,1:T(8,128)(2,1)} %copy.25), calls=%async_computation | async-start | bytes 3145728 | tf_op jit(solution)/shard_map/all_to_all | solution.py:98
  208.6 26.8 %collective-permute-done.5 = bf16[19,128,256]{2,1,0:T(8,128)(2,1)S(1)} collective-permute-done((bf16[19,128,256]{2,1,0:T(8,128)(2,1)S(1)}, bf16[19,128,256]{2,1,0:T(8,128)(2,1)S(1)}, u32[]{:S(2)}, u32[]{:S(2)}) %collective-permute-start.5) | collective-permute-done | bytes 1245216 | tf_op jit(solution)/shard_map/ppermute | solution.py:93
  235.4 25.5 %collective-permute-done.6 = bf16[19,128,256]{2,1,0:T(8,128)(2,1)S(1)} collective-permute-done((bf16[19,128,256]{2,1,0:T(8,128)(2,1)S(1)}, bf16[19,128,256]{2,1,0:T(8,128)(2,1)S(1)}, u32[]{:S(2)}, u32[]{:S(2)}) %collective-permute-start.6) | collective-permute-done | bytes 1245216 | tf_op jit(solution)/shard_map/ppermute | solution.py:93
  263.5 4.8 %all-to-all-start.1 = ((bf16[19,128,256]{2,0,1:T(8,128)(2,1)}), bf16[19,128,256]{2,0,1:T(8,128)(2,1)S(1)}, u32[]{:S(2)}, u32[]{:S(2)}) async-start(bf16[19,128,256]{2,0,1:T(8,128)(2,1)} %copy.29), calls=%async_computation.1 | async-start | bytes 3145728 | tf_op jit(solution)/shard_map/all_to_all | solution.py:98
  269.6 31.4 %all-to-all-done.1 = bf16[19,128,256]{2,0,1:T(8,128)(2,1)S(1)} async-done(((bf16[19,128,256]{2,0,1:T(8,128)(2,1)}), bf16[19,128,256]{2,0,1:T(8,128)(2,1)S(1)}, u32[]{:S(2)}, u32[]{:S(2)}) %all-to-all-start.1) | async-done | bytes 1245216 | tf_op jit(solution)/shard_map/all_to_all | solution.py:98
  302.3 4.7 %fusion.17 = f32[608,2048]{1,0:T(8,128)S(1)} fusion(bf16[608,1024]{1,0:T(8,128)(2,1)S(1)} %bitcast.120, bf16[2048,2048]{1,0:T(8,128)(2,1)} %maximum_maximum_fusion), kind=kOutput, calls=%fused_computation.38 | convolution fusion | flops 2550136832 | bytes 10420224 | tf_op jit(solution)/shard_map/dot_general | solution.py:133
  (69 shorter events, 48.1 us)
Async XLA Ops:
  4.7 11.7 %copy-start.2 = (s32[96]{0:T(128)S(1)}, s32[96]{0:T(128)}, u32[]{:S(2)}) copy-start(s32[96]{0:T(128)} %param.11) | copy-start | bytes 1156
  4.7 11.7 %copy-start = (s32[80]{0:T(128)S(1)}, s32[80]{0:T(128)}, u32[]{:S(2)}) copy-start(s32[80]{0:T(128)} %param.12) | copy-start | bytes 964
  4.7 14.6 %copy-start.1 = (s32[12288]{0:T(1024)S(1)}, s32[12288]{0:T(1024)}, u32[]{:S(2)}) copy-start(s32[12288]{0:T(1024)} %param.8) | copy-start | bytes 147460
  73.5 49.6 %collective-permute-start = (bf16[4,19,128,256]{3,2,1,0:T(8,128)(2,1)}, bf16[4,19,128,256]{3,2,1,0:T(8,128)(2,1)}, u32[]{:S(2)}, u32[]{:S(2)}) collective-permute-start(bf16[4,19,128,256]{3,2,1,0:T(8,128)(2,1)} %dynamic-slice_bitcast_fusion.1), channel_id=1, source_target_pairs={{0,4},{4,0},{8,12},{12,8},{16,20},{20,16},{24,28},{28,24},{1,5},{5... | collective-permute-start | bytes 14942216 | tf_op jit(solution)/shard_map/ppermute | solution.py:76
  123.0 53.6 %collective-permute-start.4 = (bf16[4,19,128,256]{3,2,1,0:T(8,128)(2,1)}, bf16[4,19,128,256]{3,2,1,0:T(8,128)(2,1)}, u32[]{:S(2)}, u32[]{:S(2)}) collective-permute-start(bf16[4,19,128,256]{3,2,1,0:T(8,128)(2,1)} %dynamic-slice_bitcast_fusion), channel_id=1, source_target_pairs={{0,4},{4,0},{8,12},{12,8},{16,20},{20,16},{24,28},{28,24},{1,5},{5... | collective-permute-start | bytes 14942216 | tf_op jit(solution)/shard_map/ppermute | solution.py:76
  131.4 51.7 %collective-permute-start.1 = (bf16[19,128,256]{2,1,0:T(8,128)(2,1)}, bf16[19,128,256]{2,1,0:T(8,128)(2,1)S(1)}, u32[]{:S(2)}, u32[]{:S(2)}) collective-permute-start(bf16[19,128,256]{2,1,0:T(8,128)(2,1)} %get-tuple-element.14), channel_id=1, source_target_pairs={{0,8},{4,12},{8,0},{12,4},{16,24},{20,28},{24,16},{28,20},{1,9},{5... | collective-permute-start | bytes 3735560 | tf_op jit(solution)/shard_map/ppermute | solution.py:93
  134.4 56.0 %collective-permute-start.2 = (bf16[19,128,256]{2,1,0:T(8,128)(2,1)}, bf16[19,128,256]{2,1,0:T(8,128)(2,1)}, u32[]{:S(2)}, u32[]{:S(2)}) collective-permute-start(bf16[19,128,256]{2,1,0:T(8,128)(2,1)} %get-tuple-element.16), channel_id=1, source_target_pairs={{0,16},{4,20},{8,24},{12,28},{16,0},{20,4},{24,8},{28,12},{1,17},{... | collective-permute-start | bytes 3735560 | tf_op jit(solution)/shard_map/ppermute | solution.py:93
  135.9 54.5 %collective-permute-start.3 = (bf16[19,128,256]{2,1,0:T(8,128)(2,1)}, bf16[19,128,256]{2,1,0:T(8,128)(2,1)}, u32[]{:S(2)}, u32[]{:S(2)}) collective-permute-start(bf16[19,128,256]{2,1,0:T(8,128)(2,1)} %get-tuple-element.15), channel_id=1, source_target_pairs={{0,24},{4,28},{8,16},{12,20},{16,8},{20,12},{24,0},{28,4},{1,25},{... | collective-permute-start | bytes 3735560 | tf_op jit(solution)/shard_map/ppermute | solution.py:93
  154.5 22.1 %slice-start = ((s8[9961472]{0:T(1024)(128)(4,1)}), s8[4194304]{0:T(1024)(128)(4,1)S(1)}, s32[]{:S(2)}) async-start(s8[9961472]{0:T(1024)(128)(4,1)} %bitcast.104), calls=%async_computation.2 | async-start | bytes 8388608
  154.5 22.1 %slice-start.1 = ((s8[9961472]{0:T(1024)(128)(4,1)}), s8[4194304]{0:T(1024)(128)(4,1)S(1)}, s32[]{:S(2)}) async-start(s8[9961472]{0:T(1024)(128)(4,1)} %bitcast.104), calls=%async_computation.3 | async-start | bytes 8388608
  159.5 17.1 %slice-start.2 = ((s8[9961472]{0:T(1024)(128)(4,1)}), s8[1572864]{0:T(1024)(128)(4,1)S(1)}, s32[]{:S(2)}) async-start(s8[9961472]{0:T(1024)(128)(4,1)} %bitcast.104), calls=%async_computation.4 | async-start | bytes 3145728
  195.7 67.9 %all-to-all-start = ((bf16[19,128,256]{2,0,1:T(8,128)(2,1)}), bf16[19,128,256]{2,0,1:T(8,128)(2,1)S(1)}, u32[]{:S(2)}, u32[]{:S(2)}) async-start(bf16[19,128,256]{2,0,1:T(8,128)(2,1)} %copy.25), calls=%async_computation | async-start | bytes 3145728 | tf_op jit(solution)/shard_map/all_to_all | solution.py:98
  205.1 30.3 %collective-permute-start.5 = (bf16[19,128,256]{2,1,0:T(8,128)(2,1)S(1)}, bf16[19,128,256]{2,1,0:T(8,128)(2,1)S(1)}, u32[]{:S(2)}, u32[]{:S(2)}) collective-permute-start(bf16[19,128,256]{2,1,0:T(8,128)(2,1)S(1)} %get-tuple-element.17), channel_id=1, source_target_pairs={{0,8},{4,12},{8,0},{12,4},{16,24},{20,28},{24,16},{28,20},{1,9},{5... | collective-permute-start | bytes 3735560 | tf_op jit(solution)/shard_map/ppermute | solution.py:93
  206.4 54.5 %collective-permute-start.6 = (bf16[19,128,256]{2,1,0:T(8,128)(2,1)S(1)}, bf16[19,128,256]{2,1,0:T(8,128)(2,1)S(1)}, u32[]{:S(2)}, u32[]{:S(2)}) collective-permute-start(bf16[19,128,256]{2,1,0:T(8,128)(2,1)S(1)} %get-tuple-element.19), channel_id=1, source_target_pairs={{0,16},{4,20},{8,24},{12,28},{16,0},{20,4},{24,8},{28,12},{1,17},{... | collective-permute-start | bytes 3735560 | tf_op jit(solution)/shard_map/ppermute | solution.py:93
  207.2 53.7 %collective-permute-start.7 = (bf16[19,128,256]{2,1,0:T(8,128)(2,1)S(1)}, bf16[19,128,256]{2,1,0:T(8,128)(2,1)S(1)}, u32[]{:S(2)}, u32[]{:S(2)}) collective-permute-start(bf16[19,128,256]{2,1,0:T(8,128)(2,1)S(1)} %get-tuple-element.18), channel_id=1, source_target_pairs={{0,24},{4,28},{8,16},{12,20},{16,8},{20,12},{24,0},{28,4},{1,25},{... | collective-permute-start | bytes 3735560 | tf_op jit(solution)/shard_map/ppermute | solution.py:93
  263.5 37.5 %all-to-all-start.1 = ((bf16[19,128,256]{2,0,1:T(8,128)(2,1)}), bf16[19,128,256]{2,0,1:T(8,128)(2,1)S(1)}, u32[]{:S(2)}, u32[]{:S(2)}) async-start(bf16[19,128,256]{2,0,1:T(8,128)(2,1)} %copy.29), calls=%async_computation.1 | async-start | bytes 3145728 | tf_op jit(solution)/shard_map/all_to_all | solution.py:98
  302.0 5.0 %slice-start.5 = ((s8[8388608]{0:T(1024)(128)(4,1)}), s8[4194304]{0:T(1024)(128)(4,1)S(1)}, s32[]{:S(2)}) async-start(s8[8388608]{0:T(1024)(128)(4,1)} %bitcast.113), calls=%async_computation.7 | async-start | bytes 8388608
  302.3 4.7 %slice-start.6 = ((s8[8388608]{0:T(1024)(128)(4,1)}), s8[4194304]{0:T(1024)(128)(4,1)S(1)}, s32[]{:S(2)}) async-start(s8[8388608]{0:T(1024)(128)(4,1)} %bitcast.113), calls=%async_computation.8 | async-start | bytes 8388608
  302.3 7.5 %slice-start.3 = ((s8[4980736]{0:T(1024)(128)(4,1)}), s8[4194304]{0:T(1024)(128)(4,1)S(1)}, s32[]{:S(2)}) async-start(s8[4980736]{0:T(1024)(128)(4,1)} %bitcast.107), calls=%async_computation.5 | async-start | bytes 8388608
  307.0 2.8 slice-start.4
  311.2 4.7 %collective-permute-start.8 = (f32[19,1024]{1,0:T(8,128)S(1)}, f32[19,1024]{1,0:T(8,128)S(1)}, u32[]{:S(2)}, u32[]{:S(2)}) collective-permute-start(f32[19,1024]{1,0:T(8,128)S(1)} %fusion.28), channel_id=1, source_target_pairs={{0,1},{1,0},{2,3},{3,2},{4,5},{5,4},{6,7},{7,6},{8,9},{9,8},{10,11... | collective-permute-start | bytes 233480 | tf_op jit(solution)/shard_map/ppermute | solution.py:56
  315.9 6.2 %collective-permute-start.9 = (f32[19,1024]{1,0:T(8,128)S(1)}, f32[19,1024]{1,0:T(8,128)S(1)}, u32[]{:S(2)}, u32[]{:S(2)}) collective-permute-start(f32[19,1024]{1,0:T(8,128)S(1)} %add.325), channel_id=1, source_target_pairs={{0,2},{1,3},{2,0},{3,1},{4,6},{5,7},{6,4},{7,5},{8,10},{9,11},{10,... | collective-permute-start | bytes 233480 | tf_op jit(solution)/shard_map/ppermute | solution.py:56

commit v10 on v9

--- a/solution.py
+++ b/solution.py
@@ -58,15 +58,14 @@
     return x
 
 
-def _gather_pair(part, matrix, pick2, parity, chip, n_owners, slots_dev):
+def _gather_pair(part, matrix, pick, parity, chip, n_owners, slots_dev):
     pairs = n_owners // 2
     contrib = jnp.einsum("bcr,brf->bcf", matrix, part, preferred_element_type=jnp.float32)
-    high = contrib.astype(jnp.bfloat16)
-    low = (contrib - high.astype(jnp.float32)).astype(jnp.bfloat16)
     partial = jnp.einsum(
         "sb,bcf->scf",
-        pick2,
-        jnp.concatenate([high, low], axis=0),
+        pick,
+        contrib,
+        precision=lax.Precision.HIGH,
         preferred_element_type=jnp.float32,
     ).astype(jnp.bfloat16)
     partial = partial.reshape((2, pairs, slots_dev) + partial.shape[1:])
@@ -114,16 +113,15 @@
     rank = rank_of_tile[block_tile]
     slot = (owner % 2) * (pairs * slots_dev) + (owner // 2) * slots_dev + rank
     n_slots = n_owners * slots_dev
-    pick = (jnp.arange(n_slots, dtype=jnp.int32)[:, None] == slot[None, :]).astype(jnp.bfloat16)
-    pick2 = jnp.concatenate([pick, pick], axis=1)
+    pick = (jnp.arange(n_slots, dtype=jnp.int32)[:, None] == slot[None, :]).astype(jnp.float32)
 
     blocks = vis.reshape(nblocks, BR, 2, chan_dev)
     cells = row_cell.reshape(nblocks, BR)
     weights = jnp.transpose(tap_weight.reshape(KT, nblocks, BR), (1, 0, 2))
     matrix = kernel_matrix(cells, weights, tap_offset)
     table = delay_table()
-    first = _gather_pair(blocks[:, :, 0, :], matrix, pick2, parity, chip, n_owners, slots_dev)
-    second = _gather_pair(blocks[:, :, 1, :], matrix, pick2, parity, chip, n_owners, slots_dev)
+    first = _gather_pair(blocks[:, :, 0, :], matrix, pick, parity, chip, n_owners, slots_dev)
+    second = _gather_pair(blocks[:, :, 1, :], matrix, pick, parity, chip, n_owners, slots_dev)
     galaxy_f = galaxy.astype(jnp.float32)
     table, galaxy_f, second = lax.optimization_barrier((table, galaxy_f, second))
     out = None

time: 329 us -> 337 us (1.024)
  matrix products: 60.3 us -> 84.3 us
  other arithmetic: 86.2 us -> 71.3 us
    dot_general x2, matrix products: 34.1 us -> 55.6 us  [_gather_pair(): jnp.einsum('sb,bcf->scf', pick, contrib, precision=lax.Precision.HIGH, pr...]
    concatenate x2 -> x0, other arithmetic: 14.9 us -> none  [_gather_pair(): jnp.concatenate([high, low], axis=0)]
  transfers between devices with their start and end apart: 12 -> 12, of which waited for: 6 -> 6; matrix products, arithmetic and copies ran while one was open for 35% -> 36% of each run, Pallas kernels for 0% -> 0%
where the time goes in v10:
time: 337 us; the launch traced here: 332 us
  waiting for transfers between devices  99 us (29%)
  matrix products  84.3 us (25%)
  other arithmetic  71.3 us (21%)
  local copies, waits for them, and re-layouts  56.9 us (17%)
  starting transfers between devices  19.2 us (6%)
    ppermute x6, waiting for transfers between devices, _scatter_pairs(): lax.ppermute(send, 'uv', _partner_pairs(n_owners, lambda i, dest=dest: de...  59.3 us
    dot_general x2, matrix products, _gather_pair(): jnp.einsum('sb,bcf->scf', pick, contrib, precision=lax.Precision.HIGH, pr...  55.6 us
    all_to_all x2, waiting for transfers between devices, _scatter_pairs(): lax.all_to_all(gridded, 'chan', split_axis=1, concat_axis=2, tiled=True)  31.4 us
    dot_general x2, matrix products, _gather_pair(): jnp.einsum('bcr,brf->bcf', matrix, part, preferred_element_type=jnp.float32)  21.2 us
    convert_element_type x2, local copies, waits for them, and re-layouts, _gather_pair(): partial = jnp.einsum('sb,bcf->scf', pick, contrib, precision=lax.Precisio...  20 us
    another operation x1, other arithmetic  18.5 us
    concatenate x1, other arithmetic, delay_table(): return jnp.concatenate([upper, lower], axis=0).astype(jnp.bfloat16)  17.3 us
    convert_element_type x2, other arithmetic, _gather_pair(): (mine.astype(jnp.float32) + got.astype(jnp.float32)).astype(jnp.bfloat16)  12.7 us
  transfers between devices with their start and end apart: 12, of which 6 were waited for; matrix products, arithmetic and copies ran while one was open for 36% of the time, Pallas kernels for 0%

profile of v10, /device:TPU:0, one launch (start us, length us, event | category | flops | bytes accessed | tf_op | source)
XLA Modules:
  0.0 332.0 jit_solution(6024310022843797444)
XLA Ops:
  4.7 11.7 %copy.17 = bf16[12288,2,256]{2,0,1:T(8,128)(2,1)} copy(bf16[12288,2,256]{2,1,0:T(2,128)(2,1)} %param.7) | data formatting | bytes 25165824 | tf_op args[0]
  19.3 5.0 %add_bitcast_fusion.7 = (s32[96,128]{1,0:T(8,128)S(1)}, s32[96,128]{1,0:T(8,128)S(1)}, s32[96,128]{1,0:T(8,128)S(1)}, s32[96,128]{1,0:T(8,128)S(1)}, s32[96,128]...) fusion(s32[12288]{0:T(1024)S(1)} %copy-done.1, s32[]{:T(128)} %bitcast.1, ...), kind=kLoop, calls=%fused_computation.81 | loop fusion | flops 98304 | bytes 442400 | tf_op jit(solution)/shard_map/add | solution.py:24
  24.3 10.6 %fusion.13 = f32[96,128,256]{2,1,0:T(8,128)} fusion(bf16[96,128,2,256]{3,1,0,2:T(8,128)(2,1)} %bitcast.107, f32[96,128]{1,0:T(8,128)S(1)} %bitcast.120, s32[96,128]{1,0:T(8,128)S(1)} %get-tuple-element.30, f32[96,128]{1,0:T(8,128)S(1)} %bitcast.122, s32[96,128]{1,0:T(8,128)S(1)} %get-tuple-element.31, f32[96,128]{1,0:T(8,128)S(1)} %bitcast.124, ...), kind=kOutput, calls=%fused_computation.16 | convolution fusion | flops 843055104 | bytes 19660800 | tf_op jit(solution)/shard_map/bcr,brf->bcf/dot_general | solution.py:63
  34.9 28.0 %fusion.6 = bf16[152,128,256]{2,0,1:T(8,128)(2,1)} fusion(f32[96,128,256]{2,1,0:T(8,128)} %fusion.13, s32[96]{0:T(128)S(1)} %fusion.42), kind=kOutput, calls=%fused_computation.11 | convolution fusion | flops 2873899264 | bytes 22544768 | tf_op jit(solution)/shard_map/sb,bcf->scf/dot_general | solution.py:64
  62.9 10.0 %copy.19 = bf16[152,128,256]{2,1,0:T(8,128)(2,1)} copy(bf16[152,128,256]{2,0,1:T(8,128)(2,1)} %fusion.6) | data formatting | bytes 19922944 | tf_op jit(solution)/shard_map/convert_element_type | solution.py:70
  72.9 5.3 %dynamic-slice_bitcast_fusion.1 = bf16[4,19,128,256]{3,2,1,0:T(8,128)(2,1)} fusion(bf16[2,4,19,128,256]{4,3,2,1,0:T(8,128)(2,1)} %bitcast.95, s32[]{:T(128)S(6)} %select_n.120), kind=kLoop, calls=%fused_computation.30 | loop fusion | bytes 9961476 | tf_op jit(solution)/shard_map/jit(dynamic_index_in_dim)/squeeze | solution.py:74
  78.7 10.6 %fusion.12 = f32[96,128,256]{2,1,0:T(8,128)} fusion(bf16[96,128,2,256]{3,1,0,2:T(8,128)(2,1)} %bitcast.108, f32[96,128]{1,0:T(8,128)S(1)} %bitcast.121, s32[96,128]{1,0:T(8,128)S(1)} %get-tuple-element.30, f32[96,128]{1,0:T(8,128)S(1)} %bitcast.123, s32[96,128]{1,0:T(8,128)S(1)} %get-tuple-element.31, f32[96,128]{1,0:T(8,128)S(1)} %bitcast.125, ...), kind=kOutput, calls=%fused_computation.14 | convolution fusion | flops 843055104 | bytes 19660800 | tf_op jit(solution)/shard_map/bcr,brf->bcf/dot_general | solution.py:63
  89.3 27.6 %fusion.9 = bf16[152,128,256]{2,0,1:T(8,128)(2,1)} fusion(f32[96,128,256]{2,1,0:T(8,128)} %fusion.12, s32[96]{0:T(128)S(1)} %fusion.42), kind=kOutput, calls=%fused_computation.12 | convolution fusion | flops 2873899264 | bytes 22544768 | tf_op jit(solution)/shard_map/sb,bcf->scf/dot_general | solution.py:64
  116.9 10.1 %copy.23 = bf16[152,128,256]{2,1,0:T(8,128)(2,1)} copy(bf16[152,128,256]{2,0,1:T(8,128)(2,1)} %fusion.9) | data formatting | bytes 19922944 | tf_op jit(solution)/shard_map/convert_element_type | solution.py:70
  127.0 5.2 %dynamic-slice_bitcast_fusion = bf16[4,19,128,256]{3,2,1,0:T(8,128)(2,1)} fusion(bf16[2,4,19,128,256]{4,3,2,1,0:T(8,128)(2,1)} %bitcast.98, s32[]{:T(128)S(6)} %select_n.120), kind=kLoop, calls=%fused_computation.29 | loop fusion | bytes 9961476 | tf_op jit(solution)/shard_map/jit(dynamic_index_in_dim)/squeeze | solution.py:74
  132.3 6.1 %fusion.5 = bf16[4,19,128,256]{3,2,1,0:T(8,128)(2,1)S(1)} fusion(bf16[4,19,128,256]{3,2,1,0:T(8,128)(2,1)} %collective-permute-done, bf16[2,4,19,128,256]{4,3,2,1,0:T(8,128)(2,1)} %bitcast.96, s32[]{:T(128)S(6)} %select_n.115), kind=kLoop, calls=%fused_computation.9 | loop fusion | flops 9961472 | bytes 14942212 | tf_op jit(solution)/shard_map/convert_element_type | solution.py:76
  144.8 18.5 %multiply_convert_fusion.1 = (bf16[1024,1024]{1,0:T(8,128)(2,1)S(1)}, bf16[1024,1024]{1,0:T(8,128)(2,1)}, bf16[1024,1024]{1,0:T(8,128)(2,1)}) fusion(f32[1024]{0:T(1024)S(1)} %subtract_multiply_fusion), kind=kLoop, calls=%fused_computation.39 | loop fusion | flops 22020096 | bytes 6295552 | tf_op jit(solution)/shard_map/convert.19
  163.4 5.0 %convert_element_type.147 = f32[19,32,2048]{2,1,0:T(8,128)} convert(bf16[19,32,2048]{2,1,0:T(8,128)(2,1)} %param.13) | non-fusion elementwise | flops 1245184 | bytes 7471104 | tf_op jit(solution)/shard_map/convert_element_type | solution.py:125
  168.4 17.3 %maximum_maximum_fusion = bf16[2048,2048]{1,0:T(8,128)(2,1)} fusion(bf16[1024,1024]{1,0:T(8,128)(2,1)} %get-tuple-element.34, bf16[1024,1024]{1,0:T(8,128)(2,1)} %get-tuple-element.33, bf16[1024,1024]{1,0:T(8,128)(2,1)S(1)} %get-tuple-element.32), kind=kLoop, calls=%fused_computation.10 | loop fusion | flops 33554432 | bytes 14680064 | tf_op jit(solution)/shard_map/concatenate | solution.py:44
  185.7 6.6 %fusion.4 = bf16[4,19,128,256]{3,2,1,0:T(8,128)(2,1)} fusion(bf16[4,19,128,256]{3,2,1,0:T(8,128)(2,1)} %collective-permute-done.4, bf16[2,4,19,128,256]{4,3,2,1,0:T(8,128)(2,1)S(1)} %bitcast.102, s32[]{:T(128)S(6)} %select_n.115), kind=kLoop, calls=%fused_computation.7 | loop fusion | flops 9961472 | bytes 14942212 | tf_op jit(solution)/shard_map/convert_element_type | solution.py:76
  192.3 7.0 %collective-permute-done.2 = bf16[19,128,256]{2,1,0:T(8,128)(2,1)} collective-permute-done((bf16[19,128,256]{2,1,0:T(8,128)(2,1)}, bf16[19,128,256]{2,1,0:T(8,128)(2,1)}, u32[]{:S(2)}, u32[]{:S(2)}) %collective-permute-start.2) | collective-permute-done | bytes 1245216 | tf_op jit(solution)/shard_map/ppermute | solution.py:92
  204.6 4.9 %all-to-all-start = ((bf16[19,128,256]{2,0,1:T(8,128)(2,1)}), bf16[19,128,256]{2,0,1:T(8,128)(2,1)S(1)}, u32[]{:S(2)}, u32[]{:S(2)}) async-start(bf16[19,128,256]{2,0,1:T(8,128)(2,1)} %copy.20), calls=%async_computation | async-start | bytes 3145728 | tf_op jit(solution)/shard_map/all_to_all | solution.py:97
  217.3 26.8 %collective-permute-done.5 = bf16[19,128,256]{2,1,0:T(8,128)(2,1)S(1)} collective-permute-done((bf16[19,128,256]{2,1,0:T(8,128)(2,1)S(1)}, bf16[19,128,256]{2,1,0:T(8,128)(2,1)S(1)}, u32[]{:S(2)}, u32[]{:S(2)}) %collective-permute-start.5) | collective-permute-done | bytes 1245216 | tf_op jit(solution)/shard_map/ppermute | solution.py:92
  244.1 25.5 %collective-permute-done.6 = bf16[19,128,256]{2,1,0:T(8,128)(2,1)S(1)} collective-permute-done((bf16[19,128,256]{2,1,0:T(8,128)(2,1)S(1)}, bf16[19,128,256]{2,1,0:T(8,128)(2,1)S(1)}, u32[]{:S(2)}, u32[]{:S(2)}) %collective-permute-start.6) | collective-permute-done | bytes 1245216 | tf_op jit(solution)/shard_map/ppermute | solution.py:92
  272.3 5.1 %all-to-all-start.1 = ((bf16[19,128,256]{2,0,1:T(8,128)(2,1)}), bf16[19,128,256]{2,0,1:T(8,128)(2,1)S(1)}, u32[]{:S(2)}, u32[]{:S(2)}) async-start(bf16[19,128,256]{2,0,1:T(8,128)(2,1)} %copy.24), calls=%async_computation.1 | async-start | bytes 3145728 | tf_op jit(solution)/shard_map/all_to_all | solution.py:97
  278.6 31.4 %all-to-all-done.1 = bf16[19,128,256]{2,0,1:T(8,128)(2,1)S(1)} async-done(((bf16[19,128,256]{2,0,1:T(8,128)(2,1)}), bf16[19,128,256]{2,0,1:T(8,128)(2,1)S(1)}, u32[]{:S(2)}, u32[]{:S(2)}) %all-to-all-start.1) | async-done | bytes 1245216 | tf_op jit(solution)/shard_map/all_to_all | solution.py:97
  311.3 4.7 %fusion.17 = f32[608,2048]{1,0:T(8,128)S(1)} fusion(bf16[608,1024]{1,0:T(8,128)(2,1)S(1)} %bitcast.116, bf16[2048,2048]{1,0:T(8,128)(2,1)} %maximum_maximum_fusion), kind=kOutput, calls=%fused_computation.34 | convolution fusion | flops 2550136832 | bytes 10420224 | tf_op jit(solution)/shard_map/dot_general | solution.py:131
  320.3 4.6 %collective-permute-done.8 = f32[19,1024]{1,0:T(8,128)S(1)} collective-permute-done((f32[19,1024]{1,0:T(8,128)S(1)}, f32[19,1024]{1,0:T(8,128)S(1)}, u32[]{:S(2)}, u32[]{:S(2)}) %collective-permute-start.8) | collective-permute-done | bytes 77856 | tf_op jit(solution)/shard_map/ppermute | solution.py:56
  327.4 3.7 %collective-permute-done.9 = f32[19,1024]{1,0:T(8,128)S(1)} collective-permute-done((f32[19,1024]{1,0:T(8,128)S(1)}, f32[19,1024]{1,0:T(8,128)S(1)}, u32[]{:S(2)}, u32[]{:S(2)}) %collective-permute-start.9) | collective-permute-done | bytes 77856 | tf_op jit(solution)/shard_map/ppermute | solution.py:56
  (66 shorter events, 39.6 us)
Async XLA Ops:
  4.7 11.8 %copy-start.2 = (s32[96]{0:T(128)S(1)}, s32[96]{0:T(128)}, u32[]{:S(2)}) copy-start(s32[96]{0:T(128)} %param.11) | copy-start | bytes 1156
  4.7 11.8 %copy-start = (s32[80]{0:T(128)S(1)}, s32[80]{0:T(128)}, u32[]{:S(2)}) copy-start(s32[80]{0:T(128)} %param.12) | copy-start | bytes 964
  4.7 14.6 %copy-start.1 = (s32[12288]{0:T(1024)S(1)}, s32[12288]{0:T(1024)}, u32[]{:S(2)}) copy-start(s32[12288]{0:T(1024)} %param.8) | copy-start | bytes 147460
  78.2 54.0 %collective-permute-start = (bf16[4,19,128,256]{3,2,1,0:T(8,128)(2,1)}, bf16[4,19,128,256]{3,2,1,0:T(8,128)(2,1)}, u32[]{:S(2)}, u32[]{:S(2)}) collective-permute-start(bf16[4,19,128,256]{3,2,1,0:T(8,128)(2,1)} %dynamic-slice_bitcast_fusion.1), channel_id=1, source_target_pairs={{0,4},{4,0},{8,12},{12,8},{16,20},{20,16},{24,28},{28,24},{1,5},{5... | collective-permute-start | bytes 14942216 | tf_op jit(solution)/shard_map/ppermute | solution.py:75
  132.2 53.5 %collective-permute-start.4 = (bf16[4,19,128,256]{3,2,1,0:T(8,128)(2,1)}, bf16[4,19,128,256]{3,2,1,0:T(8,128)(2,1)}, u32[]{:S(2)}, u32[]{:S(2)}) collective-permute-start(bf16[4,19,128,256]{3,2,1,0:T(8,128)(2,1)} %dynamic-slice_bitcast_fusion), channel_id=1, source_target_pairs={{0,4},{4,0},{8,12},{12,8},{16,20},{20,16},{24,28},{28,24},{1,5},{5... | collective-permute-start | bytes 14942216 | tf_op jit(solution)/shard_map/ppermute | solution.py:75
  140.3 52.0 %collective-permute-start.1 = (bf16[19,128,256]{2,1,0:T(8,128)(2,1)}, bf16[19,128,256]{2,1,0:T(8,128)(2,1)S(1)}, u32[]{:S(2)}, u32[]{:S(2)}) collective-permute-start(bf16[19,128,256]{2,1,0:T(8,128)(2,1)} %get-tuple-element.10), channel_id=1, source_target_pairs={{0,8},{4,12},{8,0},{12,4},{16,24},{20,28},{24,16},{28,20},{1,9},{5... | collective-permute-start | bytes 3735560 | tf_op jit(solution)/shard_map/ppermute | solution.py:92
  143.3 56.0 %collective-permute-start.2 = (bf16[19,128,256]{2,1,0:T(8,128)(2,1)}, bf16[19,128,256]{2,1,0:T(8,128)(2,1)}, u32[]{:S(2)}, u32[]{:S(2)}) collective-permute-start(bf16[19,128,256]{2,1,0:T(8,128)(2,1)} %get-tuple-element.12), channel_id=1, source_target_pairs={{0,16},{4,20},{8,24},{12,28},{16,0},{20,4},{24,8},{28,12},{1,17},{... | collective-permute-start | bytes 3735560 | tf_op jit(solution)/shard_map/ppermute | solution.py:92
  144.8 54.5 %collective-permute-start.3 = (bf16[19,128,256]{2,1,0:T(8,128)(2,1)}, bf16[19,128,256]{2,1,0:T(8,128)(2,1)}, u32[]{:S(2)}, u32[]{:S(2)}) collective-permute-start(bf16[19,128,256]{2,1,0:T(8,128)(2,1)} %get-tuple-element.11), channel_id=1, source_target_pairs={{0,24},{4,28},{8,16},{12,20},{16,8},{20,12},{24,0},{28,4},{1,25},{... | collective-permute-start | bytes 3735560 | tf_op jit(solution)/shard_map/ppermute | solution.py:92
  163.4 22.3 %slice-start = ((s8[9961472]{0:T(1024)(128)(4,1)}), s8[4194304]{0:T(1024)(128)(4,1)S(1)}, s32[]{:S(2)}) async-start(s8[9961472]{0:T(1024)(128)(4,1)} %bitcast.100), calls=%async_computation.2 | async-start | bytes 8388608
  163.4 22.3 %slice-start.1 = ((s8[9961472]{0:T(1024)(128)(4,1)}), s8[4194304]{0:T(1024)(128)(4,1)S(1)}, s32[]{:S(2)}) async-start(s8[9961472]{0:T(1024)(128)(4,1)} %bitcast.100), calls=%async_computation.3 | async-start | bytes 8388608
  168.4 17.4 %slice-start.2 = ((s8[9961472]{0:T(1024)(128)(4,1)}), s8[1572864]{0:T(1024)(128)(4,1)S(1)}, s32[]{:S(2)}) async-start(s8[9961472]{0:T(1024)(128)(4,1)} %bitcast.100), calls=%async_computation.4 | async-start | bytes 3145728
  204.6 67.6 %all-to-all-start = ((bf16[19,128,256]{2,0,1:T(8,128)(2,1)}), bf16[19,128,256]{2,0,1:T(8,128)(2,1)S(1)}, u32[]{:S(2)}, u32[]{:S(2)}) async-start(bf16[19,128,256]{2,0,1:T(8,128)(2,1)} %copy.20), calls=%async_computation | async-start | bytes 3145728 | tf_op jit(solution)/shard_map/all_to_all | solution.py:97
  213.8 30.3 %collective-permute-start.5 = (bf16[19,128,256]{2,1,0:T(8,128)(2,1)S(1)}, bf16[19,128,256]{2,1,0:T(8,128)(2,1)S(1)}, u32[]{:S(2)}, u32[]{:S(2)}) collective-permute-start(bf16[19,128,256]{2,1,0:T(8,128)(2,1)S(1)} %get-tuple-element.13), channel_id=1, source_target_pairs={{0,8},{4,12},{8,0},{12,4},{16,24},{20,28},{24,16},{28,20},{1,9},{5... | collective-permute-start | bytes 3735560 | tf_op jit(solution)/shard_map/ppermute | solution.py:92
  215.1 54.5 %collective-permute-start.6 = (bf16[19,128,256]{2,1,0:T(8,128)(2,1)S(1)}, bf16[19,128,256]{2,1,0:T(8,128)(2,1)S(1)}, u32[]{:S(2)}, u32[]{:S(2)}) collective-permute-start(bf16[19,128,256]{2,1,0:T(8,128)(2,1)S(1)} %get-tuple-element.15), channel_id=1, source_target_pairs={{0,16},{4,20},{8,24},{12,28},{16,0},{20,4},{24,8},{28,12},{1,17},{... | collective-permute-start | bytes 3735560 | tf_op jit(solution)/shard_map/ppermute | solution.py:92
  215.9 53.7 %collective-permute-start.7 = (bf16[19,128,256]{2,1,0:T(8,128)(2,1)S(1)}, bf16[19,128,256]{2,1,0:T(8,128)(2,1)S(1)}, u32[]{:S(2)}, u32[]{:S(2)}) collective-permute-start(bf16[19,128,256]{2,1,0:T(8,128)(2,1)S(1)} %get-tuple-element.14), channel_id=1, source_target_pairs={{0,24},{4,28},{8,16},{12,20},{16,8},{20,12},{24,0},{28,4},{1,25},{... | collective-permute-start | bytes 3735560 | tf_op jit(solution)/shard_map/ppermute | solution.py:92
  272.3 37.7 %all-to-all-start.1 = ((bf16[19,128,256]{2,0,1:T(8,128)(2,1)}), bf16[19,128,256]{2,0,1:T(8,128)(2,1)S(1)}, u32[]{:S(2)}, u32[]{:S(2)}) async-start(bf16[19,128,256]{2,0,1:T(8,128)(2,1)} %copy.24), calls=%async_computation.1 | async-start | bytes 3145728 | tf_op jit(solution)/shard_map/all_to_all | solution.py:97
  311.0 5.0 %slice-start.5 = ((s8[8388608]{0:T(1024)(128)(4,1)}), s8[4194304]{0:T(1024)(128)(4,1)S(1)}, s32[]{:S(2)}) async-start(s8[8388608]{0:T(1024)(128)(4,1)} %bitcast.109), calls=%async_computation.7 | async-start | bytes 8388608
  311.2 4.7 %slice-start.6 = ((s8[8388608]{0:T(1024)(128)(4,1)}), s8[4194304]{0:T(1024)(128)(4,1)S(1)}, s32[]{:S(2)}) async-start(s8[8388608]{0:T(1024)(128)(4,1)} %bitcast.109), calls=%async_computation.8 | async-start | bytes 8388608
  311.3 7.5 %slice-start.3 = ((s8[4980736]{0:T(1024)(128)(4,1)}), s8[4194304]{0:T(1024)(128)(4,1)S(1)}, s32[]{:S(2)}) async-start(s8[4980736]{0:T(1024)(128)(4,1)} %bitcast.103), calls=%async_computation.5 | async-start | bytes 8388608
  316.0 2.8 slice-start.4
  320.2 4.7 %collective-permute-start.8 = (f32[19,1024]{1,0:T(8,128)S(1)}, f32[19,1024]{1,0:T(8,128)S(1)}, u32[]{:S(2)}, u32[]{:S(2)}) collective-permute-start(f32[19,1024]{1,0:T(8,128)S(1)} %fusion.28), channel_id=1, source_target_pairs={{0,1},{1,0},{2,3},{3,2},{4,5},{5,4},{6,7},{7,6},{8,9},{9,8},{10,11... | collective-permute-start | bytes 233480 | tf_op jit(solution)/shard_map/ppermute | solution.py:56
  324.9 6.2 %collective-permute-start.9 = (f32[19,1024]{1,0:T(8,128)S(1)}, f32[19,1024]{1,0:T(8,128)S(1)}, u32[]{:S(2)}, u32[]{:S(2)}) collective-permute-start(f32[19,1024]{1,0:T(8,128)S(1)} %add.325), channel_id=1, source_target_pairs={{0,2},{1,3},{2,0},{3,1},{4,6},{5,7},{6,4},{7,5},{8,10},{9,11},{10,... | collective-permute-start | bytes 233480 | tf_op jit(solution)/shard_map/ppermute | solution.py:56

commit v11 on v6

--- a/solution.py
+++ b/solution.py
@@ -146,7 +146,14 @@
     out = None
     for k, (pair_send, own) in enumerate((first, second)):
         gridded = _scatter_pairs(pair_send, own, chip, n_owners)
-        term = _chan_delay(gridded, table[k * CH:(k + 1) * CH], n_chan)
+        half = table[k * CH:(k + 1) * CH]
+        if k == 0:
+            piece = lax.all_to_all(gridded, "chan", split_axis=1, concat_axis=2, tiled=True)
+            term = jnp.dot(
+                piece.reshape(-1, CH), half, preferred_element_type=jnp.float32
+            )
+        else:
+            term = _chan_delay(gridded, half, n_chan)
         out = term if out is None else out + term
     count, cells_part = slots_dev, TC // n_chan
     delay = out.reshape(count, cells_part, 2 * CH)

time: 356 us -> 347 us (0.975)
  matrix products: 83 us -> 74 us
  local copies, waits for them, and re-layouts: 52.9 us -> 60.1 us
  waiting for transfers between devices: 95.6 us -> 89.5 us
  starting transfers between devices: 33.1 us -> 29 us
    dot_general x8 -> x4, matrix products: 29.8 us -> 12.3 us  [_chan_delay(): jnp.dot(recv.reshape(-1, width), rows, preferred_element_type=jnp.float32)]
    dot_general x0 -> x1, matrix products: none -> 8.93 us  [body(): jnp.dot(piece.reshape(-1, CH), half, preferred_element_type=jnp.float32)]
    ppermute x6, waiting for transfers between devices: 82.3 us -> 73.9 us  [_scatter_pairs(): lax.ppermute(send, 'uv', _partner_pairs(n_owners, lambda i, dest=dest: de...]
    ppermute x6 -> x3, starting transfers between devices: 11.7 us -> 5.79 us  [_chan_delay(): lax.ppermute(send, 'chan', [(i, (i + d) % n_chan) for i in range(n_chan)])]
    all_to_all x0 -> x1, starting transfers between devices: none -> 5.24 us  [body(): lax.all_to_all(gridded, 'chan', split_axis=1, concat_axis=2, tiled=True)]
    ppermute x6 -> x3, waiting for transfers between devices: 8.2 us -> 12.2 us  [_chan_delay(): lax.ppermute(send, 'chan', [(i, (i + d) % n_chan) for i in range(n_chan)])]
    unnamed x15 -> x24, local copies, waits for them, and re-layouts: 11.7 us -> 12.1 us
  transfers between devices with their start and end apart: 16 -> 14, of which waited for: 5 -> 6; matrix products, arithmetic and copies ran while one was open for 38% -> 40% of each run, Pallas kernels for 0% -> 0%
where the time goes in v11:
time: 347 us; the launch traced here: 341 us
  waiting for transfers between devices  89.5 us (26%)
  other arithmetic  87.1 us (25%)
  matrix products  74 us (21%)
  local copies, waits for them, and re-layouts  60.1 us (17%)
  starting transfers between devices  29 us (8%)
    ppermute x6, waiting for transfers between devices, _scatter_pairs(): lax.ppermute(send, 'uv', _partner_pairs(n_owners, lambda i, dest=dest: de...  73.9 us
    dot_general x2, matrix products, _gather_pair(): jnp.einsum('sb,bcf->scf', pick2, jnp.concatenate([high, low], axis=0), pr...  34 us
    convert_element_type x2, local copies, waits for them, and re-layouts, _gather_pair(): partial = jnp.einsum('sb,bcf->scf', pick2, jnp.concatenate([high, low], a...  20.1 us
    dot_general x2, matrix products, _gather_pair(): jnp.einsum('bcr,brf->bcf', matrix, part, preferred_element_type=jnp.float32)  18.7 us
    another operation x1, other arithmetic  18.7 us
    concatenate x1, other arithmetic, delay_table(): return jnp.concatenate([upper, lower], axis=0).astype(jnp.bfloat16)  17.2 us
    concatenate x2, other arithmetic, _gather_pair(): jnp.concatenate([high, low], axis=0)  14.8 us
    dot_general x4, matrix products, _chan_delay(): jnp.dot(recv.reshape(-1, width), rows, preferred_element_type=jnp.float32)  12.3 us
  transfers between devices with their start and end apart: 14, of which 6 were waited for; matrix products, arithmetic and copies ran while one was open for 40% of the time, Pallas kernels for 0%

profile of v11, /device:TPU:0, one launch (start us, length us, event | category | flops | bytes accessed | tf_op | source)
XLA Modules:
  0.0 340.8 jit_solution(13598290178309584025)
XLA Ops:
  4.4 11.7 %copy.21 = bf16[12288,2,256]{2,0,1:T(8,128)(2,1)} copy(bf16[12288,2,256]{2,1,0:T(2,128)(2,1)} %param.7) | data formatting | bytes 25165824 | tf_op args[0]
  19.1 5.0 %add_bitcast_fusion.10 = (s32[96,128]{1,0:T(8,128)S(1)}, s32[96,128]{1,0:T(8,128)S(1)}, s32[96,128]{1,0:T(8,128)S(1)}, s32[96,128]{1,0:T(8,128)S(1)}, s32[96,128...) fusion(s32[12288]{0:T(1024)S(1)} %copy-done.4, s32[]{:T(128)} %bitcast.1, ...), kind=kLoop, calls=%fused_computation.91 | loop fusion | flops 98304 | bytes 442400 | tf_op jit(solution)/shard_map/add | solution.py:24
  24.1 9.4 %subtract_convert_fusion.1 = (bf16[96,128,256]{2,1,0:T(8,128)(2,1)S(1)}, bf16[96,128,256]{2,1,0:T(8,128)(2,1)S(1)}) fusion(bf16[96,128,2,256]{3,1,0,2:T(8,128)(2,1)} %bitcast.113, f32[96,128]{1,0:T(8,128)S(1)} %bitcast.124, s32[96,128]{1,0:T(8,128)S(1)} %get-tuple-element.36, f32[96,128]{1,0:T(8,128)S(1)} %bitcast.126, s32[96,128]{1,0:T(8,128)S(1)} %get-tuple-element.37, ...), kind=kOutput, calls=%fused_computation.9 | convolution fusion | flops 855638016 | bytes 19660800 | tf_op jit(solution)/shard_map/bcr,brf->bcf/dot_general | solution.py:63
  33.5 7.3 %pad_maximum_fusion = bf16[192,128,256]{2,1,0:T(8,128)(2,1)} fusion(bf16[96,128,256]{2,1,0:T(8,128)(2,1)S(1)} %get-tuple-element.8, bf16[96,128,256]{2,1,0:T(8,128)(2,1)S(1)} %get-tuple-element.9), kind=kLoop, calls=%fused_computation.2 | loop fusion | flops 6291456 | bytes 25165824 | tf_op jit(solution)/shard_map/concatenate | solution.py:69
  40.8 17.0 %fusion.6 = bf16[152,128,256]{2,0,1:T(8,128)(2,1)} fusion(bf16[192,128,256]{2,1,0:T(8,128)(2,1)} %pad_maximum_fusion, pred[152,96]{1,0:T(8,128)(4,1)S(1)} %iota_compare_fusion.8), kind=kOutput, calls=%fused_computation.15 | convolution fusion | flops 1917612544 | bytes 22558976 | tf_op jit(solution)/shard_map/sb,bcf->scf/dot_general | solution.py:66
  57.8 10.0 %copy.23 = bf16[152,128,256]{2,1,0:T(8,128)(2,1)} copy(bf16[152,128,256]{2,0,1:T(8,128)(2,1)} %fusion.6) | data formatting | bytes 19922944 | tf_op jit(solution)/shard_map/convert_element_type | solution.py:71
  67.8 5.2 %dynamic-slice_bitcast_fusion.1 = bf16[4,19,128,256]{3,2,1,0:T(8,128)(2,1)} fusion(bf16[2,4,19,128,256]{4,3,2,1,0:T(8,128)(2,1)} %bitcast.101, s32[]{:T(128)S(6)} %select_n.174), kind=kLoop, calls=%fused_computation.35 | loop fusion | bytes 9961476 | tf_op jit(solution)/shard_map/jit(dynamic_index_in_dim)/squeeze | solution.py:75
  73.5 9.4 %subtract_convert_fusion = (bf16[96,128,256]{2,1,0:T(8,128)(2,1)S(1)}, bf16[96,128,256]{2,1,0:T(8,128)(2,1)S(1)}) fusion(bf16[96,128,2,256]{3,1,0,2:T(8,128)(2,1)} %bitcast.114, f32[96,128]{1,0:T(8,128)S(1)} %bitcast.125, s32[96,128]{1,0:T(8,128)S(1)} %get-tuple-element.36, f32[96,128]{1,0:T(8,128)S(1)} %bitcast.127, s32[96,128]{1,0:T(8,128)S(1)} %get-tuple-element.37, ...), kind=kOutput, calls=%fused_computation.8 | convolution fusion | flops 855638016 | bytes 19660800 | tf_op jit(solution)/shard_map/bcr,brf->bcf/dot_general | solution.py:63
  82.9 7.6 %pad_maximum_fusion.1 = bf16[192,128,256]{2,1,0:T(8,128)(2,1)} fusion(bf16[96,128,256]{2,1,0:T(8,128)(2,1)S(1)} %get-tuple-element.10, bf16[96,128,256]{2,1,0:T(8,128)(2,1)S(1)} %get-tuple-element.11), kind=kLoop, calls=%fused_computation.3 | loop fusion | flops 6291456 | bytes 25165824 | tf_op jit(solution)/shard_map/concatenate | solution.py:69
  90.4 17.0 %fusion.9 = bf16[152,128,256]{2,0,1:T(8,128)(2,1)} fusion(bf16[192,128,256]{2,1,0:T(8,128)(2,1)} %pad_maximum_fusion.1, pred[152,96]{1,0:T(8,128)(4,1)S(1)} %iota_compare_fusion.8), kind=kOutput, calls=%fused_computation.16 | convolution fusion | flops 1917612544 | bytes 22558976 | tf_op jit(solution)/shard_map/sb,bcf->scf/dot_general | solution.py:66
  107.5 10.1 %copy.27 = bf16[152,128,256]{2,1,0:T(8,128)(2,1)} copy(bf16[152,128,256]{2,0,1:T(8,128)(2,1)} %fusion.9) | data formatting | bytes 19922944 | tf_op jit(solution)/shard_map/convert_element_type | solution.py:71
  117.5 5.3 %dynamic-slice_bitcast_fusion = bf16[4,19,128,256]{3,2,1,0:T(8,128)(2,1)} fusion(bf16[2,4,19,128,256]{4,3,2,1,0:T(8,128)(2,1)} %bitcast.104, s32[]{:T(128)S(6)} %select_n.174), kind=kLoop, calls=%fused_computation.34 | loop fusion | bytes 9961476 | tf_op jit(solution)/shard_map/jit(dynamic_index_in_dim)/squeeze | solution.py:75
  123.0 18.7 %multiply_convert_fusion.1 = (bf16[1024,1024]{1,0:T(8,128)(2,1)S(1)}, bf16[1024,1024]{1,0:T(8,128)(2,1)}, bf16[1024,1024]{1,0:T(8,128)(2,1)}) fusion(f32[1024]{0:T(1024)S(1)} %subtract_multiply_fusion), kind=kLoop, calls=%fused_computation.42 | loop fusion | flops 22020096 | bytes 6295552 | tf_op jit(solution)/shard_map/convert.20
  141.7 6.1 %fusion.5 = bf16[4,19,128,256]{3,2,1,0:T(8,128)(2,1)S(1)} fusion(bf16[4,19,128,256]{3,2,1,0:T(8,128)(2,1)} %collective-permute-done, bf16[2,4,19,128,256]{4,3,2,1,0:T(8,128)(2,1)} %bitcast.102, s32[]{:T(128)S(6)} %select_n.169), kind=kLoop, calls=%fused_computation.13 | loop fusion | flops 9961472 | bytes 14942212 | tf_op jit(solution)/shard_map/convert_element_type | solution.py:77
  152.8 17.2 %maximum_maximum_fusion = bf16[2048,2048]{1,0:T(8,128)(2,1)} fusion(bf16[1024,1024]{1,0:T(8,128)(2,1)} %get-tuple-element.40, bf16[1024,1024]{1,0:T(8,128)(2,1)} %get-tuple-element.39, bf16[1024,1024]{1,0:T(8,128)(2,1)S(1)} %get-tuple-element.38), kind=kLoop, calls=%fused_computation.14 | loop fusion | flops 33554432 | bytes 14680064 | tf_op jit(solution)/shard_map/concatenate | solution.py:44
  172.1 4.6 %fusion.4 = bf16[4,19,128,256]{3,2,1,0:T(8,128)(2,1)S(1)} fusion(bf16[4,19,128,256]{3,2,1,0:T(8,128)(2,1)} %collective-permute-done.4, bf16[2,4,19,128,256]{4,3,2,1,0:T(8,128)(2,1)S(1)} %bitcast.107, s32[]{:T(128)S(6)} %select_n.169), kind=kLoop, calls=%fused_computation.11 | loop fusion | flops 9961472 | bytes 14942212 | tf_op jit(solution)/shard_map/convert_element_type | solution.py:77
  185.2 4.6 %convert_element_type.185 = f32[19,32,2048]{2,1,0:T(8,128)} convert(bf16[19,32,2048]{2,1,0:T(8,128)(2,1)} %param.13) | non-fusion elementwise | flops 1245184 | bytes 7471104 | tf_op jit(solution)/shard_map/convert_element_type | solution.py:160
  189.8 4.8 %slice.91 = bf16[1024,2048]{1,0:T(8,128)(2,1)} slice(bf16[2048,2048]{1,0:T(8,128)(2,1)} %maximum_maximum_fusion), slice={[1024:2048], [0:2048]} | slice | bytes 8388608 | tf_op jit(solution)/shard_map/slice | solution.py:149
  194.6 32.6 %collective-permute-done.2 = bf16[19,128,256]{2,1,0:T(8,128)(2,1)} collective-permute-done((bf16[19,128,256]{2,1,0:T(8,128)(2,1)}, bf16[19,128,256]{2,1,0:T(8,128)(2,1)}, u32[]{:S(2)}, u32[]{:S(2)}) %collective-permute-start.2) | collective-permute-done | bytes 1245216 | tf_op jit(solution)/shard_map/ppermute | solution.py:93
  232.9 5.2 %all-to-all-start = ((bf16[19,128,256]{2,0,1:T(8,128)(2,1)}), bf16[19,128,256]{2,0,1:T(8,128)(2,1)}, u32[]{:S(2)}, u32[]{:S(2)}) async-start(bf16[19,128,256]{2,0,1:T(8,128)(2,1)} %copy.24), calls=%async_computation | async-start | bytes 3145728 | tf_op jit(solution)/shard_map/all_to_all | solution.py:151
  238.2 41.4 %collective-permute-done.6 = bf16[19,128,256]{2,1,0:T(8,128)(2,1)} collective-permute-done((bf16[19,128,256]{2,1,0:T(8,128)(2,1)}, bf16[19,128,256]{2,1,0:T(8,128)(2,1)}, u32[]{:S(2)}, u32[]{:S(2)}) %collective-permute-start.6) | collective-permute-done | bytes 1245216 | tf_op jit(solution)/shard_map/ppermute | solution.py:93
  297.7 8.8 %collective-permute-done.9 = bf16[19,32,256]{2,1,0:T(8,128)(2,1)S(1)} collective-permute-done((bf16[19,32,256]{2,1,0:T(8,128)(2,1)S(1)}, bf16[19,32,256]{2,1,0:T(8,128)(2,1)S(1)}, u32[]{:S(2)}, u32[]{:S(2)}) %collective-permute-start.9) | collective-permute-done | bytes 311328 | tf_op jit(solution)/shard_map/ppermute | solution.py:111
  315.6 8.9 %add_add_fusion = f32[608,2048]{1,0:T(8,128)S(1)} fusion(f32[608,2048]{1,0:T(8,128)S(1)} %copy-done.1, f32[608,2048]{1,0:T(8,128)} %fusion.33, f32[608,2048]{1,0:T(8,128)} %fusion.37, f32[608,2048]{1,0:T(8,128)} %fusion.35, bf16[608,1024]{1,0:T(8,128)(2,1)S(1)} %bitcast.116, bf16[2048,2048]{1,0:T(8,128)(2,1)} %maximum_maximum_fusion), kind=kOutput, calls=%fused_computation.33 | convolution fusion | flops 2555117568 | bytes 30343168 | tf_op jit(solution)/shard_map/dot_general | solution.py:152
  325.9 5.4 %collective-permute-start.11 = (f32[19,1024]{1,0:T(8,128)S(1)}, f32[19,1024]{1,0:T(8,128)S(1)}, u32[]{:S(2)}, u32[]{:S(2)}) collective-permute-start(f32[19,1024]{1,0:T(8,128)S(1)} %fusion.23), channel_id=1, source_target_pairs={{0,1},{1,0},{2,3},{3,2},{4,5},{5,4},{6,7},{7,6},{8,9},{9,8},{10,11... | collective-permute-start | bytes 233480 | tf_op jit(solution)/shard_map/ppermute | solution.py:56
  (76 shorter events, 66.4 us)
Async XLA Ops:
  4.4 11.7 %copy-start.5 = (s32[96]{0:T(128)S(1)}, s32[96]{0:T(128)}, u32[]{:S(2)}) copy-start(s32[96]{0:T(128)} %param.11) | copy-start | bytes 1156
  4.4 11.7 %copy-start = (s32[80]{0:T(128)S(1)}, s32[80]{0:T(128)}, u32[]{:S(2)}) copy-start(s32[80]{0:T(128)} %param.12) | copy-start | bytes 964
  4.4 14.6 %copy-start.4 = (s32[12288]{0:T(1024)S(1)}, s32[12288]{0:T(1024)}, u32[]{:S(2)}) copy-start(s32[12288]{0:T(1024)} %param.8) | copy-start | bytes 147460
  73.0 68.7 %collective-permute-start = (bf16[4,19,128,256]{3,2,1,0:T(8,128)(2,1)}, bf16[4,19,128,256]{3,2,1,0:T(8,128)(2,1)}, u32[]{:S(2)}, u32[]{:S(2)}) collective-permute-start(bf16[4,19,128,256]{3,2,1,0:T(8,128)(2,1)} %dynamic-slice_bitcast_fusion.1), channel_id=1, source_target_pairs={{0,4},{4,0},{8,12},{12,8},{16,20},{20,16},{24,28},{28,24},{1,5},{5... | collective-permute-start | bytes 14942216 | tf_op jit(solution)/shard_map/ppermute | solution.py:76
  122.9 49.2 %collective-permute-start.4 = (bf16[4,19,128,256]{3,2,1,0:T(8,128)(2,1)}, bf16[4,19,128,256]{3,2,1,0:T(8,128)(2,1)}, u32[]{:S(2)}, u32[]{:S(2)}) collective-permute-start(bf16[4,19,128,256]{3,2,1,0:T(8,128)(2,1)} %dynamic-slice_bitcast_fusion), channel_id=1, source_target_pairs={{0,4},{4,0},{8,12},{12,8},{16,20},{20,16},{24,28},{28,24},{1,5},{5... | collective-permute-start | bytes 14942216 | tf_op jit(solution)/shard_map/ppermute | solution.py:76
  147.8 24.3 %slice-start = ((s8[9961472]{0:T(1024)(128)(4,1)}), s8[4194304]{0:T(1024)(128)(4,1)S(1)}, s32[]{:S(2)}) async-start(s8[9961472]{0:T(1024)(128)(4,1)} %bitcast.105), calls=%async_computation.1 | async-start | bytes 8388608
  147.8 24.3 %slice-start.1 = ((s8[9961472]{0:T(1024)(128)(4,1)}), s8[4194304]{0:T(1024)(128)(4,1)S(1)}, s32[]{:S(2)}) async-start(s8[9961472]{0:T(1024)(128)(4,1)} %bitcast.105), calls=%async_computation.2 | async-start | bytes 8388608
  149.8 34.9 %collective-permute-start.1 = (bf16[19,128,256]{2,1,0:T(8,128)(2,1)}, bf16[19,128,256]{2,1,0:T(8,128)(2,1)}, u32[]{:S(2)}, u32[]{:S(2)}) collective-permute-start(bf16[19,128,256]{2,1,0:T(8,128)(2,1)} %get-tuple-element.12), channel_id=1, source_target_pairs={{0,8},{4,12},{8,0},{12,4},{16,24},{20,28},{24,16},{28,20},{1,9},{5... | collective-permute-start | bytes 3735560 | tf_op jit(solution)/shard_map/ppermute | solution.py:93
  152.8 19.3 %slice-start.2 = ((s8[9961472]{0:T(1024)(128)(4,1)}), s8[1572864]{0:T(1024)(128)(4,1)S(1)}, s32[]{:S(2)}) async-start(s8[9961472]{0:T(1024)(128)(4,1)} %bitcast.105), calls=%async_computation.3 | async-start | bytes 3145728
  169.9 57.2 %collective-permute-start.2 = (bf16[19,128,256]{2,1,0:T(8,128)(2,1)}, bf16[19,128,256]{2,1,0:T(8,128)(2,1)}, u32[]{:S(2)}, u32[]{:S(2)}) collective-permute-start(bf16[19,128,256]{2,1,0:T(8,128)(2,1)} %get-tuple-element.14), channel_id=1, source_target_pairs={{0,16},{4,20},{8,24},{12,28},{16,0},{20,4},{24,8},{28,12},{1,17},{... | collective-permute-start | bytes 3735560 | tf_op jit(solution)/shard_map/ppermute | solution.py:93
  171.6 55.6 %collective-permute-start.3 = (bf16[19,128,256]{2,1,0:T(8,128)(2,1)}, bf16[19,128,256]{2,1,0:T(8,128)(2,1)}, u32[]{:S(2)}, u32[]{:S(2)}) collective-permute-start(bf16[19,128,256]{2,1,0:T(8,128)(2,1)} %get-tuple-element.13), channel_id=1, source_target_pairs={{0,24},{4,28},{8,16},{12,20},{16,8},{20,12},{24,0},{28,4},{1,25},{... | collective-permute-start | bytes 3735560 | tf_op jit(solution)/shard_map/ppermute | solution.py:93
  181.7 56.5 %collective-permute-start.5 = (bf16[19,128,256]{2,1,0:T(8,128)(2,1)}, bf16[19,128,256]{2,1,0:T(8,128)(2,1)}, u32[]{:S(2)}, u32[]{:S(2)}) collective-permute-start(bf16[19,128,256]{2,1,0:T(8,128)(2,1)} %get-tuple-element.15), channel_id=1, source_target_pairs={{0,8},{4,12},{8,0},{12,4},{16,24},{20,28},{24,16},{28,20},{1,9},{5... | collective-permute-start | bytes 3735560 | tf_op jit(solution)/shard_map/ppermute | solution.py:93
  183.1 96.5 %collective-permute-start.6 = (bf16[19,128,256]{2,1,0:T(8,128)(2,1)}, bf16[19,128,256]{2,1,0:T(8,128)(2,1)}, u32[]{:S(2)}, u32[]{:S(2)}) collective-permute-start(bf16[19,128,256]{2,1,0:T(8,128)(2,1)} %get-tuple-element.17), channel_id=1, source_target_pairs={{0,16},{4,20},{8,24},{12,28},{16,0},{20,4},{24,8},{28,12},{1,17},{... | collective-permute-start | bytes 3735560 | tf_op jit(solution)/shard_map/ppermute | solution.py:93
  184.7 94.8 %collective-permute-start.7 = (bf16[19,128,256]{2,1,0:T(8,128)(2,1)}, bf16[19,128,256]{2,1,0:T(8,128)(2,1)}, u32[]{:S(2)}, u32[]{:S(2)}) collective-permute-start(bf16[19,128,256]{2,1,0:T(8,128)(2,1)} %get-tuple-element.16), channel_id=1, source_target_pairs={{0,24},{4,28},{8,16},{12,20},{16,8},{20,12},{24,0},{28,4},{1,25},{... | collective-permute-start | bytes 3735560 | tf_op jit(solution)/shard_map/ppermute | solution.py:93
  194.6 85.0 %copy-start.3 = (f32[19,128,256]{2,1,0:T(8,128)S(1)}, f32[19,128,256]{2,1,0:T(8,128)}, u32[]{:S(2)}) copy-start(f32[19,128,256]{2,1,0:T(8,128)} %convert_add_fusion.2) | copy-start | bytes 7471108
  232.9 79.8 %all-to-all-start = ((bf16[19,128,256]{2,0,1:T(8,128)(2,1)}), bf16[19,128,256]{2,0,1:T(8,128)(2,1)}, u32[]{:S(2)}, u32[]{:S(2)}) async-start(bf16[19,128,256]{2,0,1:T(8,128)(2,1)} %copy.24), calls=%async_computation | async-start | bytes 3145728 | tf_op jit(solution)/shard_map/all_to_all | solution.py:151
  238.2 50.1 %copy-start.2 = (bf16[1024,2048]{1,0:T(8,128)(2,1)S(1)}, bf16[1024,2048]{1,0:T(8,128)(2,1)}, u32[]{:S(2)}) copy-start(bf16[1024,2048]{1,0:T(8,128)(2,1)} %slice.91) | copy-start | bytes 12582916
  282.5 12.2 %collective-permute-start.8 = (bf16[19,32,256]{2,1,0:T(8,128)(2,1)S(1)}, bf16[19,32,256]{2,1,0:T(8,128)(2,1)S(1)}, u32[]{:S(2)}, u32[]{:S(2)}) collective-permute-start(bf16[19,32,256]{2,1,0:T(8,128)(2,1)S(1)} %get-tuple-element.18), channel_id=1, source_target_pairs={{0,1},{1,2},{2,3},{3,0},{4,5},{5,6},{6,7},{7,4},{8,9},{9,10},{10,1... | collective-permute-start | bytes 933896 | tf_op jit(solution)/shard_map/ppermute | solution.py:111
  284.3 22.2 %collective-permute-start.9 = (bf16[19,32,256]{2,1,0:T(8,128)(2,1)S(1)}, bf16[19,32,256]{2,1,0:T(8,128)(2,1)S(1)}, u32[]{:S(2)}, u32[]{:S(2)}) collective-permute-start(bf16[19,32,256]{2,1,0:T(8,128)(2,1)S(1)} %get-tuple-element.20), channel_id=1, source_target_pairs={{0,2},{1,3},{2,0},{3,1},{4,6},{5,7},{6,4},{7,5},{8,10},{9,11},{10,... | collective-permute-start | bytes 933896 | tf_op jit(solution)/shard_map/ppermute | solution.py:111
  286.9 22.7 %collective-permute-start.10 = (bf16[19,32,256]{2,1,0:T(8,128)(2,1)S(1)}, bf16[19,32,256]{2,1,0:T(8,128)(2,1)S(1)}, u32[]{:S(2)}, u32[]{:S(2)}) collective-permute-start(bf16[19,32,256]{2,1,0:T(8,128)(2,1)S(1)} %get-tuple-element.19), channel_id=1, source_target_pairs={{0,3},{1,0},{2,1},{3,2},{4,7},{5,4},{6,5},{7,6},{8,11},{9,8},{10,9... | collective-permute-start | bytes 933896 | tf_op jit(solution)/shard_map/ppermute | solution.py:111
  315.2 9.3 %slice-start.3 = ((s8[4980736]{0:T(1024)(128)(4,1)}), s8[4194304]{0:T(1024)(128)(4,1)S(1)}, s32[]{:S(2)}) async-start(s8[4980736]{0:T(1024)(128)(4,1)} %bitcast.111), calls=%async_computation.4 | async-start | bytes 8388608
  315.6 9.0 %slice-start.4 = ((s8[4980736]{0:T(1024)(128)(4,1)}), s8[786432]{0:T(1024)(128)(4,1)S(1)}, s32[]{:S(2)}) async-start(s8[4980736]{0:T(1024)(128)(4,1)} %bitcast.111), calls=%async_computation.5 | async-start | bytes 1572864
  325.9 8.0 %collective-permute-start.11 = (f32[19,1024]{1,0:T(8,128)S(1)}, f32[19,1024]{1,0:T(8,128)S(1)}, u32[]{:S(2)}, u32[]{:S(2)}) collective-permute-start(f32[19,1024]{1,0:T(8,128)S(1)} %fusion.23), channel_id=1, source_target_pairs={{0,1},{1,0},{2,3},{3,2},{4,5},{5,4},{6,7},{7,6},{8,9},{9,8},{10,11... | collective-permute-start | bytes 233480 | tf_op jit(solution)/shard_map/ppermute | solution.py:56
  333.9 6.0 %collective-permute-start.12 = (f32[19,1024]{1,0:T(8,128)S(1)}, f32[19,1024]{1,0:T(8,128)S(1)}, u32[]{:S(2)}, u32[]{:S(2)}) collective-permute-start(f32[19,1024]{1,0:T(8,128)S(1)} %add.413), channel_id=1, source_target_pairs={{0,2},{1,3},{2,0},{3,1},{4,6},{5,7},{6,4},{7,5},{8,10},{9,11},{10,... | collective-permute-start | bytes 233480 | tf_op jit(solution)/shard_map/ppermute | solution.py:56
  (1 other events, 2.9 us)

commit v12 on v11

--- a/solution.py
+++ b/solution.py
@@ -142,10 +142,11 @@
     table = delay_table()
     first = _gather_pair(blocks[:, :, 0, :], matrix, pick2, parity, chip, n_owners, slots_dev)
     second = _gather_pair(blocks[:, :, 1, :], matrix, pick2, parity, chip, n_owners, slots_dev)
-    table, second = lax.optimization_barrier((table, second))
     out = None
     for k, (pair_send, own) in enumerate((first, second)):
         gridded = _scatter_pairs(pair_send, own, chip, n_owners)
+        if k == 0:
+            table, gridded = lax.optimization_barrier((table, gridded))
         half = table[k * CH:(k + 1) * CH]
         if k == 0:
             piece = lax.all_to_all(gridded, "chan", split_axis=1, concat_axis=2, tiled=True)

time: 347 us -> 355 us (1.023)
  waiting for transfers between devices: 89.5 us -> 105 us
  starting transfers between devices: 29 us -> 20.7 us
    ppermute x3, waiting for transfers between devices: 12.2 us -> 46 us  [_chan_delay(): lax.ppermute(send, 'chan', [(i, (i + d) % n_chan) for i in range(n_chan)])]
    ppermute x6, waiting for transfers between devices: 73.9 us -> 50.5 us  [_scatter_pairs(): lax.ppermute(send, 'uv', _partner_pairs(n_owners, lambda i, dest=dest: de...]
    ppermute x2, starting transfers between devices: 8.85 us -> 0.14 us  [_allreduce_sum(): x = x + lax.ppermute(x, axis, _partner_pairs(n, lambda i, d=d: i ^ d))]
    ppermute x2, waiting for transfers between devices: 3.37 us -> 8.77 us  [_allreduce_sum(): x = x + lax.ppermute(x, axis, _partner_pairs(n, lambda i, d=d: i ^ d))]
    convert_element_type x2, other arithmetic: 10.7 us -> 15.1 us  [_gather_pair(): (mine.astype(jnp.float32) + got.astype(jnp.float32)).astype(jnp.bfloat16)]
    squeeze x2, local copies, waits for them, and re-layouts: 3.94 us -> 7.76 us  [_scatter_pairs(): lax.dynamic_index_in_dim(pair_send, dest(chip), axis=0, keepdims=False)]
    unnamed x24 -> x28, local copies, waits for them, and re-layouts: 12.1 us -> 14.3 us
  transfers between devices with their start and end apart: 14 -> 14, of which waited for: 6 -> 7; matrix products, arithmetic and copies ran while one was open for 40% -> 40% of each run, Pallas kernels for 0% -> 0%
where the time goes in v12:
time: 355 us; the launch traced here: 349 us
  waiting for transfers between devices  105 us (30%)
  other arithmetic  86.8 us (24%)
  matrix products  74.1 us (21%)
  local copies, waits for them, and re-layouts  61.3 us (17%)
  starting transfers between devices  20.7 us (6%)
    ppermute x6, waiting for transfers between devices, _scatter_pairs(): lax.ppermute(send, 'uv', _partner_pairs(n_owners, lambda i, dest=dest: de...  50.5 us
    ppermute x3, waiting for transfers between devices, _chan_delay(): lax.ppermute(send, 'chan', [(i, (i + d) % n_chan) for i in range(n_chan)])  46 us
    dot_general x2, matrix products, _gather_pair(): jnp.einsum('sb,bcf->scf', pick2, jnp.concatenate([high, low], axis=0), pr...  34 us
    convert_element_type x2, local copies, waits for them, and re-layouts, _gather_pair(): partial = jnp.einsum('sb,bcf->scf', pick2, jnp.concatenate([high, low], a...  20 us
    dot_general x2, matrix products, _gather_pair(): jnp.einsum('bcr,brf->bcf', matrix, part, preferred_element_type=jnp.float32)  18.7 us
    another operation x1, other arithmetic  18.4 us
    concatenate x1, other arithmetic, delay_table(): return jnp.concatenate([upper, lower], axis=0).astype(jnp.bfloat16)  17.1 us
    convert_element_type x2, other arithmetic, _gather_pair(): (mine.astype(jnp.float32) + got.astype(jnp.float32)).astype(jnp.bfloat16)  15.1 us
  transfers between devices with their start and end apart: 14, of which 7 were waited for; matrix products, arithmetic and copies ran while one was open for 40% of the time, Pallas kernels for 0%

profile of v12, /device:TPU:0, one launch (start us, length us, event | category | flops | bytes accessed | tf_op | source)
XLA Modules:
  0.0 349.4 jit_solution(17533668078754102419)
XLA Ops:
  0.7 11.8 %copy.20 = bf16[12288,2,256]{2,0,1:T(8,128)(2,1)} copy(bf16[12288,2,256]{2,1,0:T(2,128)(2,1)} %param.7) | data formatting | bytes 25165824 | tf_op args[0]
  16.4 5.0 %add_bitcast_fusion.10 = (s32[96,128]{1,0:T(8,128)S(1)}, s32[96,128]{1,0:T(8,128)S(1)}, s32[96,128]{1,0:T(8,128)S(1)}, s32[96,128]{1,0:T(8,128)S(1)}, s32[96,128...) fusion(s32[12288]{0:T(1024)S(1)} %copy-done.5, s32[]{:T(128)} %bitcast.1, ...), kind=kLoop, calls=%fused_computation.94 | loop fusion | flops 98304 | bytes 442400 | tf_op jit(solution)/shard_map/add | solution.py:24
  21.4 9.4 %subtract_convert_fusion.1 = (bf16[96,128,256]{2,1,0:T(8,128)(2,1)S(1)}, bf16[96,128,256]{2,1,0:T(8,128)(2,1)S(1)}) fusion(bf16[96,128,2,256]{3,1,0,2:T(8,128)(2,1)} %bitcast.113, f32[96,128]{1,0:T(8,128)S(1)} %bitcast.125, s32[96,128]{1,0:T(8,128)S(1)} %get-tuple-element.34, f32[96,128]{1,0:T(8,128)S(1)} %bitcast.127, s32[96,128]{1,0:T(8,128)S(1)} %get-tuple-element.35, ...), kind=kOutput, calls=%fused_computation.9 | convolution fusion | flops 855638016 | bytes 19660800 | tf_op jit(solution)/shard_map/bcr,brf->bcf/dot_general | solution.py:63
  30.8 7.3 %pad_maximum_fusion = bf16[192,128,256]{2,1,0:T(8,128)(2,1)} fusion(bf16[96,128,256]{2,1,0:T(8,128)(2,1)S(1)} %get-tuple-element.8, bf16[96,128,256]{2,1,0:T(8,128)(2,1)S(1)} %get-tuple-element.9), kind=kLoop, calls=%fused_computation.2 | loop fusion | flops 6291456 | bytes 25165824 | tf_op jit(solution)/shard_map/concatenate | solution.py:69
  38.1 17.0 %fusion.6 = bf16[152,128,256]{2,0,1:T(8,128)(2,1)} fusion(bf16[192,128,256]{2,1,0:T(8,128)(2,1)} %pad_maximum_fusion, pred[152,96]{1,0:T(8,128)(4,1)S(1)} %iota_compare_fusion.8), kind=kOutput, calls=%fused_computation.15 | convolution fusion | flops 1917612544 | bytes 22558976 | tf_op jit(solution)/shard_map/sb,bcf->scf/dot_general | solution.py:66
  55.1 10.1 %copy.22 = bf16[152,128,256]{2,1,0:T(8,128)(2,1)} copy(bf16[152,128,256]{2,0,1:T(8,128)(2,1)} %fusion.6) | data formatting | bytes 19922944 | tf_op jit(solution)/shard_map/convert_element_type | solution.py:71
  65.2 5.2 %dynamic-slice_bitcast_fusion.1 = bf16[4,19,128,256]{3,2,1,0:T(8,128)(2,1)} fusion(bf16[2,4,19,128,256]{4,3,2,1,0:T(8,128)(2,1)} %bitcast.101, s32[]{:T(128)S(6)} %select_n.175), kind=kLoop, calls=%fused_computation.35 | loop fusion | bytes 9961476 | tf_op jit(solution)/shard_map/jit(dynamic_index_in_dim)/squeeze | solution.py:75
  70.9 9.4 %subtract_convert_fusion = (bf16[96,128,256]{2,1,0:T(8,128)(2,1)S(1)}, bf16[96,128,256]{2,1,0:T(8,128)(2,1)S(1)}) fusion(bf16[96,128,2,256]{3,1,0,2:T(8,128)(2,1)} %bitcast.114, f32[96,128]{1,0:T(8,128)S(1)} %bitcast.126, s32[96,128]{1,0:T(8,128)S(1)} %get-tuple-element.34, f32[96,128]{1,0:T(8,128)S(1)} %bitcast.128, s32[96,128]{1,0:T(8,128)S(1)} %get-tuple-element.35, ...), kind=kOutput, calls=%fused_computation.8 | convolution fusion | flops 855638016 | bytes 19660800 | tf_op jit(solution)/shard_map/bcr,brf->bcf/dot_general | solution.py:63
  80.2 7.5 %pad_maximum_fusion.1 = bf16[192,128,256]{2,1,0:T(8,128)(2,1)} fusion(bf16[96,128,256]{2,1,0:T(8,128)(2,1)S(1)} %get-tuple-element.6, bf16[96,128,256]{2,1,0:T(8,128)(2,1)S(1)} %get-tuple-element.7), kind=kLoop, calls=%fused_computation.3 | loop fusion | flops 6291456 | bytes 25165824 | tf_op jit(solution)/shard_map/concatenate | solution.py:69
  87.7 17.0 %fusion.9 = bf16[152,128,256]{2,0,1:T(8,128)(2,1)} fusion(bf16[192,128,256]{2,1,0:T(8,128)(2,1)} %pad_maximum_fusion.1, pred[152,96]{1,0:T(8,128)(4,1)S(1)} %iota_compare_fusion.8), kind=kOutput, calls=%fused_computation.16 | convolution fusion | flops 1917612544 | bytes 22558976 | tf_op jit(solution)/shard_map/sb,bcf->scf/dot_general | solution.py:66
  104.7 10.0 %copy.26 = bf16[152,128,256]{2,1,0:T(8,128)(2,1)} copy(bf16[152,128,256]{2,0,1:T(8,128)(2,1)} %fusion.9) | data formatting | bytes 19922944 | tf_op jit(solution)/shard_map/convert_element_type | solution.py:71
  114.7 5.5 %dynamic-slice_bitcast_fusion = bf16[4,19,128,256]{3,2,1,0:T(8,128)(2,1)} fusion(bf16[2,4,19,128,256]{4,3,2,1,0:T(8,128)(2,1)} %bitcast.104, s32[]{:T(128)S(6)} %select_n.175), kind=kLoop, calls=%fused_computation.34 | loop fusion | bytes 9961476 | tf_op jit(solution)/shard_map/jit(dynamic_index_in_dim)/squeeze | solution.py:75
  120.2 8.6 %fusion.5 = bf16[4,19,128,256]{3,2,1,0:T(8,128)(2,1)} fusion(bf16[4,19,128,256]{3,2,1,0:T(8,128)(2,1)} %collective-permute-done, bf16[2,4,19,128,256]{4,3,2,1,0:T(8,128)(2,1)} %bitcast.102, s32[]{:T(128)S(6)} %select_n.170), kind=kLoop, calls=%fused_computation.13 | loop fusion | flops 9961472 | bytes 14942212 | tf_op jit(solution)/shard_map/convert_element_type | solution.py:77
  136.8 6.5 %fusion.4 = bf16[4,19,128,256]{3,2,1,0:T(8,128)(2,1)} fusion(bf16[4,19,128,256]{3,2,1,0:T(8,128)(2,1)} %collective-permute-done.4, bf16[2,4,19,128,256]{4,3,2,1,0:T(8,128)(2,1)S(1)} %bitcast.108, s32[]{:T(128)S(6)} %select_n.170), kind=kLoop, calls=%fused_computation.11 | loop fusion | flops 9961472 | bytes 14942212 | tf_op jit(solution)/shard_map/convert_element_type | solution.py:77
  151.1 13.9 %collective-permute-done.3 = bf16[19,128,256]{2,1,0:T(8,128)(2,1)S(1)} collective-permute-done((bf16[19,128,256]{2,1,0:T(8,128)(2,1)S(1)}, bf16[19,128,256]{2,1,0:T(8,128)(2,1)S(1)}, u32[]{:S(2)}, u32[]{:S(2)}) %collective-permute-start.3) | collective-permute-done | bytes 1245216 | tf_op jit(solution)/shard_map/ppermute | solution.py:93
  168.0 18.4 %multiply_convert_fusion.1 = (bf16[1024,1024]{1,0:T(8,128)(2,1)S(1)}, bf16[1024,1024]{1,0:T(8,128)(2,1)}, bf16[1024,1024]{1,0:T(8,128)(2,1)}) fusion(f32[1024]{0:T(1024)S(1)} %subtract_multiply_fusion), kind=kLoop, calls=%fused_computation.42 | loop fusion | flops 22020096 | bytes 6295552 | tf_op jit(solution)/shard_map/convert.20
  186.4 4.5 %convert_element_type.185 = f32[19,32,2048]{2,1,0:T(8,128)} convert(bf16[19,32,2048]{2,1,0:T(8,128)(2,1)} %param.13) | non-fusion elementwise | flops 1245184 | bytes 7471104 | tf_op jit(solution)/shard_map/convert_element_type | solution.py:161
  190.9 17.1 %maximum_maximum_fusion = bf16[2048,2048]{1,0:T(8,128)(2,1)} fusion(bf16[1024,1024]{1,0:T(8,128)(2,1)} %get-tuple-element.38, bf16[1024,1024]{1,0:T(8,128)(2,1)} %get-tuple-element.37, bf16[1024,1024]{1,0:T(8,128)(2,1)S(1)} %get-tuple-element.36), kind=kLoop, calls=%fused_computation.14 | loop fusion | flops 33554432 | bytes 14680064 | tf_op jit(solution)/shard_map/concatenate | solution.py:44
  208.0 36.3 %collective-permute-done.2 = bf16[19,128,256]{2,1,0:T(8,128)(2,1)} collective-permute-done((bf16[19,128,256]{2,1,0:T(8,128)(2,1)}, bf16[19,128,256]{2,1,0:T(8,128)(2,1)}, u32[]{:S(2)}, u32[]{:S(2)}) %collective-permute-start.2) | collective-permute-done | bytes 1245216 | tf_op jit(solution)/shard_map/ppermute | solution.py:93
  250.0 5.1 %all-to-all-start = ((bf16[19,128,256]{2,0,1:T(8,128)(2,1)}), bf16[19,128,256]{2,0,1:T(8,128)(2,1)S(1)}, u32[]{:S(2)}, u32[]{:S(2)}) async-start(bf16[19,128,256]{2,0,1:T(8,128)(2,1)} %copy.23), calls=%async_computation | async-start | bytes 3145728 | tf_op jit(solution)/shard_map/all_to_all | solution.py:152
  269.8 18.6 %collective-permute-done.10 = bf16[19,32,256]{2,1,0:T(8,128)(2,1)S(1)} collective-permute-done((bf16[19,32,256]{2,1,0:T(8,128)(2,1)S(1)}, bf16[19,32,256]{2,1,0:T(8,128)(2,1)S(1)}, u32[]{:S(2)}, u32[]{:S(2)}) %collective-permute-start.10) | collective-permute-done | bytes 311328 | tf_op jit(solution)/shard_map/ppermute | solution.py:111
  291.4 27.4 %collective-permute-done.9 = bf16[19,32,256]{2,1,0:T(8,128)(2,1)S(1)} collective-permute-done((bf16[19,32,256]{2,1,0:T(8,128)(2,1)S(1)}, bf16[19,32,256]{2,1,0:T(8,128)(2,1)S(1)}, u32[]{:S(2)}, u32[]{:S(2)}) %collective-permute-start.9) | collective-permute-done | bytes 311328 | tf_op jit(solution)/shard_map/ppermute | solution.py:111
  327.3 9.1 %add_add_fusion = f32[608,2048]{1,0:T(8,128)S(1)} fusion(f32[608,2048]{1,0:T(8,128)} %fusion.33, f32[608,2048]{1,0:T(8,128)} %fusion.35, f32[608,2048]{1,0:T(8,128)} %fusion.39, f32[608,2048]{1,0:T(8,128)S(1)} %copy-done.1, bf16[608,1024]{1,0:T(8,128)(2,1)S(1)} %bitcast.117, bf16[2048,2048]{1,0:T(8,128)(2,1)} %maximum_maximum_fusion), kind=kOutput, calls=%fused_computation.33 | convolution fusion | flops 2555117568 | bytes 30343168 | tf_op jit(solution)/shard_map/dot_general | solution.py:153
  337.9 4.6 %collective-permute-done.11 = f32[19,1024]{1,0:T(8,128)S(1)} collective-permute-done((f32[19,1024]{1,0:T(8,128)S(1)}, f32[19,1024]{1,0:T(8,128)S(1)}, u32[]{:S(2)}, u32[]{:S(2)}) %collective-permute-start.11) | collective-permute-done | bytes 77856 | tf_op jit(solution)/shard_map/ppermute | solution.py:56
  (79 shorter events, 63.0 us)
Async XLA Ops:
  0.6 11.8 %copy-start.4 = (bf16[8,12288]{1,0:T(8,128)(2,1)S(1)}, bf16[8,12288]{1,0:T(8,128)(2,1)}, u32[]{:S(2)}) copy-start(bf16[8,12288]{1,0:T(8,128)(2,1)} %param.9) | copy-start | bytes 589828
  0.7 12.1 %copy-start.6 = (s32[8]{0:T(128)S(1)}, s32[8]{0:T(128)}, u32[]{:S(2)}) copy-start(s32[8]{0:T(128)} %param.10) | copy-start | bytes 100
  0.7 12.8 %copy-start = (s32[80]{0:T(128)S(1)}, s32[80]{0:T(128)}, u32[]{:S(2)}) copy-start(s32[80]{0:T(128)} %param.12) | copy-start | bytes 964
  0.7 13.1 %copy-start.7 = (s32[96]{0:T(128)S(1)}, s32[96]{0:T(128)}, u32[]{:S(2)}) copy-start(s32[96]{0:T(128)} %param.11) | copy-start | bytes 1156
  0.7 15.7 %copy-start.5 = (s32[12288]{0:T(1024)S(1)}, s32[12288]{0:T(1024)}, u32[]{:S(2)}) copy-start(s32[12288]{0:T(1024)} %param.8) | copy-start | bytes 147460
  70.4 49.8 %collective-permute-start = (bf16[4,19,128,256]{3,2,1,0:T(8,128)(2,1)}, bf16[4,19,128,256]{3,2,1,0:T(8,128)(2,1)}, u32[]{:S(2)}, u32[]{:S(2)}) collective-permute-start(bf16[4,19,128,256]{3,2,1,0:T(8,128)(2,1)} %dynamic-slice_bitcast_fusion.1), channel_id=1, source_target_pairs={{0,4},{4,0},{8,12},{12,8},{16,20},{20,16},{24,28},{28,24},{1,5},{5... | collective-permute-start | bytes 14942216 | tf_op jit(solution)/shard_map/ppermute | solution.py:76
  114.7 22.1 %slice-start = ((s8[9961472]{0:T(1024)(128)(4,1)}), s8[1572864]{0:T(1024)(128)(4,1)S(1)}, s32[]{:S(2)}) async-start(s8[9961472]{0:T(1024)(128)(4,1)} %bitcast.106), calls=%async_computation.1 | async-start | bytes 3145728
  120.1 16.6 %collective-permute-start.4 = (bf16[4,19,128,256]{3,2,1,0:T(8,128)(2,1)}, bf16[4,19,128,256]{3,2,1,0:T(8,128)(2,1)}, u32[]{:S(2)}, u32[]{:S(2)}) collective-permute-start(bf16[4,19,128,256]{3,2,1,0:T(8,128)(2,1)} %dynamic-slice_bitcast_fusion), channel_id=1, source_target_pairs={{0,4},{4,0},{8,12},{12,8},{16,20},{20,16},{24,28},{28,24},{1,5},{5... | collective-permute-start | bytes 14942216 | tf_op jit(solution)/shard_map/ppermute | solution.py:76
  120.2 16.6 %slice-start.1 = ((s8[9961472]{0:T(1024)(128)(4,1)}), s8[4194304]{0:T(1024)(128)(4,1)S(1)}, s32[]{:S(2)}) async-start(s8[9961472]{0:T(1024)(128)(4,1)} %bitcast.106), calls=%async_computation.2 | async-start | bytes 8388608
  120.2 16.6 %slice-start.2 = ((s8[9961472]{0:T(1024)(128)(4,1)}), s8[4194304]{0:T(1024)(128)(4,1)S(1)}, s32[]{:S(2)}) async-start(s8[9961472]{0:T(1024)(128)(4,1)} %bitcast.106), calls=%async_computation.3 | async-start | bytes 8388608
  132.7 32.2 %collective-permute-start.3 = (bf16[19,128,256]{2,1,0:T(8,128)(2,1)S(1)}, bf16[19,128,256]{2,1,0:T(8,128)(2,1)S(1)}, u32[]{:S(2)}, u32[]{:S(2)}) collective-permute-start(bf16[19,128,256]{2,1,0:T(8,128)(2,1)S(1)} %get-tuple-element.14), channel_id=1, source_target_pairs={{0,24},{4,28},{8,16},{12,20},{16,8},{20,12},{24,0},{28,4},{1,25},{... | collective-permute-start | bytes 3735560 | tf_op jit(solution)/shard_map/ppermute | solution.py:93
  147.1 108.0 %collective-permute-start.7 = (bf16[19,128,256]{2,1,0:T(8,128)(2,1)}, bf16[19,128,256]{2,1,0:T(8,128)(2,1)}, u32[]{:S(2)}, u32[]{:S(2)}) collective-permute-start(bf16[19,128,256]{2,1,0:T(8,128)(2,1)} %get-tuple-element.11), channel_id=1, source_target_pairs={{0,24},{4,28},{8,16},{12,20},{16,8},{20,12},{24,0},{28,4},{1,25},{... | collective-permute-start | bytes 3735560 | tf_op jit(solution)/shard_map/ppermute | solution.py:93
  147.1 108.0 %collective-permute-start.6 = (bf16[19,128,256]{2,1,0:T(8,128)(2,1)}, bf16[19,128,256]{2,1,0:T(8,128)(2,1)}, u32[]{:S(2)}, u32[]{:S(2)}) collective-permute-start(bf16[19,128,256]{2,1,0:T(8,128)(2,1)} %get-tuple-element.12), channel_id=1, source_target_pairs={{0,16},{4,20},{8,24},{12,28},{16,0},{20,4},{24,8},{28,12},{1,17},{... | collective-permute-start | bytes 3735560 | tf_op jit(solution)/shard_map/ppermute | solution.py:93
  149.1 106.0 %collective-permute-start.5 = (bf16[19,128,256]{2,1,0:T(8,128)(2,1)S(1)}, bf16[19,128,256]{2,1,0:T(8,128)(2,1)}, u32[]{:S(2)}, u32[]{:S(2)}) collective-permute-start(bf16[19,128,256]{2,1,0:T(8,128)(2,1)S(1)} %get-tuple-element.10), channel_id=1, source_target_pairs={{0,8},{4,12},{8,0},{12,4},{16,24},{20,28},{24,16},{28,20},{1,9},{5... | collective-permute-start | bytes 3735560 | tf_op jit(solution)/shard_map/ppermute | solution.py:93
  150.6 93.8 %collective-permute-start.2 = (bf16[19,128,256]{2,1,0:T(8,128)(2,1)}, bf16[19,128,256]{2,1,0:T(8,128)(2,1)}, u32[]{:S(2)}, u32[]{:S(2)}) collective-permute-start(bf16[19,128,256]{2,1,0:T(8,128)(2,1)} %get-tuple-element.15), channel_id=1, source_target_pairs={{0,16},{4,20},{8,24},{12,28},{16,0},{20,4},{24,8},{28,12},{1,17},{... | collective-permute-start | bytes 3735560 | tf_op jit(solution)/shard_map/ppermute | solution.py:93
  166.0 78.6 %collective-permute-start.1 = (bf16[19,128,256]{2,1,0:T(8,128)(2,1)}, bf16[19,128,256]{2,1,0:T(8,128)(2,1)}, u32[]{:S(2)}, u32[]{:S(2)}) collective-permute-start(bf16[19,128,256]{2,1,0:T(8,128)(2,1)} %get-tuple-element.13), channel_id=1, source_target_pairs={{0,8},{4,12},{8,0},{12,4},{16,24},{20,28},{24,16},{28,20},{1,9},{5... | collective-permute-start | bytes 3735560 | tf_op jit(solution)/shard_map/ppermute | solution.py:93
  190.9 53.7 %copy-start.3 = (bf16[19,128,256]{2,1,0:T(8,128)(2,1)S(1)}, bf16[19,128,256]{2,1,0:T(8,128)(2,1)}, u32[]{:S(2)}) copy-start(bf16[19,128,256]{2,1,0:T(8,128)(2,1)} %copy-done.2) | copy-start | bytes 3735556
  250.0 74.9 %all-to-all-start = ((bf16[19,128,256]{2,0,1:T(8,128)(2,1)}), bf16[19,128,256]{2,0,1:T(8,128)(2,1)S(1)}, u32[]{:S(2)}, u32[]{:S(2)}) async-start(bf16[19,128,256]{2,0,1:T(8,128)(2,1)} %copy.23), calls=%async_computation | async-start | bytes 3145728 | tf_op jit(solution)/shard_map/all_to_all | solution.py:152
  259.1 29.3 %collective-permute-start.10 = (bf16[19,32,256]{2,1,0:T(8,128)(2,1)S(1)}, bf16[19,32,256]{2,1,0:T(8,128)(2,1)S(1)}, u32[]{:S(2)}, u32[]{:S(2)}) collective-permute-start(bf16[19,32,256]{2,1,0:T(8,128)(2,1)S(1)} %get-tuple-element.17), channel_id=1, source_target_pairs={{0,3},{1,0},{2,1},{3,2},{4,7},{5,4},{6,5},{7,6},{8,11},{9,8},{10,9... | collective-permute-start | bytes 933896 | tf_op jit(solution)/shard_map/ppermute | solution.py:111
  265.4 53.4 %collective-permute-start.9 = (bf16[19,32,256]{2,1,0:T(8,128)(2,1)S(1)}, bf16[19,32,256]{2,1,0:T(8,128)(2,1)S(1)}, u32[]{:S(2)}, u32[]{:S(2)}) collective-permute-start(bf16[19,32,256]{2,1,0:T(8,128)(2,1)S(1)} %get-tuple-element.18), channel_id=1, source_target_pairs={{0,2},{1,3},{2,0},{3,1},{4,6},{5,7},{6,4},{7,5},{8,10},{9,11},{10,... | collective-permute-start | bytes 933896 | tf_op jit(solution)/shard_map/ppermute | solution.py:111
  265.5 56.4 %collective-permute-start.8 = (bf16[19,32,256]{2,1,0:T(8,128)(2,1)S(1)}, bf16[19,32,256]{2,1,0:T(8,128)(2,1)S(1)}, u32[]{:S(2)}, u32[]{:S(2)}) collective-permute-start(bf16[19,32,256]{2,1,0:T(8,128)(2,1)S(1)} %get-tuple-element.16), channel_id=1, source_target_pairs={{0,1},{1,2},{2,3},{3,0},{4,5},{5,6},{6,7},{7,4},{8,9},{9,10},{10,1... | collective-permute-start | bytes 933896 | tf_op jit(solution)/shard_map/ppermute | solution.py:111
  325.9 10.5 %slice-start.3 = ((s8[4980736]{0:T(1024)(128)(4,1)}), s8[4194304]{0:T(1024)(128)(4,1)S(1)}, s32[]{:S(2)}) async-start(s8[4980736]{0:T(1024)(128)(4,1)} %bitcast.111), calls=%async_computation.4 | async-start | bytes 8388608
  337.8 4.7 %collective-permute-start.11 = (f32[19,1024]{1,0:T(8,128)S(1)}, f32[19,1024]{1,0:T(8,128)S(1)}, u32[]{:S(2)}, u32[]{:S(2)}) collective-permute-start(f32[19,1024]{1,0:T(8,128)S(1)} %fusion.23), channel_id=1, source_target_pairs={{0,1},{1,0},{2,3},{3,2},{4,5},{5,4},{6,7},{7,6},{8,9},{9,8},{10,11... | collective-permute-start | bytes 233480 | tf_op jit(solution)/shard_map/ppermute | solution.py:56
  342.5 6.1 %collective-permute-start.12 = (f32[19,1024]{1,0:T(8,128)S(1)}, f32[19,1024]{1,0:T(8,128)S(1)}, u32[]{:S(2)}, u32[]{:S(2)}) collective-permute-start(f32[19,1024]{1,0:T(8,128)S(1)} %add.413), channel_id=1, source_target_pairs={{0,2},{1,3},{2,0},{3,1},{4,6},{5,7},{6,4},{7,5},{8,10},{9,11},{10,... | collective-permute-start | bytes 233480 | tf_op jit(solution)/shard_map/ppermute | solution.py:56
  (3 other events, 12.6 us)

commit v13 on v5

--- a/solution.py
+++ b/solution.py
@@ -121,6 +121,7 @@
     cells = row_cell.reshape(nblocks, BR)
     weights = jnp.transpose(tap_weight.reshape(KT, nblocks, BR), (1, 0, 2))
     matrix = kernel_matrix(cells, weights, tap_offset)
+    matrix = lax.optimization_barrier(matrix)
     table = delay_table()
     first = _gather_pair(blocks[:, :, 0, :], matrix, pick2, parity, chip, n_owners, slots_dev)
     second = _gather_pair(blocks[:, :, 1, :], matrix, pick2, parity, chip, n_owners, slots_dev)

time: 329 us -> 339 us (1.030)
  other arithmetic: 87.5 us -> 101 us
  matrix products: 60.4 us -> 56.3 us
    concatenate x2, other arithmetic: 14.9 us -> 21.5 us  [_gather_pair(): jnp.concatenate([high, low], axis=0)]
    convert_element_type x0 -> x1, other arithmetic: none -> 6.23 us  [kernel_matrix(): return total.astype(jnp.bfloat16)]
    dot_general x2, matrix products: 18.7 us -> 14.7 us  [_gather_pair(): jnp.einsum('bcr,brf->bcf', matrix, part, preferred_element_type=jnp.float32)]
    unnamed x17 -> x15, local copies, waits for them, and re-layouts: 12.2 us -> 12.2 us
  transfers between devices with their start and end apart: 12 -> 12, of which waited for: 6 -> 6; matrix products, arithmetic and copies ran while one was open for 36% -> 35% of each run, Pallas kernels for 0% -> 0%
where the time goes in v13:
time: 339 us; the launch traced here: 333 us
  other arithmetic  101 us (30%)
  waiting for transfers between devices  98 us (29%)
  local copies, waits for them, and re-layouts  56.7 us (17%)
  matrix products  56.3 us (17%)
  starting transfers between devices  19.3 us (6%)
    ppermute x6, waiting for transfers between devices, _scatter_pairs(): lax.ppermute(send, 'uv', _partner_pairs(n_owners, lambda i, dest=dest: de...  62.8 us
    dot_general x2, matrix products, _gather_pair(): jnp.einsum('sb,bcf->scf', pick2, jnp.concatenate([high, low], axis=0), pr...  34.1 us
    all_to_all x2, waiting for transfers between devices, _scatter_pairs(): lax.all_to_all(gridded, 'chan', split_axis=1, concat_axis=2, tiled=True)  26.8 us
    concatenate x2, other arithmetic, _gather_pair(): jnp.concatenate([high, low], axis=0)  21.5 us
    convert_element_type x2, local copies, waits for them, and re-layouts, _gather_pair(): partial = jnp.einsum('sb,bcf->scf', pick2, jnp.concatenate([high, low], a...  20 us
    another operation x1, other arithmetic  18.5 us
    concatenate x1, other arithmetic, delay_table(): return jnp.concatenate([upper, lower], axis=0).astype(jnp.bfloat16)  17.1 us
    dot_general x2, matrix products, _gather_pair(): jnp.einsum('bcr,brf->bcf', matrix, part, preferred_element_type=jnp.float32)  14.7 us
  transfers between devices with their start and end apart: 12, of which 6 were waited for; matrix products, arithmetic and copies ran while one was open for 35% of the time, Pallas kernels for 0%

profile of v13, /device:TPU:0, one launch (start us, length us, event | category | flops | bytes accessed | tf_op | source)
XLA Modules:
  0.0 332.6 jit_solution(2757011699044182922)
XLA Ops:
  4.4 6.0 %add_bitcast_fusion.10 = (s32[96,128]{1,0:T(8,128)S(1)}, s32[96,128]{1,0:T(8,128)S(1)}, s32[96,128]{1,0:T(8,128)S(1)}, s32[96,128]{1,0:T(8,128)S(1)}, s32[96,128...) fusion(s32[12288]{0:T(1024)} %param.8, s32[]{:T(128)} %bitcast.1, ...), kind=kLoop, calls=%fused_computation.85 | loop fusion | flops 98304 | bytes 442400 | tf_op jit(solution)/shard_map/add | solution.py:24
  10.4 6.2 %add_convert_fusion = bf16[96,128,128]{2,1,0:T(8,128)(2,1)S(1)} fusion(f32[96,128]{1,0:T(8,128)S(1)} %bitcast.123, s32[96,128]{1,0:T(8,128)S(1)} %get-tuple-element.32, f32[96,128]{1,0:T(8,128)S(1)} %bitcast.124, s32[96,128]{1,0:T(8,128)S(1)} %get-tuple-element.33, f32[96,128]{1,0:T(8,128)S(1)} %bitcast.125, s32[96,128]{1,0:T(8,128)S(1)} %get-tuple-element.27, ...), kind=kLoop, calls=%fused_computation.24 | loop fusion | flops 37748736 | bytes 3932160 | tf_op jit(solution)/shard_map/convert_element_type | solution.py:29
  16.7 11.7 %copy.22 = bf16[12288,2,256]{2,0,1:T(8,128)(2,1)} copy(bf16[12288,2,256]{2,1,0:T(2,128)(2,1)} %param.7) | data formatting | bytes 25165824 | tf_op args[0]
  31.3 7.2 %subtract_convert_fusion.1 = (bf16[96,128,256]{2,1,0:T(8,128)(2,1)S(1)}, bf16[96,128,256]{2,1,0:T(8,128)(2,1)}) fusion(bf16[96,128,128]{2,1,0:T(8,128)(2,1)S(1)} %add_convert_fusion, bf16[96,128,2,256]{3,1,0,2:T(8,128)(2,1)} %bitcast.101), kind=kOutput, calls=%fused_computation.9 | convolution fusion | flops 817889280 | bytes 22020096 | tf_op jit(solution)/shard_map/bcr,brf->bcf/dot_general | solution.py:63
  38.5 10.9 %pad_maximum_fusion = bf16[192,128,256]{2,1,0:T(8,128)(2,1)} fusion(bf16[96,128,256]{2,1,0:T(8,128)(2,1)S(1)} %get-tuple-element.8, bf16[96,128,256]{2,1,0:T(8,128)(2,1)} %get-tuple-element.9), kind=kLoop, calls=%fused_computation.2 | loop fusion | flops 6291456 | bytes 25165824 | tf_op jit(solution)/shard_map/concatenate | solution.py:69
  49.4 17.1 %fusion.6 = bf16[152,128,256]{2,0,1:T(8,128)(2,1)} fusion(bf16[192,128,256]{2,1,0:T(8,128)(2,1)} %pad_maximum_fusion, pred[152,96]{1,0:T(8,128)(4,1)S(1)} %iota_compare_fusion.8), kind=kOutput, calls=%fused_computation.15 | convolution fusion | flops 1917612544 | bytes 22558976 | tf_op jit(solution)/shard_map/sb,bcf->scf/dot_general | solution.py:66
  66.5 10.1 %copy.24 = bf16[152,128,256]{2,1,0:T(8,128)(2,1)} copy(bf16[152,128,256]{2,0,1:T(8,128)(2,1)} %fusion.6) | data formatting | bytes 19922944 | tf_op jit(solution)/shard_map/convert_element_type | solution.py:71
  76.6 5.2 %dynamic-slice_bitcast_fusion.1 = bf16[4,19,128,256]{3,2,1,0:T(8,128)(2,1)} fusion(bf16[2,4,19,128,256]{4,3,2,1,0:T(8,128)(2,1)} %bitcast.103, s32[]{:T(128)S(6)} %select_n.120), kind=kLoop, calls=%fused_computation.34 | loop fusion | bytes 9961476 | tf_op jit(solution)/shard_map/jit(dynamic_index_in_dim)/squeeze | solution.py:75
  82.3 7.4 %subtract_convert_fusion = (bf16[96,128,256]{2,1,0:T(8,128)(2,1)S(1)}, bf16[96,128,256]{2,1,0:T(8,128)(2,1)}) fusion(bf16[96,128,128]{2,1,0:T(8,128)(2,1)S(1)} %add_convert_fusion, bf16[96,128,2,256]{3,1,0,2:T(8,128)(2,1)} %bitcast.102), kind=kOutput, calls=%fused_computation.8 | convolution fusion | flops 817889280 | bytes 22020096 | tf_op jit(solution)/shard_map/bcr,brf->bcf/dot_general | solution.py:63
  89.7 10.5 %pad_maximum_fusion.1 = bf16[192,128,256]{2,1,0:T(8,128)(2,1)} fusion(bf16[96,128,256]{2,1,0:T(8,128)(2,1)S(1)} %get-tuple-element.10, bf16[96,128,256]{2,1,0:T(8,128)(2,1)} %get-tuple-element.11), kind=kLoop, calls=%fused_computation.3 | loop fusion | flops 6291456 | bytes 25165824 | tf_op jit(solution)/shard_map/concatenate | solution.py:69
  100.2 17.0 %fusion.9 = bf16[152,128,256]{2,0,1:T(8,128)(2,1)} fusion(bf16[192,128,256]{2,1,0:T(8,128)(2,1)} %pad_maximum_fusion.1, pred[152,96]{1,0:T(8,128)(4,1)S(1)} %iota_compare_fusion.8), kind=kOutput, calls=%fused_computation.16 | convolution fusion | flops 1917612544 | bytes 22558976 | tf_op jit(solution)/shard_map/sb,bcf->scf/dot_general | solution.py:66
  117.3 9.9 %copy.28 = bf16[152,128,256]{2,1,0:T(8,128)(2,1)} copy(bf16[152,128,256]{2,0,1:T(8,128)(2,1)} %fusion.9) | data formatting | bytes 19922944 | tf_op jit(solution)/shard_map/convert_element_type | solution.py:71
  127.2 5.2 %dynamic-slice_bitcast_fusion = bf16[4,19,128,256]{3,2,1,0:T(8,128)(2,1)} fusion(bf16[2,4,19,128,256]{4,3,2,1,0:T(8,128)(2,1)} %bitcast.106, s32[]{:T(128)S(6)} %select_n.120), kind=kLoop, calls=%fused_computation.33 | loop fusion | bytes 9961476 | tf_op jit(solution)/shard_map/jit(dynamic_index_in_dim)/squeeze | solution.py:75
  132.5 6.3 %fusion.5 = bf16[4,19,128,256]{3,2,1,0:T(8,128)(2,1)S(1)} fusion(bf16[4,19,128,256]{3,2,1,0:T(8,128)(2,1)} %collective-permute-done, bf16[2,4,19,128,256]{4,3,2,1,0:T(8,128)(2,1)} %bitcast.104, s32[]{:T(128)S(6)} %select_n.115), kind=kLoop, calls=%fused_computation.13 | loop fusion | flops 9961472 | bytes 14942212 | tf_op jit(solution)/shard_map/convert_element_type | solution.py:77
  145.2 18.5 %multiply_convert_fusion.1 = (bf16[1024,1024]{1,0:T(8,128)(2,1)S(1)}, bf16[1024,1024]{1,0:T(8,128)(2,1)}, bf16[1024,1024]{1,0:T(8,128)(2,1)}) fusion(f32[1024]{0:T(1024)S(1)} %subtract_multiply_fusion), kind=kLoop, calls=%fused_computation.43 | loop fusion | flops 22020096 | bytes 6295552 | tf_op jit(solution)/shard_map/convert.20
  163.8 17.1 %maximum_maximum_fusion = bf16[2048,2048]{1,0:T(8,128)(2,1)} fusion(bf16[1024,1024]{1,0:T(8,128)(2,1)} %get-tuple-element.36, bf16[1024,1024]{1,0:T(8,128)(2,1)} %get-tuple-element.35, bf16[1024,1024]{1,0:T(8,128)(2,1)S(1)} %get-tuple-element.34), kind=kLoop, calls=%fused_computation.14 | loop fusion | flops 33554432 | bytes 14680064 | tf_op jit(solution)/shard_map/concatenate | solution.py:44
  180.8 8.4 %fusion.4 = bf16[4,19,128,256]{3,2,1,0:T(8,128)(2,1)} fusion(bf16[4,19,128,256]{3,2,1,0:T(8,128)(2,1)} %collective-permute-done.4, bf16[2,4,19,128,256]{4,3,2,1,0:T(8,128)(2,1)} %bitcast.107, s32[]{:T(128)S(6)} %select_n.115), kind=kLoop, calls=%fused_computation.11 | loop fusion | flops 9961472 | bytes 14942212 | tf_op jit(solution)/shard_map/convert_element_type | solution.py:77
  189.2 10.5 %collective-permute-done.2 = bf16[19,128,256]{2,1,0:T(8,128)(2,1)} collective-permute-done((bf16[19,128,256]{2,1,0:T(8,128)(2,1)}, bf16[19,128,256]{2,1,0:T(8,128)(2,1)}, u32[]{:S(2)}, u32[]{:S(2)}) %collective-permute-start.2) | collective-permute-done | bytes 1245216 | tf_op jit(solution)/shard_map/ppermute | solution.py:93
  205.0 5.1 %all-to-all-start = ((bf16[19,128,256]{2,0,1:T(8,128)(2,1)}), bf16[19,128,256]{2,0,1:T(8,128)(2,1)S(1)}, u32[]{:S(2)}, u32[]{:S(2)}) async-start(bf16[19,128,256]{2,0,1:T(8,128)(2,1)} %copy.25), calls=%async_computation | async-start | bytes 3145728 | tf_op jit(solution)/shard_map/all_to_all | solution.py:98
  218.0 26.8 %collective-permute-done.5 = bf16[19,128,256]{2,1,0:T(8,128)(2,1)S(1)} collective-permute-done((bf16[19,128,256]{2,1,0:T(8,128)(2,1)S(1)}, bf16[19,128,256]{2,1,0:T(8,128)(2,1)S(1)}, u32[]{:S(2)}, u32[]{:S(2)}) %collective-permute-start.5) | collective-permute-done | bytes 1245216 | tf_op jit(solution)/shard_map/ppermute | solution.py:93
  244.8 25.5 %collective-permute-done.6 = bf16[19,128,256]{2,1,0:T(8,128)(2,1)S(1)} collective-permute-done((bf16[19,128,256]{2,1,0:T(8,128)(2,1)S(1)}, bf16[19,128,256]{2,1,0:T(8,128)(2,1)S(1)}, u32[]{:S(2)}, u32[]{:S(2)}) %collective-permute-start.6) | collective-permute-done | bytes 1245216 | tf_op jit(solution)/shard_map/ppermute | solution.py:93
  272.9 4.8 %all-to-all-start.1 = ((bf16[19,128,256]{2,0,1:T(8,128)(2,1)}), bf16[19,128,256]{2,0,1:T(8,128)(2,1)S(1)}, u32[]{:S(2)}, u32[]{:S(2)}) async-start(bf16[19,128,256]{2,0,1:T(8,128)(2,1)} %copy.29), calls=%async_computation.1 | async-start | bytes 3145728 | tf_op jit(solution)/shard_map/all_to_all | solution.py:98
  283.6 26.8 %all-to-all-done.1 = bf16[19,128,256]{2,0,1:T(8,128)(2,1)S(1)} async-done(((bf16[19,128,256]{2,0,1:T(8,128)(2,1)}), bf16[19,128,256]{2,0,1:T(8,128)(2,1)S(1)}, u32[]{:S(2)}, u32[]{:S(2)}) %all-to-all-start.1) | async-done | bytes 1245216 | tf_op jit(solution)/shard_map/all_to_all | solution.py:98
  311.7 4.7 %fusion.17 = f32[608,2048]{1,0:T(8,128)S(1)} fusion(bf16[608,1024]{1,0:T(8,128)(2,1)S(1)} %bitcast.120, bf16[2048,2048]{1,0:T(8,128)(2,1)} %maximum_maximum_fusion), kind=kOutput, calls=%fused_computation.38 | convolution fusion | flops 2550136832 | bytes 10420224 | tf_op jit(solution)/shard_map/dot_general | solution.py:133
  (61 shorter events, 52.2 us)
Async XLA Ops:
  16.6 11.7 %copy-start.1 = (s32[96]{0:T(128)S(1)}, s32[96]{0:T(128)}, u32[]{:S(2)}) copy-start(s32[96]{0:T(128)} %param.11) | copy-start | bytes 1156
  16.6 11.7 %copy-start = (s32[80]{0:T(128)S(1)}, s32[80]{0:T(128)}, u32[]{:S(2)}) copy-start(s32[80]{0:T(128)} %param.12) | copy-start | bytes 964
  81.8 50.7 %collective-permute-start = (bf16[4,19,128,256]{3,2,1,0:T(8,128)(2,1)}, bf16[4,19,128,256]{3,2,1,0:T(8,128)(2,1)}, u32[]{:S(2)}, u32[]{:S(2)}) collective-permute-start(bf16[4,19,128,256]{3,2,1,0:T(8,128)(2,1)} %dynamic-slice_bitcast_fusion.1), channel_id=1, source_target_pairs={{0,4},{4,0},{8,12},{12,8},{16,20},{20,16},{24,28},{28,24},{1,5},{5... | collective-permute-start | bytes 14942216 | tf_op jit(solution)/shard_map/ppermute | solution.py:76
  132.4 48.4 %collective-permute-start.4 = (bf16[4,19,128,256]{3,2,1,0:T(8,128)(2,1)}, bf16[4,19,128,256]{3,2,1,0:T(8,128)(2,1)}, u32[]{:S(2)}, u32[]{:S(2)}) collective-permute-start(bf16[4,19,128,256]{3,2,1,0:T(8,128)(2,1)} %dynamic-slice_bitcast_fusion), channel_id=1, source_target_pairs={{0,4},{4,0},{8,12},{12,8},{16,20},{20,16},{24,28},{28,24},{1,5},{5... | collective-permute-start | bytes 14942216 | tf_op jit(solution)/shard_map/ppermute | solution.py:76
  140.7 48.4 %collective-permute-start.1 = (bf16[19,128,256]{2,1,0:T(8,128)(2,1)}, bf16[19,128,256]{2,1,0:T(8,128)(2,1)S(1)}, u32[]{:S(2)}, u32[]{:S(2)}) collective-permute-start(bf16[19,128,256]{2,1,0:T(8,128)(2,1)} %get-tuple-element.12), channel_id=1, source_target_pairs={{0,8},{4,12},{8,0},{12,4},{16,24},{20,28},{24,16},{28,20},{1,9},{5... | collective-permute-start | bytes 3735560 | tf_op jit(solution)/shard_map/ppermute | solution.py:93
  143.7 56.0 %collective-permute-start.2 = (bf16[19,128,256]{2,1,0:T(8,128)(2,1)}, bf16[19,128,256]{2,1,0:T(8,128)(2,1)}, u32[]{:S(2)}, u32[]{:S(2)}) collective-permute-start(bf16[19,128,256]{2,1,0:T(8,128)(2,1)} %get-tuple-element.14), channel_id=1, source_target_pairs={{0,16},{4,20},{8,24},{12,28},{16,0},{20,4},{24,8},{28,12},{1,17},{... | collective-permute-start | bytes 3735560 | tf_op jit(solution)/shard_map/ppermute | solution.py:93
  145.2 54.5 %collective-permute-start.3 = (bf16[19,128,256]{2,1,0:T(8,128)(2,1)}, bf16[19,128,256]{2,1,0:T(8,128)(2,1)}, u32[]{:S(2)}, u32[]{:S(2)}) collective-permute-start(bf16[19,128,256]{2,1,0:T(8,128)(2,1)} %get-tuple-element.13), channel_id=1, source_target_pairs={{0,24},{4,28},{8,16},{12,20},{16,8},{20,12},{24,0},{28,4},{1,25},{... | collective-permute-start | bytes 3735560 | tf_op jit(solution)/shard_map/ppermute | solution.py:93
  205.0 67.9 %all-to-all-start = ((bf16[19,128,256]{2,0,1:T(8,128)(2,1)}), bf16[19,128,256]{2,0,1:T(8,128)(2,1)S(1)}, u32[]{:S(2)}, u32[]{:S(2)}) async-start(bf16[19,128,256]{2,0,1:T(8,128)(2,1)} %copy.25), calls=%async_computation | async-start | bytes 3145728 | tf_op jit(solution)/shard_map/all_to_all | solution.py:98
  214.5 30.3 %collective-permute-start.5 = (bf16[19,128,256]{2,1,0:T(8,128)(2,1)S(1)}, bf16[19,128,256]{2,1,0:T(8,128)(2,1)S(1)}, u32[]{:S(2)}, u32[]{:S(2)}) collective-permute-start(bf16[19,128,256]{2,1,0:T(8,128)(2,1)S(1)} %get-tuple-element.15), channel_id=1, source_target_pairs={{0,8},{4,12},{8,0},{12,4},{16,24},{20,28},{24,16},{28,20},{1,9},{5... | collective-permute-start | bytes 3735560 | tf_op jit(solution)/shard_map/ppermute | solution.py:93
  215.8 54.5 %collective-permute-start.6 = (bf16[19,128,256]{2,1,0:T(8,128)(2,1)S(1)}, bf16[19,128,256]{2,1,0:T(8,128)(2,1)S(1)}, u32[]{:S(2)}, u32[]{:S(2)}) collective-permute-start(bf16[19,128,256]{2,1,0:T(8,128)(2,1)S(1)} %get-tuple-element.17), channel_id=1, source_target_pairs={{0,16},{4,20},{8,24},{12,28},{16,0},{20,4},{24,8},{28,12},{1,17},{... | collective-permute-start | bytes 3735560 | tf_op jit(solution)/shard_map/ppermute | solution.py:93
  216.6 53.7 %collective-permute-start.7 = (bf16[19,128,256]{2,1,0:T(8,128)(2,1)S(1)}, bf16[19,128,256]{2,1,0:T(8,128)(2,1)S(1)}, u32[]{:S(2)}, u32[]{:S(2)}) collective-permute-start(bf16[19,128,256]{2,1,0:T(8,128)(2,1)S(1)} %get-tuple-element.16), channel_id=1, source_target_pairs={{0,24},{4,28},{8,16},{12,20},{16,8},{20,12},{24,0},{28,4},{1,25},{... | collective-permute-start | bytes 3735560 | tf_op jit(solution)/shard_map/ppermute | solution.py:93
  272.9 37.5 %all-to-all-start.1 = ((bf16[19,128,256]{2,0,1:T(8,128)(2,1)}), bf16[19,128,256]{2,0,1:T(8,128)(2,1)S(1)}, u32[]{:S(2)}, u32[]{:S(2)}) async-start(bf16[19,128,256]{2,0,1:T(8,128)(2,1)} %copy.29), calls=%async_computation.1 | async-start | bytes 3145728 | tf_op jit(solution)/shard_map/all_to_all | solution.py:98
  311.4 5.0 %slice-start.2 = ((s8[8388608]{0:T(1024)(128)(4,1)}), s8[4194304]{0:T(1024)(128)(4,1)S(1)}, s32[]{:S(2)}) async-start(s8[8388608]{0:T(1024)(128)(4,1)} %bitcast.113), calls=%async_computation.4 | async-start | bytes 8388608
  311.7 4.7 %slice-start.3 = ((s8[8388608]{0:T(1024)(128)(4,1)}), s8[4194304]{0:T(1024)(128)(4,1)S(1)}, s32[]{:S(2)}) async-start(s8[8388608]{0:T(1024)(128)(4,1)} %bitcast.113), calls=%async_computation.5 | async-start | bytes 8388608
  311.7 7.5 %slice-start = ((s8[4980736]{0:T(1024)(128)(4,1)}), s8[4194304]{0:T(1024)(128)(4,1)S(1)}, s32[]{:S(2)}) async-start(s8[4980736]{0:T(1024)(128)(4,1)} %bitcast.109), calls=%async_computation.2 | async-start | bytes 8388608
  316.4 2.8 slice-start.1
  320.6 4.7 %collective-permute-start.8 = (f32[19,1024]{1,0:T(8,128)S(1)}, f32[19,1024]{1,0:T(8,128)S(1)}, u32[]{:S(2)}, u32[]{:S(2)}) collective-permute-start(f32[19,1024]{1,0:T(8,128)S(1)} %fusion.28), channel_id=1, source_target_pairs={{0,1},{1,0},{2,3},{3,2},{4,5},{5,4},{6,7},{7,6},{8,9},{9,8},{10,11... | collective-permute-start | bytes 233480 | tf_op jit(solution)/shard_map/ppermute | solution.py:56
  325.3 6.2 %collective-permute-start.9 = (f32[19,1024]{1,0:T(8,128)S(1)}, f32[19,1024]{1,0:T(8,128)S(1)}, u32[]{:S(2)}, u32[]{:S(2)}) collective-permute-start(f32[19,1024]{1,0:T(8,128)S(1)} %add.325), channel_id=1, source_target_pairs={{0,2},{1,3},{2,0},{3,1},{4,6},{5,7},{6,4},{7,5},{8,10},{9,11},{10,... | collective-permute-start | bytes 233480 | tf_op jit(solution)/shard_map/ppermute | solution.py:56

commit v14 on v9

--- a/solution.py
+++ b/solution.py
@@ -124,8 +124,8 @@
     table = delay_table()
     first = _gather_pair(blocks[:, :, 0, :], matrix, pick2, parity, chip, n_owners, slots_dev)
     second = _gather_pair(blocks[:, :, 1, :], matrix, pick2, parity, chip, n_owners, slots_dev)
+    table, second = lax.optimization_barrier((table, second))
     galaxy_f = galaxy.astype(jnp.float32)
-    table, galaxy_f, second = lax.optimization_barrier((table, galaxy_f, second))
     out = None
     for k, (pair_send, own) in enumerate((first, second)):
         piece = _scatter_pairs(pair_send, own, chip, n_owners)
@@ -135,10 +135,13 @@
             table[k * CH:(k + 1) * CH],
             preferred_element_type=jnp.float32,
         )
-        out = term if out is None else out + term
-    delay = out.reshape(count, cells_part, 2 * CH)
-    product = delay[..., :CH] * galaxy_f[..., :CH] + delay[..., CH:] * galaxy_f[..., CH:]
-    local_power = jnp.sum(product, axis=1)
+        part = term.reshape(count, cells_part, 2 * CH)
+        power_part = jnp.sum(
+            part[..., :CH] * galaxy_f[..., :CH] + part[..., CH:] * galaxy_f[..., CH:], axis=1
+        )
+        out = part if out is None else out + part
+        local_power = power_part if k == 0 else local_power + power_part
+    delay = out
     power = _allreduce_sum(local_power, "chan", n_chan) / jnp.float32(math.sqrt(TC))
     return (delay.astype(jnp.bfloat16), power)
 

time: 329 us -> 334 us (1.015)
  local copies, waits for them, and re-layouts: 56.8 us -> 61.8 us
  matrix products: 60.3 us -> 64.1 us
  waiting for transfers between devices: 99.2 us -> 95.5 us
    all_to_all x2, waiting for transfers between devices: 31.4 us -> 22.5 us  [_scatter_pairs(): lax.all_to_all(gridded, 'chan', split_axis=1, concat_axis=2, tiled=True)]
    dot_general x0 -> x2, local copies, waits for them, and re-layouts: none -> 4.44 us  [body(): jnp.dot(piece.reshape(count * cells_part, CH), table[k * CH:(k + 1) * CH]...]
    dot_general x2, matrix products: 7.48 us -> 11.2 us  [body(): jnp.dot(piece.reshape(count * cells_part, CH), table[k * CH:(k + 1) * CH]...]
    ppermute x6, waiting for transfers between devices: 59.5 us -> 62.9 us  [_scatter_pairs(): lax.ppermute(send, 'uv', _partner_pairs(n_owners, lambda i, dest=dest: de...]
    unnamed x23 -> x13, local copies, waits for them, and re-layouts: 12.2 us -> 11.7 us
  transfers between devices with their start and end apart: 12 -> 12, of which waited for: 6 -> 6; matrix products, arithmetic and copies ran while one was open for 35% -> 36% of each run, Pallas kernels for 0% -> 0%
where the time goes in v14:
time: 334 us; the launch traced here: 328 us
  waiting for transfers between devices  95.5 us (29%)
  other arithmetic  86.1 us (26%)
  matrix products  64.1 us (19%)
  local copies, waits for them, and re-layouts  61.8 us (19%)
  starting transfers between devices  19.2 us (6%)
    ppermute x6, waiting for transfers between devices, _scatter_pairs(): lax.ppermute(send, 'uv', _partner_pairs(n_owners, lambda i, dest=dest: de...  62.9 us
    dot_general x2, matrix products, _gather_pair(): jnp.einsum('sb,bcf->scf', pick2, jnp.concatenate([high, low], axis=0), pr...  34.1 us
    all_to_all x2, waiting for transfers between devices, _scatter_pairs(): lax.all_to_all(gridded, 'chan', split_axis=1, concat_axis=2, tiled=True)  22.5 us
    convert_element_type x2, local copies, waits for them, and re-layouts, _gather_pair(): partial = jnp.einsum('sb,bcf->scf', pick2, jnp.concatenate([high, low], a...  20 us
    dot_general x2, matrix products, _gather_pair(): jnp.einsum('bcr,brf->bcf', matrix, part, preferred_element_type=jnp.float32)  18.7 us
    another operation x1, other arithmetic  18.5 us
    concatenate x1, other arithmetic, delay_table(): return jnp.concatenate([upper, lower], axis=0).astype(jnp.bfloat16)  17 us
    concatenate x2, other arithmetic, _gather_pair(): jnp.concatenate([high, low], axis=0)  14.9 us
  transfers between devices with their start and end apart: 12, of which 6 were waited for; matrix products, arithmetic and copies ran while one was open for 36% of the time, Pallas kernels for 0%

profile of v14, /device:TPU:0, one launch (start us, length us, event | category | flops | bytes accessed | tf_op | source)
XLA Modules:
  0.0 327.8 jit_solution(10581420469435054773)
XLA Ops:
  4.4 11.7 %copy.24 = bf16[12288,2,256]{2,0,1:T(8,128)(2,1)} copy(bf16[12288,2,256]{2,1,0:T(2,128)(2,1)} %param.7) | data formatting | bytes 25165824 | tf_op args[0]
  19.1 5.1 %add_bitcast_fusion.10 = (s32[96,128]{1,0:T(8,128)S(1)}, s32[96,128]{1,0:T(8,128)S(1)}, s32[96,128]{1,0:T(8,128)S(1)}, s32[96,128]{1,0:T(8,128)S(1)}, s32[96,128...) fusion(s32[12288]{0:T(1024)S(1)} %copy-done.2, s32[]{:T(128)} %bitcast.1, ...), kind=kLoop, calls=%fused_computation.93 | loop fusion | flops 98304 | bytes 442400 | tf_op jit(solution)/shard_map/add | solution.py:24
  24.2 9.4 %subtract_convert_fusion.1 = (bf16[96,128,256]{2,1,0:T(8,128)(2,1)S(1)}, bf16[96,128,256]{2,1,0:T(8,128)(2,1)S(1)}) fusion(bf16[96,128,2,256]{3,1,0,2:T(8,128)(2,1)} %bitcast.112, f32[96,128]{1,0:T(8,128)S(1)} %bitcast.121, s32[96,128]{1,0:T(8,128)S(1)} %get-tuple-element.34, f32[96,128]{1,0:T(8,128)S(1)} %bitcast.123, s32[96,128]{1,0:T(8,128)S(1)} %get-tuple-element.35, ...), kind=kOutput, calls=%fused_computation.9 | convolution fusion | flops 855638016 | bytes 19660800 | tf_op jit(solution)/shard_map/bcr,brf->bcf/dot_general | solution.py:63
  33.6 7.3 %pad_maximum_fusion = bf16[192,128,256]{2,1,0:T(8,128)(2,1)} fusion(bf16[96,128,256]{2,1,0:T(8,128)(2,1)S(1)} %get-tuple-element.12, bf16[96,128,256]{2,1,0:T(8,128)(2,1)S(1)} %get-tuple-element.13), kind=kLoop, calls=%fused_computation.2 | loop fusion | flops 6291456 | bytes 25165824 | tf_op jit(solution)/shard_map/concatenate | solution.py:69
  40.8 17.1 %fusion.6 = bf16[152,128,256]{2,0,1:T(8,128)(2,1)} fusion(bf16[192,128,256]{2,1,0:T(8,128)(2,1)} %pad_maximum_fusion, pred[152,96]{1,0:T(8,128)(4,1)S(1)} %iota_compare_fusion.8), kind=kOutput, calls=%fused_computation.15 | convolution fusion | flops 1917612544 | bytes 22558976 | tf_op jit(solution)/shard_map/sb,bcf->scf/dot_general | solution.py:66
  57.9 10.1 %copy.26 = bf16[152,128,256]{2,1,0:T(8,128)(2,1)} copy(bf16[152,128,256]{2,0,1:T(8,128)(2,1)} %fusion.6) | data formatting | bytes 19922944 | tf_op jit(solution)/shard_map/convert_element_type | solution.py:71
  68.0 5.3 %dynamic-slice_bitcast_fusion.1 = bf16[4,19,128,256]{3,2,1,0:T(8,128)(2,1)} fusion(bf16[2,4,19,128,256]{4,3,2,1,0:T(8,128)(2,1)} %bitcast.104, s32[]{:T(128)S(6)} %select_n.120), kind=kLoop, calls=%fused_computation.35 | loop fusion | bytes 9961476 | tf_op jit(solution)/shard_map/jit(dynamic_index_in_dim)/squeeze | solution.py:75
  73.8 9.4 %subtract_convert_fusion = (bf16[96,128,256]{2,1,0:T(8,128)(2,1)S(1)}, bf16[96,128,256]{2,1,0:T(8,128)(2,1)S(1)}) fusion(bf16[96,128,2,256]{3,1,0,2:T(8,128)(2,1)} %bitcast.113, f32[96,128]{1,0:T(8,128)S(1)} %bitcast.122, s32[96,128]{1,0:T(8,128)S(1)} %get-tuple-element.34, f32[96,128]{1,0:T(8,128)S(1)} %bitcast.124, s32[96,128]{1,0:T(8,128)S(1)} %get-tuple-element.35, ...), kind=kOutput, calls=%fused_computation.8 | convolution fusion | flops 855638016 | bytes 19660800 | tf_op jit(solution)/shard_map/bcr,brf->bcf/dot_general | solution.py:63
  83.1 7.6 %pad_maximum_fusion.1 = bf16[192,128,256]{2,1,0:T(8,128)(2,1)} fusion(bf16[96,128,256]{2,1,0:T(8,128)(2,1)S(1)} %get-tuple-element.10, bf16[96,128,256]{2,1,0:T(8,128)(2,1)S(1)} %get-tuple-element.11), kind=kLoop, calls=%fused_computation.3 | loop fusion | flops 6291456 | bytes 25165824 | tf_op jit(solution)/shard_map/concatenate | solution.py:69
  90.7 17.0 %fusion.9 = bf16[152,128,256]{2,0,1:T(8,128)(2,1)} fusion(bf16[192,128,256]{2,1,0:T(8,128)(2,1)} %pad_maximum_fusion.1, pred[152,96]{1,0:T(8,128)(4,1)S(1)} %iota_compare_fusion.8), kind=kOutput, calls=%fused_computation.16 | convolution fusion | flops 1917612544 | bytes 22558976 | tf_op jit(solution)/shard_map/sb,bcf->scf/dot_general | solution.py:66
  107.7 9.9 %copy.30 = bf16[152,128,256]{2,1,0:T(8,128)(2,1)} copy(bf16[152,128,256]{2,0,1:T(8,128)(2,1)} %fusion.9) | data formatting | bytes 19922944 | tf_op jit(solution)/shard_map/convert_element_type | solution.py:71
  117.7 5.2 %dynamic-slice_bitcast_fusion = bf16[4,19,128,256]{3,2,1,0:T(8,128)(2,1)} fusion(bf16[2,4,19,128,256]{4,3,2,1,0:T(8,128)(2,1)} %bitcast.107, s32[]{:T(128)S(6)} %select_n.120), kind=kLoop, calls=%fused_computation.34 | loop fusion | bytes 9961476 | tf_op jit(solution)/shard_map/jit(dynamic_index_in_dim)/squeeze | solution.py:75
  123.0 6.2 %fusion.5 = bf16[4,19,128,256]{3,2,1,0:T(8,128)(2,1)S(1)} fusion(bf16[4,19,128,256]{3,2,1,0:T(8,128)(2,1)} %collective-permute-done, bf16[2,4,19,128,256]{4,3,2,1,0:T(8,128)(2,1)} %bitcast.105, s32[]{:T(128)S(6)} %select_n.115), kind=kLoop, calls=%fused_computation.13 | loop fusion | flops 9961472 | bytes 14942212 | tf_op jit(solution)/shard_map/convert_element_type | solution.py:77
  135.6 18.5 %multiply_convert_fusion.1 = (bf16[1024,1024]{1,0:T(8,128)(2,1)S(1)}, bf16[1024,1024]{1,0:T(8,128)(2,1)}, bf16[1024,1024]{1,0:T(8,128)(2,1)}) fusion(f32[1024]{0:T(1024)S(1)} %subtract_multiply_fusion), kind=kLoop, calls=%fused_computation.46 | loop fusion | flops 22020096 | bytes 6295552 | tf_op jit(solution)/shard_map/convert.20
  154.2 17.0 %maximum_maximum_fusion = bf16[2048,2048]{1,0:T(8,128)(2,1)} fusion(bf16[1024,1024]{1,0:T(8,128)(2,1)} %get-tuple-element.38, bf16[1024,1024]{1,0:T(8,128)(2,1)} %get-tuple-element.37, bf16[1024,1024]{1,0:T(8,128)(2,1)S(1)} %get-tuple-element.36), kind=kLoop, calls=%fused_computation.14 | loop fusion | flops 33554432 | bytes 14680064 | tf_op jit(solution)/shard_map/concatenate | solution.py:44
  171.1 8.4 %fusion.4 = bf16[4,19,128,256]{3,2,1,0:T(8,128)(2,1)} fusion(bf16[4,19,128,256]{3,2,1,0:T(8,128)(2,1)} %collective-permute-done.4, bf16[2,4,19,128,256]{4,3,2,1,0:T(8,128)(2,1)} %bitcast.108, s32[]{:T(128)S(6)} %select_n.115), kind=kLoop, calls=%fused_computation.11 | loop fusion | flops 9961472 | bytes 14942212 | tf_op jit(solution)/shard_map/convert_element_type | solution.py:77
  179.5 10.6 %collective-permute-done.2 = bf16[19,128,256]{2,1,0:T(8,128)(2,1)} collective-permute-done((bf16[19,128,256]{2,1,0:T(8,128)(2,1)}, bf16[19,128,256]{2,1,0:T(8,128)(2,1)}, u32[]{:S(2)}, u32[]{:S(2)}) %collective-permute-start.2) | collective-permute-done | bytes 1245216 | tf_op jit(solution)/shard_map/ppermute | solution.py:93
  195.4 5.1 %all-to-all-start = ((bf16[19,128,256]{2,0,1:T(8,128)(2,1)}), bf16[19,128,256]{2,0,1:T(8,128)(2,1)S(1)}, u32[]{:S(2)}, u32[]{:S(2)}) async-start(bf16[19,128,256]{2,0,1:T(8,128)(2,1)} %copy.27), calls=%async_computation | async-start | bytes 3145728 | tf_op jit(solution)/shard_map/all_to_all | solution.py:98
  208.3 26.8 %collective-permute-done.5 = bf16[19,128,256]{2,1,0:T(8,128)(2,1)S(1)} collective-permute-done((bf16[19,128,256]{2,1,0:T(8,128)(2,1)S(1)}, bf16[19,128,256]{2,1,0:T(8,128)(2,1)S(1)}, u32[]{:S(2)}, u32[]{:S(2)}) %collective-permute-start.5) | collective-permute-done | bytes 1245216 | tf_op jit(solution)/shard_map/ppermute | solution.py:93
  235.1 25.5 %collective-permute-done.6 = bf16[19,128,256]{2,1,0:T(8,128)(2,1)S(1)} collective-permute-done((bf16[19,128,256]{2,1,0:T(8,128)(2,1)S(1)}, bf16[19,128,256]{2,1,0:T(8,128)(2,1)S(1)}, u32[]{:S(2)}, u32[]{:S(2)}) %collective-permute-start.6) | collective-permute-done | bytes 1245216 | tf_op jit(solution)/shard_map/ppermute | solution.py:93
  263.3 4.8 %all-to-all-start.1 = ((bf16[19,128,256]{2,0,1:T(8,128)(2,1)}), bf16[19,128,256]{2,0,1:T(8,128)(2,1)S(1)}, u32[]{:S(2)}, u32[]{:S(2)}) async-start(bf16[19,128,256]{2,0,1:T(8,128)(2,1)} %copy.31), calls=%async_computation.1 | async-start | bytes 3145728 | tf_op jit(solution)/shard_map/all_to_all | solution.py:98
  278.3 22.5 %all-to-all-done.1 = bf16[19,128,256]{2,0,1:T(8,128)(2,1)S(1)} async-done(((bf16[19,128,256]{2,0,1:T(8,128)(2,1)}), bf16[19,128,256]{2,0,1:T(8,128)(2,1)S(1)}, u32[]{:S(2)}, u32[]{:S(2)}) %all-to-all-start.1) | async-done | bytes 1245216 | tf_op jit(solution)/shard_map/all_to_all | solution.py:98
  307.4 6.5 %add_convert_fusion.1 = (bf16[19,32,2048]{2,1,0:T(8,128)(2,1)}, f32[19,32,2048]{2,1,0:T(8,128)S(1)}) fusion(f32[19,32,2048]{2,1,0:T(8,128)S(1)} %fusion.17, bf16[19,32,1024]{2,1,0:T(8,128)(2,1)S(1)} %copy-done.1, bf16[2048,2048]{1,0:T(8,128)(2,1)} %maximum_maximum_fusion), kind=kOutput, calls=%fused_computation.33 | convolution fusion | flops 2552627200 | bytes 17891328 | tf_op jit(solution)/shard_map/dot_general | solution.py:133
  321.4 5.5 %collective-permute-done.9 = f32[19,1024]{1,0:T(8,128)S(1)} collective-permute-done((f32[19,1024]{1,0:T(8,128)S(1)}, f32[19,1024]{1,0:T(8,128)S(1)}, u32[]{:S(2)}, u32[]{:S(2)}) %collective-permute-start.9) | collective-permute-done | bytes 77856 | tf_op jit(solution)/shard_map/ppermute | solution.py:56
  (59 shorter events, 54.3 us)
Async XLA Ops:
  4.4 11.8 %copy-start.3 = (s32[96]{0:T(128)S(1)}, s32[96]{0:T(128)}, u32[]{:S(2)}) copy-start(s32[96]{0:T(128)} %param.11) | copy-start | bytes 1156
  4.4 11.8 %copy-start = (s32[80]{0:T(128)S(1)}, s32[80]{0:T(128)}, u32[]{:S(2)}) copy-start(s32[80]{0:T(128)} %param.12) | copy-start | bytes 964
  4.4 14.7 %copy-start.2 = (s32[12288]{0:T(1024)S(1)}, s32[12288]{0:T(1024)}, u32[]{:S(2)}) copy-start(s32[12288]{0:T(1024)} %param.8) | copy-start | bytes 147460
  73.3 49.7 %collective-permute-start = (bf16[4,19,128,256]{3,2,1,0:T(8,128)(2,1)}, bf16[4,19,128,256]{3,2,1,0:T(8,128)(2,1)}, u32[]{:S(2)}, u32[]{:S(2)}) collective-permute-start(bf16[4,19,128,256]{3,2,1,0:T(8,128)(2,1)} %dynamic-slice_bitcast_fusion.1), channel_id=1, source_target_pairs={{0,4},{4,0},{8,12},{12,8},{16,20},{20,16},{24,28},{28,24},{1,5},{5... | collective-permute-start | bytes 14942216 | tf_op jit(solution)/shard_map/ppermute | solution.py:76
  122.9 48.3 %collective-permute-start.4 = (bf16[4,19,128,256]{3,2,1,0:T(8,128)(2,1)}, bf16[4,19,128,256]{3,2,1,0:T(8,128)(2,1)}, u32[]{:S(2)}, u32[]{:S(2)}) collective-permute-start(bf16[4,19,128,256]{3,2,1,0:T(8,128)(2,1)} %dynamic-slice_bitcast_fusion), channel_id=1, source_target_pairs={{0,4},{4,0},{8,12},{12,8},{16,20},{20,16},{24,28},{28,24},{1,5},{5... | collective-permute-start | bytes 14942216 | tf_op jit(solution)/shard_map/ppermute | solution.py:76
  131.1 48.4 %collective-permute-start.1 = (bf16[19,128,256]{2,1,0:T(8,128)(2,1)}, bf16[19,128,256]{2,1,0:T(8,128)(2,1)S(1)}, u32[]{:S(2)}, u32[]{:S(2)}) collective-permute-start(bf16[19,128,256]{2,1,0:T(8,128)(2,1)} %get-tuple-element.17), channel_id=1, source_target_pairs={{0,8},{4,12},{8,0},{12,4},{16,24},{20,28},{24,16},{28,20},{1,9},{5... | collective-permute-start | bytes 3735560 | tf_op jit(solution)/shard_map/ppermute | solution.py:93
  134.1 56.0 %collective-permute-start.2 = (bf16[19,128,256]{2,1,0:T(8,128)(2,1)}, bf16[19,128,256]{2,1,0:T(8,128)(2,1)}, u32[]{:S(2)}, u32[]{:S(2)}) collective-permute-start(bf16[19,128,256]{2,1,0:T(8,128)(2,1)} %get-tuple-element.19), channel_id=1, source_target_pairs={{0,16},{4,20},{8,24},{12,28},{16,0},{20,4},{24,8},{28,12},{1,17},{... | collective-permute-start | bytes 3735560 | tf_op jit(solution)/shard_map/ppermute | solution.py:93
  135.6 54.5 %collective-permute-start.3 = (bf16[19,128,256]{2,1,0:T(8,128)(2,1)}, bf16[19,128,256]{2,1,0:T(8,128)(2,1)}, u32[]{:S(2)}, u32[]{:S(2)}) collective-permute-start(bf16[19,128,256]{2,1,0:T(8,128)(2,1)} %get-tuple-element.18), channel_id=1, source_target_pairs={{0,24},{4,28},{8,16},{12,20},{16,8},{20,12},{24,0},{28,4},{1,25},{... | collective-permute-start | bytes 3735560 | tf_op jit(solution)/shard_map/ppermute | solution.py:93
  195.4 67.9 %all-to-all-start = ((bf16[19,128,256]{2,0,1:T(8,128)(2,1)}), bf16[19,128,256]{2,0,1:T(8,128)(2,1)S(1)}, u32[]{:S(2)}, u32[]{:S(2)}) async-start(bf16[19,128,256]{2,0,1:T(8,128)(2,1)} %copy.27), calls=%async_computation | async-start | bytes 3145728 | tf_op jit(solution)/shard_map/all_to_all | solution.py:98
  204.8 30.3 %collective-permute-start.5 = (bf16[19,128,256]{2,1,0:T(8,128)(2,1)S(1)}, bf16[19,128,256]{2,1,0:T(8,128)(2,1)S(1)}, u32[]{:S(2)}, u32[]{:S(2)}) collective-permute-start(bf16[19,128,256]{2,1,0:T(8,128)(2,1)S(1)} %get-tuple-element.14), channel_id=1, source_target_pairs={{0,8},{4,12},{8,0},{12,4},{16,24},{20,28},{24,16},{28,20},{1,9},{5... | collective-permute-start | bytes 3735560 | tf_op jit(solution)/shard_map/ppermute | solution.py:93
  206.1 54.6 %collective-permute-start.6 = (bf16[19,128,256]{2,1,0:T(8,128)(2,1)S(1)}, bf16[19,128,256]{2,1,0:T(8,128)(2,1)S(1)}, u32[]{:S(2)}, u32[]{:S(2)}) collective-permute-start(bf16[19,128,256]{2,1,0:T(8,128)(2,1)S(1)} %get-tuple-element.16), channel_id=1, source_target_pairs={{0,16},{4,20},{8,24},{12,28},{16,0},{20,4},{24,8},{28,12},{1,17},{... | collective-permute-start | bytes 3735560 | tf_op jit(solution)/shard_map/ppermute | solution.py:93
  206.9 53.7 %collective-permute-start.7 = (bf16[19,128,256]{2,1,0:T(8,128)(2,1)S(1)}, bf16[19,128,256]{2,1,0:T(8,128)(2,1)S(1)}, u32[]{:S(2)}, u32[]{:S(2)}) collective-permute-start(bf16[19,128,256]{2,1,0:T(8,128)(2,1)S(1)} %get-tuple-element.15), channel_id=1, source_target_pairs={{0,24},{4,28},{8,16},{12,20},{16,8},{20,12},{24,0},{28,4},{1,25},{... | collective-permute-start | bytes 3735560 | tf_op jit(solution)/shard_map/ppermute | solution.py:93
  263.3 37.5 %all-to-all-start.1 = ((bf16[19,128,256]{2,0,1:T(8,128)(2,1)}), bf16[19,128,256]{2,0,1:T(8,128)(2,1)S(1)}, u32[]{:S(2)}, u32[]{:S(2)}) async-start(bf16[19,128,256]{2,0,1:T(8,128)(2,1)} %copy.31), calls=%async_computation.1 | async-start | bytes 3145728 | tf_op jit(solution)/shard_map/all_to_all | solution.py:98
  302.6 4.7 %copy-start.1 = (bf16[19,32,1024]{2,1,0:T(8,128)(2,1)S(1)}, bf16[19,32,1024]{2,1,0:T(8,128)(2,1)}, u32[]{:S(2)}) copy-start(bf16[19,32,1024]{2,1,0:T(8,128)(2,1)} %dot_general.24) | copy-start | bytes 3735556
  302.7 11.2 %slice-start = ((s8[4980736]{0:T(1024)(128)(4,1)}), s8[4194304]{0:T(1024)(128)(4,1)S(1)}, s32[]{:S(2)}) async-start(s8[4980736]{0:T(1024)(128)(4,1)} %bitcast.110), calls=%async_computation.2 | async-start | bytes 8388608
  307.4 6.5 %slice-start.1 = ((s8[4980736]{0:T(1024)(128)(4,1)}), s8[786432]{0:T(1024)(128)(4,1)S(1)}, s32[]{:S(2)}) async-start(s8[4980736]{0:T(1024)(128)(4,1)} %bitcast.110), calls=%async_computation.3 | async-start | bytes 1572864
  316.0 4.7 %collective-permute-start.8 = (f32[19,1024]{1,0:T(8,128)S(1)}, f32[19,1024]{1,0:T(8,128)S(1)}, u32[]{:S(2)}, u32[]{:S(2)}) collective-permute-start(f32[19,1024]{1,0:T(8,128)S(1)} %add.332), channel_id=1, source_target_pairs={{0,1},{1,0},{2,3},{3,2},{4,5},{5,4},{6,7},{7,6},{8,9},{9,8},{10,11... | collective-permute-start | bytes 233480 | tf_op jit(solution)/shard_map/ppermute | solution.py:56
  320.7 6.2 %collective-permute-start.9 = (f32[19,1024]{1,0:T(8,128)S(1)}, f32[19,1024]{1,0:T(8,128)S(1)}, u32[]{:S(2)}, u32[]{:S(2)}) collective-permute-start(f32[19,1024]{1,0:T(8,128)S(1)} %add.333), channel_id=1, source_target_pairs={{0,2},{1,3},{2,0},{3,1},{4,6},{5,7},{6,4},{7,5},{8,10},{9,11},{10,... | collective-permute-start | bytes 233480 | tf_op jit(solution)/shard_map/ppermute | solution.py:56

commit v15 on v5

--- a/solution.py
+++ b/solution.py
@@ -126,7 +126,7 @@
     second = _gather_pair(blocks[:, :, 1, :], matrix, pick2, parity, chip, n_owners, slots_dev)
     table, second = lax.optimization_barrier((table, second))
     out = None
-    for k, (pair_send, own) in enumerate((first, second)):
+    for k, (pair_send, own) in ((1, second), (0, first)):
         piece = _scatter_pairs(pair_send, own, chip, n_owners)
         count, cells_part = piece.shape[0], piece.shape[1]
         term = jnp.dot(

time: 329 us -> 387 us (1.18)
  waiting for transfers between devices: 98 us -> 142 us
  other arithmetic: 87.5 us -> 103 us
    ppermute x6, waiting for transfers between devices: 62.8 us -> 106 us  [_scatter_pairs(): lax.ppermute(send, 'uv', _partner_pairs(n_owners, lambda i, dest=dest: de...]
    concatenate x1, other arithmetic: 17.1 us -> 37 us  [delay_table(): return jnp.concatenate([upper, lower], axis=0).astype(jnp.bfloat16)]
    unnamed x17 -> x23, local copies, waits for them, and re-layouts: 12.2 us -> 12.3 us
  transfers between devices with their start and end apart: 12 -> 12, of which waited for: 6 -> 7; matrix products, arithmetic and copies ran while one was open for 36% -> 36% of each run, Pallas kernels for 0% -> 0%
where the time goes in v15:
time: 387 us; the launch traced here: 381 us
  waiting for transfers between devices  142 us (37%)
  other arithmetic  103 us (27%)
  matrix products  60.3 us (16%)
  local copies, waits for them, and re-layouts  55.4 us (14%)
  starting transfers between devices  19.3 us (5%)
    ppermute x6, waiting for transfers between devices, _scatter_pairs(): lax.ppermute(send, 'uv', _partner_pairs(n_owners, lambda i, dest=dest: de...  106 us
    concatenate x1, other arithmetic, delay_table(): return jnp.concatenate([upper, lower], axis=0).astype(jnp.bfloat16)  37 us
    dot_general x2, matrix products, _gather_pair(): jnp.einsum('sb,bcf->scf', pick2, jnp.concatenate([high, low], axis=0), pr...  34.1 us
    all_to_all x2, waiting for transfers between devices, _scatter_pairs(): lax.all_to_all(gridded, 'chan', split_axis=1, concat_axis=2, tiled=True)  26.8 us
    convert_element_type x2, local copies, waits for them, and re-layouts, _gather_pair(): partial = jnp.einsum('sb,bcf->scf', pick2, jnp.concatenate([high, low], a...  20.1 us
    dot_general x2, matrix products, _gather_pair(): jnp.einsum('bcr,brf->bcf', matrix, part, preferred_element_type=jnp.float32)  18.7 us
    another operation x1, other arithmetic  17.7 us
    concatenate x2, other arithmetic, _gather_pair(): jnp.concatenate([high, low], axis=0)  14.7 us
  transfers between devices with their start and end apart: 12, of which 7 were waited for; matrix products, arithmetic and copies ran while one was open for 36% of the time, Pallas kernels for 0%

profile of v15, /device:TPU:0, one launch (start us, length us, event | category | flops | bytes accessed | tf_op | source)
XLA Modules:
  0.0 381.0 jit_solution(11057607801994032073)
XLA Ops:
  4.4 11.7 %copy.22 = bf16[12288,2,256]{2,0,1:T(8,128)(2,1)} copy(bf16[12288,2,256]{2,1,0:T(2,128)(2,1)} %param.7) | data formatting | bytes 25165824 | tf_op args[0]
  19.1 5.0 %add_bitcast_fusion.10 = (s32[96,128]{1,0:T(8,128)S(1)}, s32[96,128]{1,0:T(8,128)S(1)}, s32[96,128]{1,0:T(8,128)S(1)}, s32[96,128]{1,0:T(8,128)S(1)}, s32[96,128...) fusion(s32[12288]{0:T(1024)S(1)} %copy-done.1, s32[]{:T(128)} %bitcast.1, ...), kind=kLoop, calls=%fused_computation.85 | loop fusion | flops 98304 | bytes 442400 | tf_op jit(solution)/shard_map/add | solution.py:24
  24.1 9.4 %subtract_convert_fusion.1 = (bf16[96,128,256]{2,1,0:T(8,128)(2,1)S(1)}, bf16[96,128,256]{2,1,0:T(8,128)(2,1)S(1)}) fusion(bf16[96,128,2,256]{3,1,0,2:T(8,128)(2,1)} %bitcast.111, f32[96,128]{1,0:T(8,128)S(1)} %bitcast.124, s32[96,128]{1,0:T(8,128)S(1)} %get-tuple-element.32, f32[96,128]{1,0:T(8,128)S(1)} %bitcast.126, s32[96,128]{1,0:T(8,128)S(1)} %get-tuple-element.33, ...), kind=kOutput, calls=%fused_computation.9 | convolution fusion | flops 855638016 | bytes 19660800 | tf_op jit(solution)/shard_map/bcr,brf->bcf/dot_general | solution.py:63
  33.5 7.1 %pad_maximum_fusion = bf16[192,128,256]{2,1,0:T(8,128)(2,1)} fusion(bf16[96,128,256]{2,1,0:T(8,128)(2,1)S(1)} %get-tuple-element.8, bf16[96,128,256]{2,1,0:T(8,128)(2,1)S(1)} %get-tuple-element.9), kind=kLoop, calls=%fused_computation.2 | loop fusion | flops 6291456 | bytes 25165824 | tf_op jit(solution)/shard_map/concatenate | solution.py:69
  40.7 17.0 %fusion.6 = bf16[152,128,256]{2,0,1:T(8,128)(2,1)} fusion(bf16[192,128,256]{2,1,0:T(8,128)(2,1)} %pad_maximum_fusion, pred[152,96]{1,0:T(8,128)(4,1)S(1)} %iota_compare_fusion.8), kind=kOutput, calls=%fused_computation.15 | convolution fusion | flops 1917612544 | bytes 22558976 | tf_op jit(solution)/shard_map/sb,bcf->scf/dot_general | solution.py:66
  57.7 10.0 %copy.24 = bf16[152,128,256]{2,1,0:T(8,128)(2,1)} copy(bf16[152,128,256]{2,0,1:T(8,128)(2,1)} %fusion.6) | data formatting | bytes 19922944 | tf_op jit(solution)/shard_map/convert_element_type | solution.py:71
  67.7 5.2 %dynamic-slice_bitcast_fusion.1 = bf16[4,19,128,256]{3,2,1,0:T(8,128)(2,1)} fusion(bf16[2,4,19,128,256]{4,3,2,1,0:T(8,128)(2,1)} %bitcast.102, s32[]{:T(128)S(6)} %select_n.117), kind=kLoop, calls=%fused_computation.34 | loop fusion | bytes 9961476 | tf_op jit(solution)/shard_map/jit(dynamic_index_in_dim)/squeeze | solution.py:75
  73.4 9.4 %subtract_convert_fusion = (bf16[96,128,256]{2,1,0:T(8,128)(2,1)S(1)}, bf16[96,128,256]{2,1,0:T(8,128)(2,1)S(1)}) fusion(bf16[96,128,2,256]{3,1,0,2:T(8,128)(2,1)} %bitcast.112, f32[96,128]{1,0:T(8,128)S(1)} %bitcast.125, s32[96,128]{1,0:T(8,128)S(1)} %get-tuple-element.32, f32[96,128]{1,0:T(8,128)S(1)} %bitcast.127, s32[96,128]{1,0:T(8,128)S(1)} %get-tuple-element.33, ...), kind=kOutput, calls=%fused_computation.8 | convolution fusion | flops 855638016 | bytes 19660800 | tf_op jit(solution)/shard_map/bcr,brf->bcf/dot_general | solution.py:63
  82.7 7.6 %pad_maximum_fusion.1 = bf16[192,128,256]{2,1,0:T(8,128)(2,1)} fusion(bf16[96,128,256]{2,1,0:T(8,128)(2,1)S(1)} %get-tuple-element.10, bf16[96,128,256]{2,1,0:T(8,128)(2,1)S(1)} %get-tuple-element.11), kind=kLoop, calls=%fused_computation.3 | loop fusion | flops 6291456 | bytes 25165824 | tf_op jit(solution)/shard_map/concatenate | solution.py:69
  90.3 17.0 %fusion.9 = bf16[152,128,256]{2,0,1:T(8,128)(2,1)} fusion(bf16[192,128,256]{2,1,0:T(8,128)(2,1)} %pad_maximum_fusion.1, pred[152,96]{1,0:T(8,128)(4,1)S(1)} %iota_compare_fusion.8), kind=kOutput, calls=%fused_computation.16 | convolution fusion | flops 1917612544 | bytes 22558976 | tf_op jit(solution)/shard_map/sb,bcf->scf/dot_general | solution.py:66
  107.4 10.1 %copy.28 = bf16[152,128,256]{2,1,0:T(8,128)(2,1)} copy(bf16[152,128,256]{2,0,1:T(8,128)(2,1)} %fusion.9) | data formatting | bytes 19922944 | tf_op jit(solution)/shard_map/convert_element_type | solution.py:71
  117.5 5.3 %dynamic-slice_bitcast_fusion = bf16[4,19,128,256]{3,2,1,0:T(8,128)(2,1)} fusion(bf16[2,4,19,128,256]{4,3,2,1,0:T(8,128)(2,1)} %bitcast.99, s32[]{:T(128)S(6)} %select_n.117), kind=kLoop, calls=%fused_computation.33 | loop fusion | bytes 9961476 | tf_op jit(solution)/shard_map/jit(dynamic_index_in_dim)/squeeze | solution.py:75
  122.9 17.7 %multiply_convert_fusion.1 = (bf16[1024,1024]{1,0:T(8,128)(2,1)S(1)}, bf16[1024,1024]{1,0:T(8,128)(2,1)S(1)}, bf16[1024,1024]{1,0:T(8,128)(2,1)S(1)}) fusion(f32[1024]{0:T(1024)S(1)} %subtract_multiply_fusion), kind=kLoop, calls=%fused_computation.43 | loop fusion | flops 22020096 | bytes 6295552 | tf_op jit(solution)/shard_map/convert.20
  140.6 37.0 %maximum_maximum_fusion = bf16[2048,2048]{1,0:T(8,128)(2,1)} fusion(bf16[1024,1024]{1,0:T(8,128)(2,1)S(1)} %get-tuple-element.36, bf16[1024,1024]{1,0:T(8,128)(2,1)S(1)} %get-tuple-element.35, bf16[1024,1024]{1,0:T(8,128)(2,1)S(1)} %get-tuple-element.34), kind=kLoop, calls=%fused_computation.14 | loop fusion | flops 33554432 | bytes 14680064 | tf_op jit(solution)/shard_map/concatenate | solution.py:44
  179.3 6.5 %fusion.5 = bf16[4,19,128,256]{3,2,1,0:T(8,128)(2,1)} fusion(bf16[4,19,128,256]{3,2,1,0:T(8,128)(2,1)} %collective-permute-done, bf16[2,4,19,128,256]{4,3,2,1,0:T(8,128)(2,1)S(1)} %bitcast.106, s32[]{:T(128)S(6)} %select_n.116), kind=kLoop, calls=%fused_computation.13 | loop fusion | flops 9961472 | bytes 14942212 | tf_op jit(solution)/shard_map/convert_element_type | solution.py:77
  192.7 26.7 %collective-permute-done.1 = bf16[19,128,256]{2,1,0:T(8,128)(2,1)S(1)} collective-permute-done((bf16[19,128,256]{2,1,0:T(8,128)(2,1)S(1)}, bf16[19,128,256]{2,1,0:T(8,128)(2,1)S(1)}, u32[]{:S(2)}, u32[]{:S(2)}) %collective-permute-start.1) | collective-permute-done | bytes 1245216 | tf_op jit(solution)/shard_map/ppermute | solution.py:93
  219.3 27.5 %collective-permute-done.2 = bf16[19,128,256]{2,1,0:T(8,128)(2,1)S(1)} collective-permute-done((bf16[19,128,256]{2,1,0:T(8,128)(2,1)S(1)}, bf16[19,128,256]{2,1,0:T(8,128)(2,1)S(1)}, u32[]{:S(2)}, u32[]{:S(2)}) %collective-permute-start.2) | collective-permute-done | bytes 1245216 | tf_op jit(solution)/shard_map/ppermute | solution.py:93
  249.5 4.9 %all-to-all-start = ((bf16[19,128,256]{2,0,1:T(8,128)(2,1)}), bf16[19,128,256]{2,0,1:T(8,128)(2,1)S(1)}, u32[]{:S(2)}, u32[]{:S(2)}) async-start(bf16[19,128,256]{2,0,1:T(8,128)(2,1)} %copy.25), calls=%async_computation | async-start | bytes 3145728 | tf_op jit(solution)/shard_map/all_to_all | solution.py:98
  254.4 6.1 %fusion.4 = bf16[4,19,128,256]{3,2,1,0:T(8,128)(2,1)S(1)} fusion(bf16[4,19,128,256]{3,2,1,0:T(8,128)(2,1)} %collective-permute-done.4, bf16[2,4,19,128,256]{4,3,2,1,0:T(8,128)(2,1)} %bitcast.100, s32[]{:T(128)S(6)} %select_n.116), kind=kLoop, calls=%fused_computation.11 | loop fusion | flops 9961472 | bytes 14942212 | tf_op jit(solution)/shard_map/convert_element_type | solution.py:77
  264.4 26.8 %collective-permute-done.5 = bf16[19,128,256]{2,1,0:T(8,128)(2,1)S(1)} collective-permute-done((bf16[19,128,256]{2,1,0:T(8,128)(2,1)S(1)}, bf16[19,128,256]{2,1,0:T(8,128)(2,1)S(1)}, u32[]{:S(2)}, u32[]{:S(2)}) %collective-permute-start.5) | collective-permute-done | bytes 1245216 | tf_op jit(solution)/shard_map/ppermute | solution.py:93
  291.2 25.5 %collective-permute-done.6 = bf16[19,128,256]{2,1,0:T(8,128)(2,1)S(1)} collective-permute-done((bf16[19,128,256]{2,1,0:T(8,128)(2,1)S(1)}, bf16[19,128,256]{2,1,0:T(8,128)(2,1)S(1)}, u32[]{:S(2)}, u32[]{:S(2)}) %collective-permute-start.6) | collective-permute-done | bytes 1245216 | tf_op jit(solution)/shard_map/ppermute | solution.py:93
  321.3 5.1 %all-to-all-start.1 = ((bf16[19,128,256]{2,0,1:T(8,128)(2,1)}), bf16[19,128,256]{2,0,1:T(8,128)(2,1)S(1)}, u32[]{:S(2)}, u32[]{:S(2)}) async-start(bf16[19,128,256]{2,0,1:T(8,128)(2,1)} %copy.29), calls=%async_computation.1 | async-start | bytes 3145728 | tf_op jit(solution)/shard_map/all_to_all | solution.py:98
  332.2 26.8 %all-to-all-done.1 = bf16[19,128,256]{2,0,1:T(8,128)(2,1)S(1)} async-done(((bf16[19,128,256]{2,0,1:T(8,128)(2,1)}), bf16[19,128,256]{2,0,1:T(8,128)(2,1)S(1)}, u32[]{:S(2)}, u32[]{:S(2)}) %all-to-all-start.1) | async-done | bytes 1245216 | tf_op jit(solution)/shard_map/all_to_all | solution.py:98
  360.3 4.7 %fusion.17 = f32[608,2048]{1,0:T(8,128)S(1)} fusion(bf16[608,1024]{1,0:T(8,128)(2,1)S(1)} %bitcast.120, bf16[2048,2048]{1,0:T(8,128)(2,1)} %maximum_maximum_fusion), kind=kOutput, calls=%fused_computation.38 | convolution fusion | flops 2550136832 | bytes 10420224 | tf_op jit(solution)/shard_map/dot_general | solution.py:132
  (69 shorter events, 49.7 us)
Async XLA Ops:
  4.4 11.8 %copy-start.2 = (s32[96]{0:T(128)S(1)}, s32[96]{0:T(128)}, u32[]{:S(2)}) copy-start(s32[96]{0:T(128)} %param.11) | copy-start | bytes 1156
  4.4 11.8 %copy-start = (s32[80]{0:T(128)S(1)}, s32[80]{0:T(128)}, u32[]{:S(2)}) copy-start(s32[80]{0:T(128)} %param.12) | copy-start | bytes 964
  4.4 14.7 %copy-start.1 = (s32[12288]{0:T(1024)S(1)}, s32[12288]{0:T(1024)}, u32[]{:S(2)}) copy-start(s32[12288]{0:T(1024)} %param.8) | copy-start | bytes 147460
  72.9 104.8 %collective-permute-start = (bf16[4,19,128,256]{3,2,1,0:T(8,128)(2,1)}, bf16[4,19,128,256]{3,2,1,0:T(8,128)(2,1)}, u32[]{:S(2)}, u32[]{:S(2)}) collective-permute-start(bf16[4,19,128,256]{3,2,1,0:T(8,128)(2,1)} %dynamic-slice_bitcast_fusion.1), channel_id=1, source_target_pairs={{0,4},{4,0},{8,12},{12,8},{16,20},{20,16},{24,28},{28,24},{1,5},{5... | collective-permute-start | bytes 14942216 | tf_op jit(solution)/shard_map/ppermute | solution.py:76
  117.5 60.2 %slice-start = ((s8[9961472]{0:T(1024)(128)(4,1)}), s8[1572864]{0:T(1024)(128)(4,1)S(1)}, s32[]{:S(2)}) async-start(s8[9961472]{0:T(1024)(128)(4,1)} %bitcast.103), calls=%async_computation.2 | async-start | bytes 3145728
  122.8 131.6 %collective-permute-start.4 = (bf16[4,19,128,256]{3,2,1,0:T(8,128)(2,1)}, bf16[4,19,128,256]{3,2,1,0:T(8,128)(2,1)}, u32[]{:S(2)}, u32[]{:S(2)}) collective-permute-start(bf16[4,19,128,256]{3,2,1,0:T(8,128)(2,1)} %dynamic-slice_bitcast_fusion), channel_id=1, source_target_pairs={{0,4},{4,0},{8,12},{12,8},{16,20},{20,16},{24,28},{28,24},{1,5},{5... | collective-permute-start | bytes 14942216 | tf_op jit(solution)/shard_map/ppermute | solution.py:76
  122.9 54.8 %slice-start.1 = ((s8[9961472]{0:T(1024)(128)(4,1)}), s8[4194304]{0:T(1024)(128)(4,1)S(1)}, s32[]{:S(2)}) async-start(s8[9961472]{0:T(1024)(128)(4,1)} %bitcast.103), calls=%async_computation.3 | async-start | bytes 8388608
  140.6 37.1 %slice-start.2 = ((s8[9961472]{0:T(1024)(128)(4,1)}), s8[4194304]{0:T(1024)(128)(4,1)S(1)}, s32[]{:S(2)}) async-start(s8[9961472]{0:T(1024)(128)(4,1)} %bitcast.103), calls=%async_computation.4 | async-start | bytes 8388608
  188.1 31.3 %collective-permute-start.1 = (bf16[19,128,256]{2,1,0:T(8,128)(2,1)S(1)}, bf16[19,128,256]{2,1,0:T(8,128)(2,1)S(1)}, u32[]{:S(2)}, u32[]{:S(2)}) collective-permute-start(bf16[19,128,256]{2,1,0:T(8,128)(2,1)S(1)} %get-tuple-element.12), channel_id=1, source_target_pairs={{0,8},{4,12},{8,0},{12,4},{16,24},{20,28},{24,16},{28,20},{1,9},{5... | collective-permute-start | bytes 3735560 | tf_op jit(solution)/shard_map/ppermute | solution.py:93
  191.1 55.7 %collective-permute-start.2 = (bf16[19,128,256]{2,1,0:T(8,128)(2,1)S(1)}, bf16[19,128,256]{2,1,0:T(8,128)(2,1)S(1)}, u32[]{:S(2)}, u32[]{:S(2)}) collective-permute-start(bf16[19,128,256]{2,1,0:T(8,128)(2,1)S(1)} %get-tuple-element.14), channel_id=1, source_target_pairs={{0,16},{4,20},{8,24},{12,28},{16,0},{20,4},{24,8},{28,12},{1,17},{... | collective-permute-start | bytes 3735560 | tf_op jit(solution)/shard_map/ppermute | solution.py:93
  192.6 54.2 %collective-permute-start.3 = (bf16[19,128,256]{2,1,0:T(8,128)(2,1)S(1)}, bf16[19,128,256]{2,1,0:T(8,128)(2,1)S(1)}, u32[]{:S(2)}, u32[]{:S(2)}) collective-permute-start(bf16[19,128,256]{2,1,0:T(8,128)(2,1)S(1)} %get-tuple-element.13), channel_id=1, source_target_pairs={{0,24},{4,28},{8,16},{12,20},{16,8},{20,12},{24,0},{28,4},{1,25},{... | collective-permute-start | bytes 3735560 | tf_op jit(solution)/shard_map/ppermute | solution.py:93
  249.5 71.7 %all-to-all-start = ((bf16[19,128,256]{2,0,1:T(8,128)(2,1)}), bf16[19,128,256]{2,0,1:T(8,128)(2,1)S(1)}, u32[]{:S(2)}, u32[]{:S(2)}) async-start(bf16[19,128,256]{2,0,1:T(8,128)(2,1)} %copy.25), calls=%async_computation | async-start | bytes 3145728 | tf_op jit(solution)/shard_map/all_to_all | solution.py:98
  260.9 30.3 %collective-permute-start.5 = (bf16[19,128,256]{2,1,0:T(8,128)(2,1)S(1)}, bf16[19,128,256]{2,1,0:T(8,128)(2,1)S(1)}, u32[]{:S(2)}, u32[]{:S(2)}) collective-permute-start(bf16[19,128,256]{2,1,0:T(8,128)(2,1)S(1)} %get-tuple-element.15), channel_id=1, source_target_pairs={{0,8},{4,12},{8,0},{12,4},{16,24},{20,28},{24,16},{28,20},{1,9},{5... | collective-permute-start | bytes 3735560 | tf_op jit(solution)/shard_map/ppermute | solution.py:93
  262.2 54.5 %collective-permute-start.6 = (bf16[19,128,256]{2,1,0:T(8,128)(2,1)S(1)}, bf16[19,128,256]{2,1,0:T(8,128)(2,1)S(1)}, u32[]{:S(2)}, u32[]{:S(2)}) collective-permute-start(bf16[19,128,256]{2,1,0:T(8,128)(2,1)S(1)} %get-tuple-element.17), channel_id=1, source_target_pairs={{0,16},{4,20},{8,24},{12,28},{16,0},{20,4},{24,8},{28,12},{1,17},{... | collective-permute-start | bytes 3735560 | tf_op jit(solution)/shard_map/ppermute | solution.py:93
  263.0 53.7 %collective-permute-start.7 = (bf16[19,128,256]{2,1,0:T(8,128)(2,1)S(1)}, bf16[19,128,256]{2,1,0:T(8,128)(2,1)S(1)}, u32[]{:S(2)}, u32[]{:S(2)}) collective-permute-start(bf16[19,128,256]{2,1,0:T(8,128)(2,1)S(1)} %get-tuple-element.16), channel_id=1, source_target_pairs={{0,24},{4,28},{8,16},{12,20},{16,8},{20,12},{24,0},{28,4},{1,25},{... | collective-permute-start | bytes 3735560 | tf_op jit(solution)/shard_map/ppermute | solution.py:93
  321.3 37.7 %all-to-all-start.1 = ((bf16[19,128,256]{2,0,1:T(8,128)(2,1)}), bf16[19,128,256]{2,0,1:T(8,128)(2,1)S(1)}, u32[]{:S(2)}, u32[]{:S(2)}) async-start(bf16[19,128,256]{2,0,1:T(8,128)(2,1)} %copy.29), calls=%async_computation.1 | async-start | bytes 3145728 | tf_op jit(solution)/shard_map/all_to_all | solution.py:98
  360.0 5.0 %slice-start.5 = ((s8[8388608]{0:T(1024)(128)(4,1)}), s8[4194304]{0:T(1024)(128)(4,1)S(1)}, s32[]{:S(2)}) async-start(s8[8388608]{0:T(1024)(128)(4,1)} %bitcast.113), calls=%async_computation.7 | async-start | bytes 8388608
  360.2 4.7 %slice-start.6 = ((s8[8388608]{0:T(1024)(128)(4,1)}), s8[4194304]{0:T(1024)(128)(4,1)S(1)}, s32[]{:S(2)}) async-start(s8[8388608]{0:T(1024)(128)(4,1)} %bitcast.113), calls=%async_computation.8 | async-start | bytes 8388608
  360.2 7.5 %slice-start.3 = ((s8[4980736]{0:T(1024)(128)(4,1)}), s8[4194304]{0:T(1024)(128)(4,1)S(1)}, s32[]{:S(2)}) async-start(s8[4980736]{0:T(1024)(128)(4,1)} %bitcast.107), calls=%async_computation.5 | async-start | bytes 8388608
  365.0 2.8 slice-start.4
  369.2 4.7 %collective-permute-start.8 = (f32[19,1024]{1,0:T(8,128)S(1)}, f32[19,1024]{1,0:T(8,128)S(1)}, u32[]{:S(2)}, u32[]{:S(2)}) collective-permute-start(f32[19,1024]{1,0:T(8,128)S(1)} %fusion.28), channel_id=1, source_target_pairs={{0,1},{1,0},{2,3},{3,2},{4,5},{5,4},{6,7},{7,6},{8,9},{9,8},{10,11... | collective-permute-start | bytes 233480 | tf_op jit(solution)/shard_map/ppermute | solution.py:56
  373.9 6.2 %collective-permute-start.9 = (f32[19,1024]{1,0:T(8,128)S(1)}, f32[19,1024]{1,0:T(8,128)S(1)}, u32[]{:S(2)}, u32[]{:S(2)}) collective-permute-start(f32[19,1024]{1,0:T(8,128)S(1)} %add.325), channel_id=1, source_target_pairs={{0,2},{1,3},{2,0},{3,1},{4,6},{5,7},{6,4},{7,5},{8,10},{9,11},{10,... | collective-permute-start | bytes 233480 | tf_op jit(solution)/shard_map/ppermute | solution.py:56

commit v16 on v5

--- a/solution.py
+++ b/solution.py
@@ -125,6 +125,7 @@
     first = _gather_pair(blocks[:, :, 0, :], matrix, pick2, parity, chip, n_owners, slots_dev)
     second = _gather_pair(blocks[:, :, 1, :], matrix, pick2, parity, chip, n_owners, slots_dev)
     table, second = lax.optimization_barrier((table, second))
+    galaxy = lax.optimization_barrier((galaxy, first[1]))[0]
     out = None
     for k, (pair_send, own) in enumerate((first, second)):
         piece = _scatter_pairs(pair_send, own, chip, n_owners)

time: 329 us -> 329 us (level)
  no operation moved by 1% of the time
where the time goes in v16:
time: 329 us; the launch traced here: 323 us
  waiting for transfers between devices  98 us (30%)
  other arithmetic  87.5 us (27%)
  matrix products  60.4 us (18%)
  local copies, waits for them, and re-layouts  56.7 us (17%)
  starting transfers between devices  19.2 us (6%)
    ppermute x6, waiting for transfers between devices, _scatter_pairs(): lax.ppermute(send, 'uv', _partner_pairs(n_owners, lambda i, dest=dest: de...  62.8 us
    dot_general x2, matrix products, _gather_pair(): jnp.einsum('sb,bcf->scf', pick2, jnp.concatenate([high, low], axis=0), pr...  34.1 us
    all_to_all x2, waiting for transfers between devices, _scatter_pairs(): lax.all_to_all(gridded, 'chan', split_axis=1, concat_axis=2, tiled=True)  26.8 us
    convert_element_type x2, local copies, waits for them, and re-layouts, _gather_pair(): partial = jnp.einsum('sb,bcf->scf', pick2, jnp.concatenate([high, low], a...  20 us
    dot_general x2, matrix products, _gather_pair(): jnp.einsum('bcr,brf->bcf', matrix, part, preferred_element_type=jnp.float32)  18.7 us
    another operation x1, other arithmetic  18.5 us
    concatenate x1, other arithmetic, delay_table(): return jnp.concatenate([upper, lower], axis=0).astype(jnp.bfloat16)  17.1 us
    concatenate x2, other arithmetic, _gather_pair(): jnp.concatenate([high, low], axis=0)  14.9 us
  transfers between devices with their start and end apart: 12, of which 6 were waited for; matrix products, arithmetic and copies ran while one was open for 36% of the time, Pallas kernels for 0%

profile of v16, /device:TPU:0, one launch (start us, length us, event | category | flops | bytes accessed | tf_op | source)
XLA Modules:
  0.0 322.9 jit_solution(1897229221736697006)
XLA Ops:
  4.4 11.7 %copy.22 = bf16[12288,2,256]{2,0,1:T(8,128)(2,1)} copy(bf16[12288,2,256]{2,1,0:T(2,128)(2,1)} %param.7) | data formatting | bytes 25165824 | tf_op args[0]
  19.1 5.2 %add_bitcast_fusion.10 = (s32[96,128]{1,0:T(8,128)S(1)}, s32[96,128]{1,0:T(8,128)S(1)}, s32[96,128]{1,0:T(8,128)S(1)}, s32[96,128]{1,0:T(8,128)S(1)}, s32[96,128...) fusion(s32[12288]{0:T(1024)S(1)} %copy-done.1, s32[]{:T(128)} %bitcast.1, ...), kind=kLoop, calls=%fused_computation.82 | loop fusion | flops 98304 | bytes 442400 | tf_op jit(solution)/shard_map/add | solution.py:24
  24.3 9.4 %subtract_convert_fusion.1 = (bf16[96,128,256]{2,1,0:T(8,128)(2,1)S(1)}, bf16[96,128,256]{2,1,0:T(8,128)(2,1)S(1)}) fusion(bf16[96,128,2,256]{3,1,0,2:T(8,128)(2,1)} %bitcast.111, f32[96,128]{1,0:T(8,128)S(1)} %bitcast.124, s32[96,128]{1,0:T(8,128)S(1)} %get-tuple-element.36, f32[96,128]{1,0:T(8,128)S(1)} %bitcast.126, s32[96,128]{1,0:T(8,128)S(1)} %get-tuple-element.37, ...), kind=kOutput, calls=%fused_computation.9 | convolution fusion | flops 855638016 | bytes 19660800 | tf_op jit(solution)/shard_map/bcr,brf->bcf/dot_general | solution.py:63
  33.7 7.3 %pad_maximum_fusion = bf16[192,128,256]{2,1,0:T(8,128)(2,1)} fusion(bf16[96,128,256]{2,1,0:T(8,128)(2,1)S(1)} %get-tuple-element.12, bf16[96,128,256]{2,1,0:T(8,128)(2,1)S(1)} %get-tuple-element.13), kind=kLoop, calls=%fused_computation.2 | loop fusion | flops 6291456 | bytes 25165824 | tf_op jit(solution)/shard_map/concatenate | solution.py:69
  41.0 17.1 %fusion.6 = bf16[152,128,256]{2,0,1:T(8,128)(2,1)} fusion(bf16[192,128,256]{2,1,0:T(8,128)(2,1)} %pad_maximum_fusion, pred[152,96]{1,0:T(8,128)(4,1)S(1)} %iota_compare_fusion.8), kind=kOutput, calls=%fused_computation.15 | convolution fusion | flops 1917612544 | bytes 22558976 | tf_op jit(solution)/shard_map/sb,bcf->scf/dot_general | solution.py:66
  58.1 10.1 %copy.24 = bf16[152,128,256]{2,1,0:T(8,128)(2,1)} copy(bf16[152,128,256]{2,0,1:T(8,128)(2,1)} %fusion.6) | data formatting | bytes 19922944 | tf_op jit(solution)/shard_map/convert_element_type | solution.py:71
  68.1 5.2 %dynamic-slice_bitcast_fusion.1 = bf16[4,19,128,256]{3,2,1,0:T(8,128)(2,1)} fusion(bf16[2,4,19,128,256]{4,3,2,1,0:T(8,128)(2,1)} %bitcast.101, s32[]{:T(128)S(6)} %select_n.120), kind=kLoop, calls=%fused_computation.34 | loop fusion | bytes 9961476 | tf_op jit(solution)/shard_map/jit(dynamic_index_in_dim)/squeeze | solution.py:75
  73.8 9.4 %subtract_convert_fusion = (bf16[96,128,256]{2,1,0:T(8,128)(2,1)S(1)}, bf16[96,128,256]{2,1,0:T(8,128)(2,1)S(1)}) fusion(bf16[96,128,2,256]{3,1,0,2:T(8,128)(2,1)} %bitcast.112, f32[96,128]{1,0:T(8,128)S(1)} %bitcast.125, s32[96,128]{1,0:T(8,128)S(1)} %get-tuple-element.36, f32[96,128]{1,0:T(8,128)S(1)} %bitcast.127, s32[96,128]{1,0:T(8,128)S(1)} %get-tuple-element.37, ...), kind=kOutput, calls=%fused_computation.8 | convolution fusion | flops 855638016 | bytes 19660800 | tf_op jit(solution)/shard_map/bcr,brf->bcf/dot_general | solution.py:63
  83.2 7.6 %pad_maximum_fusion.1 = bf16[192,128,256]{2,1,0:T(8,128)(2,1)} fusion(bf16[96,128,256]{2,1,0:T(8,128)(2,1)S(1)} %get-tuple-element.14, bf16[96,128,256]{2,1,0:T(8,128)(2,1)S(1)} %get-tuple-element.15), kind=kLoop, calls=%fused_computation.3 | loop fusion | flops 6291456 | bytes 25165824 | tf_op jit(solution)/shard_map/concatenate | solution.py:69
  90.8 17.0 %fusion.9 = bf16[152,128,256]{2,0,1:T(8,128)(2,1)} fusion(bf16[192,128,256]{2,1,0:T(8,128)(2,1)} %pad_maximum_fusion.1, pred[152,96]{1,0:T(8,128)(4,1)S(1)} %iota_compare_fusion.8), kind=kOutput, calls=%fused_computation.16 | convolution fusion | flops 1917612544 | bytes 22558976 | tf_op jit(solution)/shard_map/sb,bcf->scf/dot_general | solution.py:66
  107.8 9.9 %copy.28 = bf16[152,128,256]{2,1,0:T(8,128)(2,1)} copy(bf16[152,128,256]{2,0,1:T(8,128)(2,1)} %fusion.9) | data formatting | bytes 19922944 | tf_op jit(solution)/shard_map/convert_element_type | solution.py:71
  117.8 5.2 %dynamic-slice_bitcast_fusion = bf16[4,19,128,256]{3,2,1,0:T(8,128)(2,1)} fusion(bf16[2,4,19,128,256]{4,3,2,1,0:T(8,128)(2,1)} %bitcast.104, s32[]{:T(128)S(6)} %select_n.120), kind=kLoop, calls=%fused_computation.33 | loop fusion | bytes 9961476 | tf_op jit(solution)/shard_map/jit(dynamic_index_in_dim)/squeeze | solution.py:75
  123.1 6.2 %fusion.5 = bf16[4,19,128,256]{3,2,1,0:T(8,128)(2,1)S(1)} fusion(bf16[4,19,128,256]{3,2,1,0:T(8,128)(2,1)} %collective-permute-done, bf16[2,4,19,128,256]{4,3,2,1,0:T(8,128)(2,1)} %bitcast.102, s32[]{:T(128)S(6)} %select_n.115), kind=kLoop, calls=%fused_computation.13 | loop fusion | flops 9961472 | bytes 14942212 | tf_op jit(solution)/shard_map/convert_element_type | solution.py:77
  135.8 18.5 %multiply_convert_fusion.1 = (bf16[1024,1024]{1,0:T(8,128)(2,1)S(1)}, bf16[1024,1024]{1,0:T(8,128)(2,1)}, bf16[1024,1024]{1,0:T(8,128)(2,1)}) fusion(f32[1024]{0:T(1024)S(1)} %subtract_multiply_fusion), kind=kLoop, calls=%fused_computation.43 | loop fusion | flops 22020096 | bytes 6295552 | tf_op jit(solution)/shard_map/convert.20
  154.3 17.1 %maximum_maximum_fusion = bf16[2048,2048]{1,0:T(8,128)(2,1)} fusion(bf16[1024,1024]{1,0:T(8,128)(2,1)} %get-tuple-element.40, bf16[1024,1024]{1,0:T(8,128)(2,1)} %get-tuple-element.39, bf16[1024,1024]{1,0:T(8,128)(2,1)S(1)} %get-tuple-element.38), kind=kLoop, calls=%fused_computation.14 | loop fusion | flops 33554432 | bytes 14680064 | tf_op jit(solution)/shard_map/concatenate | solution.py:44
  171.4 8.4 %fusion.4 = bf16[4,19,128,256]{3,2,1,0:T(8,128)(2,1)} fusion(bf16[4,19,128,256]{3,2,1,0:T(8,128)(2,1)} %collective-permute-done.4, bf16[2,4,19,128,256]{4,3,2,1,0:T(8,128)(2,1)} %bitcast.105, s32[]{:T(128)S(6)} %select_n.115), kind=kLoop, calls=%fused_computation.11 | loop fusion | flops 9961472 | bytes 14942212 | tf_op jit(solution)/shard_map/convert_element_type | solution.py:77
  179.7 10.5 %collective-permute-done.2 = bf16[19,128,256]{2,1,0:T(8,128)(2,1)} collective-permute-done((bf16[19,128,256]{2,1,0:T(8,128)(2,1)}, bf16[19,128,256]{2,1,0:T(8,128)(2,1)}, u32[]{:S(2)}, u32[]{:S(2)}) %collective-permute-start.2) | collective-permute-done | bytes 1245216 | tf_op jit(solution)/shard_map/ppermute | solution.py:93
  195.6 5.1 %all-to-all-start = ((bf16[19,128,256]{2,0,1:T(8,128)(2,1)}), bf16[19,128,256]{2,0,1:T(8,128)(2,1)S(1)}, u32[]{:S(2)}, u32[]{:S(2)}) async-start(bf16[19,128,256]{2,0,1:T(8,128)(2,1)} %copy.25), calls=%async_computation | async-start | bytes 3145728 | tf_op jit(solution)/shard_map/all_to_all | solution.py:98
  208.5 26.8 %collective-permute-done.5 = bf16[19,128,256]{2,1,0:T(8,128)(2,1)S(1)} collective-permute-done((bf16[19,128,256]{2,1,0:T(8,128)(2,1)S(1)}, bf16[19,128,256]{2,1,0:T(8,128)(2,1)S(1)}, u32[]{:S(2)}, u32[]{:S(2)}) %collective-permute-start.5) | collective-permute-done | bytes 1245216 | tf_op jit(solution)/shard_map/ppermute | solution.py:93
  235.3 25.5 %collective-permute-done.6 = bf16[19,128,256]{2,1,0:T(8,128)(2,1)S(1)} collective-permute-done((bf16[19,128,256]{2,1,0:T(8,128)(2,1)S(1)}, bf16[19,128,256]{2,1,0:T(8,128)(2,1)S(1)}, u32[]{:S(2)}, u32[]{:S(2)}) %collective-permute-start.6) | collective-permute-done | bytes 1245216 | tf_op jit(solution)/shard_map/ppermute | solution.py:93
  263.4 4.8 %all-to-all-start.1 = ((bf16[19,128,256]{2,0,1:T(8,128)(2,1)}), bf16[19,128,256]{2,0,1:T(8,128)(2,1)S(1)}, u32[]{:S(2)}, u32[]{:S(2)}) async-start(bf16[19,128,256]{2,0,1:T(8,128)(2,1)} %copy.29), calls=%async_computation.1 | async-start | bytes 3145728 | tf_op jit(solution)/shard_map/all_to_all | solution.py:98
  274.1 26.8 %all-to-all-done.1 = bf16[19,128,256]{2,0,1:T(8,128)(2,1)S(1)} async-done(((bf16[19,128,256]{2,0,1:T(8,128)(2,1)}), bf16[19,128,256]{2,0,1:T(8,128)(2,1)S(1)}, u32[]{:S(2)}, u32[]{:S(2)}) %all-to-all-start.1) | async-done | bytes 1245216 | tf_op jit(solution)/shard_map/all_to_all | solution.py:98
  302.2 4.7 %fusion.17 = f32[608,2048]{1,0:T(8,128)S(1)} fusion(bf16[608,1024]{1,0:T(8,128)(2,1)S(1)} %bitcast.120, bf16[2048,2048]{1,0:T(8,128)(2,1)} %maximum_maximum_fusion), kind=kOutput, calls=%fused_computation.38 | convolution fusion | flops 2550136832 | bytes 10420224 | tf_op jit(solution)/shard_map/dot_general | solution.py:133
  311.2 4.6 %collective-permute-done.8 = f32[19,1024]{1,0:T(8,128)S(1)} collective-permute-done((f32[19,1024]{1,0:T(8,128)S(1)}, f32[19,1024]{1,0:T(8,128)S(1)}, u32[]{:S(2)}, u32[]{:S(2)}) %collective-permute-start.8) | collective-permute-done | bytes 77856 | tf_op jit(solution)/shard_map/ppermute | solution.py:56
  (62 shorter events, 47.6 us)
Async XLA Ops:
  4.4 11.7 %copy-start.2 = (s32[96]{0:T(128)S(1)}, s32[96]{0:T(128)}, u32[]{:S(2)}) copy-start(s32[96]{0:T(128)} %param.11) | copy-start | bytes 1156
  4.4 11.7 %copy-start = (s32[80]{0:T(128)S(1)}, s32[80]{0:T(128)}, u32[]{:S(2)}) copy-start(s32[80]{0:T(128)} %param.12) | copy-start | bytes 964
  4.4 14.6 %copy-start.1 = (s32[12288]{0:T(1024)S(1)}, s32[12288]{0:T(1024)}, u32[]{:S(2)}) copy-start(s32[12288]{0:T(1024)} %param.8) | copy-start | bytes 147460
  73.3 49.7 %collective-permute-start = (bf16[4,19,128,256]{3,2,1,0:T(8,128)(2,1)}, bf16[4,19,128,256]{3,2,1,0:T(8,128)(2,1)}, u32[]{:S(2)}, u32[]{:S(2)}) collective-permute-start(bf16[4,19,128,256]{3,2,1,0:T(8,128)(2,1)} %dynamic-slice_bitcast_fusion.1), channel_id=1, source_target_pairs={{0,4},{4,0},{8,12},{12,8},{16,20},{20,16},{24,28},{28,24},{1,5},{5... | collective-permute-start | bytes 14942216 | tf_op jit(solution)/shard_map/ppermute | solution.py:76
  123.0 48.4 %collective-permute-start.4 = (bf16[4,19,128,256]{3,2,1,0:T(8,128)(2,1)}, bf16[4,19,128,256]{3,2,1,0:T(8,128)(2,1)}, u32[]{:S(2)}, u32[]{:S(2)}) collective-permute-start(bf16[4,19,128,256]{3,2,1,0:T(8,128)(2,1)} %dynamic-slice_bitcast_fusion), channel_id=1, source_target_pairs={{0,4},{4,0},{8,12},{12,8},{16,20},{20,16},{24,28},{28,24},{1,5},{5... | collective-permute-start | bytes 14942216 | tf_op jit(solution)/shard_map/ppermute | solution.py:76
  131.3 48.4 %collective-permute-start.1 = (bf16[19,128,256]{2,1,0:T(8,128)(2,1)}, bf16[19,128,256]{2,1,0:T(8,128)(2,1)S(1)}, u32[]{:S(2)}, u32[]{:S(2)}) collective-permute-start(bf16[19,128,256]{2,1,0:T(8,128)(2,1)} %get-tuple-element.16), channel_id=1, source_target_pairs={{0,8},{4,12},{8,0},{12,4},{16,24},{20,28},{24,16},{28,20},{1,9},{5... | collective-permute-start | bytes 3735560 | tf_op jit(solution)/shard_map/ppermute | solution.py:93
  134.2 56.0 %collective-permute-start.2 = (bf16[19,128,256]{2,1,0:T(8,128)(2,1)}, bf16[19,128,256]{2,1,0:T(8,128)(2,1)}, u32[]{:S(2)}, u32[]{:S(2)}) collective-permute-start(bf16[19,128,256]{2,1,0:T(8,128)(2,1)} %get-tuple-element.18), channel_id=1, source_target_pairs={{0,16},{4,20},{8,24},{12,28},{16,0},{20,4},{24,8},{28,12},{1,17},{... | collective-permute-start | bytes 3735560 | tf_op jit(solution)/shard_map/ppermute | solution.py:93
  135.8 54.5 %collective-permute-start.3 = (bf16[19,128,256]{2,1,0:T(8,128)(2,1)}, bf16[19,128,256]{2,1,0:T(8,128)(2,1)}, u32[]{:S(2)}, u32[]{:S(2)}) collective-permute-start(bf16[19,128,256]{2,1,0:T(8,128)(2,1)} %get-tuple-element.17), channel_id=1, source_target_pairs={{0,24},{4,28},{8,16},{12,20},{16,8},{20,12},{24,0},{28,4},{1,25},{... | collective-permute-start | bytes 3735560 | tf_op jit(solution)/shard_map/ppermute | solution.py:93
  195.6 67.9 %all-to-all-start = ((bf16[19,128,256]{2,0,1:T(8,128)(2,1)}), bf16[19,128,256]{2,0,1:T(8,128)(2,1)S(1)}, u32[]{:S(2)}, u32[]{:S(2)}) async-start(bf16[19,128,256]{2,0,1:T(8,128)(2,1)} %copy.25), calls=%async_computation | async-start | bytes 3145728 | tf_op jit(solution)/shard_map/all_to_all | solution.py:98
  205.0 30.3 %collective-permute-start.5 = (bf16[19,128,256]{2,1,0:T(8,128)(2,1)S(1)}, bf16[19,128,256]{2,1,0:T(8,128)(2,1)S(1)}, u32[]{:S(2)}, u32[]{:S(2)}) collective-permute-start(bf16[19,128,256]{2,1,0:T(8,128)(2,1)S(1)} %get-tuple-element.19), channel_id=1, source_target_pairs={{0,8},{4,12},{8,0},{12,4},{16,24},{20,28},{24,16},{28,20},{1,9},{5... | collective-permute-start | bytes 3735560 | tf_op jit(solution)/shard_map/ppermute | solution.py:93
  206.2 54.5 %collective-permute-start.6 = (bf16[19,128,256]{2,1,0:T(8,128)(2,1)S(1)}, bf16[19,128,256]{2,1,0:T(8,128)(2,1)S(1)}, u32[]{:S(2)}, u32[]{:S(2)}) collective-permute-start(bf16[19,128,256]{2,1,0:T(8,128)(2,1)S(1)} %get-tuple-element.21), channel_id=1, source_target_pairs={{0,16},{4,20},{8,24},{12,28},{16,0},{20,4},{24,8},{28,12},{1,17},{... | collective-permute-start | bytes 3735560 | tf_op jit(solution)/shard_map/ppermute | solution.py:93
  207.1 53.7 %collective-permute-start.7 = (bf16[19,128,256]{2,1,0:T(8,128)(2,1)S(1)}, bf16[19,128,256]{2,1,0:T(8,128)(2,1)S(1)}, u32[]{:S(2)}, u32[]{:S(2)}) collective-permute-start(bf16[19,128,256]{2,1,0:T(8,128)(2,1)S(1)} %get-tuple-element.20), channel_id=1, source_target_pairs={{0,24},{4,28},{8,16},{12,20},{16,8},{20,12},{24,0},{28,4},{1,25},{... | collective-permute-start | bytes 3735560 | tf_op jit(solution)/shard_map/ppermute | solution.py:93
  263.4 37.5 %all-to-all-start.1 = ((bf16[19,128,256]{2,0,1:T(8,128)(2,1)}), bf16[19,128,256]{2,0,1:T(8,128)(2,1)S(1)}, u32[]{:S(2)}, u32[]{:S(2)}) async-start(bf16[19,128,256]{2,0,1:T(8,128)(2,1)} %copy.29), calls=%async_computation.1 | async-start | bytes 3145728 | tf_op jit(solution)/shard_map/all_to_all | solution.py:98
  301.9 5.0 %slice-start.2 = ((s8[8388608]{0:T(1024)(128)(4,1)}), s8[4194304]{0:T(1024)(128)(4,1)S(1)}, s32[]{:S(2)}) async-start(s8[8388608]{0:T(1024)(128)(4,1)} %bitcast.113), calls=%async_computation.4 | async-start | bytes 8388608
  302.2 4.7 %slice-start.3 = ((s8[8388608]{0:T(1024)(128)(4,1)}), s8[4194304]{0:T(1024)(128)(4,1)S(1)}, s32[]{:S(2)}) async-start(s8[8388608]{0:T(1024)(128)(4,1)} %bitcast.113), calls=%async_computation.5 | async-start | bytes 8388608
  302.2 7.5 %slice-start = ((s8[4980736]{0:T(1024)(128)(4,1)}), s8[4194304]{0:T(1024)(128)(4,1)S(1)}, s32[]{:S(2)}) async-start(s8[4980736]{0:T(1024)(128)(4,1)} %bitcast.107), calls=%async_computation.2 | async-start | bytes 8388608
  306.9 2.8 slice-start.1
  311.1 4.7 %collective-permute-start.8 = (f32[19,1024]{1,0:T(8,128)S(1)}, f32[19,1024]{1,0:T(8,128)S(1)}, u32[]{:S(2)}, u32[]{:S(2)}) collective-permute-start(f32[19,1024]{1,0:T(8,128)S(1)} %fusion.28), channel_id=1, source_target_pairs={{0,1},{1,0},{2,3},{3,2},{4,5},{5,4},{6,7},{7,6},{8,9},{9,8},{10,11... | collective-permute-start | bytes 233480 | tf_op jit(solution)/shard_map/ppermute | solution.py:56
  315.8 6.2 %collective-permute-start.9 = (f32[19,1024]{1,0:T(8,128)S(1)}, f32[19,1024]{1,0:T(8,128)S(1)}, u32[]{:S(2)}, u32[]{:S(2)}) collective-permute-start(f32[19,1024]{1,0:T(8,128)S(1)} %add.325), channel_id=1, source_target_pairs={{0,2},{1,3},{2,0},{3,1},{4,6},{5,7},{6,4},{7,5},{8,10},{9,11},{10,... | collective-permute-start | bytes 233480 | tf_op jit(solution)/shard_map/ppermute | solution.py:56
